TPU v7x, 512 devices: a whole 4x4x16 slice. The times are simulated.
512 devices in a mesh: tm: 16 (over z_hi, y), space: 32 (over z_lo, x, core).
Axes of the slice: x: 4, y: 4, z: 16 (z_hi: 4, z_lo: 4; z = z_hi * 4 + z_lo), core: 2. Of those that a mesh axis runs over, the one named last changes fastest.
Arguments:
- queries: bfloat16 [128, 2048, 256], P('tm', 'space'), as said below
- keys: bfloat16 [128, 2048, 256], P('tm', 'space'), as said below
- label_values: bfloat16 [128, 2048, 64], P('tm', 'space'), may hold values from -6 to 6
- class_ids: int32 [128, 2048], P(None, 'space'), may hold values from 0 to 63
- valid_pixels: int32 [128], replicated, may hold values from 1024 to 2048
- keyframe_index: int32 [2, 2], replicated, may hold values from 0 to 127, as said below
Outputs:
- readout: bfloat16 [128, 2048, 64], P('tm', 'space')
- confidence: float32 [2, 2, 2048], P(None, None, 'space')
Inputs may be any that keep to these rules, and one draw needn't show every extreme that they name: `queries`: queries and keys are real-valued embeddings. `keys`: Real-valued embeddings. `keyframe_index`: all 4 entries are different frames.
All inputs are finite; a program needn't handle non-finite values.
Results may differ from a plain program's by a relative error of at most 0.0053.
Values may be sent and summed in bfloat16 or wider, within the bound.
No kernel may reach another device: no remote copies, remote signals or barrier semaphores. Data moves between devices by JAX's collectives and lax.ppermute only.
A program may use at most 192 MiB of HBM per device.

v0:
```python
import math

import jax
import jax.numpy as jnp
from jax import lax
from jax.sharding import PartitionSpec as P


def from_root(value, axis, root):
    mine = lax.axis_index(axis) == root
    return lax.psum(jnp.where(mine, value, jnp.zeros_like(value)), axis)


def body(queries, keys, label_values, class_ids, valid_pixels, keyframe_index):
    fr_dev, pix_dev, width = queries.shape
    channels = label_values.shape[2]
    total_steps, keyframes = keyframe_index.shape
    pix_all = pix_dev * lax.axis_size("space")
    mem_width = keyframes * pix_all
    time_pos = lax.axis_index("tm")
    space_pos = lax.axis_index("space")
    rows = fr_dev * pix_dev
    block_rows = 512
    blocks = rows // block_rows
    frame_valid = lax.dynamic_slice_in_dim(valid_pixels, time_pos * fr_dev, fr_dev)
    pixel_ids = space_pos * pix_dev + jnp.arange(pix_dev, dtype=jnp.int32)
    row_valid = (pixel_ids[None, :] < frame_valid[:, None]).reshape(blocks, block_rows)
    query_blocks = queries.reshape(blocks, block_rows, width)
    scale = 3.0 / math.sqrt(width)
    class_range = jnp.arange(channels, dtype=jnp.int32)
    current = label_values
    confidences = []
    readout = label_values
    for step in range(total_steps):
        chosen = keyframe_index[step]
        owners = chosen // fr_dev
        slots = chosen % fr_dev
        local_keys = jnp.take(keys, slots, axis=0)
        local_values = jnp.take(current, slots, axis=0)
        joined = jnp.concatenate([local_keys, local_values], axis=2)
        fetched = []
        for number in range(keyframes):
            fetched.append(from_root(joined[number], "tm", owners[number]))
        fetched = jnp.stack(fetched)
        part_keys = fetched[:, :, :width]
        part_values = fetched[:, :, width:]
        part_ids = jnp.take(class_ids, chosen, axis=0).astype(jnp.bfloat16)
        mem_keys, mem_values, mem_ids = (
            lax.all_gather(part_keys, "space", axis=1, tiled=True),
            lax.all_gather(part_values, "space", axis=1, tiled=True),
            lax.all_gather(part_ids, "space", axis=1, tiled=True),
        )
        mem_keys = mem_keys.reshape(mem_width, width)
        mem_values = mem_values.reshape(mem_width, channels)
        mem_ids = mem_ids.reshape(mem_width).astype(jnp.int32)
        key_valid = (
            jnp.arange(pix_all, dtype=jnp.int32)[None, :] < jnp.take(valid_pixels, chosen)[:, None]
        ).reshape(mem_width)
        class_match = mem_ids[None, :] == class_range[:, None]
        onehot_t = class_match.astype(jnp.bfloat16)

        def score_block(query_rows):
            raw = lax.dot_general(
                query_rows, mem_keys, (((1,), (1,)), ((), ())), preferred_element_type=jnp.float32
            )
            return raw * scale

        def forward(scores, valid_rows):
            masked = jnp.where(key_valid[None, :], scores, -1e30)
            row_max = jnp.max(masked, axis=1, keepdims=True)
            weights = jnp.where(key_valid[None, :], jnp.exp(scores - row_max), 0.0)
            total = jnp.sum(weights, axis=1, keepdims=True)
            mixed = (
                jnp.dot(
                    weights.astype(jnp.bfloat16), mem_values, preferred_element_type=jnp.float32
                )
                / total
            )
            return jnp.where(valid_rows[:, None], mixed, 0.0).astype(jnp.bfloat16)

        lowest = jnp.full((mem_width,), -1e30, jnp.float32)
        zeros_col = jnp.zeros((mem_width,), jnp.float32)

        def first_pass(col_max, inputs):
            query_rows, valid_rows = inputs
            scores = score_block(query_rows)
            block_out = forward(scores, valid_rows)
            local_max = jnp.max(jnp.where(valid_rows[:, None], scores, -1e30), axis=0)
            return (jnp.maximum(col_max, local_max), block_out)

        col_max, out_blocks = lax.scan(first_pass, lowest, (query_blocks, row_valid))
        col_max = lax.pmax(col_max, ("tm", "space"))

        def second_pass(carry, inputs):
            query_rows, valid_rows, block_out = inputs
            scores = score_block(query_rows)
            expo = jnp.where(valid_rows[:, None], jnp.exp(scores - col_max[None, :]), 0.0)
            picked = jnp.dot(block_out, onehot_t, preferred_element_type=jnp.float32)
            return (
                (carry[0] + jnp.sum(expo, axis=0), carry[1] + jnp.sum(expo * picked, axis=0)),
                None,
            )

        (col_total, col_num), unused = lax.scan(
            second_pass, (zeros_col, zeros_col), (query_blocks, row_valid, out_blocks)
        )
        col_total, col_num = lax.psum((col_total, col_num), ("tm", "space"))
        readout = out_blocks.reshape(fr_dev, pix_dev, channels)
        hits = (class_match & key_valid[None, :]).astype(jnp.int32)
        counts = jnp.sum(hits, axis=1)
        all_count = jnp.sum(counts)
        own = jnp.sum(jnp.where(class_match, counts[:, None], 0), axis=0)
        own_safe = jnp.where(key_valid, own, 1)
        factor = jnp.sqrt(all_count.astype(jnp.float32) / (channels * own_safe.astype(jnp.float32)))
        conf_full = jnp.where(key_valid, col_num / col_total * factor, 0.0).reshape(
            keyframes, pix_all
        )
        confidences.append(lax.dynamic_slice_in_dim(conf_full, space_pos * pix_dev, pix_dev, 1))
        current = readout
    return (readout, jnp.stack(confidences))


def solution(mesh):
    placed = (
        P("tm", "space", None),
        P("tm", "space", None),
        P("tm", "space", None),
        P(None, "space"),
        P(),
        P(),
    )
    return jax.shard_map(
        body,
        mesh=mesh,
        in_specs=placed,
        out_specs=(P("tm", "space", None), P(None, None, "space")),
        check_vma=False,
    )
```

profile of v0, /device:TPU:1, one launch (start us, length us, event | category | flops | bytes accessed | tf_op | source)
XLA Modules:
  0.0 1291.4 jit_solution(1095203512651782425)
XLA Ops:
  8.0 1.5 gather_fusion.3
  9.5 1.5 gather_fusion.4
  13.9 188.7 %all-reduce.11.cloned.1.call-done = (bf16[1,64,320]{2,1,0:T(8,128)(2,1)}, bf16[1,64,320]{2,1,0:T(8,128)(2,1)}) async-done(((bf16[1,64,320]{2,1,0:T(8,128)(2,1)}, bf16[1,64,320]{2,1,0:T(8,128)(2,1)}), (bf16[1,64,320]{2,1,0:T(8,128)(2,1)}, bf16[1,64,320]{2,1,0:T(8,128)(2,1)})) %all-reduce.11.cloned.1.call-update) | async-done | bytes 81936 | tf_op jit(solution)/shard_map/psum | solution.py:11
  206.6 1.3 gather_fusion.2
  207.9 1.3 gather_fusion
  209.4 1.5 gather_fusion.1
  212.3 56.8 %all_gather.19 = bf16[2,2048,64]{2,1,0:T(8,128)(2,1)S(1)} all-gather(bf16[2,64,64]{2,1,0:T(8,128)(2,1)S(1)} %slice.75), channel_id=1, replica_groups=mesh['tm'=16,'space'=32] {'space'}, dimensions={1}, use_global_device_ids=true | all-gather | bytes 540672 | tf_op jit(solution)/shard_map/all_gather | solution.py:50
  269.1 13.7 %all-gather.5.cloned.1.call-done = bf16[2,2048,256]{2,1,0:T(8,128)(2,1)} async-done(((bf16[2,64,256]{2,1,0:T(8,128)(2,1)}), bf16[2,2048,256]{2,1,0:T(8,128)(2,1)}) %all-gather.5.cloned.1.call-update) | async-done | bytes 2097168 | tf_op jit(solution)/shard_map/all_gather | solution.py:49
  282.8 6.0 select_reduce_fusion.1
  288.9 104.7 %pmax.14 = f32[4096]{0:T(1024)S(1)} all-reduce(f32[4096]{0:T(1024)S(1)} %broadcast_maximum_fusion.1), channel_id=1, replica_groups=mesh['tm'=16,'space'=32] {'tm','space'}, use_global_device_ids=true, to_apply=%region_9.13 | all-reduce | flops 4096 | bytes 32768 | tf_op jit(solution)/shard_map/pmax | solution.py:92
  393.5 7.0 fusion.6
  400.6 1.5 fusion.20
  403.6 176.6 %all-reduce.9.cloned.1.call-done = (bf16[1,64,320]{2,1,0:T(8,128)(2,1)}, bf16[1,64,320]{2,1,0:T(8,128)(2,1)}) async-done(((bf16[1,64,320]{2,1,0:T(8,128)(2,1)}, bf16[1,64,320]{2,1,0:T(8,128)(2,1)}), (bf16[1,64,320]{2,1,0:T(8,128)(2,1)}, bf16[1,64,320]{2,1,0:T(8,128)(2,1)})) %all-reduce.9.cloned.1.call-update) | async-done | bytes 81936 | tf_op jit(solution)/shard_map/psum | solution.py:11
  583.8 53.1 %all-gather = bf16[32,64,2]{1,2,0:T(2,128)(2,1)S(1)} all-gather(bf16[1,64,2]{1,2,0:T(2,128)(2,1)S(1)} %fusion.42), channel_id=1, replica_groups=mesh['tm'=16,'space'=32] {'space'}, dimensions={0}, use_global_device_ids=true | all-gather | bytes 8448 | tf_op jit(solution)/shard_map/all_gather | solution.py:51
  637.2 37.6 %all-gather.1 = bf16[32,64,2]{1,2,0:T(2,128)(2,1)S(1)} all-gather(bf16[1,64,2]{1,2,0:T(2,128)(2,1)S(1)} %fusion.43), channel_id=1, replica_groups=mesh['tm'=16,'space'=32] {'space'}, dimensions={0}, use_global_device_ids=true | all-gather | bytes 8448 | tf_op jit(solution)/shard_map/all_gather | solution.py:51
  674.9 1.1 convert_reduce_fusion.3
  677.2 5.3 fusion.1
  682.5 42.2 %all_gather.21 = bf16[2,2048,64]{2,1,0:T(8,128)(2,1)S(1)} all-gather(bf16[2,64,64]{2,1,0:T(8,128)(2,1)S(1)} %slice.79), channel_id=1, replica_groups=mesh['tm'=16,'space'=32] {'space'}, dimensions={1}, use_global_device_ids=true | all-gather | bytes 540672 | tf_op jit(solution)/shard_map/all_gather | solution.py:50
  724.7 6.0 select_reduce_fusion
  730.7 101.4 %pmax.15 = f32[4096]{0:T(1024)S(1)} all-reduce(f32[4096]{0:T(1024)S(1)} %broadcast_maximum_fusion), channel_id=1, replica_groups=mesh['tm'=16,'space'=32] {'tm','space'}, use_global_device_ids=true, to_apply=%region_18.23 | all-reduce | flops 4096 | bytes 32768 | tf_op jit(solution)/shard_map/pmax | solution.py:92
  832.1 7.0 fusion.7
  839.1 1.5 fusion.29
  840.6 3.2 fusion
  846.2 436.3 %all-reduce.7.cloned.1.call-done = (f32[4096]{0:T(1024)}, f32[4096]{0:T(1024)}, f32[4096]{0:T(1024)}, f32[4096]{0:T(1024)}) async-done(((f32[4096]{0:T(1024)}, f32[4096]{0:T(1024)}, f32[4096]{0:T(1024)}, f32[4096]{0:T(1024)}), (f32[4096]{0:T(1024)}, f32[4096]{0:T(1024)}, f32[4096]{0:T(1024)}, f32[4096]{0:T(1024)})) %all-reduce.7.cloned.1.call-update) | async-done | bytes 65552 | tf_op jit(solution)/shard_map/psum | solution.py:107
  (76 shorter events, 16.5 us)
Async XLA Ops:
  7.2 275.7 %copy-start = (bf16[8,64,256]{2,1,0:T(8,128)(2,1)S(1)}, bf16[8,64,256]{2,1,0:T(8,128)(2,1)}, u32[]{:S(2)}) copy-start(bf16[8,64,256]{2,1,0:T(8,128)(2,1)} %param.14) | copy-start | bytes 786436
  7.2 195.5 %all-reduce.11.cloned.1.call-start = ((), (), s32[]{:S(2)}) async-start(), calls=%async_computation.4 | async-start | bytes 196608 | tf_op jit(solution)/shard_map/psum | solution.py:11
  13.9 269.0 %all-gather.5.cloned.1.call-start = ((), (), s32[]{:S(2)}) async-start(), calls=%async_computation | async-start | bytes 2162688 | tf_op jit(solution)/shard_map/all_gather | solution.py:49
  204.9 375.2 %all-reduce.9.cloned.1.call-start = ((), (), s32[]{:S(2)}) async-start(), calls=%async_computation.3 | async-start | bytes 196608 | tf_op jit(solution)/shard_map/psum | solution.py:11
  393.5 7.0 copy-start.1
  393.5 188.9 %copy-start.3 = (s32[128,64]{0,1:T(8,128)S(1)}, s32[128,64]{0,1:T(8,128)}, u32[]{:S(2)}) copy-start(s32[128,64]{0,1:T(8,128)} %param.17) | copy-start | bytes 98308
  403.5 321.1 %all-gather.7.cloned.1.call-start = ((), (), s32[]{:S(2)}) async-start(), calls=%async_computation.1 | async-start | bytes 2162688 | tf_op jit(solution)/shard_map/all_gather | solution.py:49
  582.4 700.1 %all-reduce.7.cloned.1.call-start = ((), (), s32[]{:S(2)}) async-start(), calls=%async_computation.2 | async-start | bytes 131072 | tf_op jit(solution)/shard_map/psum | solution.py:107
  832.1 7.0 copy-start.2
Sparse Core Ops, SparseCore 0:
  14.0 188.6 all-reduce.10
  205.6 77.1 all-gather.4
  403.7 176.4 all-reduce.8
  582.7 77.0 all-gather.6
  844.0 438.5 all-reduce.6
where the time goes:
time: 1290 us
  waiting for transfers between devices  815 us (63%)
  blocking collectives  396 us (31%)
  matrix products  23.6 us (2%)
  other arithmetic  22.3 us (2%)
  between operations  17.9 us (1%)
  local copies, waits for them, and re-layouts  16.1 us (1%)
    psum x1, waiting for transfers between devices, body(): col_total, col_num = lax.psum((col_total, col_num), ('tm', 'space'))  436 us
    psum x2, waiting for transfers between devices, from_root(): return lax.psum(jnp.where(mine, value, jnp.zeros_like(value)), axis)  365 us
    pmax x2, blocking collectives, body(): col_max = lax.pmax(col_max, ('tm', 'space'))  206 us
    all_gather x2, blocking collectives, body(): lax.all_gather(part_values, 'space', axis=1, tiled=True)  99 us
    all_gather x2, blocking collectives, body(): lax.all_gather(part_ids, 'space', axis=1, tiled=True)  90.7 us
  transfers between devices with their start and end apart: 5, of which 4 were waited for; matrix products, arithmetic and copies ran while one was open for 1% of the time, Pallas kernels for 0%

commit v1 on v0

v1 whole, which is shorter than its diff:
```python
import math

import jax
import jax.numpy as jnp
from jax import lax
from jax.sharding import PartitionSpec as P

LOWEST = -1e30


def broadcast_tm(values, owners, axis):
    size = lax.axis_size(axis)
    me = lax.axis_index(axis)
    rounds = size.bit_length() - 1
    assert (1 << rounds) == size
    for r in range(rounds):
        bit = 1 << r
        pairs = [(i, i ^ bit) for i in range(size)]
        received = lax.ppermute(values, axis, pairs)
        out = []
        for value, owner, got in zip(values, owners, received):
            take = ((me ^ owner) >> r) == 1
            take = take.reshape(take.shape + (1,) * (value.ndim - take.ndim))
            out.append(jnp.where(take, got, value))
        values = tuple(out)
    return values


def merge_stats(col_max, col_total, col_num, axis):
    top = jnp.max(col_max, axis=axis, keepdims=True)
    keep = jnp.exp(col_max - top)
    total = jnp.sum(col_total * keep, axis=axis)
    num = jnp.sum(col_num * keep, axis=axis)
    return jnp.squeeze(top, axis), total, num


def body(queries, keys, label_values, class_ids, valid_pixels, keyframe_index):
    fr_dev, pix_dev, width = queries.shape
    channels = label_values.shape[2]
    total_steps, keyframes = keyframe_index.shape
    n_space = lax.axis_size("space")
    pix_all = pix_dev * n_space
    mem_width = keyframes * pix_all
    time_pos = lax.axis_index("tm")
    space_pos = lax.axis_index("space")
    rows = fr_dev * pix_dev
    scale = 3.0 / math.sqrt(width)
    class_range = jnp.arange(channels, dtype=jnp.int32)

    frame_valid = lax.dynamic_slice_in_dim(valid_pixels, time_pos * fr_dev, fr_dev)
    pixel_ids = space_pos * pix_dev + jnp.arange(pix_dev, dtype=jnp.int32)
    row_valid = (pixel_ids[None, :] < frame_valid[:, None]).reshape(rows)
    query_rows = queries.reshape(rows, width)

    flat_kf = keyframe_index.reshape(-1)
    owners = flat_kf // fr_dev
    slots = flat_kf % fr_dev
    later = keyframes * (total_steps - 1)

    kf_keys = jnp.take(keys, slots, axis=0)
    kf_values = jnp.take(label_values, slots[:keyframes], axis=0)
    kf_queries = jnp.take(queries, slots[keyframes:], axis=0)
    kf_keys, kf_values, kf_queries = broadcast_tm(
        (kf_keys, kf_values, kf_queries),
        (owners, owners[:keyframes], owners[keyframes:]),
        "tm",
    )

    kf_ids = jnp.take(class_ids, flat_kf, axis=0).astype(jnp.bfloat16)
    kf_ids = kf_ids.reshape(total_steps, keyframes, pix_dev).transpose(1, 2, 0)
    step_keys = kf_keys.reshape(total_steps, keyframes, pix_dev, width)
    packed = jnp.concatenate(
        [step_keys[s] for s in range(total_steps)] + [kf_values, kf_ids], axis=2
    )
    gathered = lax.all_gather(packed, "space", axis=1, tiled=True)
    mem_keys = [
        gathered[:, :, s * width:(s + 1) * width].reshape(mem_width, width)
        for s in range(total_steps)
    ]
    base = total_steps * width
    mem_values = gathered[:, :, base:base + channels].reshape(mem_width, channels)
    mem_ids = [
        gathered[:, :, base + channels + s].reshape(mem_width).astype(jnp.int32)
        for s in range(total_steps)
    ]

    extra_queries = kf_queries.reshape(later, pix_dev, width)
    extra_valid = pixel_ids[None, :] < jnp.take(valid_pixels, flat_kf[keyframes:])[:, None]

    stats = []
    readout = None
    for step in range(total_steps):
        chosen = keyframe_index[step]
        key_valid = (
            jnp.arange(pix_all, dtype=jnp.int32)[None, :]
            < jnp.take(valid_pixels, chosen)[:, None]
        ).reshape(mem_width)
        ids = mem_ids[step]
        onehot_t = (ids[None, :] == class_range[:, None]).astype(jnp.bfloat16)
        if step + 1 < total_steps:
            extra = extra_queries[step * keyframes:(step + 1) * keyframes].reshape(-1, width)
            extra_ok = extra_valid[step * keyframes:(step + 1) * keyframes].reshape(-1)
            q = jnp.concatenate([query_rows, extra], axis=0)
            q_valid = jnp.concatenate([row_valid, extra_ok], axis=0)
        else:
            q = query_rows
            q_valid = row_valid
        scores = lax.dot_general(
            q, mem_keys[step], (((1,), (1,)), ((), ())), preferred_element_type=jnp.float32
        ) * scale
        masked = jnp.where(key_valid[None, :], scores, LOWEST)
        row_max = jnp.max(masked, axis=1, keepdims=True)
        weights = jnp.where(key_valid[None, :], jnp.exp(scores - row_max), 0.0)
        total = jnp.sum(weights, axis=1, keepdims=True)
        mixed = (
            jnp.dot(weights.astype(jnp.bfloat16), mem_values, preferred_element_type=jnp.float32)
            / total
        )
        out = jnp.where(q_valid[:, None], mixed, 0.0).astype(jnp.bfloat16)
        readout = out[:rows]
        own_scores = scores[:rows]
        picked = jnp.dot(readout, onehot_t, preferred_element_type=jnp.float32)
        col_max = jnp.max(jnp.where(row_valid[:, None], own_scores, LOWEST), axis=0)
        expo = jnp.where(row_valid[:, None], jnp.exp(own_scores - col_max[None, :]), 0.0)
        col_total = jnp.sum(expo, axis=0)
        col_num = jnp.sum(expo * picked, axis=0)
        stats.append(jnp.stack([col_max, col_total, col_num]))
        if step + 1 < total_steps:
            part = out[rows:].reshape(keyframes, pix_dev, channels)
            mem_values = lax.all_gather(part, "space", axis=1, tiled=True).reshape(
                mem_width, channels
            )

    local = jnp.stack(stats).reshape(total_steps, 3, keyframes, n_space, pix_dev)
    local = local.transpose(3, 1, 0, 2, 4)
    spread = lax.all_to_all(local, "space", 0, 0, tiled=True)
    m, t, n = merge_stats(spread[:, 0], spread[:, 1], spread[:, 2], 0)
    joined = lax.all_gather(jnp.stack([m, t, n]), "tm", axis=0, tiled=False)
    m, col_total, col_num = merge_stats(joined[:, 0], joined[:, 1], joined[:, 2], 0)

    confidences = []
    for step in range(total_steps):
        chosen = keyframe_index[step]
        key_valid = (
            jnp.arange(pix_all, dtype=jnp.int32)[None, :]
            < jnp.take(valid_pixels, chosen)[:, None]
        ).reshape(mem_width)
        class_match = mem_ids[step][None, :] == class_range[:, None]
        hits = (class_match & key_valid[None, :]).astype(jnp.int32)
        counts = jnp.sum(hits, axis=1)
        all_count = jnp.sum(counts)
        own_ids = lax.dynamic_slice_in_dim(
            mem_ids[step].reshape(keyframes, pix_all), space_pos * pix_dev, pix_dev, 1
        )
        own_valid = pixel_ids[None, :] < jnp.take(valid_pixels, chosen)[:, None]
        own = jnp.take(counts, own_ids)
        own_safe = jnp.where(own_valid, own, 1)
        factor = jnp.sqrt(all_count.astype(jnp.float32) / (channels * own_safe.astype(jnp.float32)))
        conf = jnp.where(own_valid, col_num[step] / col_total[step] * factor, 0.0)
        confidences.append(conf)
    return (readout.reshape(fr_dev, pix_dev, channels), jnp.stack(confidences))


def solution(mesh):
    placed = (
        P("tm", "space", None),
        P("tm", "space", None),
        P("tm", "space", None),
        P(None, "space"),
        P(),
        P(),
    )
    return jax.shard_map(
        body,
        mesh=mesh,
        in_specs=placed,
        out_specs=(P("tm", "space", None), P(None, None, "space")),
        check_vma=False,
    )
```

time: 1290 us -> 317 us (0.25)
  the two profiles are of different devices: /device:TPU:1 before, /device:TPU:2 now
where the time goes in v1:
time: 317 us; the launch traced here: 316 us
  blocking collectives  94 us (30%)
  starting transfers between devices  74 us (23%)
  waiting for transfers between devices  59.7 us (19%)
  other arithmetic  30.3 us (10%)
  local copies, waits for them, and re-layouts  23.8 us (8%)
  matrix products  18.7 us (6%)
  between operations  15.8 us (5%)
    ppermute x12, starting transfers between devices, broadcast_tm(): received = lax.ppermute(values, axis, pairs)  67.4 us
    all_gather x1, blocking collectives, body(): joined = lax.all_gather(jnp.stack([m, t, n]), 'tm', axis=0, tiled=False)  50.9 us
    all_gather x1, blocking collectives, body(): lax.all_gather(part, 'space', axis=1, tiled=True)  43.1 us
    ppermute x12, waiting for transfers between devices, broadcast_tm(): received = lax.ppermute(values, axis, pairs)  35.7 us
    all_gather x1, waiting for transfers between devices, body(): gathered = lax.all_gather(packed, 'space', axis=1, tiled=True)  23.9 us
    reduce_sum x2, other arithmetic, body(): col_total = jnp.sum(expo, axis=0)  8.21 us
    dot_general x2, matrix products, body(): lax.dot_general(q, mem_keys[step], (((1,), (1,)), ((), ())), preferred_el...  7.93 us
    dot_general x2, matrix products, body(): picked = jnp.dot(readout, onehot_t, preferred_element_type=jnp.float32)  7.4 us
  transfers between devices with their start and end apart: 14, of which 7 were waited for; matrix products, arithmetic and copies ran while one was open for 6% of the time, Pallas kernels for 0%

profile of v1, /device:TPU:2, one launch (start us, length us, event | category | flops | bytes accessed | tf_op | source)
XLA Modules:
  0.0 316.3 jit_solution(2012742104391452579)
XLA Ops:
  9.5 3.5 %collective-permute-start = (bf16[4,64,256]{2,1,0:T(8,128)(2,1)S(1)}, bf16[4,64,256]{2,1,0:T(8,128)(2,1)S(1)}, u32[]{:S(2)}, u32[]{:S(2)}) collective-permute-start(bf16[4,64,256]{2,1,0:T(8,128)(2,1)S(1)} %broadcast_select_fusion), channel_id=1, source_target_pairs={{0,32},{32,0},{64,96},{96,64},{128,160},{160,128},{192,224},{224,1... | collective-permute-start | bytes 393224 | tf_op jit(solution)/shard_map/ppermute | solution.py:19
  20.5 4.8 %collective-permute-start.5 = (bf16[2,64,64]{2,1,0:T(8,128)(2,1)S(1)}, bf16[2,64,64]{2,1,0:T(8,128)(2,1)S(1)}, u32[]{:S(2)}, u32[]{:S(2)}) collective-permute-start(bf16[2,64,64]{2,1,0:T(8,128)(2,1)S(1)} %broadcast_select_fusion.11), channel_id=1, source_target_pairs={{0,64},{32,96},{64,0},{96,32},{128,192},{160,224},{192,128},{224,1... | collective-permute-start | bytes 49160 | tf_op jit(solution)/shard_map/ppermute | solution.py:19
  28.1 9.1 %collective-permute-start.6 = (bf16[2,64,64]{2,1,0:T(8,128)(2,1)S(1)}, bf16[2,64,64]{2,1,0:T(8,128)(2,1)S(1)}, u32[]{:S(2)}, u32[]{:S(2)}) collective-permute-start(bf16[2,64,64]{2,1,0:T(8,128)(2,1)S(1)} %broadcast_select_fusion.12), channel_id=1, source_target_pairs={{0,128},{32,160},{64,192},{96,224},{128,0},{160,32},{192,64},{224,... | collective-permute-start | bytes 49160 | tf_op jit(solution)/shard_map/ppermute | solution.py:19
  37.2 5.7 %collective-permute-start.2 = (bf16[4,64,256]{2,1,0:T(8,128)(2,1)S(1)}, bf16[4,64,256]{2,1,0:T(8,128)(2,1)S(1)}, u32[]{:S(2)}, u32[]{:S(2)}) collective-permute-start(bf16[4,64,256]{2,1,0:T(8,128)(2,1)S(1)} %broadcast_select_fusion.2), channel_id=1, source_target_pairs={{0,128},{32,160},{64,192},{96,224},{128,0},{160,32},{192,64},{224,... | collective-permute-start | bytes 393224 | tf_op jit(solution)/shard_map/ppermute | solution.py:19
  43.1 10.9 %collective-permute-start.7 = (bf16[2,64,64]{2,1,0:T(8,128)(2,1)S(1)}, bf16[2,64,64]{2,1,0:T(8,128)(2,1)S(1)}, u32[]{:S(2)}, u32[]{:S(2)}) collective-permute-start(bf16[2,64,64]{2,1,0:T(8,128)(2,1)S(1)} %broadcast_select_fusion.13), channel_id=1, source_target_pairs={{0,256},{32,288},{64,320},{96,352},{128,384},{160,416},{192,448},{... | collective-permute-start | bytes 49160 | tf_op jit(solution)/shard_map/ppermute | solution.py:19
  54.6 14.0 %collective-permute-start.3 = (bf16[4,64,256]{2,1,0:T(8,128)(2,1)S(1)}, bf16[4,64,256]{2,1,0:T(8,128)(2,1)S(1)}, u32[]{:S(2)}, u32[]{:S(2)}) collective-permute-start(bf16[4,64,256]{2,1,0:T(8,128)(2,1)S(1)} %broadcast_select_fusion.3), channel_id=1, source_target_pairs={{0,256},{32,288},{64,320},{96,352},{128,384},{160,416},{192,448},{... | collective-permute-start | bytes 393224 | tf_op jit(solution)/shard_map/ppermute | solution.py:19
  68.8 11.4 %collective-permute-done.3 = bf16[4,64,256]{2,1,0:T(8,128)(2,1)S(1)} collective-permute-done((bf16[4,64,256]{2,1,0:T(8,128)(2,1)S(1)}, bf16[4,64,256]{2,1,0:T(8,128)(2,1)S(1)}, u32[]{:S(2)}, u32[]{:S(2)}) %collective-permute-start.3) | collective-permute-done | bytes 131104 | tf_op jit(solution)/shard_map/ppermute | solution.py:19
  89.9 4.3 %collective-permute-start.9 = (bf16[2,64,256]{2,1,0:T(8,128)(2,1)S(1)}, bf16[2,64,256]{2,1,0:T(8,128)(2,1)S(1)}, u32[]{:S(2)}, u32[]{:S(2)}) collective-permute-start(bf16[2,64,256]{2,1,0:T(8,128)(2,1)S(1)} %broadcast_select_fusion.6), channel_id=1, source_target_pairs={{0,64},{32,96},{64,0},{96,32},{128,192},{160,224},{192,128},{224,1... | collective-permute-start | bytes 196616 | tf_op jit(solution)/shard_map/ppermute | solution.py:19
  94.3 3.3 %collective-permute-done.9 = bf16[2,64,256]{2,1,0:T(8,128)(2,1)S(1)} collective-permute-done((bf16[2,64,256]{2,1,0:T(8,128)(2,1)S(1)}, bf16[2,64,256]{2,1,0:T(8,128)(2,1)S(1)}, u32[]{:S(2)}, u32[]{:S(2)}) %collective-permute-start.9) | collective-permute-done | bytes 65568 | tf_op jit(solution)/shard_map/ppermute | solution.py:19
  99.8 9.3 %collective-permute-done.10 = bf16[2,64,256]{2,1,0:T(8,128)(2,1)S(1)} collective-permute-done((bf16[2,64,256]{2,1,0:T(8,128)(2,1)S(1)}, bf16[2,64,256]{2,1,0:T(8,128)(2,1)S(1)}, u32[]{:S(2)}, u32[]{:S(2)}) %collective-permute-start.10) | collective-permute-done | bytes 65568 | tf_op jit(solution)/shard_map/ppermute | solution.py:19
  109.2 6.2 %collective-permute-start.11 = (bf16[2,64,256]{2,1,0:T(8,128)(2,1)S(1)}, bf16[2,64,256]{2,1,0:T(8,128)(2,1)S(1)}, u32[]{:S(2)}, u32[]{:S(2)}) collective-permute-start(bf16[2,64,256]{2,1,0:T(8,128)(2,1)S(1)} %broadcast_select_fusion.8), channel_id=1, source_target_pairs={{0,256},{32,288},{64,320},{96,352},{128,384},{160,416},{192,448},{... | collective-permute-start | bytes 196616 | tf_op jit(solution)/shard_map/ppermute | solution.py:19
  115.4 10.2 %collective-permute-done.11 = bf16[2,64,256]{2,1,0:T(8,128)(2,1)S(1)} collective-permute-done((bf16[2,64,256]{2,1,0:T(8,128)(2,1)S(1)}, bf16[2,64,256]{2,1,0:T(8,128)(2,1)S(1)}, u32[]{:S(2)}, u32[]{:S(2)}) %collective-permute-start.11) | collective-permute-done | bytes 65568 | tf_op jit(solution)/shard_map/ppermute | solution.py:19
  125.7 23.9 %all-gather.3.cloned.1.call-done = bf16[2,2048,578]{2,1,0:T(8,128)(2,1)} async-done(((bf16[2,64,578]{2,1,0:T(8,128)(2,1)}), bf16[2,2048,578]{2,1,0:T(8,128)(2,1)}) %all-gather.3.cloned.1.call-update) | async-done | bytes 4734992 | tf_op jit(solution)/shard_map/all_gather | solution.py:75
  149.7 3.8 %fusion.62 = (bf16[2,2048,256]{2,1,0:T(8,128)(2,1)}, bf16[2,2048,256]{2,1,0:T(8,128)(2,1)S(1)}) fusion(bf16[2,2048,578]{2,1,0:T(8,128)(2,1)} %all-gather.3.cloned.1.call-done), kind=kLoop, calls=%fused_computation.167 | loop fusion | bytes 8388608 | tf_op jit(solution)/shard_map/slice | solution.py:77
  161.2 6.1 %fusion = f32[640]{0:T(1024)S(1)} fusion(f32[640,4096]{1,0:T(8,128)} %copy-done.1, f32[640]{0:T(1024)S(1)} %get-tuple-element.70, pred[4096]{0:T(1024)(128)(4,1)S(1)} %lt.185), kind=kLoop, calls=%fused_computation.10 | loop fusion | flops 7863680 | bytes 10494976 | tf_op jit(solution)/shard_map/reduce_sum | solution.py:114
  167.3 3.4 %fusion.35 = (s32[2,2048]{1,0:T(2,128)S(1)}, s32[2,2048]{1,0:T(2,128)S(1)}) fusion(bf16[2,2048,578]{2,1,0:T(8,128)(2,1)} %all-gather.3.cloned.1.call-done), kind=kLoop, calls=%fused_computation.49 | loop fusion | flops 8192 | bytes 49152 | tf_op jit(solution)/shard_map/convert_element_type | solution.py:83
  172.7 2.7 multiply_reduce_fusion
  176.8 43.1 %all_gather.13 = bf16[2,2048,64]{2,0,1:T(2,128)(2,1)S(1)} all-gather(bf16[2,64,64]{2,0,1:T(2,128)(2,1)S(1)} %copy.47), channel_id=1, replica_groups=mesh['tm'=16,'space'=32] {'space'}, dimensions={1}, use_global_device_ids=true | all-gather | bytes 540672 | tf_op jit(solution)/shard_map/all_gather | solution.py:130
  220.9 6.1 %select_reduce_fusion.1 = (f32[4096]{0:T(1024)S(1)}, f32[512]{0:T(512)S(1)}, f32[4096,512]{0,1:T(8,128)}) fusion(pred[512]{0:T(512)(128)(4,1)S(1)} %lt.168, pred[4096]{0:T(1024)(128)(4,1)S(1)} %lt.172, bf16[4096,256]{1,0:T(8,128)(2,1)} %bitcast.117, bf16[512,256]{1,0:T(8,128)(2,1)S(1)} %bitcast.135), kind=kOutput, calls=%fused_computation.15 | convolution fusion | flops 1084222976 | bytes 10770944 | tf_op jit(solution)/shard_map/dot_general | solution.py:108
  227.0 6.4 %fusion.5 = (f32[4096]{0:T(1024)S(1)}, f32[512]{0:T(512)S(1)}) fusion(f32[4096,512]{0,1:T(8,128)} %get-tuple-element.72, f32[4096]{0:T(1024)S(1)} %get-tuple-element.16, pred[512]{0:T(512)(128)(4,1)S(1)} %lt.168, f32[512]{0:T(512)S(1)} %get-tuple-element.17, pred[4096]{0:T(1024)(128)(4,1)S(1)} %lt.172), kind=kLoop, calls=%fused_computation.24 | loop fusion | flops 12578304 | bytes 8430080 | tf_op jit(solution)/shard_map/reduce_sum | solution.py:125
  235.8 4.7 %fusion.2 = f32[4096]{0:T(1024)S(1)} fusion(f32[4096,512]{0,1:T(8,128)} %get-tuple-element.72, bf16[512,64]{0,1:T(8,128)(2,1)S(1)} %fusion.19, f32[4096]{0:T(1024)S(1)} %get-tuple-element.16, pred[512]{0:T(512)(128)(4,1)S(1)} %lt.168, s32[4096]{0:T(1024)S(1)} %bitcast.129), kind=kOutput, calls=%fused_computation.13 | convolution fusion | flops 277082112 | bytes 8503808 | tf_op jit(solution)/shard_map/dot_general | solution.py:122
  241.6 6.5 %all-to-all-start = ((f32[32,1,768]{2,1,0:T(1,128)}), f32[32,1,768]{2,1,0:T(1,128)S(1)}, u32[]{:S(2)}, u32[]{:S(2)}) async-start(f32[32,1,768]{2,1,0:T(1,128)} %reshape.454), calls=%async_computation | async-start | bytes 196608 | tf_op jit(solution)/shard_map/all_to_all | solution.py:136
  248.1 2.6 slice_convert_fusion.1
  257.8 50.9 %all-gather = f32[48,2,2,64]{3,2,1,0:T(2,128)S(1)} all-gather(f32[3,2,2,64]{3,2,1,0:T(2,128)S(1)} %pad_maximum_fusion.1), channel_id=2, replica_groups=mesh['tm'=16,'space'=32] {'tm'}, dimensions={0}, use_global_device_ids=true | all-gather | bytes 52224 | tf_op jit(solution)/shard_map/all_gather | solution.py:138
  (127 shorter events, 47.5 us)
Async XLA Ops:
  7.2 1.7 copy-start
  7.2 146.3 %copy-start.4 = (bf16[8,64,256]{2,1,0:T(8,128)(2,1)S(1)}, bf16[8,64,256]{2,1,0:T(8,128)(2,1)}, u32[]{:S(2)}) copy-start(bf16[8,64,256]{2,1,0:T(8,128)(2,1)} %param.10) | copy-start | bytes 786436
  7.2 142.5 %all-gather.3.cloned.1.call-start = ((), (), s32[]{:S(2)}) async-start(), calls=%async_computation.1 | async-start | bytes 5406720 | tf_op jit(solution)/shard_map/all_gather | solution.py:75
  9.5 15.8 %collective-permute-start = (bf16[4,64,256]{2,1,0:T(8,128)(2,1)S(1)}, bf16[4,64,256]{2,1,0:T(8,128)(2,1)S(1)}, u32[]{:S(2)}, u32[]{:S(2)}) collective-permute-start(bf16[4,64,256]{2,1,0:T(8,128)(2,1)S(1)} %broadcast_select_fusion), channel_id=1, source_target_pairs={{0,32},{32,0},{64,96},{96,64},{128,160},{160,128},{192,224},{224,1... | collective-permute-start | bytes 393224 | tf_op jit(solution)/shard_map/ppermute | solution.py:19
  14.6 5.8 %collective-permute-start.4 = (bf16[2,64,64]{2,1,0:T(8,128)(2,1)S(1)}, bf16[2,64,64]{2,1,0:T(8,128)(2,1)S(1)}, u32[]{:S(2)}, u32[]{:S(2)}) collective-permute-start(bf16[2,64,64]{2,1,0:T(8,128)(2,1)S(1)} %broadcast_select_fusion.10), channel_id=1, source_target_pairs={{0,32},{32,0},{64,96},{96,64},{128,160},{160,128},{192,224},{224,1... | collective-permute-start | bytes 49160 | tf_op jit(solution)/shard_map/ppermute | solution.py:19
  20.5 7.5 %collective-permute-start.5 = (bf16[2,64,64]{2,1,0:T(8,128)(2,1)S(1)}, bf16[2,64,64]{2,1,0:T(8,128)(2,1)S(1)}, u32[]{:S(2)}, u32[]{:S(2)}) collective-permute-start(bf16[2,64,64]{2,1,0:T(8,128)(2,1)S(1)} %broadcast_select_fusion.11), channel_id=1, source_target_pairs={{0,64},{32,96},{64,0},{96,32},{128,192},{160,224},{192,128},{224,1... | collective-permute-start | bytes 49160 | tf_op jit(solution)/shard_map/ppermute | solution.py:19
  25.4 11.7 %collective-permute-start.1 = (bf16[4,64,256]{2,1,0:T(8,128)(2,1)S(1)}, bf16[4,64,256]{2,1,0:T(8,128)(2,1)S(1)}, u32[]{:S(2)}, u32[]{:S(2)}) collective-permute-start(bf16[4,64,256]{2,1,0:T(8,128)(2,1)S(1)} %broadcast_select_fusion.1), channel_id=1, source_target_pairs={{0,64},{32,96},{64,0},{96,32},{128,192},{160,224},{192,128},{224,1... | collective-permute-start | bytes 393224 | tf_op jit(solution)/shard_map/ppermute | solution.py:19
  28.1 14.9 %collective-permute-start.6 = (bf16[2,64,64]{2,1,0:T(8,128)(2,1)S(1)}, bf16[2,64,64]{2,1,0:T(8,128)(2,1)S(1)}, u32[]{:S(2)}, u32[]{:S(2)}) collective-permute-start(bf16[2,64,64]{2,1,0:T(8,128)(2,1)S(1)} %broadcast_select_fusion.12), channel_id=1, source_target_pairs={{0,128},{32,160},{64,192},{96,224},{128,0},{160,32},{192,64},{224,... | collective-permute-start | bytes 49160 | tf_op jit(solution)/shard_map/ppermute | solution.py:19
  37.2 17.3 %collective-permute-start.2 = (bf16[4,64,256]{2,1,0:T(8,128)(2,1)S(1)}, bf16[4,64,256]{2,1,0:T(8,128)(2,1)S(1)}, u32[]{:S(2)}, u32[]{:S(2)}) collective-permute-start(bf16[4,64,256]{2,1,0:T(8,128)(2,1)S(1)} %broadcast_select_fusion.2), channel_id=1, source_target_pairs={{0,128},{32,160},{64,192},{96,224},{128,0},{160,32},{192,64},{224,... | collective-permute-start | bytes 393224 | tf_op jit(solution)/shard_map/ppermute | solution.py:19
  43.1 25.6 %collective-permute-start.7 = (bf16[2,64,64]{2,1,0:T(8,128)(2,1)S(1)}, bf16[2,64,64]{2,1,0:T(8,128)(2,1)S(1)}, u32[]{:S(2)}, u32[]{:S(2)}) collective-permute-start(bf16[2,64,64]{2,1,0:T(8,128)(2,1)S(1)} %broadcast_select_fusion.13), channel_id=1, source_target_pairs={{0,256},{32,288},{64,320},{96,352},{128,384},{160,416},{192,448},{... | collective-permute-start | bytes 49160 | tf_op jit(solution)/shard_map/ppermute | solution.py:19
  54.6 25.5 %collective-permute-start.3 = (bf16[4,64,256]{2,1,0:T(8,128)(2,1)S(1)}, bf16[4,64,256]{2,1,0:T(8,128)(2,1)S(1)}, u32[]{:S(2)}, u32[]{:S(2)}) collective-permute-start(bf16[4,64,256]{2,1,0:T(8,128)(2,1)S(1)} %broadcast_select_fusion.3), channel_id=1, source_target_pairs={{0,256},{32,288},{64,320},{96,352},{128,384},{160,416},{192,448},{... | collective-permute-start | bytes 393224 | tf_op jit(solution)/shard_map/ppermute | solution.py:19
  82.6 7.2 %collective-permute-start.8 = (bf16[2,64,256]{2,1,0:T(8,128)(2,1)S(1)}, bf16[2,64,256]{2,1,0:T(8,128)(2,1)S(1)}, u32[]{:S(2)}, u32[]{:S(2)}) collective-permute-start(bf16[2,64,256]{2,1,0:T(8,128)(2,1)S(1)} %broadcast_select_fusion.5), channel_id=1, source_target_pairs={{0,32},{32,0},{64,96},{96,64},{128,160},{160,128},{192,224},{224,1... | collective-permute-start | bytes 196616 | tf_op jit(solution)/shard_map/ppermute | solution.py:19
  89.9 7.7 %collective-permute-start.9 = (bf16[2,64,256]{2,1,0:T(8,128)(2,1)S(1)}, bf16[2,64,256]{2,1,0:T(8,128)(2,1)S(1)}, u32[]{:S(2)}, u32[]{:S(2)}) collective-permute-start(bf16[2,64,256]{2,1,0:T(8,128)(2,1)S(1)} %broadcast_select_fusion.6), channel_id=1, source_target_pairs={{0,64},{32,96},{64,0},{96,32},{128,192},{160,224},{192,128},{224,1... | collective-permute-start | bytes 196616 | tf_op jit(solution)/shard_map/ppermute | solution.py:19
  97.6 11.5 %collective-permute-start.10 = (bf16[2,64,256]{2,1,0:T(8,128)(2,1)S(1)}, bf16[2,64,256]{2,1,0:T(8,128)(2,1)S(1)}, u32[]{:S(2)}, u32[]{:S(2)}) collective-permute-start(bf16[2,64,256]{2,1,0:T(8,128)(2,1)S(1)} %broadcast_select_fusion.7), channel_id=1, source_target_pairs={{0,128},{32,160},{64,192},{96,224},{128,0},{160,32},{192,64},{224,... | collective-permute-start | bytes 196616 | tf_op jit(solution)/shard_map/ppermute | solution.py:19
  109.2 16.4 %collective-permute-start.11 = (bf16[2,64,256]{2,1,0:T(8,128)(2,1)S(1)}, bf16[2,64,256]{2,1,0:T(8,128)(2,1)S(1)}, u32[]{:S(2)}, u32[]{:S(2)}) collective-permute-start(bf16[2,64,256]{2,1,0:T(8,128)(2,1)S(1)} %broadcast_select_fusion.8), channel_id=1, source_target_pairs={{0,256},{32,288},{64,320},{96,352},{128,384},{160,416},{192,448},{... | collective-permute-start | bytes 196616 | tf_op jit(solution)/shard_map/ppermute | solution.py:19
  155.3 4.0 %copy-start.1 = (f32[640,4096]{1,0:T(8,128)}, f32[640,4096]{1,0:T(8,128)S(1)}, u32[]{:S(2)}) copy-start(f32[640,4096]{1,0:T(8,128)S(1)} %get-tuple-element.71) | copy-start | bytes 31457284
  161.1 9.7 %slice-start = ((bf16[2,2048,578]{2,1,0:T(8,128)(2,1)}), bf16[2,2048,64]{2,1,0:T(8,128)(2,1)S(1)}, s32[]{:S(2)}) async-start(bf16[2,2048,578]{2,1,0:T(8,128)(2,1)} %all-gather.3.cloned.1.call-done), calls=%async_computation.2 | async-start | bytes 2097152 | tf_op jit(solution)/shard_map/slice | solution.py:81
  161.2 9.6 %copy-start.2 = (f32[640,4096]{1,0:T(8,128)S(1)}, f32[640,4096]{1,0:T(8,128)}, u32[]{:S(2)}) copy-start(f32[640,4096]{1,0:T(8,128)} %copy-done.1) | copy-start | bytes 31457284
  227.0 6.4 %copy-start.3 = (f32[4096,512]{0,1:T(8,128)S(1)}, f32[4096,512]{0,1:T(8,128)}, u32[]{:S(2)}) copy-start(f32[4096,512]{0,1:T(8,128)} %get-tuple-element.72) | copy-start | bytes 25165828
  241.6 14.4 %all-to-all-start = ((f32[32,1,768]{2,1,0:T(1,128)}), f32[32,1,768]{2,1,0:T(1,128)S(1)}, u32[]{:S(2)}, u32[]{:S(2)}) async-start(f32[32,1,768]{2,1,0:T(1,128)} %reshape.454), calls=%async_computation | async-start | bytes 196608 | tf_op jit(solution)/shard_map/all_to_all | solution.py:136
Sparse Core Ops, SparseCore 0:
  81.1 68.4 all-gather.2

commit v2 on v1

--- a/solution.py
+++ b/solution.py
@@ -8,7 +8,7 @@
 LOWEST = -1e30
 
 
-def broadcast_tm(values, owners, axis):
+def broadcast_tm(value, owner, axis):
     size = lax.axis_size(axis)
     me = lax.axis_index(axis)
     rounds = size.bit_length() - 1
@@ -16,14 +16,16 @@
     for r in range(rounds):
         bit = 1 << r
         pairs = [(i, i ^ bit) for i in range(size)]
-        received = lax.ppermute(values, axis, pairs)
-        out = []
-        for value, owner, got in zip(values, owners, received):
-            take = ((me ^ owner) >> r) == 1
-            take = take.reshape(take.shape + (1,) * (value.ndim - take.ndim))
-            out.append(jnp.where(take, got, value))
-        values = tuple(out)
-    return values
+        got = lax.ppermute(value, axis, pairs)
+        take = ((me ^ owner) >> r) == 1
+        value = jnp.where(take[:, None], got, value)
+    return value
+
+
+def gather_all(value, axis):
+    size = lax.axis_size(axis)
+    spread = jnp.broadcast_to(value[None], (size,) + value.shape)
+    return lax.all_to_all(spread, axis, 0, 0, tiled=True)
 
 
 def merge_stats(col_max, col_total, col_num, axis):
@@ -60,11 +62,17 @@
     kf_keys = jnp.take(keys, slots, axis=0)
     kf_values = jnp.take(label_values, slots[:keyframes], axis=0)
     kf_queries = jnp.take(queries, slots[keyframes:], axis=0)
-    kf_keys, kf_values, kf_queries = broadcast_tm(
-        (kf_keys, kf_values, kf_queries),
-        (owners, owners[:keyframes], owners[keyframes:]),
-        "tm",
+    parts = [kf_keys, kf_queries, kf_values]
+    part_owners = [owners, owners[keyframes:], owners[:keyframes]]
+    flat = jnp.concatenate([p.reshape(-1, width) for p in parts], axis=0)
+    row_owner = jnp.concatenate(
+        [jnp.repeat(o, p[0].size // width) for p, o in zip(parts, part_owners)]
     )
+    flat = broadcast_tm(flat, row_owner, "tm")
+    sizes = [p.size // width for p in parts]
+    kf_keys = flat[:sizes[0]].reshape(kf_keys.shape)
+    kf_queries = flat[sizes[0]:sizes[0] + sizes[1]].reshape(kf_queries.shape)
+    kf_values = flat[sizes[0] + sizes[1]:].reshape(kf_values.shape)
 
     kf_ids = jnp.take(class_ids, flat_kf, axis=0).astype(jnp.bfloat16)
     kf_ids = kf_ids.reshape(total_steps, keyframes, pix_dev).transpose(1, 2, 0)
@@ -127,7 +135,7 @@
         stats.append(jnp.stack([col_max, col_total, col_num]))
         if step + 1 < total_steps:
             part = out[rows:].reshape(keyframes, pix_dev, channels)
-            mem_values = lax.all_gather(part, "space", axis=1, tiled=True).reshape(
+            mem_values = gather_all(part, "space").transpose(1, 0, 2, 3).reshape(
                 mem_width, channels
             )
 
@@ -135,7 +143,7 @@
     local = local.transpose(3, 1, 0, 2, 4)
     spread = lax.all_to_all(local, "space", 0, 0, tiled=True)
     m, t, n = merge_stats(spread[:, 0], spread[:, 1], spread[:, 2], 0)
-    joined = lax.all_gather(jnp.stack([m, t, n]), "tm", axis=0, tiled=False)
+    joined = gather_all(jnp.stack([m, t, n]), "tm")
     m, col_total, col_num = merge_stats(joined[:, 0], joined[:, 1], joined[:, 2], 0)
 
     confidences = []

time: 317 us -> 275 us (0.87)
  the two profiles are of different devices: /device:TPU:2 before, /device:TPU:1 now
where the time goes in v2:
time: 275 us
  waiting for transfers between devices  114 us (41%)
  starting transfers between devices  63.7 us (23%)
  local copies, waits for them, and re-layouts  31.5 us (11%)
  other arithmetic  29.9 us (11%)
  matrix products  20 us (7%)
  between operations  15.8 us (6%)
    all_gather x1, waiting for transfers between devices, body(): gathered = lax.all_gather(packed, 'space', axis=1, tiled=True)  60.5 us
    ppermute x4, starting transfers between devices, broadcast_tm(): got = lax.ppermute(value, axis, pairs)  39.2 us
    ppermute x4, waiting for transfers between devices, broadcast_tm(): got = lax.ppermute(value, axis, pairs)  36.7 us
    all_to_all x2, starting transfers between devices, gather_all(): return lax.all_to_all(spread, axis, 0, 0, tiled=True)  18.3 us
    unnamed x23, local copies, waits for them, and re-layouts  10.2 us
    all_to_all x2, waiting for transfers between devices, gather_all(): return lax.all_to_all(spread, axis, 0, 0, tiled=True)  9.58 us
    dot_general x2, matrix products, body(): lax.dot_general(q, mem_keys[step], (((1,), (1,)), ((), ())), preferred_el...  7.87 us
    reduce_sum x2, other arithmetic, body(): col_total = jnp.sum(expo, axis=0)  7.44 us
  transfers between devices with their start and end apart: 8, of which 8 were waited for; matrix products, arithmetic and copies ran while one was open for 10% of the time, Pallas kernels for 0%

profile of v2, /device:TPU:1, one launch (start us, length us, event | category | flops | bytes accessed | tf_op | source)
XLA Modules:
  0.0 274.7 jit_solution(15955193458045880197)
XLA Ops:
  13.2 4.0 %collective-permute-start = (bf16[416,256]{1,0:T(8,128)(2,1)S(1)}, bf16[416,256]{1,0:T(8,128)(2,1)S(1)}, u32[]{:S(2)}, u32[]{:S(2)}) collective-permute-start(bf16[416,256]{1,0:T(8,128)(2,1)S(1)} %pad_maximum_fusion), channel_id=1, source_target_pairs={{0,32},{32,0},{64,96},{96,64},{128,160},{160,128},{192,224},{224,1... | collective-permute-start | bytes 638984 | tf_op jit(solution)/shard_map/ppermute | solution.py:19
  17.8 2.6 collective-permute-done
  20.6 6.4 %collective-permute-start.1 = (bf16[416,256]{1,0:T(8,128)(2,1)S(1)}, bf16[416,256]{1,0:T(8,128)(2,1)S(1)}, u32[]{:S(2)}, u32[]{:S(2)}) collective-permute-start(bf16[416,256]{1,0:T(8,128)(2,1)S(1)} %broadcast_select_fusion), channel_id=1, source_target_pairs={{0,64},{32,96},{64,0},{96,32},{128,192},{160,224},{192,128},{224,1... | collective-permute-start | bytes 638984 | tf_op jit(solution)/shard_map/ppermute | solution.py:19
  30.4 9.4 %collective-permute-start.2 = (bf16[416,256]{1,0:T(8,128)(2,1)S(1)}, bf16[416,256]{1,0:T(8,128)(2,1)S(1)}, u32[]{:S(2)}, u32[]{:S(2)}) collective-permute-start(bf16[416,256]{1,0:T(8,128)(2,1)S(1)} %broadcast_select_fusion.1), channel_id=1, source_target_pairs={{0,128},{32,160},{64,192},{96,224},{128,0},{160,32},{192,64},{224,... | collective-permute-start | bytes 638984 | tf_op jit(solution)/shard_map/ppermute | solution.py:19
  40.5 17.2 %collective-permute-done.2 = bf16[416,256]{1,0:T(8,128)(2,1)S(1)} collective-permute-done((bf16[416,256]{1,0:T(8,128)(2,1)S(1)}, bf16[416,256]{1,0:T(8,128)(2,1)S(1)}, u32[]{:S(2)}, u32[]{:S(2)}) %collective-permute-start.2) | collective-permute-done | bytes 213024 | tf_op jit(solution)/shard_map/ppermute | solution.py:19
  57.8 19.4 %collective-permute-start.3 = (bf16[416,256]{1,0:T(8,128)(2,1)S(1)}, bf16[416,256]{1,0:T(8,128)(2,1)S(1)}, u32[]{:S(2)}, u32[]{:S(2)}) collective-permute-start(bf16[416,256]{1,0:T(8,128)(2,1)S(1)} %broadcast_select_fusion.2), channel_id=1, source_target_pairs={{0,256},{32,288},{64,320},{96,352},{128,384},{160,416},{192,448},{... | collective-permute-start | bytes 638984 | tf_op jit(solution)/shard_map/ppermute | solution.py:19
  77.2 15.2 %collective-permute-done.3 = bf16[416,256]{1,0:T(8,128)(2,1)S(1)} collective-permute-done((bf16[416,256]{1,0:T(8,128)(2,1)S(1)}, bf16[416,256]{1,0:T(8,128)(2,1)S(1)}, u32[]{:S(2)}, u32[]{:S(2)}) %collective-permute-start.3) | collective-permute-done | bytes 213024 | tf_op jit(solution)/shard_map/ppermute | solution.py:19
  98.9 60.5 %all-gather.2.cloned.1.call-done = bf16[2,2048,578]{2,1,0:T(8,128)(2,1)} async-done(((bf16[2,64,578]{2,1,0:T(8,128)(2,1)}), bf16[2,2048,578]{2,1,0:T(8,128)(2,1)}) %all-gather.2.cloned.1.call-update) | async-done | bytes 4734992 | tf_op jit(solution)/shard_map/all_gather | solution.py:83
  159.4 3.8 %fusion.62 = (bf16[2,2048,256]{2,1,0:T(8,128)(2,1)}, bf16[2,2048,256]{2,1,0:T(8,128)(2,1)S(1)}) fusion(bf16[2,2048,578]{2,1,0:T(8,128)(2,1)} %all-gather.2.cloned.1.call-done), kind=kLoop, calls=%fused_computation.150 | loop fusion | bytes 8388608 | tf_op jit(solution)/shard_map/slice | solution.py:85
  166.4 2.6 copy-done.1
  171.0 6.1 %fusion = f32[640]{0:T(1024)S(1)} fusion(f32[640,4096]{1,0:T(8,128)} %copy-done.1, f32[640]{0:T(1024)S(1)} %get-tuple-element.61, pred[4096]{0:T(1024)(128)(4,1)S(1)} %lt.186), kind=kLoop, calls=%fused_computation.10 | loop fusion | flops 7863680 | bytes 10494976 | tf_op jit(solution)/shard_map/reduce_sum | solution.py:122
  177.1 3.4 %fusion.35 = (s32[2,2048]{1,0:T(2,128)S(1)}, s32[2,2048]{1,0:T(2,128)S(1)}) fusion(bf16[2,2048,578]{2,1,0:T(8,128)(2,1)} %all-gather.2.cloned.1.call-done), kind=kLoop, calls=%fused_computation.49 | loop fusion | flops 8192 | bytes 49152 | tf_op jit(solution)/shard_map/convert_element_type | solution.py:91
  180.6 1.9 fusion.28
  182.5 2.7 multiply_reduce_fusion
  187.9 5.3 %all-to-all-start = ((bf16[32,2,4096]{2,1,0:T(2,128)(2,1)}), bf16[32,2,4096]{2,1,0:T(2,128)(2,1)S(1)}, u32[]{:S(2)}, u32[]{:S(2)}) async-start(bf16[32,2,4096]{2,1,0:T(2,128)(2,1)} %reshape.467), calls=%async_computation | async-start | bytes 1048576 | tf_op jit(solution)/shard_map/all_to_all | solution.py:28
  193.2 6.1 %select_reduce_fusion.1 = (f32[4096]{0:T(1024)S(1)}, f32[512]{0:T(512)S(1)}, f32[4096,512]{0,1:T(8,128)}) fusion(pred[512]{0:T(512)(128)(4,1)S(1)} %lt.168, pred[4096]{0:T(1024)(128)(4,1)S(1)} %lt.172, bf16[4096,256]{1,0:T(8,128)(2,1)} %bitcast.128, bf16[512,256]{1,0:T(8,128)(2,1)S(1)} %bitcast.144), kind=kOutput, calls=%fused_computation.15 | convolution fusion | flops 1084222976 | bytes 10770944 | tf_op jit(solution)/shard_map/dot_general | solution.py:116
  199.4 5.7 %fusion.5 = (f32[4096]{0:T(1024)S(1)}, f32[512]{0:T(512)S(1)}) fusion(f32[4096,512]{0,1:T(8,128)} %get-tuple-element.63, f32[4096]{0:T(1024)S(1)} %get-tuple-element.20, pred[512]{0:T(512)(128)(4,1)S(1)} %lt.168, f32[512]{0:T(512)S(1)} %get-tuple-element.21, pred[4096]{0:T(1024)(128)(4,1)S(1)} %lt.172), kind=kLoop, calls=%fused_computation.24 | loop fusion | flops 12578304 | bytes 8430080 | tf_op jit(solution)/shard_map/reduce_sum | solution.py:133
  205.1 2.6 slice_convert_fusion.1
  213.2 5.0 %fusion.19 = bf16[512,64]{0,1:T(8,128)(2,1)S(1)} fusion(bf16[4096,64]{0,1:T(8,128)(2,1)S(1)} %reshape.375, f32[4096,512]{0,1:T(8,128)} %get-tuple-element.63, f32[512]{0:T(512)S(1)} %get-tuple-element.21, pred[4096]{0:T(1024)(128)(4,1)S(1)} %lt.172, f32[512]{0:T(512)S(1)} %get-tuple-element.19, pred[512]{0:T(512)(128)(4,1)S(1)} %lt.168), kind=kOutput, calls=%fused_computation.37 | convolution fusion | flops 274825216 | bytes 8987136 | tf_op jit(solution)/shard_map/dot_general | solution.py:124
  219.0 2.6 fusion.2
  222.7 6.2 %all-to-all-start.1 = ((f32[32,1,768]{2,1,0:T(1,128)}), f32[32,1,768]{2,1,0:T(1,128)S(1)}, u32[]{:S(2)}, u32[]{:S(2)}) async-start(f32[32,1,768]{2,1,0:T(1,128)} %reshape.469), calls=%async_computation.1 | async-start | bytes 196608 | tf_op jit(solution)/shard_map/all_to_all | solution.py:144
  230.1 6.9 %all-to-all-done.1 = f32[32,1,768]{2,1,0:T(1,128)S(1)} async-done(((f32[32,1,768]{2,1,0:T(1,128)}), f32[32,1,768]{2,1,0:T(1,128)S(1)}, u32[]{:S(2)}, u32[]{:S(2)}) %all-to-all-start.1) | async-done | bytes 98336 | tf_op jit(solution)/shard_map/all_to_all | solution.py:144
  239.5 13.0 %all-to-all-start.2 = ((f32[16,1,768]{2,1,0:T(1,128)}), f32[16,1,768]{2,1,0:T(1,128)S(1)}, u32[]{:S(2)}, u32[]{:S(2)}) async-start(f32[16,1,768]{2,1,0:T(1,128)} %reshape.471), calls=%async_computation.2 | async-start | bytes 98304 | tf_op jit(solution)/shard_map/all_to_all | solution.py:28
  258.2 8.0 %all-to-all-done.2 = f32[16,1,768]{2,1,0:T(1,128)S(1)} async-done(((f32[16,1,768]{2,1,0:T(1,128)}), f32[16,1,768]{2,1,0:T(1,128)S(1)}, u32[]{:S(2)}, u32[]{:S(2)}) %all-to-all-start.2) | async-done | bytes 49184 | tf_op jit(solution)/shard_map/all_to_all | solution.py:28
  (127 shorter events, 42.2 us)
Async XLA Ops:
  7.2 5.3 %copy-start = (bf16[8,64,256]{2,1,0:T(8,128)(2,1)S(1)}, bf16[8,64,256]{2,1,0:T(8,128)(2,1)}, u32[]{:S(2)}) copy-start(bf16[8,64,256]{2,1,0:T(8,128)(2,1)} %param.11) | copy-start | bytes 786436
  7.2 156.0 %copy-start.3 = (bf16[8,64,256]{2,1,0:T(8,128)(2,1)S(1)}, bf16[8,64,256]{2,1,0:T(8,128)(2,1)}, u32[]{:S(2)}) copy-start(bf16[8,64,256]{2,1,0:T(8,128)(2,1)} %param.10) | copy-start | bytes 786436
  7.2 152.2 %all-gather.2.cloned.1.call-start = ((), (), s32[]{:S(2)}) async-start(), calls=%async_computation.3 | async-start | bytes 5406720 | tf_op jit(solution)/shard_map/all_gather | solution.py:83
  13.2 7.3 %collective-permute-start = (bf16[416,256]{1,0:T(8,128)(2,1)S(1)}, bf16[416,256]{1,0:T(8,128)(2,1)S(1)}, u32[]{:S(2)}, u32[]{:S(2)}) collective-permute-start(bf16[416,256]{1,0:T(8,128)(2,1)S(1)} %pad_maximum_fusion), channel_id=1, source_target_pairs={{0,32},{32,0},{64,96},{96,64},{128,160},{160,128},{192,224},{224,1... | collective-permute-start | bytes 638984 | tf_op jit(solution)/shard_map/ppermute | solution.py:19
  20.6 9.6 %collective-permute-start.1 = (bf16[416,256]{1,0:T(8,128)(2,1)S(1)}, bf16[416,256]{1,0:T(8,128)(2,1)S(1)}, u32[]{:S(2)}, u32[]{:S(2)}) collective-permute-start(bf16[416,256]{1,0:T(8,128)(2,1)S(1)} %broadcast_select_fusion), channel_id=1, source_target_pairs={{0,64},{32,96},{64,0},{96,32},{128,192},{160,224},{192,128},{224,1... | collective-permute-start | bytes 638984 | tf_op jit(solution)/shard_map/ppermute | solution.py:19
  30.4 27.3 %collective-permute-start.2 = (bf16[416,256]{1,0:T(8,128)(2,1)S(1)}, bf16[416,256]{1,0:T(8,128)(2,1)S(1)}, u32[]{:S(2)}, u32[]{:S(2)}) collective-permute-start(bf16[416,256]{1,0:T(8,128)(2,1)S(1)} %broadcast_select_fusion.1), channel_id=1, source_target_pairs={{0,128},{32,160},{64,192},{96,224},{128,0},{160,32},{192,64},{224,... | collective-permute-start | bytes 638984 | tf_op jit(solution)/shard_map/ppermute | solution.py:19
  57.8 34.6 %collective-permute-start.3 = (bf16[416,256]{1,0:T(8,128)(2,1)S(1)}, bf16[416,256]{1,0:T(8,128)(2,1)S(1)}, u32[]{:S(2)}, u32[]{:S(2)}) collective-permute-start(bf16[416,256]{1,0:T(8,128)(2,1)S(1)} %broadcast_select_fusion.2), channel_id=1, source_target_pairs={{0,256},{32,288},{64,320},{96,352},{128,384},{160,416},{192,448},{... | collective-permute-start | bytes 638984 | tf_op jit(solution)/shard_map/ppermute | solution.py:19
  165.0 4.0 %copy-start.1 = (f32[640,4096]{1,0:T(8,128)}, f32[640,4096]{1,0:T(8,128)S(1)}, u32[]{:S(2)}) copy-start(f32[640,4096]{1,0:T(8,128)S(1)} %get-tuple-element.62) | copy-start | bytes 31457284
  170.8 9.8 %slice-start = ((bf16[2,2048,578]{2,1,0:T(8,128)(2,1)}), bf16[2,2048,64]{2,1,0:T(8,128)(2,1)S(1)}, s32[]{:S(2)}) async-start(bf16[2,2048,578]{2,1,0:T(8,128)(2,1)} %all-gather.2.cloned.1.call-done), calls=%async_computation.4 | async-start | bytes 2097152 | tf_op jit(solution)/shard_map/slice | solution.py:89
  171.0 9.6 %copy-start.2 = (f32[640,4096]{1,0:T(8,128)S(1)}, f32[640,4096]{1,0:T(8,128)}, u32[]{:S(2)}) copy-start(f32[640,4096]{1,0:T(8,128)} %copy-done.1) | copy-start | bytes 31457284
  187.9 21.7 %all-to-all-start = ((bf16[32,2,4096]{2,1,0:T(2,128)(2,1)}), bf16[32,2,4096]{2,1,0:T(2,128)(2,1)S(1)}, u32[]{:S(2)}, u32[]{:S(2)}) async-start(bf16[32,2,4096]{2,1,0:T(2,128)(2,1)} %reshape.467), calls=%async_computation | async-start | bytes 1048576 | tf_op jit(solution)/shard_map/all_to_all | solution.py:28
  213.2 5.0 %slice-start.1 = ((s8[8388608]{0:T(1024)(128)(4,1)}), s8[4194304]{0:T(1024)(128)(4,1)S(1)}, s32[]{:S(2)}) async-start(s8[8388608]{0:T(1024)(128)(4,1)} %bitcast.126), calls=%async_computation.5 | async-start | bytes 8388608
  213.2 5.8 %slice-start.2 = ((s8[8388608]{0:T(1024)(128)(4,1)}), s8[4194304]{0:T(1024)(128)(4,1)S(1)}, s32[]{:S(2)}) async-start(s8[8388608]{0:T(1024)(128)(4,1)} %bitcast.126), calls=%async_computation.6 | async-start | bytes 8388608
  222.7 14.3 %all-to-all-start.1 = ((f32[32,1,768]{2,1,0:T(1,128)}), f32[32,1,768]{2,1,0:T(1,128)S(1)}, u32[]{:S(2)}, u32[]{:S(2)}) async-start(f32[32,1,768]{2,1,0:T(1,128)} %reshape.469), calls=%async_computation.1 | async-start | bytes 196608 | tf_op jit(solution)/shard_map/all_to_all | solution.py:144
  239.5 26.7 %all-to-all-start.2 = ((f32[16,1,768]{2,1,0:T(1,128)}), f32[16,1,768]{2,1,0:T(1,128)S(1)}, u32[]{:S(2)}, u32[]{:S(2)}) async-start(f32[16,1,768]{2,1,0:T(1,128)} %reshape.471), calls=%async_computation.2 | async-start | bytes 98304 | tf_op jit(solution)/shard_map/all_to_all | solution.py:28
Sparse Core Ops, SparseCore 0:
  93.6 65.7 all-gather.1

commit v3 on v2

--- a/solution.py
+++ b/solution.py
@@ -6,19 +6,36 @@
 from jax.sharding import PartitionSpec as P
 
 LOWEST = -1e30
-
-
-def broadcast_tm(value, owner, axis):
+NEAR_TM = 4
+
+
+def broadcast_tm(value, owner, axis, inner):
     size = lax.axis_size(axis)
     me = lax.axis_index(axis)
-    rounds = size.bit_length() - 1
-    assert (1 << rounds) == size
+    rounds = inner.bit_length() - 1
+    assert (1 << rounds) == inner and size % inner == 0
     for r in range(rounds):
         bit = 1 << r
         pairs = [(i, i ^ bit) for i in range(size)]
         got = lax.ppermute(value, axis, pairs)
-        take = ((me ^ owner) >> r) == 1
+        take = ((me ^ owner) % inner >> r) == 1
         value = jnp.where(take[:, None], got, value)
+    groups = size // inner
+    rel = (me // inner - owner // inner) % groups
+    ahead = [(i, (i + inner) % size) for i in range(size)]
+    behind = [(i, (i - inner) % size) for i in range(size)]
+    half = value.shape[0] // 2
+    for k in range(1, groups // 2 + 1):
+        if 2 * k == groups:
+            got_a = lax.ppermute(value[:half], axis, ahead)
+            got_b = lax.ppermute(value[half:], axis, behind)
+            got = jnp.concatenate([got_a, got_b], axis=0)
+            value = jnp.where((rel == k)[:, None], got, value)
+        else:
+            got_a = lax.ppermute(value, axis, ahead)
+            got_b = lax.ppermute(value, axis, behind)
+            value = jnp.where((rel == k)[:, None], got_a, value)
+            value = jnp.where((rel == groups - k)[:, None], got_b, value)
     return value
 
 
@@ -68,7 +85,7 @@
     row_owner = jnp.concatenate(
         [jnp.repeat(o, p[0].size // width) for p, o in zip(parts, part_owners)]
     )
-    flat = broadcast_tm(flat, row_owner, "tm")
+    flat = broadcast_tm(flat, row_owner, "tm", NEAR_TM)
     sizes = [p.size // width for p in parts]
     kf_keys = flat[:sizes[0]].reshape(kf_keys.shape)
     kf_queries = flat[sizes[0]:sizes[0] + sizes[1]].reshape(kf_queries.shape)
@@ -77,20 +94,17 @@
     kf_ids = jnp.take(class_ids, flat_kf, axis=0).astype(jnp.bfloat16)
     kf_ids = kf_ids.reshape(total_steps, keyframes, pix_dev).transpose(1, 2, 0)
     step_keys = kf_keys.reshape(total_steps, keyframes, pix_dev, width)
-    packed = jnp.concatenate(
-        [step_keys[s] for s in range(total_steps)] + [kf_values, kf_ids], axis=2
-    )
+    packed = jnp.concatenate([step_keys[0], kf_values, kf_ids], axis=2)
     gathered = lax.all_gather(packed, "space", axis=1, tiled=True)
-    mem_keys = [
-        gathered[:, :, s * width:(s + 1) * width].reshape(mem_width, width)
+    mem_keys = [gathered[:, :, :width].reshape(mem_width, width)]
+    mem_values = gathered[:, :, width:width + channels].reshape(mem_width, channels)
+    mem_ids = [
+        gathered[:, :, width + channels + s].reshape(mem_width).astype(jnp.int32)
         for s in range(total_steps)
     ]
-    base = total_steps * width
-    mem_values = gathered[:, :, base:base + channels].reshape(mem_width, channels)
-    mem_ids = [
-        gathered[:, :, base + channels + s].reshape(mem_width).astype(jnp.int32)
-        for s in range(total_steps)
-    ]
+    rest_keys, unused = lax.optimization_barrier((step_keys[1:], gathered))
+    rest_keys = lax.all_gather(rest_keys, "space", axis=2, tiled=True)
+    mem_keys += [rest_keys[s].reshape(mem_width, width) for s in range(total_steps - 1)]
 
     extra_queries = kf_queries.reshape(later, pix_dev, width)
     extra_valid = pixel_ids[None, :] < jnp.take(valid_pixels, flat_kf[keyframes:])[:, None]

time: 275 us -> 292 us (1.062)
  waiting for transfers between devices: 114 us -> 130 us
    ppermute x4 -> x2, waiting for transfers between devices: 36.7 us -> 3.43 us  [broadcast_tm(): got = lax.ppermute(value, axis, pairs)]
    ppermute x4 -> x2, starting transfers between devices: 39.2 us -> 10.4 us  [broadcast_tm(): got = lax.ppermute(value, axis, pairs)]
    ppermute x0 -> x4, starting transfers between devices: none -> 27.7 us  [the longest x1 13 us: broadcast_tm(): got_b = lax.ppermute(value, axis, behind)]
    all_gather x0 -> x1, waiting for transfers between devices: none -> 25.9 us  [body(): rest_keys = lax.all_gather(rest_keys, 'space', axis=2, tiled=True)]
    ppermute x0 -> x4, waiting for transfers between devices: none -> 18.7 us  [the longest x1 13.3 us: broadcast_tm(): got_b = lax.ppermute(value, axis, behind)]
    all_gather x1, waiting for transfers between devices: 60.5 us -> 67 us  [body(): gathered = lax.all_gather(packed, 'space', axis=1, tiled=True)]
    reduce_sum x1, other arithmetic: 6.14 us -> 2.01 us  [body(): total = jnp.sum(weights, axis=1, keepdims=True)]
    dot_general x2, matrix products: 6.88 us -> 3.34 us  [body(): jnp.dot(weights.astype(jnp.bfloat16), mem_values, preferred_element_type=...]
  transfers between devices with their start and end apart: 8 -> 11, of which waited for: 8 -> 9; matrix products, arithmetic and copies ran while one was open for 10% -> 18% of each run, Pallas kernels for 0% -> 0%
where the time goes in v3:
time: 292 us; the launch traced here: 291 us
  waiting for transfers between devices  130 us (45%)
  starting transfers between devices  61.9 us (21%)
  local copies, waits for them, and re-layouts  32.4 us (11%)
  other arithmetic  30.6 us (10%)
  matrix products  20.1 us (7%)
  between operations  16 us (5%)
    all_gather x1, waiting for transfers between devices, body(): gathered = lax.all_gather(packed, 'space', axis=1, tiled=True)  67 us
    all_gather x1, waiting for transfers between devices, body(): rest_keys = lax.all_gather(rest_keys, 'space', axis=2, tiled=True)  25.9 us
    all_to_all x2, starting transfers between devices, gather_all(): return lax.all_to_all(spread, axis, 0, 0, tiled=True)  17.4 us
    ppermute x1, waiting for transfers between devices, broadcast_tm(): got_b = lax.ppermute(value, axis, behind)  13.3 us
    ppermute x1, starting transfers between devices, broadcast_tm(): got_b = lax.ppermute(value, axis, behind)  13 us
    reduce_sum x2, other arithmetic, body(): col_total = jnp.sum(expo, axis=0)  10.8 us
    ppermute x2, starting transfers between devices, broadcast_tm(): got = lax.ppermute(value, axis, pairs)  10.4 us
    unnamed x49, local copies, waits for them, and re-layouts  10.3 us
  transfers between devices with their start and end apart: 11, of which 9 were waited for; matrix products, arithmetic and copies ran while one was open for 18% of the time, Pallas kernels for 0%

profile of v3, /device:TPU:1, one launch (start us, length us, event | category | flops | bytes accessed | tf_op | source)
XLA Modules:
  0.0 290.9 jit_solution(16868599560397090585)
XLA Ops:
  13.2 4.0 %collective-permute-start = (bf16[416,256]{1,0:T(8,128)(2,1)S(1)}, bf16[416,256]{1,0:T(8,128)(2,1)S(1)}, u32[]{:S(2)}, u32[]{:S(2)}) collective-permute-start(bf16[416,256]{1,0:T(8,128)(2,1)S(1)} %pad_maximum_fusion), channel_id=1, source_target_pairs={{0,32},{32,0},{64,96},{96,64},{128,160},{160,128},{192,224},{224,1... | collective-permute-start | bytes 638984 | tf_op jit(solution)/shard_map/ppermute | solution.py:20
  20.6 6.4 %collective-permute-start.1 = (bf16[416,256]{1,0:T(8,128)(2,1)S(1)}, bf16[416,256]{1,0:T(8,128)(2,1)S(1)}, u32[]{:S(2)}, u32[]{:S(2)}) collective-permute-start(bf16[416,256]{1,0:T(8,128)(2,1)S(1)} %broadcast_select_fusion), channel_id=1, source_target_pairs={{0,64},{32,96},{64,0},{96,32},{128,192},{160,224},{192,128},{224,1... | collective-permute-start | bytes 638984 | tf_op jit(solution)/shard_map/ppermute | solution.py:20
  27.8 2.4 collective-permute-done.1
  30.4 13.0 %collective-permute-start.2 = (bf16[416,256]{1,0:T(8,128)(2,1)S(1)}, bf16[416,256]{1,0:T(8,128)(2,1)S(1)}, u32[]{:S(2)}, u32[]{:S(2)}) collective-permute-start(bf16[416,256]{1,0:T(8,128)(2,1)S(1)} %broadcast_select_fusion.1), channel_id=1, source_target_pairs={{0,384},{32,416},{64,448},{96,480},{128,0},{160,32},{192,64},{224,... | collective-permute-start | bytes 638984 | tf_op jit(solution)/shard_map/ppermute | solution.py:36
  45.3 13.3 %collective-permute-done.2 = bf16[416,256]{1,0:T(8,128)(2,1)S(1)} collective-permute-done((bf16[416,256]{1,0:T(8,128)(2,1)S(1)}, bf16[416,256]{1,0:T(8,128)(2,1)S(1)}, u32[]{:S(2)}, u32[]{:S(2)}) %collective-permute-start.2) | collective-permute-done | bytes 213024 | tf_op jit(solution)/shard_map/ppermute | solution.py:36
  58.9 8.8 %collective-permute-start.4 = (bf16[208,256]{1,0:T(8,128)(2,1)S(1)}, bf16[208,256]{1,0:T(8,128)(2,1)S(1)}, u32[]{:S(2)}, u32[]{:S(2)}) collective-permute-start(bf16[208,256]{1,0:T(8,128)(2,1)S(1)} %get-tuple-element.49), channel_id=1, source_target_pairs={{0,128},{32,160},{64,192},{96,224},{128,256},{160,288},{192,320},{... | collective-permute-start | bytes 319496 | tf_op jit(solution)/shard_map/ppermute | solution.py:30
  67.6 4.1 %collective-permute-start.5 = (bf16[208,256]{1,0:T(8,128)(2,1)S(1)}, bf16[208,256]{1,0:T(8,128)(2,1)S(1)}, u32[]{:S(2)}, u32[]{:S(2)}) collective-permute-start(bf16[208,256]{1,0:T(8,128)(2,1)S(1)} %get-tuple-element.50), channel_id=1, source_target_pairs={{0,384},{32,416},{64,448},{96,480},{128,0},{160,32},{192,64},{224,... | collective-permute-start | bytes 319496 | tf_op jit(solution)/shard_map/ppermute | solution.py:31
  72.7 4.3 %collective-permute-done.5 = bf16[208,256]{1,0:T(8,128)(2,1)S(1)} collective-permute-done((bf16[208,256]{1,0:T(8,128)(2,1)S(1)}, bf16[208,256]{1,0:T(8,128)(2,1)S(1)}, u32[]{:S(2)}, u32[]{:S(2)}) %collective-permute-start.5) | collective-permute-done | bytes 106528 | tf_op jit(solution)/shard_map/ppermute | solution.py:31
  85.1 67.0 %all-gather.3.cloned.1.call-done = bf16[2,2048,322]{2,1,0:T(8,128)(2,1)} async-done(((bf16[2,64,322]{2,1,0:T(8,128)(2,1)}), bf16[2,2048,322]{2,1,0:T(8,128)(2,1)}) %all-gather.3.cloned.1.call-update) | async-done | bytes 2637840 | tf_op jit(solution)/shard_map/all_gather | solution.py:98
  155.7 2.0 fusion
  162.8 5.4 %all-to-all-start = ((bf16[32,2,4096]{2,1,0:T(2,128)(2,1)}), bf16[32,2,4096]{2,1,0:T(2,128)(2,1)}, u32[]{:S(2)}, u32[]{:S(2)}) async-start(bf16[32,2,4096]{2,1,0:T(2,128)(2,1)} %reshape.649), calls=%async_computation | async-start | bytes 1048576 | tf_op jit(solution)/shard_map/all_to_all | solution.py:45
  168.2 4.8 %select_reduce_fusion.2 = f32[4096]{0:T(1024)S(1)} fusion(f32[640,4096]{1,0:T(8,128)} %copy-done.1, pred[512]{0:T(512)(128)(4,1)S(1)} %lt.180), kind=kLoop, calls=%fused_computation.18 | loop fusion | flops 4190208 | bytes 8405504 | tf_op jit(solution)/shard_map/reduce_max | solution.py:145
  173.1 4.4 %fusion.6 = f32[4096]{0:T(1024)S(1)} fusion(f32[640,4096]{1,0:T(8,128)} %copy-done.1, f32[4096]{0:T(1024)S(1)} %select_reduce_fusion.2, pred[512]{0:T(512)(128)(4,1)S(1)} %lt.180), kind=kLoop, calls=%fused_computation.26 | loop fusion | flops 6287360 | bytes 8421888 | tf_op jit(solution)/shard_map/reduce_sum | solution.py:147
  179.4 5.2 %multiply_reduce_fusion = f32[4096]{0:T(1024)} fusion(f32[640,4096]{1,0:T(8,128)} %copy-done.1, f32[4096]{0:T(1024)S(1)} %select_reduce_fusion.2, pred[512]{0:T(512)(128)(4,1)S(1)} %lt.180, s32[4096]{0:T(1024)S(1)} %bitcast.137, bf16[640,64]{0,1:T(8,128)(2,1)} %copy-done.15), kind=kOutput, calls=%fused_computation.16 | convolution fusion | flops 277082112 | bytes 8503808 | tf_op jit(solution)/shard_map/dot_general | solution.py:144
  185.3 2.2 slice_convert_fusion.1
  188.8 3.2 %reshape.650 = bf16[32,64,2,64]{3,2,1,0:T(2,128)(2,1)S(1)} reshape(bf16[32,2,4096]{2,1,0:T(2,128)(2,1)} %all-to-all-done) | data formatting | bytes 1048576
  194.9 25.9 %all-gather.5.cloned.1.call-done = bf16[1,2,2048,256]{3,2,1,0:T(8,128)(2,1)} async-done(((bf16[1,2,64,256]{3,2,1,0:T(8,128)(2,1)}), bf16[1,2,2048,256]{3,2,1,0:T(8,128)(2,1)}) %all-gather.5.cloned.1.call-update) | async-done | bytes 2097168 | tf_op jit(solution)/shard_map/all_gather | solution.py:106
  220.8 7.2 %select_reduce_fusion.1 = (f32[4096]{0:T(1024)S(1)}, f32[512]{0:T(512)S(1)}, f32[4096,512]{0,1:T(8,128)}) fusion(pred[512]{0:T(512)(128)(4,1)S(1)} %copy-done.9, pred[4096]{0:T(1024)(128)(4,1)} %lt.184, bf16[4096,256]{1,0:T(8,128)(2,1)} %bitcast.145, bf16[512,256]{1,0:T(8,128)(2,1)} %bitcast.140), kind=kOutput, calls=%fused_computation.15 | convolution fusion | flops 1084222976 | bytes 10770944 | tf_op jit(solution)/shard_map/dot_general | solution.py:130
  228.0 6.4 %fusion.5 = (f32[4096]{0:T(1024)S(1)}, f32[512]{0:T(512)S(1)}) fusion(f32[4096,512]{0,1:T(8,128)} %get-tuple-element.69, f32[4096]{0:T(1024)S(1)} %get-tuple-element.22, pred[512]{0:T(512)(128)(4,1)S(1)} %copy-done.9, f32[512]{0:T(512)S(1)} %get-tuple-element.23, pred[4096]{0:T(1024)(128)(4,1)S(1)} %copy-done.4), kind=kLoop, calls=%fused_computation.24 | loop fusion | flops 12578304 | bytes 8430080 | tf_op jit(solution)/shard_map/reduce_sum | solution.py:147
  236.0 2.6 fusion.2
  239.8 6.2 %all-to-all-start.1 = ((f32[32,1,768]{2,1,0:T(1,128)}), f32[32,1,768]{2,1,0:T(1,128)S(1)}, u32[]{:S(2)}, u32[]{:S(2)}) async-start(f32[32,1,768]{2,1,0:T(1,128)} %reshape.651), calls=%async_computation.1 | async-start | bytes 196608 | tf_op jit(solution)/shard_map/all_to_all | solution.py:158
  247.2 6.9 %all-to-all-done.1 = f32[32,1,768]{2,1,0:T(1,128)S(1)} async-done(((f32[32,1,768]{2,1,0:T(1,128)}), f32[32,1,768]{2,1,0:T(1,128)S(1)}, u32[]{:S(2)}, u32[]{:S(2)}) %all-to-all-start.1) | async-done | bytes 98336 | tf_op jit(solution)/shard_map/all_to_all | solution.py:158
  256.6 12.0 %all-to-all-start.2 = ((f32[16,1,768]{2,1,0:T(1,128)}), f32[16,1,768]{2,1,0:T(1,128)S(1)}, u32[]{:S(2)}, u32[]{:S(2)}) async-start(f32[16,1,768]{2,1,0:T(1,128)} %reshape.653), calls=%async_computation.2 | async-start | bytes 98304 | tf_op jit(solution)/shard_map/all_to_all | solution.py:45
  274.3 8.0 %all-to-all-done.2 = f32[16,1,768]{2,1,0:T(1,128)S(1)} async-done(((f32[16,1,768]{2,1,0:T(1,128)}), f32[16,1,768]{2,1,0:T(1,128)S(1)}, u32[]{:S(2)}, u32[]{:S(2)}) %all-to-all-start.2) | async-done | bytes 49184 | tf_op jit(solution)/shard_map/all_to_all | solution.py:45
  (164 shorter events, 49.1 us)
Async XLA Ops:
  7.2 146.6 %copy-start.7 = (bf16[8,64,256]{2,1,0:T(8,128)(2,1)S(1)}, bf16[8,64,256]{2,1,0:T(8,128)(2,1)}, u32[]{:S(2)}) copy-start(bf16[8,64,256]{2,1,0:T(8,128)(2,1)} %param.10) | copy-start | bytes 786436
  7.2 144.9 %all-gather.3.cloned.1.call-start = ((), (), s32[]{:S(2)}) async-start(), calls=%async_computation.3 | async-start | bytes 3244032 | tf_op jit(solution)/shard_map/all_gather | solution.py:98
  13.2 7.3 %collective-permute-start = (bf16[416,256]{1,0:T(8,128)(2,1)S(1)}, bf16[416,256]{1,0:T(8,128)(2,1)S(1)}, u32[]{:S(2)}, u32[]{:S(2)}) collective-permute-start(bf16[416,256]{1,0:T(8,128)(2,1)S(1)} %pad_maximum_fusion), channel_id=1, source_target_pairs={{0,32},{32,0},{64,96},{96,64},{128,160},{160,128},{192,224},{224,1... | collective-permute-start | bytes 638984 | tf_op jit(solution)/shard_map/ppermute | solution.py:20
  20.6 9.6 %collective-permute-start.1 = (bf16[416,256]{1,0:T(8,128)(2,1)S(1)}, bf16[416,256]{1,0:T(8,128)(2,1)S(1)}, u32[]{:S(2)}, u32[]{:S(2)}) collective-permute-start(bf16[416,256]{1,0:T(8,128)(2,1)S(1)} %broadcast_select_fusion), channel_id=1, source_target_pairs={{0,64},{32,96},{64,0},{96,32},{128,192},{160,224},{192,128},{224,1... | collective-permute-start | bytes 638984 | tf_op jit(solution)/shard_map/ppermute | solution.py:20
  30.4 28.3 %collective-permute-start.2 = (bf16[416,256]{1,0:T(8,128)(2,1)S(1)}, bf16[416,256]{1,0:T(8,128)(2,1)S(1)}, u32[]{:S(2)}, u32[]{:S(2)}) collective-permute-start(bf16[416,256]{1,0:T(8,128)(2,1)S(1)} %broadcast_select_fusion.1), channel_id=1, source_target_pairs={{0,384},{32,416},{64,448},{96,480},{128,0},{160,32},{192,64},{224,... | collective-permute-start | bytes 638984 | tf_op jit(solution)/shard_map/ppermute | solution.py:36
  43.4 15.3 %collective-permute-start.3 = (bf16[416,256]{1,0:T(8,128)(2,1)S(1)}, bf16[416,256]{1,0:T(8,128)(2,1)S(1)}, u32[]{:S(2)}, u32[]{:S(2)}) collective-permute-start(bf16[416,256]{1,0:T(8,128)(2,1)S(1)} %broadcast_select_fusion.1), channel_id=1, source_target_pairs={{0,128},{32,160},{64,192},{96,224},{128,256},{160,288},{192,320},{... | collective-permute-start | bytes 638984 | tf_op jit(solution)/shard_map/ppermute | solution.py:35
  58.9 13.9 %collective-permute-start.4 = (bf16[208,256]{1,0:T(8,128)(2,1)S(1)}, bf16[208,256]{1,0:T(8,128)(2,1)S(1)}, u32[]{:S(2)}, u32[]{:S(2)}) collective-permute-start(bf16[208,256]{1,0:T(8,128)(2,1)S(1)} %get-tuple-element.49), channel_id=1, source_target_pairs={{0,128},{32,160},{64,192},{96,224},{128,256},{160,288},{192,320},{... | collective-permute-start | bytes 319496 | tf_op jit(solution)/shard_map/ppermute | solution.py:30
  67.6 9.4 %collective-permute-start.5 = (bf16[208,256]{1,0:T(8,128)(2,1)S(1)}, bf16[208,256]{1,0:T(8,128)(2,1)S(1)}, u32[]{:S(2)}, u32[]{:S(2)}) collective-permute-start(bf16[208,256]{1,0:T(8,128)(2,1)S(1)} %get-tuple-element.50), channel_id=1, source_target_pairs={{0,384},{32,416},{64,448},{96,480},{128,0},{160,32},{192,64},{224,... | collective-permute-start | bytes 319496 | tf_op jit(solution)/shard_map/ppermute | solution.py:31
  78.7 142.1 %all-gather.5.cloned.1.call-start = ((), (), s32[]{:S(2)}) async-start(), calls=%async_computation.4 | async-start | bytes 2162688 | tf_op jit(solution)/shard_map/all_gather | solution.py:106
  82.9 71.0 %copy-start.11 = (s32[2]{0:T(128)}, s32[2]{0:T(128)S(1)}, u32[]{:S(2)}) copy-start(s32[2]{0:T(128)S(1)} %get-tuple-element.57) | copy-start | bytes 28
  82.9 71.0 %copy-start.13 = (s32[2]{0:T(128)}, s32[2]{0:T(128)S(1)}, u32[]{:S(2)}) copy-start(s32[2]{0:T(128)S(1)} %get-tuple-element.58) | copy-start | bytes 28
  83.0 74.7 %copy-start.5 = (pred[4096]{0:T(1024)(128)(4,1)}, pred[4096]{0:T(1024)(128)(4,1)S(1)}, u32[]{:S(2)}) copy-start(pred[4096]{0:T(1024)(128)(4,1)S(1)} %lt.200) | copy-start | bytes 12292
  83.9 95.5 %copy-start.8 = (pred[512]{0:T(512)(128)(4,1)}, pred[512]{0:T(512)(128)(4,1)S(1)}, u32[]{:S(2)}) copy-start(pred[512]{0:T(512)(128)(4,1)S(1)} %lt.180) | copy-start | bytes 1540
  162.8 25.9 %all-to-all-start = ((bf16[32,2,4096]{2,1,0:T(2,128)(2,1)}), bf16[32,2,4096]{2,1,0:T(2,128)(2,1)}, u32[]{:S(2)}, u32[]{:S(2)}) async-start(bf16[32,2,4096]{2,1,0:T(2,128)(2,1)} %reshape.649), calls=%async_computation | async-start | bytes 1048576 | tf_op jit(solution)/shard_map/all_to_all | solution.py:45
  168.2 9.3 %copy-start.2 = (bf16[2,2048,322]{2,1,0:T(8,128)(2,1)S(1)}, bf16[2,2048,322]{2,1,0:T(8,128)(2,1)}, u32[]{:S(2)}) copy-start(bf16[2,2048,322]{2,1,0:T(8,128)(2,1)} %all-gather.3.cloned.1.call-done) | copy-start | bytes 7913476
  185.3 35.4 %copy-start.9 = (pred[512]{0:T(512)(128)(4,1)S(1)}, pred[512]{0:T(512)(128)(4,1)}, u32[]{:S(2)}) copy-start(pred[512]{0:T(512)(128)(4,1)} %copy-done.8) | copy-start | bytes 1540
  220.8 7.2 %copy-start.4 = (pred[4096]{0:T(1024)(128)(4,1)S(1)}, pred[4096]{0:T(1024)(128)(4,1)}, u32[]{:S(2)}) copy-start(pred[4096]{0:T(1024)(128)(4,1)} %lt.184) | copy-start | bytes 12292
  228.0 6.4 %copy-start.3 = (f32[4096,512]{0,1:T(8,128)S(1)}, f32[4096,512]{0,1:T(8,128)}, u32[]{:S(2)}) copy-start(f32[4096,512]{0,1:T(8,128)} %get-tuple-element.69) | copy-start | bytes 25165828
  235.9 10.2 %copy-start.6 = (pred[4096]{0:T(1024)(128)(4,1)S(1)}, pred[4096]{0:T(1024)(128)(4,1)}, u32[]{:S(2)}) copy-start(pred[4096]{0:T(1024)(128)(4,1)} %copy-done.5) | copy-start | bytes 12292
  235.9 47.4 %copy-start.12 = (s32[2]{0:T(128)S(1)}, s32[2]{0:T(128)}, u32[]{:S(2)}) copy-start(s32[2]{0:T(128)} %copy-done.11) | copy-start | bytes 28
  236.0 47.4 %copy-start.14 = (s32[2]{0:T(128)S(1)}, s32[2]{0:T(128)}, u32[]{:S(2)}) copy-start(s32[2]{0:T(128)} %copy-done.13) | copy-start | bytes 28
  236.0 47.4 %copy-start.17 = (s32[64]{0:T(128)S(1)}, s32[64]{0:T(128)}, u32[]{:S(2)}) copy-start(s32[64]{0:T(128)} %copy-done.16) | copy-start | bytes 772
  239.8 14.3 %all-to-all-start.1 = ((f32[32,1,768]{2,1,0:T(1,128)}), f32[32,1,768]{2,1,0:T(1,128)S(1)}, u32[]{:S(2)}, u32[]{:S(2)}) async-start(f32[32,1,768]{2,1,0:T(1,128)} %reshape.651), calls=%async_computation.1 | async-start | bytes 196608 | tf_op jit(solution)/shard_map/all_to_all | solution.py:158
  256.6 25.7 %all-to-all-start.2 = ((f32[16,1,768]{2,1,0:T(1,128)}), f32[16,1,768]{2,1,0:T(1,128)S(1)}, u32[]{:S(2)}, u32[]{:S(2)}) async-start(f32[16,1,768]{2,1,0:T(1,128)} %reshape.653), calls=%async_computation.2 | async-start | bytes 98304 | tf_op jit(solution)/shard_map/all_to_all | solution.py:45
  (6 other events, 14.1 us)
Sparse Core Ops, SparseCore 0:
  78.8 73.1 all-gather.2
  154.2 66.5 all-gather.4

commit v4 on v3

--- a/solution.py
+++ b/solution.py
@@ -94,17 +94,21 @@
     kf_ids = jnp.take(class_ids, flat_kf, axis=0).astype(jnp.bfloat16)
     kf_ids = kf_ids.reshape(total_steps, keyframes, pix_dev).transpose(1, 2, 0)
     step_keys = kf_keys.reshape(total_steps, keyframes, pix_dev, width)
-    packed = jnp.concatenate([step_keys[0], kf_values, kf_ids], axis=2)
-    gathered = lax.all_gather(packed, "space", axis=1, tiled=True)
-    mem_keys = [gathered[:, :, :width].reshape(mem_width, width)]
-    mem_values = gathered[:, :, width:width + channels].reshape(mem_width, channels)
-    mem_ids = [
-        gathered[:, :, width + channels + s].reshape(mem_width).astype(jnp.int32)
+    packed = jnp.concatenate(
+        [step_keys[s] for s in range(total_steps)] + [kf_values, kf_ids], axis=2
+    )
+    gathered = gather_all(packed, "space").transpose(1, 0, 2, 3)
+    gathered = gathered.reshape(keyframes, pix_all, packed.shape[2])
+    mem_keys = [
+        gathered[:, :, s * width:(s + 1) * width].reshape(mem_width, width)
         for s in range(total_steps)
     ]
-    rest_keys, unused = lax.optimization_barrier((step_keys[1:], gathered))
-    rest_keys = lax.all_gather(rest_keys, "space", axis=2, tiled=True)
-    mem_keys += [rest_keys[s].reshape(mem_width, width) for s in range(total_steps - 1)]
+    base = total_steps * width
+    mem_values = gathered[:, :, base:base + channels].reshape(mem_width, channels)
+    mem_ids = [
+        gathered[:, :, base + channels + s].reshape(mem_width).astype(jnp.int32)
+        for s in range(total_steps)
+    ]
 
     extra_queries = kf_queries.reshape(later, pix_dev, width)
     extra_valid = pixel_ids[None, :] < jnp.take(valid_pixels, flat_kf[keyframes:])[:, None]

time: 292 us -> 314 us (1.075)
  waiting for transfers between devices: 130 us -> 153 us
  starting transfers between devices: 61.9 us -> 76.7 us
  between operations: 16 us -> 2.54 us
  other arithmetic: 30.6 us -> 26.2 us
    all_to_all x2 -> x3, waiting for transfers between devices: 8.03 us -> 124 us  [gather_all(): return lax.all_to_all(spread, axis, 0, 0, tiled=True)]
    all_gather x2 -> x0, waiting for transfers between devices: 92.8 us -> none  [the longest x1 67 us: body(): gathered = lax.all_gather(packed, 'space', axis=1, tiled=True)]
    all_to_all x2 -> x3, starting transfers between devices: 17.4 us -> 32.3 us  [gather_all(): return lax.all_to_all(spread, axis, 0, 0, tiled=True)]
    reduce_sum x1, other arithmetic: 2.01 us -> 6.14 us  [body(): total = jnp.sum(weights, axis=1, keepdims=True)]
    dot_general x2, matrix products: 3.34 us -> 6.87 us  [body(): jnp.dot(weights.astype(jnp.bfloat16), mem_values, preferred_element_type=...]
    reduce_max x1, other arithmetic: 4.8 us -> 1.37 us  [body(): col_max = jnp.max(jnp.where(row_valid[:, None], own_scores, LOWEST), axis=0)]
    reduce_sum x2, other arithmetic: 10.8 us -> 7.44 us  [body(): col_total = jnp.sum(expo, axis=0)]
    transpose x0 -> x2, local copies, waits for them, and re-layouts: none -> 3.15 us  [the longest x1 3.02 us: body(): gathered = gather_all(packed, 'space').transpose(1, 0, 2, 3)]
  transfers between devices with their start and end apart: 11 -> 10, of which waited for: 9 -> 9; matrix products, arithmetic and copies ran while one was open for 18% -> 8% of each run, Pallas kernels for 0% -> 0%
where the time goes in v4:
time: 314 us; the launch traced here: 313 us
  waiting for transfers between devices  153 us (49%)
  starting transfers between devices  76.7 us (24%)
  local copies, waits for them, and re-layouts  34.5 us (11%)
  other arithmetic  26.2 us (8%)
  matrix products  20.3 us (6%)
    all_to_all x3, waiting for transfers between devices, gather_all(): return lax.all_to_all(spread, axis, 0, 0, tiled=True)  124 us
    all_to_all x3, starting transfers between devices, gather_all(): return lax.all_to_all(spread, axis, 0, 0, tiled=True)  32.3 us
    ppermute x1, starting transfers between devices, broadcast_tm(): got_b = lax.ppermute(value, axis, behind)  13 us
    ppermute x1, waiting for transfers between devices, broadcast_tm(): got_b = lax.ppermute(value, axis, behind)  12.7 us
    unnamed x31, local copies, waits for them, and re-layouts  11 us
    ppermute x2, starting transfers between devices, broadcast_tm(): got = lax.ppermute(value, axis, pairs)  10.4 us
    ppermute x1, starting transfers between devices, broadcast_tm(): got_a = lax.ppermute(value[:half], axis, ahead)  8.76 us
    dot_general x2, matrix products, body(): lax.dot_general(q, mem_keys[step], (((1,), (1,)), ((), ())), preferred_el...  7.89 us
  transfers between devices with their start and end apart: 10, of which 9 were waited for; matrix products, arithmetic and copies ran while one was open for 8% of the time, Pallas kernels for 0%

profile of v4, /device:TPU:1, one launch (start us, length us, event | category | flops | bytes accessed | tf_op | source)
XLA Modules:
  0.0 313.1 jit_solution(2839852621653130229)
XLA Ops:
  6.6 4.0 %collective-permute-start = (bf16[416,256]{1,0:T(8,128)(2,1)S(1)}, bf16[416,256]{1,0:T(8,128)(2,1)S(1)}, u32[]{:S(2)}, u32[]{:S(2)}) collective-permute-start(bf16[416,256]{1,0:T(8,128)(2,1)S(1)} %pad_maximum_fusion), channel_id=1, source_target_pairs={{0,32},{32,0},{64,96},{96,64},{128,160},{160,128},{192,224},{224,1... | collective-permute-start | bytes 638984 | tf_op jit(solution)/shard_map/ppermute | solution.py:20
  14.0 6.4 %collective-permute-start.1 = (bf16[416,256]{1,0:T(8,128)(2,1)S(1)}, bf16[416,256]{1,0:T(8,128)(2,1)S(1)}, u32[]{:S(2)}, u32[]{:S(2)}) collective-permute-start(bf16[416,256]{1,0:T(8,128)(2,1)S(1)} %broadcast_select_fusion), channel_id=1, source_target_pairs={{0,64},{32,96},{64,0},{96,32},{128,192},{160,224},{192,128},{224,1... | collective-permute-start | bytes 638984 | tf_op jit(solution)/shard_map/ppermute | solution.py:20
  20.4 3.2 %collective-permute-done.1 = bf16[416,256]{1,0:T(8,128)(2,1)S(1)} collective-permute-done((bf16[416,256]{1,0:T(8,128)(2,1)S(1)}, bf16[416,256]{1,0:T(8,128)(2,1)S(1)}, u32[]{:S(2)}, u32[]{:S(2)}) %collective-permute-start.1) | collective-permute-done | bytes 213024 | tf_op jit(solution)/shard_map/ppermute | solution.py:20
  23.8 13.0 %collective-permute-start.2 = (bf16[416,256]{1,0:T(8,128)(2,1)S(1)}, bf16[416,256]{1,0:T(8,128)(2,1)S(1)}, u32[]{:S(2)}, u32[]{:S(2)}) collective-permute-start(bf16[416,256]{1,0:T(8,128)(2,1)S(1)} %broadcast_select_fusion.1), channel_id=1, source_target_pairs={{0,384},{32,416},{64,448},{96,480},{128,0},{160,32},{192,64},{224,... | collective-permute-start | bytes 638984 | tf_op jit(solution)/shard_map/ppermute | solution.py:36
  39.4 12.7 %collective-permute-done.2 = bf16[416,256]{1,0:T(8,128)(2,1)S(1)} collective-permute-done((bf16[416,256]{1,0:T(8,128)(2,1)S(1)}, bf16[416,256]{1,0:T(8,128)(2,1)S(1)}, u32[]{:S(2)}, u32[]{:S(2)}) %collective-permute-start.2) | collective-permute-done | bytes 213024 | tf_op jit(solution)/shard_map/ppermute | solution.py:36
  52.3 8.8 %collective-permute-start.4 = (bf16[208,256]{1,0:T(8,128)(2,1)S(1)}, bf16[208,256]{1,0:T(8,128)(2,1)S(1)}, u32[]{:S(2)}, u32[]{:S(2)}) collective-permute-start(bf16[208,256]{1,0:T(8,128)(2,1)S(1)} %get-tuple-element.49), channel_id=1, source_target_pairs={{0,128},{32,160},{64,192},{96,224},{128,256},{160,288},{192,320},{... | collective-permute-start | bytes 319496 | tf_op jit(solution)/shard_map/ppermute | solution.py:30
  61.0 4.1 %collective-permute-start.5 = (bf16[208,256]{1,0:T(8,128)(2,1)S(1)}, bf16[208,256]{1,0:T(8,128)(2,1)S(1)}, u32[]{:S(2)}, u32[]{:S(2)}) collective-permute-start(bf16[208,256]{1,0:T(8,128)(2,1)S(1)} %get-tuple-element.50), channel_id=1, source_target_pairs={{0,384},{32,416},{64,448},{96,480},{128,0},{160,32},{192,64},{224,... | collective-permute-start | bytes 319496 | tf_op jit(solution)/shard_map/ppermute | solution.py:31
  66.1 4.3 %collective-permute-done.5 = bf16[208,256]{1,0:T(8,128)(2,1)S(1)} collective-permute-done((bf16[208,256]{1,0:T(8,128)(2,1)S(1)}, bf16[208,256]{1,0:T(8,128)(2,1)S(1)}, u32[]{:S(2)}, u32[]{:S(2)}) %collective-permute-start.5) | collective-permute-done | bytes 106528 | tf_op jit(solution)/shard_map/ppermute | solution.py:31
  70.9 3.1 broadcast_in_dim.279
  74.0 15.1 %all-to-all-start = ((bf16[32,2,64,578]{3,2,1,0:T(8,128)(2,1)}), bf16[32,2,64,578]{3,2,1,0:T(8,128)(2,1)}, u32[]{:S(2)}, u32[]{:S(2)}) async-start(bf16[32,2,64,578]{3,2,1,0:T(8,128)(2,1)} %broadcast_in_dim.279), calls=%async_computation | async-start | bytes 10485760 | tf_op jit(solution)/shard_map/all_to_all | solution.py:45
  91.1 114.1 %all-to-all-done = bf16[32,2,64,578]{3,2,1,0:T(8,128)(2,1)} async-done(((bf16[32,2,64,578]{3,2,1,0:T(8,128)(2,1)}), bf16[32,2,64,578]{3,2,1,0:T(8,128)(2,1)}, u32[]{:S(2)}, u32[]{:S(2)}) %all-to-all-start) | async-done | bytes 4735008 | tf_op jit(solution)/shard_map/all_to_all | solution.py:45
  205.2 3.0 copy.60
  215.1 2.6 copy-done.2
  219.7 6.1 %fusion = f32[640]{0:T(1024)S(1)} fusion(f32[640,4096]{1,0:T(8,128)} %copy-done.2, f32[640]{0:T(1024)S(1)} %get-tuple-element.67, pred[4096]{0:T(1024)(128)(4,1)S(1)} %lt.200), kind=kLoop, calls=%fused_computation.10 | loop fusion | flops 7863680 | bytes 10494976 | tf_op jit(solution)/shard_map/reduce_sum | solution.py:140
  228.5 2.9 multiply_reduce_fusion
  234.1 6.1 %all-to-all-start.1 = ((bf16[32,2,4096]{2,1,0:T(2,128)(2,1)}), bf16[32,2,4096]{2,1,0:T(2,128)(2,1)S(1)}, u32[]{:S(2)}, u32[]{:S(2)}) async-start(bf16[32,2,4096]{2,1,0:T(2,128)(2,1)} %reshape.659), calls=%async_computation.1 | async-start | bytes 1048576 | tf_op jit(solution)/shard_map/all_to_all | solution.py:45
  240.3 6.1 %select_reduce_fusion.1 = (f32[4096]{0:T(1024)S(1)}, f32[512]{0:T(512)S(1)}, f32[4096,512]{0,1:T(8,128)}) fusion(pred[512]{0:T(512)(128)(4,1)S(1)} %lt.180, pred[4096]{0:T(1024)(128)(4,1)S(1)} %lt.184, bf16[4096,256]{1,0:T(8,128)(2,1)} %bitcast.133, bf16[512,256]{1,0:T(8,128)(2,1)S(1)} %bitcast.150), kind=kOutput, calls=%fused_computation.15 | convolution fusion | flops 1084222976 | bytes 10770944 | tf_op jit(solution)/shard_map/dot_general | solution.py:134
  246.4 5.7 %fusion.5 = (f32[4096]{0:T(1024)S(1)}, f32[512]{0:T(512)S(1)}) fusion(f32[4096,512]{0,1:T(8,128)} %get-tuple-element.69, f32[4096]{0:T(1024)S(1)} %get-tuple-element.20, pred[512]{0:T(512)(128)(4,1)S(1)} %lt.180, f32[512]{0:T(512)S(1)} %get-tuple-element.21, pred[4096]{0:T(1024)(128)(4,1)S(1)} %lt.184), kind=kLoop, calls=%fused_computation.24 | loop fusion | flops 12578304 | bytes 8430080 | tf_op jit(solution)/shard_map/reduce_sum | solution.py:151
  252.2 2.6 slice_convert_fusion.1
  260.3 5.0 %fusion.19 = bf16[512,64]{0,1:T(8,128)(2,1)S(1)} fusion(bf16[4096,64]{0,1:T(8,128)(2,1)S(1)} %reshape.567, f32[4096,512]{0,1:T(8,128)} %get-tuple-element.69, f32[512]{0:T(512)S(1)} %get-tuple-element.21, pred[4096]{0:T(1024)(128)(4,1)S(1)} %lt.184, f32[512]{0:T(512)S(1)} %get-tuple-element.19, pred[512]{0:T(512)(128)(4,1)S(1)} %lt.180), kind=kOutput, calls=%fused_computation.37 | convolution fusion | flops 274825216 | bytes 8987136 | tf_op jit(solution)/shard_map/dot_general | solution.py:142
  269.8 6.2 %all-to-all-start.2 = ((f32[32,1,768]{2,1,0:T(1,128)}), f32[32,1,768]{2,1,0:T(1,128)S(1)}, u32[]{:S(2)}, u32[]{:S(2)}) async-start(f32[32,1,768]{2,1,0:T(1,128)} %reshape.661), calls=%async_computation.2 | async-start | bytes 196608 | tf_op jit(solution)/shard_map/all_to_all | solution.py:162
  277.2 6.9 %all-to-all-done.2 = f32[32,1,768]{2,1,0:T(1,128)S(1)} async-done(((f32[32,1,768]{2,1,0:T(1,128)}), f32[32,1,768]{2,1,0:T(1,128)S(1)}, u32[]{:S(2)}, u32[]{:S(2)}) %all-to-all-start.2) | async-done | bytes 98336 | tf_op jit(solution)/shard_map/all_to_all | solution.py:162
  286.6 11.1 %all-to-all-start.3 = ((f32[16,1,768]{2,1,0:T(1,128)}), f32[16,1,768]{2,1,0:T(1,128)S(1)}, u32[]{:S(2)}, u32[]{:S(2)}) async-start(f32[16,1,768]{2,1,0:T(1,128)} %reshape.663), calls=%async_computation.3 | async-start | bytes 98304 | tf_op jit(solution)/shard_map/all_to_all | solution.py:45
  303.4 8.0 %all-to-all-done.3 = f32[16,1,768]{2,1,0:T(1,128)S(1)} async-done(((f32[16,1,768]{2,1,0:T(1,128)}), f32[16,1,768]{2,1,0:T(1,128)S(1)}, u32[]{:S(2)}, u32[]{:S(2)}) %all-to-all-start.3) | async-done | bytes 49184 | tf_op jit(solution)/shard_map/all_to_all | solution.py:45
  (143 shorter events, 49.3 us)
Async XLA Ops:
  0.6 5.3 %copy-start = (bf16[8,64,256]{2,1,0:T(8,128)(2,1)S(1)}, bf16[8,64,256]{2,1,0:T(8,128)(2,1)}, u32[]{:S(2)}) copy-start(bf16[8,64,256]{2,1,0:T(8,128)(2,1)} %param.11) | copy-start | bytes 786436
  6.6 7.3 %collective-permute-start = (bf16[416,256]{1,0:T(8,128)(2,1)S(1)}, bf16[416,256]{1,0:T(8,128)(2,1)S(1)}, u32[]{:S(2)}, u32[]{:S(2)}) collective-permute-start(bf16[416,256]{1,0:T(8,128)(2,1)S(1)} %pad_maximum_fusion), channel_id=1, source_target_pairs={{0,32},{32,0},{64,96},{96,64},{128,160},{160,128},{192,224},{224,1... | collective-permute-start | bytes 638984 | tf_op jit(solution)/shard_map/ppermute | solution.py:20
  14.0 9.6 %collective-permute-start.1 = (bf16[416,256]{1,0:T(8,128)(2,1)S(1)}, bf16[416,256]{1,0:T(8,128)(2,1)S(1)}, u32[]{:S(2)}, u32[]{:S(2)}) collective-permute-start(bf16[416,256]{1,0:T(8,128)(2,1)S(1)} %broadcast_select_fusion), channel_id=1, source_target_pairs={{0,64},{32,96},{64,0},{96,32},{128,192},{160,224},{192,128},{224,1... | collective-permute-start | bytes 638984 | tf_op jit(solution)/shard_map/ppermute | solution.py:20
  23.8 28.3 %collective-permute-start.2 = (bf16[416,256]{1,0:T(8,128)(2,1)S(1)}, bf16[416,256]{1,0:T(8,128)(2,1)S(1)}, u32[]{:S(2)}, u32[]{:S(2)}) collective-permute-start(bf16[416,256]{1,0:T(8,128)(2,1)S(1)} %broadcast_select_fusion.1), channel_id=1, source_target_pairs={{0,384},{32,416},{64,448},{96,480},{128,0},{160,32},{192,64},{224,... | collective-permute-start | bytes 638984 | tf_op jit(solution)/shard_map/ppermute | solution.py:36
  36.8 15.3 %collective-permute-start.3 = (bf16[416,256]{1,0:T(8,128)(2,1)S(1)}, bf16[416,256]{1,0:T(8,128)(2,1)S(1)}, u32[]{:S(2)}, u32[]{:S(2)}) collective-permute-start(bf16[416,256]{1,0:T(8,128)(2,1)S(1)} %broadcast_select_fusion.1), channel_id=1, source_target_pairs={{0,128},{32,160},{64,192},{96,224},{128,256},{160,288},{192,320},{... | collective-permute-start | bytes 638984 | tf_op jit(solution)/shard_map/ppermute | solution.py:35
  52.3 13.9 %collective-permute-start.4 = (bf16[208,256]{1,0:T(8,128)(2,1)S(1)}, bf16[208,256]{1,0:T(8,128)(2,1)S(1)}, u32[]{:S(2)}, u32[]{:S(2)}) collective-permute-start(bf16[208,256]{1,0:T(8,128)(2,1)S(1)} %get-tuple-element.49), channel_id=1, source_target_pairs={{0,128},{32,160},{64,192},{96,224},{128,256},{160,288},{192,320},{... | collective-permute-start | bytes 319496 | tf_op jit(solution)/shard_map/ppermute | solution.py:30
  61.0 9.4 %collective-permute-start.5 = (bf16[208,256]{1,0:T(8,128)(2,1)S(1)}, bf16[208,256]{1,0:T(8,128)(2,1)S(1)}, u32[]{:S(2)}, u32[]{:S(2)}) collective-permute-start(bf16[208,256]{1,0:T(8,128)(2,1)S(1)} %get-tuple-element.50), channel_id=1, source_target_pairs={{0,384},{32,416},{64,448},{96,480},{128,0},{160,32},{192,64},{224,... | collective-permute-start | bytes 319496 | tf_op jit(solution)/shard_map/ppermute | solution.py:31
  70.6 18.5 %copy-start.6 = (s32[2,2]{1,0:T(2,128)S(1)}, s32[2,2]{1,0:T(2,128)}, u32[]{:S(2)}) copy-start(s32[2,2]{1,0:T(2,128)} %param.15) | copy-start | bytes 52
  70.6 18.5 %copy-start.1 = (s32[128]{0:T(128)S(1)}, s32[128]{0:T(128)}, u32[]{:S(2)}) copy-start(s32[128]{0:T(128)} %param.14) | copy-start | bytes 1540
  74.0 131.2 %all-to-all-start = ((bf16[32,2,64,578]{3,2,1,0:T(8,128)(2,1)}), bf16[32,2,64,578]{3,2,1,0:T(8,128)(2,1)}, u32[]{:S(2)}, u32[]{:S(2)}) async-start(bf16[32,2,64,578]{3,2,1,0:T(8,128)(2,1)} %broadcast_in_dim.279), calls=%async_computation | async-start | bytes 10485760 | tf_op jit(solution)/shard_map/all_to_all | solution.py:45
  208.2 3.6 %copy-start.4 = (bf16[2,32,64,578]{3,2,1,0:T(8,128)(2,1)}, bf16[2,32,64,578]{3,2,1,0:T(8,128)(2,1)S(1)}, u32[]{:S(2)}) copy-start(bf16[2,32,64,578]{3,2,1,0:T(8,128)(2,1)S(1)} %copy.60) | copy-start | bytes 14204932
  208.3 3.6 %copy-start.5 = (bf16[8,64,256]{2,1,0:T(8,128)(2,1)S(1)}, bf16[8,64,256]{2,1,0:T(8,128)(2,1)}, u32[]{:S(2)}) copy-start(bf16[8,64,256]{2,1,0:T(8,128)(2,1)} %param.10) | copy-start | bytes 786436
  213.7 4.0 %copy-start.2 = (f32[640,4096]{1,0:T(8,128)}, f32[640,4096]{1,0:T(8,128)S(1)}, u32[]{:S(2)}) copy-start(f32[640,4096]{1,0:T(8,128)S(1)} %get-tuple-element.68) | copy-start | bytes 31457284
  219.7 7.0 %copy-start.3 = (f32[640,4096]{1,0:T(8,128)S(1)}, f32[640,4096]{1,0:T(8,128)}, u32[]{:S(2)}) copy-start(f32[640,4096]{1,0:T(8,128)} %copy-done.2) | copy-start | bytes 31457284
  234.1 22.6 %all-to-all-start.1 = ((bf16[32,2,4096]{2,1,0:T(2,128)(2,1)}), bf16[32,2,4096]{2,1,0:T(2,128)(2,1)S(1)}, u32[]{:S(2)}, u32[]{:S(2)}) async-start(bf16[32,2,4096]{2,1,0:T(2,128)(2,1)} %reshape.659), calls=%async_computation.1 | async-start | bytes 1048576 | tf_op jit(solution)/shard_map/all_to_all | solution.py:45
  260.2 5.0 %slice-start = ((s8[8388608]{0:T(1024)(128)(4,1)}), s8[4194304]{0:T(1024)(128)(4,1)S(1)}, s32[]{:S(2)}) async-start(s8[8388608]{0:T(1024)(128)(4,1)} %bitcast.131), calls=%async_computation.4 | async-start | bytes 8388608
  260.3 5.8 %slice-start.1 = ((s8[8388608]{0:T(1024)(128)(4,1)}), s8[4194304]{0:T(1024)(128)(4,1)S(1)}, s32[]{:S(2)}) async-start(s8[8388608]{0:T(1024)(128)(4,1)} %bitcast.131), calls=%async_computation.5 | async-start | bytes 8388608
  269.8 14.3 %all-to-all-start.2 = ((f32[32,1,768]{2,1,0:T(1,128)}), f32[32,1,768]{2,1,0:T(1,128)S(1)}, u32[]{:S(2)}, u32[]{:S(2)}) async-start(f32[32,1,768]{2,1,0:T(1,128)} %reshape.661), calls=%async_computation.2 | async-start | bytes 196608 | tf_op jit(solution)/shard_map/all_to_all | solution.py:162
  286.6 24.8 %all-to-all-start.3 = ((f32[16,1,768]{2,1,0:T(1,128)}), f32[16,1,768]{2,1,0:T(1,128)S(1)}, u32[]{:S(2)}, u32[]{:S(2)}) async-start(f32[16,1,768]{2,1,0:T(1,128)} %reshape.663), calls=%async_computation.3 | async-start | bytes 98304 | tf_op jit(solution)/shard_map/all_to_all | solution.py:45

commit v5 on v4

--- a/solution.py
+++ b/solution.py
@@ -97,8 +97,7 @@
     packed = jnp.concatenate(
         [step_keys[s] for s in range(total_steps)] + [kf_values, kf_ids], axis=2
     )
-    gathered = gather_all(packed, "space").transpose(1, 0, 2, 3)
-    gathered = gathered.reshape(keyframes, pix_all, packed.shape[2])
+    gathered = lax.all_gather(packed, "space", axis=1, tiled=True)
     mem_keys = [
         gathered[:, :, s * width:(s + 1) * width].reshape(mem_width, width)
         for s in range(total_steps)

time: 314 us -> 271 us (0.86)
  waiting for transfers between devices: 153 us -> 110 us
  starting transfers between devices: 76.7 us -> 62.7 us
  between operations: 2.54 us -> 15.9 us
  other arithmetic: 26.2 us -> 30 us
    all_to_all x3 -> x2, waiting for transfers between devices: 124 us -> 9.57 us  [gather_all(): return lax.all_to_all(spread, axis, 0, 0, tiled=True)]
    all_gather x0 -> x1, waiting for transfers between devices: none -> 71.2 us  [body(): gathered = lax.all_gather(packed, 'space', axis=1, tiled=True)]
    all_to_all x3 -> x2, starting transfers between devices: 32.3 us -> 18.3 us  [gather_all(): return lax.all_to_all(spread, axis, 0, 0, tiled=True)]
    transpose x2 -> x0, local copies, waits for them, and re-layouts: 3.15 us -> none  [the longest x1 3.02 us: body(): gathered = gather_all(packed, 'space').transpose(1, 0, 2, 3)]
    unnamed x31 -> x25, local copies, waits for them, and re-layouts: 11 us -> 10.2 us
  transfers between devices with their start and end apart: 10 -> 10, of which waited for: 9 -> 9; matrix products, arithmetic and copies ran while one was open for 8% -> 11% of each run, Pallas kernels for 0% -> 0%
where the time goes in v5:
time: 271 us; the launch traced here: 270 us
  waiting for transfers between devices  110 us (41%)
  starting transfers between devices  62.7 us (23%)
  local copies, waits for them, and re-layouts  31.6 us (12%)
  other arithmetic  30 us (11%)
  matrix products  20.1 us (7%)
  between operations  15.9 us (6%)
    all_gather x1, waiting for transfers between devices, body(): gathered = lax.all_gather(packed, 'space', axis=1, tiled=True)  71.2 us
    all_to_all x2, starting transfers between devices, gather_all(): return lax.all_to_all(spread, axis, 0, 0, tiled=True)  18.3 us
    ppermute x1, waiting for transfers between devices, broadcast_tm(): got_b = lax.ppermute(value, axis, behind)  13.3 us
    ppermute x1, starting transfers between devices, broadcast_tm(): got_b = lax.ppermute(value, axis, behind)  13 us
    ppermute x2, starting transfers between devices, broadcast_tm(): got = lax.ppermute(value, axis, pairs)  10.4 us
    unnamed x25, local copies, waits for them, and re-layouts  10.2 us
    all_to_all x2, waiting for transfers between devices, gather_all(): return lax.all_to_all(spread, axis, 0, 0, tiled=True)  9.57 us
    ppermute x1, starting transfers between devices, broadcast_tm(): got_a = lax.ppermute(value[:half], axis, ahead)  8.76 us
  transfers between devices with their start and end apart: 10, of which 9 were waited for; matrix products, arithmetic and copies ran while one was open for 11% of the time, Pallas kernels for 0%

profile of v5, /device:TPU:1, one launch (start us, length us, event | category | flops | bytes accessed | tf_op | source)
XLA Modules:
  0.0 270.0 jit_solution(14113356932138235534)
XLA Ops:
  13.2 4.0 %collective-permute-start = (bf16[416,256]{1,0:T(8,128)(2,1)S(1)}, bf16[416,256]{1,0:T(8,128)(2,1)S(1)}, u32[]{:S(2)}, u32[]{:S(2)}) collective-permute-start(bf16[416,256]{1,0:T(8,128)(2,1)S(1)} %pad_maximum_fusion), channel_id=1, source_target_pairs={{0,32},{32,0},{64,96},{96,64},{128,160},{160,128},{192,224},{224,1... | collective-permute-start | bytes 638984 | tf_op jit(solution)/shard_map/ppermute | solution.py:20
  20.6 6.4 %collective-permute-start.1 = (bf16[416,256]{1,0:T(8,128)(2,1)S(1)}, bf16[416,256]{1,0:T(8,128)(2,1)S(1)}, u32[]{:S(2)}, u32[]{:S(2)}) collective-permute-start(bf16[416,256]{1,0:T(8,128)(2,1)S(1)} %broadcast_select_fusion), channel_id=1, source_target_pairs={{0,64},{32,96},{64,0},{96,32},{128,192},{160,224},{192,128},{224,1... | collective-permute-start | bytes 638984 | tf_op jit(solution)/shard_map/ppermute | solution.py:20
  27.8 2.4 collective-permute-done.1
  30.4 13.0 %collective-permute-start.2 = (bf16[416,256]{1,0:T(8,128)(2,1)S(1)}, bf16[416,256]{1,0:T(8,128)(2,1)S(1)}, u32[]{:S(2)}, u32[]{:S(2)}) collective-permute-start(bf16[416,256]{1,0:T(8,128)(2,1)S(1)} %broadcast_select_fusion.1), channel_id=1, source_target_pairs={{0,384},{32,416},{64,448},{96,480},{128,0},{160,32},{192,64},{224,... | collective-permute-start | bytes 638984 | tf_op jit(solution)/shard_map/ppermute | solution.py:36
  45.3 13.3 %collective-permute-done.2 = bf16[416,256]{1,0:T(8,128)(2,1)S(1)} collective-permute-done((bf16[416,256]{1,0:T(8,128)(2,1)S(1)}, bf16[416,256]{1,0:T(8,128)(2,1)S(1)}, u32[]{:S(2)}, u32[]{:S(2)}) %collective-permute-start.2) | collective-permute-done | bytes 213024 | tf_op jit(solution)/shard_map/ppermute | solution.py:36
  58.9 8.8 %collective-permute-start.4 = (bf16[208,256]{1,0:T(8,128)(2,1)S(1)}, bf16[208,256]{1,0:T(8,128)(2,1)S(1)}, u32[]{:S(2)}, u32[]{:S(2)}) collective-permute-start(bf16[208,256]{1,0:T(8,128)(2,1)S(1)} %get-tuple-element.49), channel_id=1, source_target_pairs={{0,128},{32,160},{64,192},{96,224},{128,256},{160,288},{192,320},{... | collective-permute-start | bytes 319496 | tf_op jit(solution)/shard_map/ppermute | solution.py:30
  67.6 4.1 %collective-permute-start.5 = (bf16[208,256]{1,0:T(8,128)(2,1)S(1)}, bf16[208,256]{1,0:T(8,128)(2,1)S(1)}, u32[]{:S(2)}, u32[]{:S(2)}) collective-permute-start(bf16[208,256]{1,0:T(8,128)(2,1)S(1)} %get-tuple-element.50), channel_id=1, source_target_pairs={{0,384},{32,416},{64,448},{96,480},{128,0},{160,32},{192,64},{224,... | collective-permute-start | bytes 319496 | tf_op jit(solution)/shard_map/ppermute | solution.py:31
  72.7 4.3 %collective-permute-done.5 = bf16[208,256]{1,0:T(8,128)(2,1)S(1)} collective-permute-done((bf16[208,256]{1,0:T(8,128)(2,1)S(1)}, bf16[208,256]{1,0:T(8,128)(2,1)S(1)}, u32[]{:S(2)}, u32[]{:S(2)}) %collective-permute-start.5) | collective-permute-done | bytes 106528 | tf_op jit(solution)/shard_map/ppermute | solution.py:31
  83.5 71.2 %all-gather.2.cloned.1.call-done = bf16[2,2048,578]{2,1,0:T(8,128)(2,1)} async-done(((bf16[2,64,578]{2,1,0:T(8,128)(2,1)}), bf16[2,2048,578]{2,1,0:T(8,128)(2,1)}) %all-gather.2.cloned.1.call-update) | async-done | bytes 4734992 | tf_op jit(solution)/shard_map/all_gather | solution.py:100
  154.7 3.8 %fusion.67 = (bf16[2,2048,256]{2,1,0:T(8,128)(2,1)}, bf16[2,2048,256]{2,1,0:T(8,128)(2,1)S(1)}) fusion(bf16[2,2048,578]{2,1,0:T(8,128)(2,1)} %all-gather.2.cloned.1.call-done), kind=kLoop, calls=%fused_computation.169 | loop fusion | bytes 8388608 | tf_op jit(solution)/shard_map/slice | solution.py:102
  161.7 2.6 copy-done.1
  166.3 6.1 %fusion = f32[640]{0:T(1024)S(1)} fusion(f32[640,4096]{1,0:T(8,128)} %copy-done.1, f32[640]{0:T(1024)S(1)} %get-tuple-element.67, pred[4096]{0:T(1024)(128)(4,1)S(1)} %lt.200), kind=kLoop, calls=%fused_computation.10 | loop fusion | flops 7863680 | bytes 10494976 | tf_op jit(solution)/shard_map/reduce_sum | solution.py:139
  172.4 3.4 %fusion.35 = (s32[2,2048]{1,0:T(2,128)S(1)}, s32[2,2048]{1,0:T(2,128)S(1)}) fusion(bf16[2,2048,578]{2,1,0:T(8,128)(2,1)} %all-gather.2.cloned.1.call-done), kind=kLoop, calls=%fused_computation.49 | loop fusion | flops 8192 | bytes 49152 | tf_op jit(solution)/shard_map/convert_element_type | solution.py:108
  177.8 2.7 %multiply_reduce_fusion = f32[4096]{0:T(1024)S(1)} fusion(f32[640,4096]{1,0:T(8,128)S(1)} %copy-done.2, f32[4096]{0:T(1024)S(1)} %select_reduce_fusion.2, pred[512]{0:T(512)(128)(4,1)S(1)} %lt.180, s32[4096]{0:T(1024)S(1)} %bitcast.140, bf16[640,64]{0,1:T(8,128)(2,1)S(1)} %fusion.28), kind=kOutput, calls=%fused_computation.16 | convolution fusion | flops 277082112 | bytes 8503808 | tf_op jit(solution)/shard_map/dot_general | solution.py:147
  183.2 5.3 %all-to-all-start = ((bf16[32,2,4096]{2,1,0:T(2,128)(2,1)}), bf16[32,2,4096]{2,1,0:T(2,128)(2,1)S(1)}, u32[]{:S(2)}, u32[]{:S(2)}) async-start(bf16[32,2,4096]{2,1,0:T(2,128)(2,1)} %reshape.654), calls=%async_computation | async-start | bytes 1048576 | tf_op jit(solution)/shard_map/all_to_all | solution.py:45
  188.5 6.1 %select_reduce_fusion.1 = (f32[4096]{0:T(1024)S(1)}, f32[512]{0:T(512)S(1)}, f32[4096,512]{0,1:T(8,128)}) fusion(pred[512]{0:T(512)(128)(4,1)S(1)} %lt.180, pred[4096]{0:T(1024)(128)(4,1)S(1)} %lt.184, bf16[4096,256]{1,0:T(8,128)(2,1)} %bitcast.128, bf16[512,256]{1,0:T(8,128)(2,1)S(1)} %bitcast.144), kind=kOutput, calls=%fused_computation.15 | convolution fusion | flops 1084222976 | bytes 10770944 | tf_op jit(solution)/shard_map/dot_general | solution.py:133
  194.7 5.7 %fusion.5 = (f32[4096]{0:T(1024)S(1)}, f32[512]{0:T(512)S(1)}) fusion(f32[4096,512]{0,1:T(8,128)} %get-tuple-element.69, f32[4096]{0:T(1024)S(1)} %get-tuple-element.20, pred[512]{0:T(512)(128)(4,1)S(1)} %lt.180, f32[512]{0:T(512)S(1)} %get-tuple-element.21, pred[4096]{0:T(1024)(128)(4,1)S(1)} %lt.184), kind=kLoop, calls=%fused_computation.24 | loop fusion | flops 12578304 | bytes 8430080 | tf_op jit(solution)/shard_map/reduce_sum | solution.py:150
  200.4 2.6 slice_convert_fusion.1
  208.5 5.0 %fusion.19 = bf16[512,64]{0,1:T(8,128)(2,1)S(1)} fusion(bf16[4096,64]{0,1:T(8,128)(2,1)S(1)} %reshape.562, f32[4096,512]{0,1:T(8,128)} %get-tuple-element.69, f32[512]{0:T(512)S(1)} %get-tuple-element.21, pred[4096]{0:T(1024)(128)(4,1)S(1)} %lt.184, f32[512]{0:T(512)S(1)} %get-tuple-element.19, pred[512]{0:T(512)(128)(4,1)S(1)} %lt.180), kind=kOutput, calls=%fused_computation.37 | convolution fusion | flops 274825216 | bytes 8987136 | tf_op jit(solution)/shard_map/dot_general | solution.py:141
  214.3 2.6 fusion.2
  218.0 6.2 %all-to-all-start.1 = ((f32[32,1,768]{2,1,0:T(1,128)}), f32[32,1,768]{2,1,0:T(1,128)S(1)}, u32[]{:S(2)}, u32[]{:S(2)}) async-start(f32[32,1,768]{2,1,0:T(1,128)} %reshape.656), calls=%async_computation.1 | async-start | bytes 196608 | tf_op jit(solution)/shard_map/all_to_all | solution.py:161
  225.4 6.9 %all-to-all-done.1 = f32[32,1,768]{2,1,0:T(1,128)S(1)} async-done(((f32[32,1,768]{2,1,0:T(1,128)}), f32[32,1,768]{2,1,0:T(1,128)S(1)}, u32[]{:S(2)}, u32[]{:S(2)}) %all-to-all-start.1) | async-done | bytes 98336 | tf_op jit(solution)/shard_map/all_to_all | solution.py:161
  234.9 13.0 %all-to-all-start.2 = ((f32[16,1,768]{2,1,0:T(1,128)}), f32[16,1,768]{2,1,0:T(1,128)S(1)}, u32[]{:S(2)}, u32[]{:S(2)}) async-start(f32[16,1,768]{2,1,0:T(1,128)} %reshape.658), calls=%async_computation.2 | async-start | bytes 98304 | tf_op jit(solution)/shard_map/all_to_all | solution.py:45
  253.5 8.0 %all-to-all-done.2 = f32[16,1,768]{2,1,0:T(1,128)S(1)} async-done(((f32[16,1,768]{2,1,0:T(1,128)}), f32[16,1,768]{2,1,0:T(1,128)S(1)}, u32[]{:S(2)}, u32[]{:S(2)}) %all-to-all-start.2) | async-done | bytes 49184 | tf_op jit(solution)/shard_map/all_to_all | solution.py:45
  (138 shorter events, 46.5 us)
Async XLA Ops:
  7.2 5.3 %copy-start = (bf16[8,64,256]{2,1,0:T(8,128)(2,1)S(1)}, bf16[8,64,256]{2,1,0:T(8,128)(2,1)}, u32[]{:S(2)}) copy-start(bf16[8,64,256]{2,1,0:T(8,128)(2,1)} %param.11) | copy-start | bytes 786436
  7.2 151.4 %copy-start.3 = (bf16[8,64,256]{2,1,0:T(8,128)(2,1)S(1)}, bf16[8,64,256]{2,1,0:T(8,128)(2,1)}, u32[]{:S(2)}) copy-start(bf16[8,64,256]{2,1,0:T(8,128)(2,1)} %param.10) | copy-start | bytes 786436
  7.2 147.5 %all-gather.2.cloned.1.call-start = ((), (), s32[]{:S(2)}) async-start(), calls=%async_computation.3 | async-start | bytes 5406720 | tf_op jit(solution)/shard_map/all_gather | solution.py:100
  13.2 7.3 %collective-permute-start = (bf16[416,256]{1,0:T(8,128)(2,1)S(1)}, bf16[416,256]{1,0:T(8,128)(2,1)S(1)}, u32[]{:S(2)}, u32[]{:S(2)}) collective-permute-start(bf16[416,256]{1,0:T(8,128)(2,1)S(1)} %pad_maximum_fusion), channel_id=1, source_target_pairs={{0,32},{32,0},{64,96},{96,64},{128,160},{160,128},{192,224},{224,1... | collective-permute-start | bytes 638984 | tf_op jit(solution)/shard_map/ppermute | solution.py:20
  20.6 9.6 %collective-permute-start.1 = (bf16[416,256]{1,0:T(8,128)(2,1)S(1)}, bf16[416,256]{1,0:T(8,128)(2,1)S(1)}, u32[]{:S(2)}, u32[]{:S(2)}) collective-permute-start(bf16[416,256]{1,0:T(8,128)(2,1)S(1)} %broadcast_select_fusion), channel_id=1, source_target_pairs={{0,64},{32,96},{64,0},{96,32},{128,192},{160,224},{192,128},{224,1... | collective-permute-start | bytes 638984 | tf_op jit(solution)/shard_map/ppermute | solution.py:20
  30.4 28.3 %collective-permute-start.2 = (bf16[416,256]{1,0:T(8,128)(2,1)S(1)}, bf16[416,256]{1,0:T(8,128)(2,1)S(1)}, u32[]{:S(2)}, u32[]{:S(2)}) collective-permute-start(bf16[416,256]{1,0:T(8,128)(2,1)S(1)} %broadcast_select_fusion.1), channel_id=1, source_target_pairs={{0,384},{32,416},{64,448},{96,480},{128,0},{160,32},{192,64},{224,... | collective-permute-start | bytes 638984 | tf_op jit(solution)/shard_map/ppermute | solution.py:36
  43.4 15.3 %collective-permute-start.3 = (bf16[416,256]{1,0:T(8,128)(2,1)S(1)}, bf16[416,256]{1,0:T(8,128)(2,1)S(1)}, u32[]{:S(2)}, u32[]{:S(2)}) collective-permute-start(bf16[416,256]{1,0:T(8,128)(2,1)S(1)} %broadcast_select_fusion.1), channel_id=1, source_target_pairs={{0,128},{32,160},{64,192},{96,224},{128,256},{160,288},{192,320},{... | collective-permute-start | bytes 638984 | tf_op jit(solution)/shard_map/ppermute | solution.py:35
  58.9 13.9 %collective-permute-start.4 = (bf16[208,256]{1,0:T(8,128)(2,1)S(1)}, bf16[208,256]{1,0:T(8,128)(2,1)S(1)}, u32[]{:S(2)}, u32[]{:S(2)}) collective-permute-start(bf16[208,256]{1,0:T(8,128)(2,1)S(1)} %get-tuple-element.49), channel_id=1, source_target_pairs={{0,128},{32,160},{64,192},{96,224},{128,256},{160,288},{192,320},{... | collective-permute-start | bytes 319496 | tf_op jit(solution)/shard_map/ppermute | solution.py:30
  67.6 9.4 %collective-permute-start.5 = (bf16[208,256]{1,0:T(8,128)(2,1)S(1)}, bf16[208,256]{1,0:T(8,128)(2,1)S(1)}, u32[]{:S(2)}, u32[]{:S(2)}) collective-permute-start(bf16[208,256]{1,0:T(8,128)(2,1)S(1)} %get-tuple-element.50), channel_id=1, source_target_pairs={{0,384},{32,416},{64,448},{96,480},{128,0},{160,32},{192,64},{224,... | collective-permute-start | bytes 319496 | tf_op jit(solution)/shard_map/ppermute | solution.py:31
  160.3 4.0 %copy-start.1 = (f32[640,4096]{1,0:T(8,128)}, f32[640,4096]{1,0:T(8,128)S(1)}, u32[]{:S(2)}) copy-start(f32[640,4096]{1,0:T(8,128)S(1)} %get-tuple-element.68) | copy-start | bytes 31457284
  166.1 9.8 %slice-start = ((bf16[2,2048,578]{2,1,0:T(8,128)(2,1)}), bf16[2,2048,64]{2,1,0:T(8,128)(2,1)S(1)}, s32[]{:S(2)}) async-start(bf16[2,2048,578]{2,1,0:T(8,128)(2,1)} %all-gather.2.cloned.1.call-done), calls=%async_computation.4 | async-start | bytes 2097152 | tf_op jit(solution)/shard_map/slice | solution.py:106
  166.3 9.6 %copy-start.2 = (f32[640,4096]{1,0:T(8,128)S(1)}, f32[640,4096]{1,0:T(8,128)}, u32[]{:S(2)}) copy-start(f32[640,4096]{1,0:T(8,128)} %copy-done.1) | copy-start | bytes 31457284
  183.2 21.7 %all-to-all-start = ((bf16[32,2,4096]{2,1,0:T(2,128)(2,1)}), bf16[32,2,4096]{2,1,0:T(2,128)(2,1)S(1)}, u32[]{:S(2)}, u32[]{:S(2)}) async-start(bf16[32,2,4096]{2,1,0:T(2,128)(2,1)} %reshape.654), calls=%async_computation | async-start | bytes 1048576 | tf_op jit(solution)/shard_map/all_to_all | solution.py:45
  208.5 5.0 %slice-start.1 = ((s8[8388608]{0:T(1024)(128)(4,1)}), s8[4194304]{0:T(1024)(128)(4,1)S(1)}, s32[]{:S(2)}) async-start(s8[8388608]{0:T(1024)(128)(4,1)} %bitcast.126), calls=%async_computation.5 | async-start | bytes 8388608
  208.5 5.8 %slice-start.2 = ((s8[8388608]{0:T(1024)(128)(4,1)}), s8[4194304]{0:T(1024)(128)(4,1)S(1)}, s32[]{:S(2)}) async-start(s8[8388608]{0:T(1024)(128)(4,1)} %bitcast.126), calls=%async_computation.6 | async-start | bytes 8388608
  218.0 14.3 %all-to-all-start.1 = ((f32[32,1,768]{2,1,0:T(1,128)}), f32[32,1,768]{2,1,0:T(1,128)S(1)}, u32[]{:S(2)}, u32[]{:S(2)}) async-start(f32[32,1,768]{2,1,0:T(1,128)} %reshape.656), calls=%async_computation.1 | async-start | bytes 196608 | tf_op jit(solution)/shard_map/all_to_all | solution.py:161
  234.9 26.7 %all-to-all-start.2 = ((f32[16,1,768]{2,1,0:T(1,128)}), f32[16,1,768]{2,1,0:T(1,128)S(1)}, u32[]{:S(2)}, u32[]{:S(2)}) async-start(f32[16,1,768]{2,1,0:T(1,128)} %reshape.658), calls=%async_computation.2 | async-start | bytes 98304 | tf_op jit(solution)/shard_map/all_to_all | solution.py:45
Sparse Core Ops, SparseCore 0:
  78.2 76.4 all-gather.1

commit v6 on v5

--- a/solution.py
+++ b/solution.py
@@ -3,6 +3,8 @@
 import jax
 import jax.numpy as jnp
 from jax import lax
+from jax.experimental import pallas as pl
+from jax.experimental.pallas import tpu as pltpu
 from jax.sharding import PartitionSpec as P
 
 LOWEST = -1e30
@@ -53,6 +55,63 @@
     return jnp.squeeze(top, axis), total, num
 
 
+BLOCK_ROWS = 128
+
+
+def step_kernel(q_ref, row_ok_ref, col_ok_ref, keys_ref, key_ok_ref, values_ref, onehot_ref,
+                out_ref, cmax_ref, ctot_ref, cnum_ref, *, scale):
+    @pl.when(pl.program_id(0) == 0)
+    def _():
+        cmax_ref[...] = jnp.full_like(cmax_ref, LOWEST)
+        ctot_ref[...] = jnp.zeros_like(ctot_ref)
+        cnum_ref[...] = jnp.zeros_like(cnum_ref)
+
+    scores = lax.dot_general(
+        q_ref[...], keys_ref[...], (((1,), (1,)), ((), ())), preferred_element_type=jnp.float32
+    ) * scale
+    key_ok = key_ok_ref[...] != 0
+    row_ok = row_ok_ref[...] != 0
+    col_ok = col_ok_ref[...] != 0
+    masked = jnp.where(key_ok, scores, LOWEST)
+    row_max = jnp.max(masked, axis=1, keepdims=True)
+    weights = jnp.where(key_ok, jnp.exp(scores - row_max), 0.0)
+    total = jnp.sum(weights, axis=1, keepdims=True)
+    mixed = jnp.dot(
+        weights.astype(jnp.bfloat16), values_ref[...], preferred_element_type=jnp.float32
+    ) / total
+    out = jnp.where(row_ok, mixed, 0.0).astype(jnp.bfloat16)
+    out_ref[...] = out
+    picked = jnp.dot(out, onehot_ref[...], preferred_element_type=jnp.float32)
+    old_max = cmax_ref[...]
+    local = jnp.max(jnp.where(col_ok, scores, LOWEST), axis=0, keepdims=True)
+    new_max = jnp.maximum(old_max, local)
+    keep = jnp.exp(old_max - new_max)
+    expo = jnp.where(col_ok, jnp.exp(scores - new_max), 0.0)
+    ctot_ref[...] = ctot_ref[...] * keep + jnp.sum(expo, axis=0, keepdims=True)
+    cnum_ref[...] = cnum_ref[...] * keep + jnp.sum(expo * picked, axis=0, keepdims=True)
+    cmax_ref[...] = new_max
+
+
+def step_pass(q, row_ok, col_ok, mem_keys, key_ok, mem_values, onehot_t, scale):
+    rows, width = q.shape
+    mem, channels = mem_values.shape
+    blocks = rows // BLOCK_ROWS
+    whole = lambda shape: pl.BlockSpec(shape, lambda i: (0, 0))
+    by_row = lambda cols: pl.BlockSpec((BLOCK_ROWS, cols), lambda i: (i, 0))
+    stat = jax.ShapeDtypeStruct((1, mem), jnp.float32)
+    return pl.pallas_call(
+        lambda *refs: step_kernel(*refs, scale=scale),
+        grid=(blocks,),
+        in_specs=[
+            by_row(width), by_row(1), by_row(1),
+            whole((mem, width)), whole((1, mem)), whole((mem, channels)), whole((channels, mem)),
+        ],
+        out_specs=[by_row(channels), whole((1, mem)), whole((1, mem)), whole((1, mem))],
+        out_shape=[jax.ShapeDtypeStruct((rows, channels), jnp.bfloat16), stat, stat, stat],
+        compiler_params=pltpu.CompilerParams(dimension_semantics=("arbitrary",)),
+    )(q, row_ok, col_ok, mem_keys, key_ok, mem_values, onehot_t)
+
+
 def body(queries, keys, label_values, class_ids, valid_pixels, keyframe_index):
     fr_dev, pix_dev, width = queries.shape
     channels = label_values.shape[2]
@@ -130,26 +189,21 @@
         else:
             q = query_rows
             q_valid = row_valid
-        scores = lax.dot_general(
-            q, mem_keys[step], (((1,), (1,)), ((), ())), preferred_element_type=jnp.float32
-        ) * scale
-        masked = jnp.where(key_valid[None, :], scores, LOWEST)
-        row_max = jnp.max(masked, axis=1, keepdims=True)
-        weights = jnp.where(key_valid[None, :], jnp.exp(scores - row_max), 0.0)
-        total = jnp.sum(weights, axis=1, keepdims=True)
-        mixed = (
-            jnp.dot(weights.astype(jnp.bfloat16), mem_values, preferred_element_type=jnp.float32)
-            / total
+        col_ok = jnp.concatenate(
+            [row_valid, jnp.zeros((q.shape[0] - rows,), jnp.bool_)], axis=0
         )
-        out = jnp.where(q_valid[:, None], mixed, 0.0).astype(jnp.bfloat16)
+        out, col_max, col_total, col_num = step_pass(
+            q,
+            q_valid.astype(jnp.int32)[:, None],
+            col_ok.astype(jnp.int32)[:, None],
+            mem_keys[step],
+            key_valid.astype(jnp.int32)[None, :],
+            mem_values,
+            onehot_t,
+            scale,
+        )
         readout = out[:rows]
-        own_scores = scores[:rows]
-        picked = jnp.dot(readout, onehot_t, preferred_element_type=jnp.float32)
-        col_max = jnp.max(jnp.where(row_valid[:, None], own_scores, LOWEST), axis=0)
-        expo = jnp.where(row_valid[:, None], jnp.exp(own_scores - col_max[None, :]), 0.0)
-        col_total = jnp.sum(expo, axis=0)
-        col_num = jnp.sum(expo * picked, axis=0)
-        stats.append(jnp.stack([col_max, col_total, col_num]))
+        stats.append(jnp.stack([col_max[0], col_total[0], col_num[0]]))
         if step + 1 < total_steps:
             part = out[rows:].reshape(keyframes, pix_dev, channels)
             mem_values = gather_all(part, "space").transpose(1, 0, 2, 3).reshape(

time: 271 us -> 281 us (1.037)
  Pallas kernels: 0 us -> 28.4 us
  matrix products: 20.1 us -> 0 us
  other arithmetic: 30 us -> 15 us
  local copies, waits for them, and re-layouts: 31.6 us -> 42.1 us
  waiting for transfers between devices: 110 us -> 118 us
    pallas_call x0 -> x2, Pallas kernels: none -> 28.4 us  [step_pass(): pl.pallas_call(lambda *refs: step_kernel(*refs, scale=scale), grid=(block...]
    dot_general x6 -> x0, matrix products: 20.1 us -> none  [the longest x2 7.88 us: body(): lax.dot_general(q, mem_keys[step], (((1,), (1,)), ((), ())), preferred_el...]
    reduce_sum x3 -> x0, other arithmetic: 13.6 us -> none  [the longest x2 7.44 us: body(): col_total = jnp.sum(expo, axis=0)]
    all_to_all x2, waiting for transfers between devices: 9.57 us -> 16.7 us  [gather_all(): return lax.all_to_all(spread, axis, 0, 0, tiled=True)]
    slice x1 -> x3, local copies, waits for them, and re-layouts: 3.82 us -> 10.6 us  [body(): gathered[:, :, s * width:(s + 1) * width].reshape(mem_width, width)]
    convert_element_type x0 -> x5, local copies, waits for them, and re-layouts: none -> 5.55 us  [the longest x2 3.69 us: body(): gathered[:, :, base + channels + s].reshape(mem_width).astype(jnp.int32)]
    unnamed x25 -> x39, local copies, waits for them, and re-layouts: 10.2 us -> 7.92 us
    convert_element_type x2 -> x1, other arithmetic: 6.06 us -> 4.58 us  [body(): gathered[:, :, base + channels + s].reshape(mem_width).astype(jnp.int32)]
  transfers between devices with their start and end apart: 10 -> 10, of which waited for: 9 -> 9; matrix products, arithmetic and copies ran while one was open for 11% -> 7% of each run, Pallas kernels for 0% -> 0%
where the time goes in v6:
time: 281 us; the launch traced here: 280 us
  waiting for transfers between devices  118 us (42%)
  starting transfers between devices  60.8 us (22%)
  local copies, waits for them, and re-layouts  42.1 us (15%)
  Pallas kernels  28.4 us (10%)
  between operations  15.9 us (6%)
  other arithmetic  15 us (5%)
    all_gather x1, waiting for transfers between devices, body(): gathered = lax.all_gather(packed, 'space', axis=1, tiled=True)  71.5 us
    pallas_call x2, Pallas kernels, step_pass(): pl.pallas_call(lambda *refs: step_kernel(*refs, scale=scale), grid=(block...  28.4 us
    all_to_all x2, starting transfers between devices, gather_all(): return lax.all_to_all(spread, axis, 0, 0, tiled=True)  18.3 us
    all_to_all x2, waiting for transfers between devices, gather_all(): return lax.all_to_all(spread, axis, 0, 0, tiled=True)  16.7 us
    ppermute x1, waiting for transfers between devices, broadcast_tm(): got_b = lax.ppermute(value, axis, behind)  13.3 us
    ppermute x1, starting transfers between devices, broadcast_tm(): got_b = lax.ppermute(value, axis, behind)  13 us
    slice x3, local copies, waits for them, and re-layouts, body(): gathered[:, :, s * width:(s + 1) * width].reshape(mem_width, width)  10.6 us
    ppermute x2, starting transfers between devices, broadcast_tm(): got = lax.ppermute(value, axis, pairs)  10.4 us
  transfers between devices with their start and end apart: 10, of which 9 were waited for; matrix products, arithmetic and copies ran while one was open for 7% of the time, Pallas kernels for 0%

profile of v6, /device:TPU:1, one launch (start us, length us, event | category | flops | bytes accessed | tf_op | source)
XLA Modules:
  0.0 280.2 jit_solution(952424063725902196)
XLA Ops:
  13.2 4.0 %collective-permute-start = (bf16[416,256]{1,0:T(8,128)(2,1)S(1)}, bf16[416,256]{1,0:T(8,128)(2,1)S(1)}, u32[]{:S(2)}, u32[]{:S(2)}) collective-permute-start(bf16[416,256]{1,0:T(8,128)(2,1)S(1)} %pad_maximum_fusion.1), channel_id=1, source_target_pairs={{0,32},{32,0},{64,96},{96,64},{128,160},{160,128},{192,224},{224,1... | collective-permute-start | bytes 638984 | tf_op jit(solution)/shard_map/ppermute | solution.py:22
  20.6 6.4 %collective-permute-start.1 = (bf16[416,256]{1,0:T(8,128)(2,1)S(1)}, bf16[416,256]{1,0:T(8,128)(2,1)S(1)}, u32[]{:S(2)}, u32[]{:S(2)}) collective-permute-start(bf16[416,256]{1,0:T(8,128)(2,1)S(1)} %broadcast_select_fusion), channel_id=1, source_target_pairs={{0,64},{32,96},{64,0},{96,32},{128,192},{160,224},{192,128},{224,1... | collective-permute-start | bytes 638984 | tf_op jit(solution)/shard_map/ppermute | solution.py:22
  27.1 3.1 %collective-permute-done.1 = bf16[416,256]{1,0:T(8,128)(2,1)S(1)} collective-permute-done((bf16[416,256]{1,0:T(8,128)(2,1)S(1)}, bf16[416,256]{1,0:T(8,128)(2,1)S(1)}, u32[]{:S(2)}, u32[]{:S(2)}) %collective-permute-start.1) | collective-permute-done | bytes 213024 | tf_op jit(solution)/shard_map/ppermute | solution.py:22
  30.4 13.0 %collective-permute-start.2 = (bf16[416,256]{1,0:T(8,128)(2,1)S(1)}, bf16[416,256]{1,0:T(8,128)(2,1)S(1)}, u32[]{:S(2)}, u32[]{:S(2)}) collective-permute-start(bf16[416,256]{1,0:T(8,128)(2,1)S(1)} %broadcast_select_fusion.1), channel_id=1, source_target_pairs={{0,384},{32,416},{64,448},{96,480},{128,0},{160,32},{192,64},{224,... | collective-permute-start | bytes 638984 | tf_op jit(solution)/shard_map/ppermute | solution.py:38
  43.4 1.9 collective-permute-start.3
  45.3 13.3 %collective-permute-done.2 = bf16[416,256]{1,0:T(8,128)(2,1)S(1)} collective-permute-done((bf16[416,256]{1,0:T(8,128)(2,1)S(1)}, bf16[416,256]{1,0:T(8,128)(2,1)S(1)}, u32[]{:S(2)}, u32[]{:S(2)}) %collective-permute-start.2) | collective-permute-done | bytes 213024 | tf_op jit(solution)/shard_map/ppermute | solution.py:38
  58.9 8.9 %collective-permute-start.4 = (bf16[208,256]{1,0:T(8,128)(2,1)S(1)}, bf16[208,256]{1,0:T(8,128)(2,1)S(1)}, u32[]{:S(2)}, u32[]{:S(2)}) collective-permute-start(bf16[208,256]{1,0:T(8,128)(2,1)S(1)} %get-tuple-element.45), channel_id=1, source_target_pairs={{0,128},{32,160},{64,192},{96,224},{128,256},{160,288},{192,320},{... | collective-permute-start | bytes 319496 | tf_op jit(solution)/shard_map/ppermute | solution.py:32
  67.8 4.1 %collective-permute-start.5 = (bf16[208,256]{1,0:T(8,128)(2,1)S(1)}, bf16[208,256]{1,0:T(8,128)(2,1)S(1)}, u32[]{:S(2)}, u32[]{:S(2)}) collective-permute-start(bf16[208,256]{1,0:T(8,128)(2,1)S(1)} %get-tuple-element.46), channel_id=1, source_target_pairs={{0,384},{32,416},{64,448},{96,480},{128,0},{160,32},{192,64},{224,... | collective-permute-start | bytes 319496 | tf_op jit(solution)/shard_map/ppermute | solution.py:33
  72.7 4.5 %collective-permute-done.5 = bf16[208,256]{1,0:T(8,128)(2,1)S(1)} collective-permute-done((bf16[208,256]{1,0:T(8,128)(2,1)S(1)}, bf16[208,256]{1,0:T(8,128)(2,1)S(1)}, u32[]{:S(2)}, u32[]{:S(2)}) %collective-permute-start.5) | collective-permute-done | bytes 106528 | tf_op jit(solution)/shard_map/ppermute | solution.py:33
  83.7 71.5 %all-gather.2.cloned.1.call-done = bf16[2,2048,578]{2,0,1:T(2,128)(2,1)} async-done(((bf16[2,64,578]{2,0,1:T(2,128)(2,1)}), bf16[2,2048,578]{2,0,1:T(2,128)(2,1)}) %all-gather.2.cloned.1.call-update) | async-done | bytes 4734992 | tf_op jit(solution)/shard_map/all_gather | solution.py:159
  155.2 5.8 %fusion.27 = (bf16[2,2048,256]{2,0,1:T(2,128)(2,1)S(1)}, bf16[2,2048,256]{2,0,1:T(2,128)(2,1)}) fusion(bf16[2,2048,578]{2,0,1:T(2,128)(2,1)} %all-gather.2.cloned.1.call-done), kind=kLoop, calls=%fused_computation.137 | loop fusion | bytes 8388608 | tf_op jit(solution)/shard_map/slice | solution.py:161
  161.0 1.6 copy.133
  162.6 4.6 %slice_convert_fusion = (s32[2,2048,1]{2,0,1:T(2,128)S(1)}, s32[2,2048,1]{2,0,1:T(2,128)}) fusion(bf16[2,2048,578]{2,0,1:T(2,128)(2,1)S(1)} %copy-done.2), kind=kLoop, calls=%fused_computation.12 | loop fusion | flops 8192 | bytes 49152 | tf_op jit(solution)/shard_map/convert_element_type | solution.py:167
  167.2 2.8 copy.135
  172.0 15.5 %shard_map.77 = (bf16[640,64]{1,0:T(8,128)(2,1)}, f32[1,4096]{1,0:T(1,128)}, f32[1,4096]{1,0:T(1,128)}, f32[1,4096]{1,0:T(1,128)}) custom-call(bf16[640,256]{1,0:T(8,128)(2,1)} %pad_maximum_fusion.refs_0_, s32[640,1]{1,0:T(8,128)} %copy.136.refs_1_, s32[640,1]{1,0:T(8,128)} %reshape.733.refs_2_, bf16[4096,256]{1,0:T(8,128)(2,1)} %bitcast.126, ...), custom_call_target="tpu_custom_call" | custom-call | tf_op jit(solution)/shard_map/pallas_call | solution.py:102
  190.1 5.6 %all-to-all-start = ((bf16[32,2,4096]{2,1,0:T(2,128)(2,1)}), bf16[32,2,4096]{2,1,0:T(2,128)(2,1)}, u32[]{:S(2)}, u32[]{:S(2)}) async-start(bf16[32,2,4096]{2,1,0:T(2,128)(2,1)} %reshape.734), calls=%async_computation | async-start | bytes 1048576 | tf_op jit(solution)/shard_map/all_to_all | solution.py:47
  197.7 3.2 %copy.132 = bf16[2,2048,256]{2,1,0:T(8,128)(2,1)} copy(bf16[2,2048,256]{2,0,1:T(2,128)(2,1)} %get-tuple-element.41) | data formatting | bytes 4194304 | tf_op jit(solution)/shard_map/slice | solution.py:161
  204.3 7.9 %all-to-all-done = bf16[32,2,4096]{2,1,0:T(2,128)(2,1)} async-done(((bf16[32,2,4096]{2,1,0:T(2,128)(2,1)}), bf16[32,2,4096]{2,1,0:T(2,128)(2,1)}, u32[]{:S(2)}, u32[]{:S(2)}) %all-to-all-start) | async-done | bytes 524320 | tf_op jit(solution)/shard_map/all_to_all | solution.py:47
  212.2 2.3 reshape.735
  215.5 12.9 %shard_map.78 = (bf16[512,64]{1,0:T(8,128)(2,1)}, f32[1,4096]{1,0:T(1,128)}, f32[1,4096]{1,0:T(1,128)}, f32[1,4096]{1,0:T(1,128)}) custom-call(bf16[512,256]{1,0:T(8,128)(2,1)} %bitcast.130, s32[512,1]{1,0:T(8,128)} %copy.140.refs_1_.refs_2_, s32[512,1]{1,0:T(8,128)} %copy.140.refs_1_.refs_2_, bf16[4096,256]{1,0:T(8,128)(2,1)} %bitcast.125, ...), custom_call_target="tpu_custom_call" | custom-call | tf_op jit(solution)/shard_map/pallas_call | solution.py:102
  230.5 4.1 %all-to-all-start.1 = ((f32[32,1,768]{2,1,0:T(1,128)}), f32[32,1,768]{2,1,0:T(1,128)S(1)}, u32[]{:S(2)}, u32[]{:S(2)}) async-start(f32[32,1,768]{2,1,0:T(1,128)} %reshape.736), calls=%async_computation.1 | async-start | bytes 196608 | tf_op jit(solution)/shard_map/all_to_all | solution.py:215
  235.7 7.0 %all-to-all-done.1 = f32[32,1,768]{2,1,0:T(1,128)S(1)} async-done(((f32[32,1,768]{2,1,0:T(1,128)}), f32[32,1,768]{2,1,0:T(1,128)S(1)}, u32[]{:S(2)}, u32[]{:S(2)}) %all-to-all-start.1) | async-done | bytes 98336 | tf_op jit(solution)/shard_map/all_to_all | solution.py:215
  245.2 12.7 %all-to-all-start.2 = ((f32[16,1,768]{2,1,0:T(1,128)}), f32[16,1,768]{2,1,0:T(1,128)S(1)}, u32[]{:S(2)}, u32[]{:S(2)}) async-start(f32[16,1,768]{2,1,0:T(1,128)} %reshape.738), calls=%async_computation.2 | async-start | bytes 98304 | tf_op jit(solution)/shard_map/all_to_all | solution.py:47
  262.9 8.8 %all-to-all-done.2 = f32[16,1,768]{2,1,0:T(1,128)S(1)} async-done(((f32[16,1,768]{2,1,0:T(1,128)}), f32[16,1,768]{2,1,0:T(1,128)S(1)}, u32[]{:S(2)}, u32[]{:S(2)}) %all-to-all-start.2) | async-done | bytes 49184 | tf_op jit(solution)/shard_map/all_to_all | solution.py:47
  (158 shorter events, 38.8 us)
Async XLA Ops:
  7.2 5.3 %copy-start = (bf16[8,64,256]{2,1,0:T(8,128)(2,1)S(1)}, bf16[8,64,256]{2,1,0:T(8,128)(2,1)}, u32[]{:S(2)}) copy-start(bf16[8,64,256]{2,1,0:T(8,128)(2,1)} %param.11) | copy-start | bytes 786436
  7.2 19.8 %copy-start.9 = (s32[2,2]{1,0:T(2,128)S(1)}, s32[2,2]{1,0:T(2,128)}, u32[]{:S(2)}) copy-start(s32[2,2]{1,0:T(2,128)} %param.15) | copy-start | bytes 52
  7.2 148.0 %all-gather.2.cloned.1.call-start = ((), (), s32[]{:S(2)}) async-start(), calls=%async_computation.3 | async-start | bytes 5406720 | tf_op jit(solution)/shard_map/all_gather | solution.py:159
  13.2 7.3 %collective-permute-start = (bf16[416,256]{1,0:T(8,128)(2,1)S(1)}, bf16[416,256]{1,0:T(8,128)(2,1)S(1)}, u32[]{:S(2)}, u32[]{:S(2)}) collective-permute-start(bf16[416,256]{1,0:T(8,128)(2,1)S(1)} %pad_maximum_fusion.1), channel_id=1, source_target_pairs={{0,32},{32,0},{64,96},{96,64},{128,160},{160,128},{192,224},{224,1... | collective-permute-start | bytes 638984 | tf_op jit(solution)/shard_map/ppermute | solution.py:22
  20.6 58.0 %copy-start.1 = (s32[128]{0:T(128)S(1)}, s32[128]{0:T(128)}, u32[]{:S(2)}) copy-start(s32[128]{0:T(128)} %param.14) | copy-start | bytes 1540
  20.6 9.6 %collective-permute-start.1 = (bf16[416,256]{1,0:T(8,128)(2,1)S(1)}, bf16[416,256]{1,0:T(8,128)(2,1)S(1)}, u32[]{:S(2)}, u32[]{:S(2)}) collective-permute-start(bf16[416,256]{1,0:T(8,128)(2,1)S(1)} %broadcast_select_fusion), channel_id=1, source_target_pairs={{0,64},{32,96},{64,0},{96,32},{128,192},{160,224},{192,128},{224,1... | collective-permute-start | bytes 638984 | tf_op jit(solution)/shard_map/ppermute | solution.py:22
  30.4 28.3 %collective-permute-start.2 = (bf16[416,256]{1,0:T(8,128)(2,1)S(1)}, bf16[416,256]{1,0:T(8,128)(2,1)S(1)}, u32[]{:S(2)}, u32[]{:S(2)}) collective-permute-start(bf16[416,256]{1,0:T(8,128)(2,1)S(1)} %broadcast_select_fusion.1), channel_id=1, source_target_pairs={{0,384},{32,416},{64,448},{96,480},{128,0},{160,32},{192,64},{224,... | collective-permute-start | bytes 638984 | tf_op jit(solution)/shard_map/ppermute | solution.py:38
  43.4 15.3 %collective-permute-start.3 = (bf16[416,256]{1,0:T(8,128)(2,1)S(1)}, bf16[416,256]{1,0:T(8,128)(2,1)S(1)}, u32[]{:S(2)}, u32[]{:S(2)}) collective-permute-start(bf16[416,256]{1,0:T(8,128)(2,1)S(1)} %broadcast_select_fusion.1), channel_id=1, source_target_pairs={{0,128},{32,160},{64,192},{96,224},{128,256},{160,288},{192,320},{... | collective-permute-start | bytes 638984 | tf_op jit(solution)/shard_map/ppermute | solution.py:37
  58.8 24.1 %copy-start.3 = (bf16[8,64,256]{2,1,0:T(8,128)(2,1)S(1)}, bf16[8,64,256]{2,1,0:T(8,128)(2,1)}, u32[]{:S(2)}) copy-start(bf16[8,64,256]{2,1,0:T(8,128)(2,1)} %param.10) | copy-start | bytes 786436
  58.9 13.8 %collective-permute-start.4 = (bf16[208,256]{1,0:T(8,128)(2,1)S(1)}, bf16[208,256]{1,0:T(8,128)(2,1)S(1)}, u32[]{:S(2)}, u32[]{:S(2)}) collective-permute-start(bf16[208,256]{1,0:T(8,128)(2,1)S(1)} %get-tuple-element.45), channel_id=1, source_target_pairs={{0,128},{32,160},{64,192},{96,224},{128,256},{160,288},{192,320},{... | collective-permute-start | bytes 319496 | tf_op jit(solution)/shard_map/ppermute | solution.py:32
  67.8 9.4 %collective-permute-start.5 = (bf16[208,256]{1,0:T(8,128)(2,1)S(1)}, bf16[208,256]{1,0:T(8,128)(2,1)S(1)}, u32[]{:S(2)}, u32[]{:S(2)}) collective-permute-start(bf16[208,256]{1,0:T(8,128)(2,1)S(1)} %get-tuple-element.46), channel_id=1, source_target_pairs={{0,384},{32,416},{64,448},{96,480},{128,0},{160,32},{192,64},{224,... | collective-permute-start | bytes 319496 | tf_op jit(solution)/shard_map/ppermute | solution.py:33
  78.7 82.4 %copy-start.10 = (s32[64]{0:T(128)}, s32[64]{0:T(128)S(1)}, u32[]{:S(2)}) copy-start(s32[64]{0:T(128)S(1)} %iota_add_fusion) | copy-start | bytes 772
  80.2 115.5 %copy-start.7 = (s32[2]{0:T(128)}, s32[2]{0:T(128)S(1)}, u32[]{:S(2)}) copy-start(s32[2]{0:T(128)S(1)} %get-tuple-element.54) | copy-start | bytes 28
  155.2 7.4 %copy-start.2 = (bf16[2,2048,578]{2,0,1:T(2,128)(2,1)S(1)}, bf16[2,2048,578]{2,0,1:T(2,128)(2,1)}, u32[]{:S(2)}) copy-start(bf16[2,2048,578]{2,0,1:T(2,128)(2,1)} %all-gather.2.cloned.1.call-done) | copy-start | bytes 14204932
  167.2 3.7 %slice-start = ((bf16[2,2048,578]{2,0,1:T(2,128)(2,1)}), bf16[2,2048,64]{2,0,1:T(2,128)(2,1)S(1)}, s32[]{:S(2)}) async-start(bf16[2,2048,578]{2,0,1:T(2,128)(2,1)} %all-gather.2.cloned.1.call-done), calls=%async_computation.4 | async-start | bytes 2097152 | tf_op jit(solution)/shard_map/slice | solution.py:165
  187.5 9.9 %copy-start.4 = (f32[1,4096]{1,0:T(1,128)S(1)}, f32[1,4096]{1,0:T(1,128)}, u32[]{:S(2)}) copy-start(f32[1,4096]{1,0:T(1,128)} %get-tuple-element.14) | copy-start | bytes 49156
  187.5 9.9 %copy-start.5 = (f32[1,4096]{1,0:T(1,128)S(1)}, f32[1,4096]{1,0:T(1,128)}, u32[]{:S(2)}) copy-start(f32[1,4096]{1,0:T(1,128)} %get-tuple-element.15) | copy-start | bytes 49156
  187.5 9.9 %copy-start.6 = (f32[1,4096]{1,0:T(1,128)S(1)}, f32[1,4096]{1,0:T(1,128)}, u32[]{:S(2)}) copy-start(f32[1,4096]{1,0:T(1,128)} %get-tuple-element.16) | copy-start | bytes 49156
  190.1 22.0 %all-to-all-start = ((bf16[32,2,4096]{2,1,0:T(2,128)(2,1)}), bf16[32,2,4096]{2,1,0:T(2,128)(2,1)}, u32[]{:S(2)}, u32[]{:S(2)}) async-start(bf16[32,2,4096]{2,1,0:T(2,128)(2,1)} %reshape.734), calls=%async_computation | async-start | bytes 1048576 | tf_op jit(solution)/shard_map/all_to_all | solution.py:47
  215.5 19.2 %copy-start.12 = (s32[128]{0:T(128)S(1)}, s32[128]{0:T(128)}, u32[]{:S(2)}) copy-start(s32[128]{0:T(128)} %reshape.725) | copy-start | bytes 1540
  229.6 43.1 %copy-start.8 = (s32[2]{0:T(128)S(1)}, s32[2]{0:T(128)}, u32[]{:S(2)}) copy-start(s32[2]{0:T(128)} %copy-done.7) | copy-start | bytes 28
  229.6 43.1 %copy-start.11 = (s32[64]{0:T(128)S(1)}, s32[64]{0:T(128)}, u32[]{:S(2)}) copy-start(s32[64]{0:T(128)} %copy-done.10) | copy-start | bytes 772
  230.5 12.2 %all-to-all-start.1 = ((f32[32,1,768]{2,1,0:T(1,128)}), f32[32,1,768]{2,1,0:T(1,128)S(1)}, u32[]{:S(2)}, u32[]{:S(2)}) async-start(f32[32,1,768]{2,1,0:T(1,128)} %reshape.736), calls=%async_computation.1 | async-start | bytes 196608 | tf_op jit(solution)/shard_map/all_to_all | solution.py:215
  245.2 26.4 %all-to-all-start.2 = ((f32[16,1,768]{2,1,0:T(1,128)}), f32[16,1,768]{2,1,0:T(1,128)S(1)}, u32[]{:S(2)}, u32[]{:S(2)}) async-start(f32[16,1,768]{2,1,0:T(1,128)} %reshape.738), calls=%async_computation.2 | async-start | bytes 98304 | tf_op jit(solution)/shard_map/all_to_all | solution.py:47
Sparse Core Ops, SparseCore 0:
  78.7 76.4 all-gather.1

commit v7 on v6

--- a/solution.py
+++ b/solution.py
@@ -58,20 +58,13 @@
 BLOCK_ROWS = 128
 
 
-def step_kernel(q_ref, row_ok_ref, col_ok_ref, keys_ref, key_ok_ref, values_ref, onehot_ref,
-                out_ref, cmax_ref, ctot_ref, cnum_ref, *, scale):
-    @pl.when(pl.program_id(0) == 0)
-    def _():
-        cmax_ref[...] = jnp.full_like(cmax_ref, LOWEST)
-        ctot_ref[...] = jnp.zeros_like(ctot_ref)
-        cnum_ref[...] = jnp.zeros_like(cnum_ref)
-
+def step_kernel(q_ref, row_ok_ref, col_ok_ref, keys_ref, key_ok_ref, values_ref, aux_ref,
+                *out_refs, scale, step, with_stats):
     scores = lax.dot_general(
         q_ref[...], keys_ref[...], (((1,), (1,)), ((), ())), preferred_element_type=jnp.float32
     ) * scale
     key_ok = key_ok_ref[...] != 0
     row_ok = row_ok_ref[...] != 0
-    col_ok = col_ok_ref[...] != 0
     masked = jnp.where(key_ok, scores, LOWEST)
     row_max = jnp.max(masked, axis=1, keepdims=True)
     weights = jnp.where(key_ok, jnp.exp(scores - row_max), 0.0)
@@ -80,8 +73,25 @@
         weights.astype(jnp.bfloat16), values_ref[...], preferred_element_type=jnp.float32
     ) / total
     out = jnp.where(row_ok, mixed, 0.0).astype(jnp.bfloat16)
-    out_ref[...] = out
-    picked = jnp.dot(out, onehot_ref[...], preferred_element_type=jnp.float32)
+    out_refs[0][...] = out
+    if not with_stats:
+        return
+    cmax_ref, ctot_ref, cnum_ref = out_refs[1:]
+
+    @pl.when(pl.program_id(0) == 0)
+    def _():
+        cmax_ref[...] = jnp.full_like(cmax_ref, LOWEST)
+        ctot_ref[...] = jnp.zeros_like(ctot_ref)
+        cnum_ref[...] = jnp.zeros_like(cnum_ref)
+
+    channels = values_ref.shape[1]
+    ids = aux_ref[:, channels + step:channels + step + 1].astype(jnp.float32)
+    classes = lax.broadcasted_iota(jnp.int32, (1, channels), 1).astype(jnp.float32)
+    onehot = (ids == classes).astype(jnp.bfloat16)
+    picked = lax.dot_general(
+        out, onehot, (((1,), (1,)), ((), ())), preferred_element_type=jnp.float32
+    )
+    col_ok = col_ok_ref[...] != 0
     old_max = cmax_ref[...]
     local = jnp.max(jnp.where(col_ok, scores, LOWEST), axis=0, keepdims=True)
     new_max = jnp.maximum(old_max, local)
@@ -92,24 +102,33 @@
     cmax_ref[...] = new_max
 
 
-def step_pass(q, row_ok, col_ok, mem_keys, key_ok, mem_values, onehot_t, scale):
+def step_pass(q, row_ok, col_ok, gathered, step, key_ok, mem_values, scale, with_stats):
     rows, width = q.shape
-    mem, channels = mem_values.shape
+    parts, mem, _ = gathered.shape
+    channels = mem_values.shape[1]
     blocks = rows // BLOCK_ROWS
     whole = lambda shape: pl.BlockSpec(shape, lambda i: (0, 0))
     by_row = lambda cols: pl.BlockSpec((BLOCK_ROWS, cols), lambda i: (i, 0))
     stat = jax.ShapeDtypeStruct((1, mem), jnp.float32)
+    out_specs = [by_row(channels)]
+    out_shape = [jax.ShapeDtypeStruct((rows, channels), jnp.bfloat16)]
+    if with_stats:
+        out_specs += [whole((1, mem))] * 3
+        out_shape += [stat] * 3
     return pl.pallas_call(
-        lambda *refs: step_kernel(*refs, scale=scale),
+        lambda *refs: step_kernel(*refs, scale=scale, step=step, with_stats=with_stats),
         grid=(blocks,),
         in_specs=[
             by_row(width), by_row(1), by_row(1),
-            whole((mem, width)), whole((1, mem)), whole((mem, channels)), whole((channels, mem)),
+            pl.BlockSpec((None, mem, width), lambda i: (step, 0, 0)),
+            whole((1, mem)),
+            whole((mem, channels)),
+            pl.BlockSpec((None, mem, 128), lambda i: (parts - 1, 0, 0)),
         ],
-        out_specs=[by_row(channels), whole((1, mem)), whole((1, mem)), whole((1, mem))],
-        out_shape=[jax.ShapeDtypeStruct((rows, channels), jnp.bfloat16), stat, stat, stat],
+        out_specs=out_specs,
+        out_shape=out_shape,
         compiler_params=pltpu.CompilerParams(dimension_semantics=("arbitrary",)),
-    )(q, row_ok, col_ok, mem_keys, key_ok, mem_values, onehot_t)
+    )(q, row_ok, col_ok, gathered, key_ok, mem_values, gathered)
 
 
 def body(queries, keys, label_values, class_ids, valid_pixels, keyframe_index):
@@ -153,19 +172,14 @@
     kf_ids = jnp.take(class_ids, flat_kf, axis=0).astype(jnp.bfloat16)
     kf_ids = kf_ids.reshape(total_steps, keyframes, pix_dev).transpose(1, 2, 0)
     step_keys = kf_keys.reshape(total_steps, keyframes, pix_dev, width)
-    packed = jnp.concatenate(
-        [step_keys[s] for s in range(total_steps)] + [kf_values, kf_ids], axis=2
-    )
-    gathered = lax.all_gather(packed, "space", axis=1, tiled=True)
-    mem_keys = [
-        gathered[:, :, s * width:(s + 1) * width].reshape(mem_width, width)
-        for s in range(total_steps)
-    ]
-    base = total_steps * width
-    mem_values = gathered[:, :, base:base + channels].reshape(mem_width, channels)
+    aux = jnp.concatenate([kf_values, kf_ids], axis=2)
+    aux = jnp.pad(aux, ((0, 0), (0, 0), (0, width - aux.shape[2])))
+    packed = jnp.concatenate([step_keys, aux[None]], axis=0)
+    gathered = lax.all_gather(packed, "space", axis=2, tiled=True)
+    gathered = gathered.reshape(total_steps + 1, mem_width, width)
+    mem_values = gathered[total_steps, :, :channels]
     mem_ids = [
-        gathered[:, :, base + channels + s].reshape(mem_width).astype(jnp.int32)
-        for s in range(total_steps)
+        gathered[total_steps, :, channels + s].astype(jnp.int32) for s in range(total_steps)
     ]
 
     extra_queries = kf_queries.reshape(later, pix_dev, width)
@@ -179,36 +193,25 @@
             jnp.arange(pix_all, dtype=jnp.int32)[None, :]
             < jnp.take(valid_pixels, chosen)[:, None]
         ).reshape(mem_width)
-        ids = mem_ids[step]
-        onehot_t = (ids[None, :] == class_range[:, None]).astype(jnp.bfloat16)
+        key_ok = key_valid.astype(jnp.int32)[None, :]
         if step + 1 < total_steps:
             extra = extra_queries[step * keyframes:(step + 1) * keyframes].reshape(-1, width)
-            extra_ok = extra_valid[step * keyframes:(step + 1) * keyframes].reshape(-1)
-            q = jnp.concatenate([query_rows, extra], axis=0)
-            q_valid = jnp.concatenate([row_valid, extra_ok], axis=0)
-        else:
-            q = query_rows
-            q_valid = row_valid
-        col_ok = jnp.concatenate(
-            [row_valid, jnp.zeros((q.shape[0] - rows,), jnp.bool_)], axis=0
+            extra_ok = extra_valid[step * keyframes:(step + 1) * keyframes].reshape(-1, 1)
+            extra_ok = extra_ok.astype(jnp.int32)
+            (part,) = step_pass(
+                extra, extra_ok, extra_ok, gathered, step, key_ok, mem_values, scale, False
+            )
+            part = part.reshape(keyframes, pix_dev, channels)
+            next_values = gather_all(part, "space").transpose(1, 0, 2, 3).reshape(
+                mem_width, channels
+            )
+        ok = row_valid.astype(jnp.int32)[:, None]
+        readout, col_max, col_total, col_num = step_pass(
+            query_rows, ok, ok, gathered, step, key_ok, mem_values, scale, True
         )
-        out, col_max, col_total, col_num = step_pass(
-            q,
-            q_valid.astype(jnp.int32)[:, None],
-            col_ok.astype(jnp.int32)[:, None],
-            mem_keys[step],
-            key_valid.astype(jnp.int32)[None, :],
-            mem_values,
-            onehot_t,
-            scale,
-        )
-        readout = out[:rows]
         stats.append(jnp.stack([col_max[0], col_total[0], col_num[0]]))
         if step + 1 < total_steps:
-            part = out[rows:].reshape(keyframes, pix_dev, channels)
-            mem_values = gather_all(part, "space").transpose(1, 0, 2, 3).reshape(
-                mem_width, channels
-            )
+            mem_values = next_values
 
     local = jnp.stack(stats).reshape(total_steps, 3, keyframes, n_space, pix_dev)
     local = local.transpose(3, 1, 0, 2, 4)

time: 281 us -> 266 us (0.947)
  local copies, waits for them, and re-layouts: 42.1 us -> 24.9 us
  Pallas kernels: 28.4 us -> 35.1 us
  waiting for transfers between devices: 118 us -> 112 us
  starting transfers between devices: 60.8 us -> 64 us
    slice x7 -> x1, local copies, waits for them, and re-layouts: 12.5 us -> 0.01 us  [body(): kf_keys = flat[:sizes[0]].reshape(kf_keys.shape)]
    all_to_all x2, waiting for transfers between devices: 16.7 us -> 8.81 us  [gather_all(): return lax.all_to_all(spread, axis, 0, 0, tiled=True)]
    pallas_call x2 -> x3, Pallas kernels: 28.4 us -> 35.1 us  [step_pass(): pl.pallas_call(lambda *refs: step_kernel(*refs, scale=scale, step=step, w...]
    convert_element_type x5 -> x4, local copies, waits for them, and re-layouts: 5.55 us -> 1.69 us  [the longest x1 0.9 us: body(): ok = row_valid.astype(jnp.int32)[:, None]]
    all_to_all x1, starting transfers between devices: 4.15 us -> 7.73 us  [body(): spread = lax.all_to_all(local, 'space', 0, 0, tiled=True)]
    convert_element_type x5 -> x3, other arithmetic: 6.41 us -> 3.53 us  [the longest x1 3.38 us: body(): gathered[total_steps, :, channels + s].astype(jnp.int32)]
    unnamed x39 -> x17, local copies, waits for them, and re-layouts: 7.92 us -> 6.19 us
  transfers between devices with their start and end apart: 10 -> 10, of which waited for: 9 -> 8; matrix products, arithmetic and copies ran while one was open for 7% -> 7% of each run, Pallas kernels for 0% -> 6%
where the time goes in v7:
time: 266 us; the launch traced here: 265 us
  waiting for transfers between devices  112 us (42%)
  starting transfers between devices  64 us (24%)
  Pallas kernels  35.1 us (13%)
  local copies, waits for them, and re-layouts  24.9 us (9%)
  between operations  15.7 us (6%)
  other arithmetic  13.5 us (5%)
    all_gather x1, waiting for transfers between devices, body(): gathered = lax.all_gather(packed, 'space', axis=2, tiled=True)  73.9 us
    pallas_call x3, Pallas kernels, step_pass(): pl.pallas_call(lambda *refs: step_kernel(*refs, scale=scale, step=step, w...  35.1 us
    all_to_all x2, starting transfers between devices, gather_all(): return lax.all_to_all(spread, axis, 0, 0, tiled=True)  18.1 us
    ppermute x1, waiting for transfers between devices, broadcast_tm(): got_b = lax.ppermute(value, axis, behind)  13.3 us
    ppermute x1, starting transfers between devices, broadcast_tm(): got_b = lax.ppermute(value, axis, behind)  13 us
    ppermute x2, starting transfers between devices, broadcast_tm(): got = lax.ppermute(value, axis, pairs)  10.4 us
    all_to_all x2, waiting for transfers between devices, gather_all(): return lax.all_to_all(spread, axis, 0, 0, tiled=True)  8.81 us
    ppermute x1, starting transfers between devices, broadcast_tm(): got_a = lax.ppermute(value[:half], axis, ahead)  8.76 us
  transfers between devices with their start and end apart: 10, of which 8 were waited for; matrix products, arithmetic and copies ran while one was open for 7% of the time, Pallas kernels for 6%

profile of v7, /device:TPU:1, one launch (start us, length us, event | category | flops | bytes accessed | tf_op | source)
XLA Modules:
  0.0 264.8 jit_solution(14996730615425907910)
XLA Ops:
  9.1 1.5 gather_fusion.2
  10.9 1.5 gather_fusion.1
  13.2 4.0 %collective-permute-start = (bf16[416,256]{1,0:T(8,128)(2,1)S(1)}, bf16[416,256]{1,0:T(8,128)(2,1)S(1)}, u32[]{:S(2)}, u32[]{:S(2)}) collective-permute-start(bf16[416,256]{1,0:T(8,128)(2,1)S(1)} %pad_maximum_fusion), channel_id=1, source_target_pairs={{0,32},{32,0},{64,96},{96,64},{128,160},{160,128},{192,224},{224,1... | collective-permute-start | bytes 638984 | tf_op jit(solution)/shard_map/ppermute | solution.py:22
  20.6 6.4 %collective-permute-start.1 = (bf16[416,256]{1,0:T(8,128)(2,1)S(1)}, bf16[416,256]{1,0:T(8,128)(2,1)S(1)}, u32[]{:S(2)}, u32[]{:S(2)}) collective-permute-start(bf16[416,256]{1,0:T(8,128)(2,1)S(1)} %broadcast_select_fusion), channel_id=1, source_target_pairs={{0,64},{32,96},{64,0},{96,32},{128,192},{160,224},{192,128},{224,1... | collective-permute-start | bytes 638984 | tf_op jit(solution)/shard_map/ppermute | solution.py:22
  27.8 2.4 collective-permute-done.1
  30.4 13.0 %collective-permute-start.2 = (bf16[416,256]{1,0:T(8,128)(2,1)S(1)}, bf16[416,256]{1,0:T(8,128)(2,1)S(1)}, u32[]{:S(2)}, u32[]{:S(2)}) collective-permute-start(bf16[416,256]{1,0:T(8,128)(2,1)S(1)} %broadcast_select_fusion.1), channel_id=1, source_target_pairs={{0,384},{32,416},{64,448},{96,480},{128,0},{160,32},{192,64},{224,... | collective-permute-start | bytes 638984 | tf_op jit(solution)/shard_map/ppermute | solution.py:38
  43.4 1.9 collective-permute-start.3
  45.3 13.3 %collective-permute-done.2 = bf16[416,256]{1,0:T(8,128)(2,1)S(1)} collective-permute-done((bf16[416,256]{1,0:T(8,128)(2,1)S(1)}, bf16[416,256]{1,0:T(8,128)(2,1)S(1)}, u32[]{:S(2)}, u32[]{:S(2)}) %collective-permute-start.2) | collective-permute-done | bytes 213024 | tf_op jit(solution)/shard_map/ppermute | solution.py:38
  58.9 8.8 %collective-permute-start.4 = (bf16[208,256]{1,0:T(8,128)(2,1)S(1)}, bf16[208,256]{1,0:T(8,128)(2,1)S(1)}, u32[]{:S(2)}, u32[]{:S(2)}) collective-permute-start(bf16[208,256]{1,0:T(8,128)(2,1)S(1)} %get-tuple-element.38), channel_id=1, source_target_pairs={{0,128},{32,160},{64,192},{96,224},{128,256},{160,288},{192,320},{... | collective-permute-start | bytes 319496 | tf_op jit(solution)/shard_map/ppermute | solution.py:32
  67.6 4.1 %collective-permute-start.5 = (bf16[208,256]{1,0:T(8,128)(2,1)S(1)}, bf16[208,256]{1,0:T(8,128)(2,1)S(1)}, u32[]{:S(2)}, u32[]{:S(2)}) collective-permute-start(bf16[208,256]{1,0:T(8,128)(2,1)S(1)} %get-tuple-element.39), channel_id=1, source_target_pairs={{0,384},{32,416},{64,448},{96,480},{128,0},{160,32},{192,64},{224,... | collective-permute-start | bytes 319496 | tf_op jit(solution)/shard_map/ppermute | solution.py:33
  72.7 4.3 %collective-permute-done.5 = bf16[208,256]{1,0:T(8,128)(2,1)S(1)} collective-permute-done((bf16[208,256]{1,0:T(8,128)(2,1)S(1)}, bf16[208,256]{1,0:T(8,128)(2,1)S(1)}, u32[]{:S(2)}, u32[]{:S(2)}) %collective-permute-start.5) | collective-permute-done | bytes 106528 | tf_op jit(solution)/shard_map/ppermute | solution.py:33
  82.4 73.9 %all-gather.2.cloned.1.call-done = bf16[3,2,2048,256]{3,2,1,0:T(8,128)(2,1)} async-done(((bf16[3,2,64,256]{3,2,1,0:T(8,128)(2,1)}), bf16[3,2,2048,256]{3,2,1,0:T(8,128)(2,1)}) %all-gather.2.cloned.1.call-update) | async-done | bytes 6291472 | tf_op jit(solution)/shard_map/all_gather | solution.py:178
  156.3 2.3 slice_bitcast_fusion.refs_5_
  158.6 4.6 %shard_map.77 = bf16[128,64]{1,0:T(8,128)(2,1)} custom-call(bf16[128,256]{1,0:T(8,128)(2,1)} %slice.120.refs_0_, s32[128,1]{1,0:T(8,128)} %reshape.705.refs_1_.refs_2_, s32[128,1]{1,0:T(8,128)} %reshape.705.refs_1_.refs_2_, bf16[3,4096,256]{2,1,0:T(8,128)(2,1)} %bitcast.111, s32[1,4096]{1,0:T(1,128)} %bitcast.125, ...), custom_call_target="tpu_custom_call" | custom-call | tf_op jit(solution)/shard_map/pallas_call | solution.py:118
  164.1 1.5 reshape.710
  165.7 5.4 %all-to-all-start = ((bf16[32,2,4096]{2,1,0:T(2,128)(2,1)}), bf16[32,2,4096]{2,1,0:T(2,128)(2,1)S(1)}, u32[]{:S(2)}, u32[]{:S(2)}) async-start(bf16[32,2,4096]{2,1,0:T(2,128)(2,1)} %reshape.710), calls=%async_computation | async-start | bytes 1048576 | tf_op jit(solution)/shard_map/all_to_all | solution.py:47
  172.9 15.3 %shard_map.79 = (bf16[512,64]{1,0:T(8,128)(2,1)}, f32[1,4096]{1,0:T(1,128)}, f32[1,4096]{1,0:T(1,128)}, f32[1,4096]{1,0:T(1,128)}) custom-call(bf16[512,256]{1,0:T(8,128)(2,1)} %bitcast.120, s32[512,1]{1,0:T(8,128)} %reshape.704.refs_1_.refs_2_, s32[512,1]{1,0:T(8,128)} %reshape.704.refs_1_.refs_2_, bf16[3,4096,256]{2,1,0:T(8,128)(2,1)} %bitcast.113, ...), custom_call_target="tpu_custom_call" | custom-call | tf_op jit(solution)/shard_map/pallas_call | solution.py:118
  189.2 3.4 %convert_reduce_fusion.1 = (s32[4096]{0:T(1024)S(1)}, s32[4096]{0:T(1024)S(1)}) fusion(bf16[3,4096,256]{2,1,0:T(8,128)(2,1)} %bitcast.115), kind=kLoop, calls=%fused_computation.9 | loop fusion | flops 8192 | bytes 49152 | tf_op jit(solution)/shard_map/convert_element_type | solution.py:182
  194.4 15.3 %shard_map.78 = (bf16[512,64]{1,0:T(8,128)(2,1)}, f32[1,4096]{1,0:T(1,128)}, f32[1,4096]{1,0:T(1,128)}, f32[1,4096]{1,0:T(1,128)}) custom-call(bf16[512,256]{1,0:T(8,128)(2,1)} %bitcast.121, s32[512,1]{1,0:T(8,128)} %reshape.704.refs_1_.refs_2_, s32[512,1]{1,0:T(8,128)} %reshape.704.refs_1_.refs_2_, bf16[3,4096,256]{2,1,0:T(8,128)(2,1)} %bitcast.116, ...), custom_call_target="tpu_custom_call" | custom-call | tf_op jit(solution)/shard_map/pallas_call | solution.py:118
  211.6 7.7 %all-to-all-start.1 = ((f32[32,1,768]{2,1,0:T(1,128)}), f32[32,1,768]{2,1,0:T(1,128)S(1)}, u32[]{:S(2)}, u32[]{:S(2)}) async-start(f32[32,1,768]{2,1,0:T(1,128)} %reshape.712), calls=%async_computation.1 | async-start | bytes 196608 | tf_op jit(solution)/shard_map/all_to_all | solution.py:218
  220.7 6.7 %all-to-all-done.1 = f32[32,1,768]{2,1,0:T(1,128)S(1)} async-done(((f32[32,1,768]{2,1,0:T(1,128)}), f32[32,1,768]{2,1,0:T(1,128)S(1)}, u32[]{:S(2)}, u32[]{:S(2)}) %all-to-all-start.1) | async-done | bytes 98336 | tf_op jit(solution)/shard_map/all_to_all | solution.py:218
  229.9 12.7 %all-to-all-start.2 = ((f32[16,1,768]{2,1,0:T(1,128)}), f32[16,1,768]{2,1,0:T(1,128)S(1)}, u32[]{:S(2)}, u32[]{:S(2)}) async-start(f32[16,1,768]{2,1,0:T(1,128)} %reshape.714), calls=%async_computation.2 | async-start | bytes 98304 | tf_op jit(solution)/shard_map/all_to_all | solution.py:47
  242.6 1.2 gather_fusion.6
  247.5 8.8 %all-to-all-done.2 = f32[16,1,768]{2,1,0:T(1,128)S(1)} async-done(((f32[16,1,768]{2,1,0:T(1,128)}), f32[16,1,768]{2,1,0:T(1,128)S(1)}, u32[]{:S(2)}, u32[]{:S(2)}) %all-to-all-start.2) | async-done | bytes 49184 | tf_op jit(solution)/shard_map/all_to_all | solution.py:47
  (116 shorter events, 29.1 us)
Async XLA Ops:
  7.2 5.3 %copy-start = (bf16[8,64,256]{2,1,0:T(8,128)(2,1)S(1)}, bf16[8,64,256]{2,1,0:T(8,128)(2,1)}, u32[]{:S(2)}) copy-start(bf16[8,64,256]{2,1,0:T(8,128)(2,1)} %param.11) | copy-start | bytes 786436
  7.2 73.0 %copy-start.2 = (s32[2,2]{1,0:T(2,128)S(1)}, s32[2,2]{1,0:T(2,128)}, u32[]{:S(2)}) copy-start(s32[2,2]{1,0:T(2,128)} %param.15) | copy-start | bytes 52
  7.2 71.7 %copy-start.1 = (s32[128]{0:T(128)S(1)}, s32[128]{0:T(128)}, u32[]{:S(2)}) copy-start(s32[128]{0:T(128)} %param.14) | copy-start | bytes 1540
  7.2 149.1 %all-gather.2.cloned.1.call-start = ((), (), s32[]{:S(2)}) async-start(), calls=%async_computation.3 | async-start | bytes 6488064 | tf_op jit(solution)/shard_map/all_gather | solution.py:178
  13.2 7.3 %collective-permute-start = (bf16[416,256]{1,0:T(8,128)(2,1)S(1)}, bf16[416,256]{1,0:T(8,128)(2,1)S(1)}, u32[]{:S(2)}, u32[]{:S(2)}) collective-permute-start(bf16[416,256]{1,0:T(8,128)(2,1)S(1)} %pad_maximum_fusion), channel_id=1, source_target_pairs={{0,32},{32,0},{64,96},{96,64},{128,160},{160,128},{192,224},{224,1... | collective-permute-start | bytes 638984 | tf_op jit(solution)/shard_map/ppermute | solution.py:22
  20.6 9.6 %collective-permute-start.1 = (bf16[416,256]{1,0:T(8,128)(2,1)S(1)}, bf16[416,256]{1,0:T(8,128)(2,1)S(1)}, u32[]{:S(2)}, u32[]{:S(2)}) collective-permute-start(bf16[416,256]{1,0:T(8,128)(2,1)S(1)} %broadcast_select_fusion), channel_id=1, source_target_pairs={{0,64},{32,96},{64,0},{96,32},{128,192},{160,224},{192,128},{224,1... | collective-permute-start | bytes 638984 | tf_op jit(solution)/shard_map/ppermute | solution.py:22
  30.4 28.3 %collective-permute-start.2 = (bf16[416,256]{1,0:T(8,128)(2,1)S(1)}, bf16[416,256]{1,0:T(8,128)(2,1)S(1)}, u32[]{:S(2)}, u32[]{:S(2)}) collective-permute-start(bf16[416,256]{1,0:T(8,128)(2,1)S(1)} %broadcast_select_fusion.1), channel_id=1, source_target_pairs={{0,384},{32,416},{64,448},{96,480},{128,0},{160,32},{192,64},{224,... | collective-permute-start | bytes 638984 | tf_op jit(solution)/shard_map/ppermute | solution.py:38
  43.4 15.3 %collective-permute-start.3 = (bf16[416,256]{1,0:T(8,128)(2,1)S(1)}, bf16[416,256]{1,0:T(8,128)(2,1)S(1)}, u32[]{:S(2)}, u32[]{:S(2)}) collective-permute-start(bf16[416,256]{1,0:T(8,128)(2,1)S(1)} %broadcast_select_fusion.1), channel_id=1, source_target_pairs={{0,128},{32,160},{64,192},{96,224},{128,256},{160,288},{192,320},{... | collective-permute-start | bytes 638984 | tf_op jit(solution)/shard_map/ppermute | solution.py:37
  58.9 13.9 %collective-permute-start.4 = (bf16[208,256]{1,0:T(8,128)(2,1)S(1)}, bf16[208,256]{1,0:T(8,128)(2,1)S(1)}, u32[]{:S(2)}, u32[]{:S(2)}) collective-permute-start(bf16[208,256]{1,0:T(8,128)(2,1)S(1)} %get-tuple-element.38), channel_id=1, source_target_pairs={{0,128},{32,160},{64,192},{96,224},{128,256},{160,288},{192,320},{... | collective-permute-start | bytes 319496 | tf_op jit(solution)/shard_map/ppermute | solution.py:32
  67.6 9.4 %collective-permute-start.5 = (bf16[208,256]{1,0:T(8,128)(2,1)S(1)}, bf16[208,256]{1,0:T(8,128)(2,1)S(1)}, u32[]{:S(2)}, u32[]{:S(2)}) collective-permute-start(bf16[208,256]{1,0:T(8,128)(2,1)S(1)} %get-tuple-element.39), channel_id=1, source_target_pairs={{0,384},{32,416},{64,448},{96,480},{128,0},{160,32},{192,64},{224,... | collective-permute-start | bytes 319496 | tf_op jit(solution)/shard_map/ppermute | solution.py:33
  165.7 26.9 %all-to-all-start = ((bf16[32,2,4096]{2,1,0:T(2,128)(2,1)}), bf16[32,2,4096]{2,1,0:T(2,128)(2,1)S(1)}, u32[]{:S(2)}, u32[]{:S(2)}) async-start(bf16[32,2,4096]{2,1,0:T(2,128)(2,1)} %reshape.710), calls=%async_computation | async-start | bytes 1048576 | tf_op jit(solution)/shard_map/all_to_all | solution.py:47
  211.6 15.8 %all-to-all-start.1 = ((f32[32,1,768]{2,1,0:T(1,128)}), f32[32,1,768]{2,1,0:T(1,128)S(1)}, u32[]{:S(2)}, u32[]{:S(2)}) async-start(f32[32,1,768]{2,1,0:T(1,128)} %reshape.712), calls=%async_computation.1 | async-start | bytes 196608 | tf_op jit(solution)/shard_map/all_to_all | solution.py:218
  229.9 26.4 %all-to-all-start.2 = ((f32[16,1,768]{2,1,0:T(1,128)}), f32[16,1,768]{2,1,0:T(1,128)S(1)}, u32[]{:S(2)}, u32[]{:S(2)}) async-start(f32[16,1,768]{2,1,0:T(1,128)} %reshape.714), calls=%async_computation.2 | async-start | bytes 98304 | tf_op jit(solution)/shard_map/all_to_all | solution.py:47
Sparse Core Ops, SparseCore 0:
  78.2 77.9 all-gather.1

commit v8 on v7

--- a/solution.py
+++ b/solution.py
@@ -76,21 +76,20 @@
     out_refs[0][...] = out
     if not with_stats:
         return
-    cmax_ref, ctot_ref, cnum_ref = out_refs[1:]
+    cmax_ref, ctot_ref, cnum_ref, onehot_ref = out_refs[1:]
 
     @pl.when(pl.program_id(0) == 0)
     def _():
         cmax_ref[...] = jnp.full_like(cmax_ref, LOWEST)
         ctot_ref[...] = jnp.zeros_like(ctot_ref)
         cnum_ref[...] = jnp.zeros_like(cnum_ref)
-
-    channels = values_ref.shape[1]
-    ids = aux_ref[:, channels + step:channels + step + 1].astype(jnp.float32)
-    classes = lax.broadcasted_iota(jnp.int32, (1, channels), 1).astype(jnp.float32)
-    onehot = (ids == classes).astype(jnp.bfloat16)
-    picked = lax.dot_general(
-        out, onehot, (((1,), (1,)), ((), ())), preferred_element_type=jnp.float32
-    )
+        channels = values_ref.shape[1]
+        ids = aux_ref[:, channels + step:channels + step + 1].astype(jnp.float32)
+        classes = lax.broadcasted_iota(jnp.int32, (1, channels), 1).astype(jnp.float32)
+        onehot = (ids == classes).astype(jnp.float32)
+        onehot_ref[...] = jnp.transpose(onehot).astype(jnp.bfloat16)
+
+    picked = jnp.dot(out, onehot_ref[...], preferred_element_type=jnp.float32)
     col_ok = col_ok_ref[...] != 0
     old_max = cmax_ref[...]
     local = jnp.max(jnp.where(col_ok, scores, LOWEST), axis=0, keepdims=True)
@@ -127,6 +126,7 @@
         ],
         out_specs=out_specs,
         out_shape=out_shape,
+        scratch_shapes=[pltpu.VMEM((channels, mem), jnp.bfloat16)] if with_stats else [],
         compiler_params=pltpu.CompilerParams(dimension_semantics=("arbitrary",)),
     )(q, row_ok, col_ok, gathered, key_ok, mem_values, gathered)
 

time: 266 us -> 265 us (level)
  no operation moved by 1% of the time
where the time goes in v8:
time: 265 us; the launch traced here: 264 us
  waiting for transfers between devices  112 us (42%)
  starting transfers between devices  64 us (24%)
  Pallas kernels  34.5 us (13%)
  local copies, waits for them, and re-layouts  24.9 us (9%)
  between operations  15.7 us (6%)
  other arithmetic  13.5 us (5%)
    all_gather x1, waiting for transfers between devices, body(): gathered = lax.all_gather(packed, 'space', axis=2, tiled=True)  73.9 us
    pallas_call x3, Pallas kernels, step_pass(): pl.pallas_call(lambda *refs: step_kernel(*refs, scale=scale, step=step, w...  34.5 us
    all_to_all x2, starting transfers between devices, gather_all(): return lax.all_to_all(spread, axis, 0, 0, tiled=True)  18.1 us
    ppermute x1, waiting for transfers between devices, broadcast_tm(): got_b = lax.ppermute(value, axis, behind)  13.3 us
    ppermute x1, starting transfers between devices, broadcast_tm(): got_b = lax.ppermute(value, axis, behind)  13 us
    ppermute x2, starting transfers between devices, broadcast_tm(): got = lax.ppermute(value, axis, pairs)  10.4 us
    all_to_all x2, waiting for transfers between devices, gather_all(): return lax.all_to_all(spread, axis, 0, 0, tiled=True)  8.81 us
    ppermute x1, starting transfers between devices, broadcast_tm(): got_a = lax.ppermute(value[:half], axis, ahead)  8.76 us
  transfers between devices with their start and end apart: 10, of which 8 were waited for; matrix products, arithmetic and copies ran while one was open for 7% of the time, Pallas kernels for 6%

profile of v8, /device:TPU:1, one launch (start us, length us, event | category | flops | bytes accessed | tf_op | source)
XLA Modules:
  0.0 264.2 jit_solution(12658888438621386516)
XLA Ops:
  9.1 1.5 gather_fusion.2
  10.9 1.5 gather_fusion.1
  13.2 4.0 %collective-permute-start = (bf16[416,256]{1,0:T(8,128)(2,1)S(1)}, bf16[416,256]{1,0:T(8,128)(2,1)S(1)}, u32[]{:S(2)}, u32[]{:S(2)}) collective-permute-start(bf16[416,256]{1,0:T(8,128)(2,1)S(1)} %pad_maximum_fusion), channel_id=1, source_target_pairs={{0,32},{32,0},{64,96},{96,64},{128,160},{160,128},{192,224},{224,1... | collective-permute-start | bytes 638984 | tf_op jit(solution)/shard_map/ppermute | solution.py:22
  20.6 6.4 %collective-permute-start.1 = (bf16[416,256]{1,0:T(8,128)(2,1)S(1)}, bf16[416,256]{1,0:T(8,128)(2,1)S(1)}, u32[]{:S(2)}, u32[]{:S(2)}) collective-permute-start(bf16[416,256]{1,0:T(8,128)(2,1)S(1)} %broadcast_select_fusion), channel_id=1, source_target_pairs={{0,64},{32,96},{64,0},{96,32},{128,192},{160,224},{192,128},{224,1... | collective-permute-start | bytes 638984 | tf_op jit(solution)/shard_map/ppermute | solution.py:22
  27.8 2.4 collective-permute-done.1
  30.4 13.0 %collective-permute-start.2 = (bf16[416,256]{1,0:T(8,128)(2,1)S(1)}, bf16[416,256]{1,0:T(8,128)(2,1)S(1)}, u32[]{:S(2)}, u32[]{:S(2)}) collective-permute-start(bf16[416,256]{1,0:T(8,128)(2,1)S(1)} %broadcast_select_fusion.1), channel_id=1, source_target_pairs={{0,384},{32,416},{64,448},{96,480},{128,0},{160,32},{192,64},{224,... | collective-permute-start | bytes 638984 | tf_op jit(solution)/shard_map/ppermute | solution.py:38
  43.4 1.9 collective-permute-start.3
  45.3 13.3 %collective-permute-done.2 = bf16[416,256]{1,0:T(8,128)(2,1)S(1)} collective-permute-done((bf16[416,256]{1,0:T(8,128)(2,1)S(1)}, bf16[416,256]{1,0:T(8,128)(2,1)S(1)}, u32[]{:S(2)}, u32[]{:S(2)}) %collective-permute-start.2) | collective-permute-done | bytes 213024 | tf_op jit(solution)/shard_map/ppermute | solution.py:38
  58.9 8.8 %collective-permute-start.4 = (bf16[208,256]{1,0:T(8,128)(2,1)S(1)}, bf16[208,256]{1,0:T(8,128)(2,1)S(1)}, u32[]{:S(2)}, u32[]{:S(2)}) collective-permute-start(bf16[208,256]{1,0:T(8,128)(2,1)S(1)} %get-tuple-element.38), channel_id=1, source_target_pairs={{0,128},{32,160},{64,192},{96,224},{128,256},{160,288},{192,320},{... | collective-permute-start | bytes 319496 | tf_op jit(solution)/shard_map/ppermute | solution.py:32
  67.6 4.1 %collective-permute-start.5 = (bf16[208,256]{1,0:T(8,128)(2,1)S(1)}, bf16[208,256]{1,0:T(8,128)(2,1)S(1)}, u32[]{:S(2)}, u32[]{:S(2)}) collective-permute-start(bf16[208,256]{1,0:T(8,128)(2,1)S(1)} %get-tuple-element.39), channel_id=1, source_target_pairs={{0,384},{32,416},{64,448},{96,480},{128,0},{160,32},{192,64},{224,... | collective-permute-start | bytes 319496 | tf_op jit(solution)/shard_map/ppermute | solution.py:33
  72.7 4.3 %collective-permute-done.5 = bf16[208,256]{1,0:T(8,128)(2,1)S(1)} collective-permute-done((bf16[208,256]{1,0:T(8,128)(2,1)S(1)}, bf16[208,256]{1,0:T(8,128)(2,1)S(1)}, u32[]{:S(2)}, u32[]{:S(2)}) %collective-permute-start.5) | collective-permute-done | bytes 106528 | tf_op jit(solution)/shard_map/ppermute | solution.py:33
  82.4 73.9 %all-gather.2.cloned.1.call-done = bf16[3,2,2048,256]{3,2,1,0:T(8,128)(2,1)} async-done(((bf16[3,2,64,256]{3,2,1,0:T(8,128)(2,1)}), bf16[3,2,2048,256]{3,2,1,0:T(8,128)(2,1)}) %all-gather.2.cloned.1.call-update) | async-done | bytes 6291472 | tf_op jit(solution)/shard_map/all_gather | solution.py:178
  156.3 2.3 slice_bitcast_fusion.refs_5_
  158.6 4.6 %shard_map.77 = bf16[128,64]{1,0:T(8,128)(2,1)} custom-call(bf16[128,256]{1,0:T(8,128)(2,1)} %slice.120.refs_0_, s32[128,1]{1,0:T(8,128)} %reshape.705.refs_1_.refs_2_, s32[128,1]{1,0:T(8,128)} %reshape.705.refs_1_.refs_2_, bf16[3,4096,256]{2,1,0:T(8,128)(2,1)} %bitcast.111, s32[1,4096]{1,0:T(1,128)} %bitcast.125, ...), custom_call_target="tpu_custom_call" | custom-call | tf_op jit(solution)/shard_map/pallas_call | solution.py:117
  164.1 1.5 reshape.710
  165.7 5.4 %all-to-all-start = ((bf16[32,2,4096]{2,1,0:T(2,128)(2,1)}), bf16[32,2,4096]{2,1,0:T(2,128)(2,1)S(1)}, u32[]{:S(2)}, u32[]{:S(2)}) async-start(bf16[32,2,4096]{2,1,0:T(2,128)(2,1)} %reshape.710), calls=%async_computation | async-start | bytes 1048576 | tf_op jit(solution)/shard_map/all_to_all | solution.py:47
  172.9 15.0 %shard_map.79 = (bf16[512,64]{1,0:T(8,128)(2,1)}, f32[1,4096]{1,0:T(1,128)}, f32[1,4096]{1,0:T(1,128)}, f32[1,4096]{1,0:T(1,128)}) custom-call(bf16[512,256]{1,0:T(8,128)(2,1)} %bitcast.120, s32[512,1]{1,0:T(8,128)} %reshape.704.refs_1_.refs_2_, s32[512,1]{1,0:T(8,128)} %reshape.704.refs_1_.refs_2_, bf16[3,4096,256]{2,1,0:T(8,128)(2,1)} %bitcast.113, ...), custom_call_target="tpu_custom_call" | custom-call | tf_op jit(solution)/shard_map/pallas_call | solution.py:117
  188.9 3.4 %convert_reduce_fusion.1 = (s32[4096]{0:T(1024)S(1)}, s32[4096]{0:T(1024)S(1)}) fusion(bf16[3,4096,256]{2,1,0:T(8,128)(2,1)} %bitcast.115), kind=kLoop, calls=%fused_computation.9 | loop fusion | flops 8192 | bytes 49152 | tf_op jit(solution)/shard_map/convert_element_type | solution.py:182
  194.1 14.9 %shard_map.78 = (bf16[512,64]{1,0:T(8,128)(2,1)}, f32[1,4096]{1,0:T(1,128)}, f32[1,4096]{1,0:T(1,128)}, f32[1,4096]{1,0:T(1,128)}) custom-call(bf16[512,256]{1,0:T(8,128)(2,1)} %bitcast.121, s32[512,1]{1,0:T(8,128)} %reshape.704.refs_1_.refs_2_, s32[512,1]{1,0:T(8,128)} %reshape.704.refs_1_.refs_2_, bf16[3,4096,256]{2,1,0:T(8,128)(2,1)} %bitcast.116, ...), custom_call_target="tpu_custom_call" | custom-call | tf_op jit(solution)/shard_map/pallas_call | solution.py:117
  211.0 7.7 %all-to-all-start.1 = ((f32[32,1,768]{2,1,0:T(1,128)}), f32[32,1,768]{2,1,0:T(1,128)S(1)}, u32[]{:S(2)}, u32[]{:S(2)}) async-start(f32[32,1,768]{2,1,0:T(1,128)} %reshape.712), calls=%async_computation.1 | async-start | bytes 196608 | tf_op jit(solution)/shard_map/all_to_all | solution.py:218
  220.0 6.7 %all-to-all-done.1 = f32[32,1,768]{2,1,0:T(1,128)S(1)} async-done(((f32[32,1,768]{2,1,0:T(1,128)}), f32[32,1,768]{2,1,0:T(1,128)S(1)}, u32[]{:S(2)}, u32[]{:S(2)}) %all-to-all-start.1) | async-done | bytes 98336 | tf_op jit(solution)/shard_map/all_to_all | solution.py:218
  229.3 12.7 %all-to-all-start.2 = ((f32[16,1,768]{2,1,0:T(1,128)}), f32[16,1,768]{2,1,0:T(1,128)S(1)}, u32[]{:S(2)}, u32[]{:S(2)}) async-start(f32[16,1,768]{2,1,0:T(1,128)} %reshape.714), calls=%async_computation.2 | async-start | bytes 98304 | tf_op jit(solution)/shard_map/all_to_all | solution.py:47
  242.0 1.2 gather_fusion.6
  246.9 8.8 %all-to-all-done.2 = f32[16,1,768]{2,1,0:T(1,128)S(1)} async-done(((f32[16,1,768]{2,1,0:T(1,128)}), f32[16,1,768]{2,1,0:T(1,128)S(1)}, u32[]{:S(2)}, u32[]{:S(2)}) %all-to-all-start.2) | async-done | bytes 49184 | tf_op jit(solution)/shard_map/all_to_all | solution.py:47
  (116 shorter events, 29.1 us)
Async XLA Ops:
  7.2 5.3 %copy-start = (bf16[8,64,256]{2,1,0:T(8,128)(2,1)S(1)}, bf16[8,64,256]{2,1,0:T(8,128)(2,1)}, u32[]{:S(2)}) copy-start(bf16[8,64,256]{2,1,0:T(8,128)(2,1)} %param.11) | copy-start | bytes 786436
  7.2 73.0 %copy-start.2 = (s32[2,2]{1,0:T(2,128)S(1)}, s32[2,2]{1,0:T(2,128)}, u32[]{:S(2)}) copy-start(s32[2,2]{1,0:T(2,128)} %param.15) | copy-start | bytes 52
  7.2 71.7 %copy-start.1 = (s32[128]{0:T(128)S(1)}, s32[128]{0:T(128)}, u32[]{:S(2)}) copy-start(s32[128]{0:T(128)} %param.14) | copy-start | bytes 1540
  7.2 149.1 %all-gather.2.cloned.1.call-start = ((), (), s32[]{:S(2)}) async-start(), calls=%async_computation.3 | async-start | bytes 6488064 | tf_op jit(solution)/shard_map/all_gather | solution.py:178
  13.2 7.3 %collective-permute-start = (bf16[416,256]{1,0:T(8,128)(2,1)S(1)}, bf16[416,256]{1,0:T(8,128)(2,1)S(1)}, u32[]{:S(2)}, u32[]{:S(2)}) collective-permute-start(bf16[416,256]{1,0:T(8,128)(2,1)S(1)} %pad_maximum_fusion), channel_id=1, source_target_pairs={{0,32},{32,0},{64,96},{96,64},{128,160},{160,128},{192,224},{224,1... | collective-permute-start | bytes 638984 | tf_op jit(solution)/shard_map/ppermute | solution.py:22
  20.6 9.6 %collective-permute-start.1 = (bf16[416,256]{1,0:T(8,128)(2,1)S(1)}, bf16[416,256]{1,0:T(8,128)(2,1)S(1)}, u32[]{:S(2)}, u32[]{:S(2)}) collective-permute-start(bf16[416,256]{1,0:T(8,128)(2,1)S(1)} %broadcast_select_fusion), channel_id=1, source_target_pairs={{0,64},{32,96},{64,0},{96,32},{128,192},{160,224},{192,128},{224,1... | collective-permute-start | bytes 638984 | tf_op jit(solution)/shard_map/ppermute | solution.py:22
  30.4 28.3 %collective-permute-start.2 = (bf16[416,256]{1,0:T(8,128)(2,1)S(1)}, bf16[416,256]{1,0:T(8,128)(2,1)S(1)}, u32[]{:S(2)}, u32[]{:S(2)}) collective-permute-start(bf16[416,256]{1,0:T(8,128)(2,1)S(1)} %broadcast_select_fusion.1), channel_id=1, source_target_pairs={{0,384},{32,416},{64,448},{96,480},{128,0},{160,32},{192,64},{224,... | collective-permute-start | bytes 638984 | tf_op jit(solution)/shard_map/ppermute | solution.py:38
  43.4 15.3 %collective-permute-start.3 = (bf16[416,256]{1,0:T(8,128)(2,1)S(1)}, bf16[416,256]{1,0:T(8,128)(2,1)S(1)}, u32[]{:S(2)}, u32[]{:S(2)}) collective-permute-start(bf16[416,256]{1,0:T(8,128)(2,1)S(1)} %broadcast_select_fusion.1), channel_id=1, source_target_pairs={{0,128},{32,160},{64,192},{96,224},{128,256},{160,288},{192,320},{... | collective-permute-start | bytes 638984 | tf_op jit(solution)/shard_map/ppermute | solution.py:37
  58.9 13.9 %collective-permute-start.4 = (bf16[208,256]{1,0:T(8,128)(2,1)S(1)}, bf16[208,256]{1,0:T(8,128)(2,1)S(1)}, u32[]{:S(2)}, u32[]{:S(2)}) collective-permute-start(bf16[208,256]{1,0:T(8,128)(2,1)S(1)} %get-tuple-element.38), channel_id=1, source_target_pairs={{0,128},{32,160},{64,192},{96,224},{128,256},{160,288},{192,320},{... | collective-permute-start | bytes 319496 | tf_op jit(solution)/shard_map/ppermute | solution.py:32
  67.6 9.4 %collective-permute-start.5 = (bf16[208,256]{1,0:T(8,128)(2,1)S(1)}, bf16[208,256]{1,0:T(8,128)(2,1)S(1)}, u32[]{:S(2)}, u32[]{:S(2)}) collective-permute-start(bf16[208,256]{1,0:T(8,128)(2,1)S(1)} %get-tuple-element.39), channel_id=1, source_target_pairs={{0,384},{32,416},{64,448},{96,480},{128,0},{160,32},{192,64},{224,... | collective-permute-start | bytes 319496 | tf_op jit(solution)/shard_map/ppermute | solution.py:33
  165.7 26.6 %all-to-all-start = ((bf16[32,2,4096]{2,1,0:T(2,128)(2,1)}), bf16[32,2,4096]{2,1,0:T(2,128)(2,1)S(1)}, u32[]{:S(2)}, u32[]{:S(2)}) async-start(bf16[32,2,4096]{2,1,0:T(2,128)(2,1)} %reshape.710), calls=%async_computation | async-start | bytes 1048576 | tf_op jit(solution)/shard_map/all_to_all | solution.py:47
  211.0 15.8 %all-to-all-start.1 = ((f32[32,1,768]{2,1,0:T(1,128)}), f32[32,1,768]{2,1,0:T(1,128)S(1)}, u32[]{:S(2)}, u32[]{:S(2)}) async-start(f32[32,1,768]{2,1,0:T(1,128)} %reshape.712), calls=%async_computation.1 | async-start | bytes 196608 | tf_op jit(solution)/shard_map/all_to_all | solution.py:218
  229.3 26.4 %all-to-all-start.2 = ((f32[16,1,768]{2,1,0:T(1,128)}), f32[16,1,768]{2,1,0:T(1,128)S(1)}, u32[]{:S(2)}, u32[]{:S(2)}) async-start(f32[16,1,768]{2,1,0:T(1,128)} %reshape.714), calls=%async_computation.2 | async-start | bytes 98304 | tf_op jit(solution)/shard_map/all_to_all | solution.py:47
Sparse Core Ops, SparseCore 0:
  78.2 77.9 all-gather.1

commit v9 on v8

--- a/solution.py
+++ b/solution.py
@@ -55,7 +55,7 @@
     return jnp.squeeze(top, axis), total, num
 
 
-BLOCK_ROWS = 128
+BLOCK_ROWS = 256
 
 
 def step_kernel(q_ref, row_ok_ref, col_ok_ref, keys_ref, key_ok_ref, values_ref, aux_ref,
@@ -105,9 +105,11 @@
     rows, width = q.shape
     parts, mem, _ = gathered.shape
     channels = mem_values.shape[1]
-    blocks = rows // BLOCK_ROWS
+    block = min(BLOCK_ROWS, rows)
+    assert rows % block == 0
+    blocks = rows // block
     whole = lambda shape: pl.BlockSpec(shape, lambda i: (0, 0))
-    by_row = lambda cols: pl.BlockSpec((BLOCK_ROWS, cols), lambda i: (i, 0))
+    by_row = lambda cols: pl.BlockSpec((block, cols), lambda i: (i, 0))
     stat = jax.ShapeDtypeStruct((1, mem), jnp.float32)
     out_specs = [by_row(channels)]
     out_shape = [jax.ShapeDtypeStruct((rows, channels), jnp.bfloat16)]

time: 265 us -> 260 us (0.981)
  Pallas kernels: 34.5 us -> 29.8 us
    pallas_call x3, Pallas kernels: 34.5 us -> 29.8 us  [step_pass(): pl.pallas_call(lambda *refs: step_kernel(*refs, scale=scale, step=step, w...]
  transfers between devices with their start and end apart: 10 -> 10, of which waited for: 8 -> 8; matrix products, arithmetic and copies ran while one was open for 7% -> 7% of each run, Pallas kernels for 6% -> 5%
where the time goes in v9:
time: 260 us
  waiting for transfers between devices  112 us (43%)
  starting transfers between devices  64 us (25%)
  Pallas kernels  29.8 us (11%)
  local copies, waits for them, and re-layouts  24.9 us (10%)
  between operations  15.7 us (6%)
  other arithmetic  13.5 us (5%)
    all_gather x1, waiting for transfers between devices, body(): gathered = lax.all_gather(packed, 'space', axis=2, tiled=True)  73.9 us
    pallas_call x3, Pallas kernels, step_pass(): pl.pallas_call(lambda *refs: step_kernel(*refs, scale=scale, step=step, w...  29.8 us
    all_to_all x2, starting transfers between devices, gather_all(): return lax.all_to_all(spread, axis, 0, 0, tiled=True)  18.1 us
    ppermute x1, waiting for transfers between devices, broadcast_tm(): got_b = lax.ppermute(value, axis, behind)  13.3 us
    ppermute x1, starting transfers between devices, broadcast_tm(): got_b = lax.ppermute(value, axis, behind)  13 us
    ppermute x2, starting transfers between devices, broadcast_tm(): got = lax.ppermute(value, axis, pairs)  10.4 us
    all_to_all x2, waiting for transfers between devices, gather_all(): return lax.all_to_all(spread, axis, 0, 0, tiled=True)  8.81 us
    ppermute x1, starting transfers between devices, broadcast_tm(): got_a = lax.ppermute(value[:half], axis, ahead)  8.76 us
  transfers between devices with their start and end apart: 10, of which 8 were waited for; matrix products, arithmetic and copies ran while one was open for 7% of the time, Pallas kernels for 5%

profile of v9, /device:TPU:1, one launch (start us, length us, event | category | flops | bytes accessed | tf_op | source)
XLA Modules:
  0.0 259.5 jit_solution(17646778782445675398)
XLA Ops:
  9.1 1.5 gather_fusion.2
  10.9 1.5 gather_fusion.1
  13.2 4.0 %collective-permute-start = (bf16[416,256]{1,0:T(8,128)(2,1)S(1)}, bf16[416,256]{1,0:T(8,128)(2,1)S(1)}, u32[]{:S(2)}, u32[]{:S(2)}) collective-permute-start(bf16[416,256]{1,0:T(8,128)(2,1)S(1)} %pad_maximum_fusion), channel_id=1, source_target_pairs={{0,32},{32,0},{64,96},{96,64},{128,160},{160,128},{192,224},{224,1... | collective-permute-start | bytes 638984 | tf_op jit(solution)/shard_map/ppermute | solution.py:22
  20.6 6.4 %collective-permute-start.1 = (bf16[416,256]{1,0:T(8,128)(2,1)S(1)}, bf16[416,256]{1,0:T(8,128)(2,1)S(1)}, u32[]{:S(2)}, u32[]{:S(2)}) collective-permute-start(bf16[416,256]{1,0:T(8,128)(2,1)S(1)} %broadcast_select_fusion), channel_id=1, source_target_pairs={{0,64},{32,96},{64,0},{96,32},{128,192},{160,224},{192,128},{224,1... | collective-permute-start | bytes 638984 | tf_op jit(solution)/shard_map/ppermute | solution.py:22
  27.8 2.4 collective-permute-done.1
  30.4 13.0 %collective-permute-start.2 = (bf16[416,256]{1,0:T(8,128)(2,1)S(1)}, bf16[416,256]{1,0:T(8,128)(2,1)S(1)}, u32[]{:S(2)}, u32[]{:S(2)}) collective-permute-start(bf16[416,256]{1,0:T(8,128)(2,1)S(1)} %broadcast_select_fusion.1), channel_id=1, source_target_pairs={{0,384},{32,416},{64,448},{96,480},{128,0},{160,32},{192,64},{224,... | collective-permute-start | bytes 638984 | tf_op jit(solution)/shard_map/ppermute | solution.py:38
  43.4 1.9 collective-permute-start.3
  45.3 13.3 %collective-permute-done.2 = bf16[416,256]{1,0:T(8,128)(2,1)S(1)} collective-permute-done((bf16[416,256]{1,0:T(8,128)(2,1)S(1)}, bf16[416,256]{1,0:T(8,128)(2,1)S(1)}, u32[]{:S(2)}, u32[]{:S(2)}) %collective-permute-start.2) | collective-permute-done | bytes 213024 | tf_op jit(solution)/shard_map/ppermute | solution.py:38
  58.9 8.8 %collective-permute-start.4 = (bf16[208,256]{1,0:T(8,128)(2,1)S(1)}, bf16[208,256]{1,0:T(8,128)(2,1)S(1)}, u32[]{:S(2)}, u32[]{:S(2)}) collective-permute-start(bf16[208,256]{1,0:T(8,128)(2,1)S(1)} %get-tuple-element.38), channel_id=1, source_target_pairs={{0,128},{32,160},{64,192},{96,224},{128,256},{160,288},{192,320},{... | collective-permute-start | bytes 319496 | tf_op jit(solution)/shard_map/ppermute | solution.py:32
  67.6 4.1 %collective-permute-start.5 = (bf16[208,256]{1,0:T(8,128)(2,1)S(1)}, bf16[208,256]{1,0:T(8,128)(2,1)S(1)}, u32[]{:S(2)}, u32[]{:S(2)}) collective-permute-start(bf16[208,256]{1,0:T(8,128)(2,1)S(1)} %get-tuple-element.39), channel_id=1, source_target_pairs={{0,384},{32,416},{64,448},{96,480},{128,0},{160,32},{192,64},{224,... | collective-permute-start | bytes 319496 | tf_op jit(solution)/shard_map/ppermute | solution.py:33
  72.7 4.3 %collective-permute-done.5 = bf16[208,256]{1,0:T(8,128)(2,1)S(1)} collective-permute-done((bf16[208,256]{1,0:T(8,128)(2,1)S(1)}, bf16[208,256]{1,0:T(8,128)(2,1)S(1)}, u32[]{:S(2)}, u32[]{:S(2)}) %collective-permute-start.5) | collective-permute-done | bytes 106528 | tf_op jit(solution)/shard_map/ppermute | solution.py:33
  82.4 73.9 %all-gather.2.cloned.1.call-done = bf16[3,2,2048,256]{3,2,1,0:T(8,128)(2,1)} async-done(((bf16[3,2,64,256]{3,2,1,0:T(8,128)(2,1)}), bf16[3,2,2048,256]{3,2,1,0:T(8,128)(2,1)}) %all-gather.2.cloned.1.call-update) | async-done | bytes 6291472 | tf_op jit(solution)/shard_map/all_gather | solution.py:180
  156.3 2.3 slice_bitcast_fusion.refs_5_
  158.6 4.6 %shard_map.77 = bf16[128,64]{1,0:T(8,128)(2,1)} custom-call(bf16[128,256]{1,0:T(8,128)(2,1)} %slice.120.refs_0_, s32[128,1]{1,0:T(8,128)} %reshape.705.refs_1_.refs_2_, s32[128,1]{1,0:T(8,128)} %reshape.705.refs_1_.refs_2_, bf16[3,4096,256]{2,1,0:T(8,128)(2,1)} %bitcast.111, s32[1,4096]{1,0:T(1,128)} %bitcast.125, ...), custom_call_target="tpu_custom_call" | custom-call | tf_op jit(solution)/shard_map/pallas_call | solution.py:119
  164.1 1.5 reshape.710
  165.7 5.4 %all-to-all-start = ((bf16[32,2,4096]{2,1,0:T(2,128)(2,1)}), bf16[32,2,4096]{2,1,0:T(2,128)(2,1)S(1)}, u32[]{:S(2)}, u32[]{:S(2)}) async-start(bf16[32,2,4096]{2,1,0:T(2,128)(2,1)} %reshape.710), calls=%async_computation | async-start | bytes 1048576 | tf_op jit(solution)/shard_map/all_to_all | solution.py:47
  172.9 12.6 %shard_map.79 = (bf16[512,64]{1,0:T(8,128)(2,1)}, f32[1,4096]{1,0:T(1,128)}, f32[1,4096]{1,0:T(1,128)}, f32[1,4096]{1,0:T(1,128)}) custom-call(bf16[512,256]{1,0:T(8,128)(2,1)} %bitcast.120, s32[512,1]{1,0:T(8,128)} %reshape.704.refs_1_.refs_2_, s32[512,1]{1,0:T(8,128)} %reshape.704.refs_1_.refs_2_, bf16[3,4096,256]{2,1,0:T(8,128)(2,1)} %bitcast.113, ...), custom_call_target="tpu_custom_call" | custom-call | tf_op jit(solution)/shard_map/pallas_call | solution.py:119
  186.6 3.4 %convert_reduce_fusion.1 = (s32[4096]{0:T(1024)S(1)}, s32[4096]{0:T(1024)S(1)}) fusion(bf16[3,4096,256]{2,1,0:T(8,128)(2,1)} %bitcast.115), kind=kLoop, calls=%fused_computation.9 | loop fusion | flops 8192 | bytes 49152 | tf_op jit(solution)/shard_map/convert_element_type | solution.py:184
  191.7 12.6 %shard_map.78 = (bf16[512,64]{1,0:T(8,128)(2,1)}, f32[1,4096]{1,0:T(1,128)}, f32[1,4096]{1,0:T(1,128)}, f32[1,4096]{1,0:T(1,128)}) custom-call(bf16[512,256]{1,0:T(8,128)(2,1)} %bitcast.121, s32[512,1]{1,0:T(8,128)} %reshape.704.refs_1_.refs_2_, s32[512,1]{1,0:T(8,128)} %reshape.704.refs_1_.refs_2_, bf16[3,4096,256]{2,1,0:T(8,128)(2,1)} %bitcast.116, ...), custom_call_target="tpu_custom_call" | custom-call | tf_op jit(solution)/shard_map/pallas_call | solution.py:119
  206.3 7.7 %all-to-all-start.1 = ((f32[32,1,768]{2,1,0:T(1,128)}), f32[32,1,768]{2,1,0:T(1,128)S(1)}, u32[]{:S(2)}, u32[]{:S(2)}) async-start(f32[32,1,768]{2,1,0:T(1,128)} %reshape.712), calls=%async_computation.1 | async-start | bytes 196608 | tf_op jit(solution)/shard_map/all_to_all | solution.py:220
  215.4 6.7 %all-to-all-done.1 = f32[32,1,768]{2,1,0:T(1,128)S(1)} async-done(((f32[32,1,768]{2,1,0:T(1,128)}), f32[32,1,768]{2,1,0:T(1,128)S(1)}, u32[]{:S(2)}, u32[]{:S(2)}) %all-to-all-start.1) | async-done | bytes 98336 | tf_op jit(solution)/shard_map/all_to_all | solution.py:220
  224.6 12.7 %all-to-all-start.2 = ((f32[16,1,768]{2,1,0:T(1,128)}), f32[16,1,768]{2,1,0:T(1,128)S(1)}, u32[]{:S(2)}, u32[]{:S(2)}) async-start(f32[16,1,768]{2,1,0:T(1,128)} %reshape.714), calls=%async_computation.2 | async-start | bytes 98304 | tf_op jit(solution)/shard_map/all_to_all | solution.py:47
  237.3 1.2 gather_fusion.6
  242.2 8.8 %all-to-all-done.2 = f32[16,1,768]{2,1,0:T(1,128)S(1)} async-done(((f32[16,1,768]{2,1,0:T(1,128)}), f32[16,1,768]{2,1,0:T(1,128)S(1)}, u32[]{:S(2)}, u32[]{:S(2)}) %all-to-all-start.2) | async-done | bytes 49184 | tf_op jit(solution)/shard_map/all_to_all | solution.py:47
  (116 shorter events, 29.1 us)
Async XLA Ops:
  7.2 5.3 %copy-start = (bf16[8,64,256]{2,1,0:T(8,128)(2,1)S(1)}, bf16[8,64,256]{2,1,0:T(8,128)(2,1)}, u32[]{:S(2)}) copy-start(bf16[8,64,256]{2,1,0:T(8,128)(2,1)} %param.11) | copy-start | bytes 786436
  7.2 73.0 %copy-start.2 = (s32[2,2]{1,0:T(2,128)S(1)}, s32[2,2]{1,0:T(2,128)}, u32[]{:S(2)}) copy-start(s32[2,2]{1,0:T(2,128)} %param.15) | copy-start | bytes 52
  7.2 71.7 %copy-start.1 = (s32[128]{0:T(128)S(1)}, s32[128]{0:T(128)}, u32[]{:S(2)}) copy-start(s32[128]{0:T(128)} %param.14) | copy-start | bytes 1540
  7.2 149.1 %all-gather.2.cloned.1.call-start = ((), (), s32[]{:S(2)}) async-start(), calls=%async_computation.3 | async-start | bytes 6488064 | tf_op jit(solution)/shard_map/all_gather | solution.py:180
  13.2 7.3 %collective-permute-start = (bf16[416,256]{1,0:T(8,128)(2,1)S(1)}, bf16[416,256]{1,0:T(8,128)(2,1)S(1)}, u32[]{:S(2)}, u32[]{:S(2)}) collective-permute-start(bf16[416,256]{1,0:T(8,128)(2,1)S(1)} %pad_maximum_fusion), channel_id=1, source_target_pairs={{0,32},{32,0},{64,96},{96,64},{128,160},{160,128},{192,224},{224,1... | collective-permute-start | bytes 638984 | tf_op jit(solution)/shard_map/ppermute | solution.py:22
  20.6 9.6 %collective-permute-start.1 = (bf16[416,256]{1,0:T(8,128)(2,1)S(1)}, bf16[416,256]{1,0:T(8,128)(2,1)S(1)}, u32[]{:S(2)}, u32[]{:S(2)}) collective-permute-start(bf16[416,256]{1,0:T(8,128)(2,1)S(1)} %broadcast_select_fusion), channel_id=1, source_target_pairs={{0,64},{32,96},{64,0},{96,32},{128,192},{160,224},{192,128},{224,1... | collective-permute-start | bytes 638984 | tf_op jit(solution)/shard_map/ppermute | solution.py:22
  30.4 28.3 %collective-permute-start.2 = (bf16[416,256]{1,0:T(8,128)(2,1)S(1)}, bf16[416,256]{1,0:T(8,128)(2,1)S(1)}, u32[]{:S(2)}, u32[]{:S(2)}) collective-permute-start(bf16[416,256]{1,0:T(8,128)(2,1)S(1)} %broadcast_select_fusion.1), channel_id=1, source_target_pairs={{0,384},{32,416},{64,448},{96,480},{128,0},{160,32},{192,64},{224,... | collective-permute-start | bytes 638984 | tf_op jit(solution)/shard_map/ppermute | solution.py:38
  43.4 15.3 %collective-permute-start.3 = (bf16[416,256]{1,0:T(8,128)(2,1)S(1)}, bf16[416,256]{1,0:T(8,128)(2,1)S(1)}, u32[]{:S(2)}, u32[]{:S(2)}) collective-permute-start(bf16[416,256]{1,0:T(8,128)(2,1)S(1)} %broadcast_select_fusion.1), channel_id=1, source_target_pairs={{0,128},{32,160},{64,192},{96,224},{128,256},{160,288},{192,320},{... | collective-permute-start | bytes 638984 | tf_op jit(solution)/shard_map/ppermute | solution.py:37
  58.9 13.9 %collective-permute-start.4 = (bf16[208,256]{1,0:T(8,128)(2,1)S(1)}, bf16[208,256]{1,0:T(8,128)(2,1)S(1)}, u32[]{:S(2)}, u32[]{:S(2)}) collective-permute-start(bf16[208,256]{1,0:T(8,128)(2,1)S(1)} %get-tuple-element.38), channel_id=1, source_target_pairs={{0,128},{32,160},{64,192},{96,224},{128,256},{160,288},{192,320},{... | collective-permute-start | bytes 319496 | tf_op jit(solution)/shard_map/ppermute | solution.py:32
  67.6 9.4 %collective-permute-start.5 = (bf16[208,256]{1,0:T(8,128)(2,1)S(1)}, bf16[208,256]{1,0:T(8,128)(2,1)S(1)}, u32[]{:S(2)}, u32[]{:S(2)}) collective-permute-start(bf16[208,256]{1,0:T(8,128)(2,1)S(1)} %get-tuple-element.39), channel_id=1, source_target_pairs={{0,384},{32,416},{64,448},{96,480},{128,0},{160,32},{192,64},{224,... | collective-permute-start | bytes 319496 | tf_op jit(solution)/shard_map/ppermute | solution.py:33
  165.7 24.3 %all-to-all-start = ((bf16[32,2,4096]{2,1,0:T(2,128)(2,1)}), bf16[32,2,4096]{2,1,0:T(2,128)(2,1)S(1)}, u32[]{:S(2)}, u32[]{:S(2)}) async-start(bf16[32,2,4096]{2,1,0:T(2,128)(2,1)} %reshape.710), calls=%async_computation | async-start | bytes 1048576 | tf_op jit(solution)/shard_map/all_to_all | solution.py:47
  206.3 15.8 %all-to-all-start.1 = ((f32[32,1,768]{2,1,0:T(1,128)}), f32[32,1,768]{2,1,0:T(1,128)S(1)}, u32[]{:S(2)}, u32[]{:S(2)}) async-start(f32[32,1,768]{2,1,0:T(1,128)} %reshape.712), calls=%async_computation.1 | async-start | bytes 196608 | tf_op jit(solution)/shard_map/all_to_all | solution.py:220
  224.6 26.4 %all-to-all-start.2 = ((f32[16,1,768]{2,1,0:T(1,128)}), f32[16,1,768]{2,1,0:T(1,128)S(1)}, u32[]{:S(2)}, u32[]{:S(2)}) async-start(f32[16,1,768]{2,1,0:T(1,128)} %reshape.714), calls=%async_computation.2 | async-start | bytes 98304 | tf_op jit(solution)/shard_map/all_to_all | solution.py:47
Sparse Core Ops, SparseCore 0:
  78.2 77.9 all-gather.1

commit v10 on v9

--- a/solution.py
+++ b/solution.py
@@ -1,3 +1,4 @@
+import functools
 import math
 
 import jax
@@ -58,8 +59,14 @@
 BLOCK_ROWS = 256
 
 
-def step_kernel(q_ref, row_ok_ref, col_ok_ref, keys_ref, key_ok_ref, values_ref, aux_ref,
-                *out_refs, scale, step, with_stats):
+def step_kernel(q_ref, row_ok_ref, col_ok_ref, keys_ref, key_ok_ref, aux_ref, *refs,
+                scale, step, with_stats, channels, values_from_aux):
+    if values_from_aux:
+        values = aux_ref[:, :channels]
+        out_refs = refs
+    else:
+        values = refs[0][...]
+        out_refs = refs[1:]
     scores = lax.dot_general(
         q_ref[...], keys_ref[...], (((1,), (1,)), ((), ())), preferred_element_type=jnp.float32
     ) * scale
@@ -70,7 +77,7 @@
     weights = jnp.where(key_ok, jnp.exp(scores - row_max), 0.0)
     total = jnp.sum(weights, axis=1, keepdims=True)
     mixed = jnp.dot(
-        weights.astype(jnp.bfloat16), values_ref[...], preferred_element_type=jnp.float32
+        weights.astype(jnp.bfloat16), values, preferred_element_type=jnp.float32
     ) / total
     out = jnp.where(row_ok, mixed, 0.0).astype(jnp.bfloat16)
     out_refs[0][...] = out
@@ -83,7 +90,6 @@
         cmax_ref[...] = jnp.full_like(cmax_ref, LOWEST)
         ctot_ref[...] = jnp.zeros_like(ctot_ref)
         cnum_ref[...] = jnp.zeros_like(cnum_ref)
-        channels = values_ref.shape[1]
         ids = aux_ref[:, channels + step:channels + step + 1].astype(jnp.float32)
         classes = lax.broadcasted_iota(jnp.int32, (1, channels), 1).astype(jnp.float32)
         onehot = (ids == classes).astype(jnp.float32)
@@ -101,10 +107,9 @@
     cmax_ref[...] = new_max
 
 
-def step_pass(q, row_ok, col_ok, gathered, step, key_ok, mem_values, scale, with_stats):
+def step_pass(q, row_ok, col_ok, gathered, step, key_ok, mem_values, channels, scale, with_stats):
     rows, width = q.shape
     parts, mem, _ = gathered.shape
-    channels = mem_values.shape[1]
     block = min(BLOCK_ROWS, rows)
     assert rows % block == 0
     blocks = rows // block
@@ -116,21 +121,29 @@
     if with_stats:
         out_specs += [whole((1, mem))] * 3
         out_shape += [stat] * 3
+    in_specs = [
+        by_row(width), by_row(1), by_row(1),
+        pl.BlockSpec((None, mem, width), lambda i: (step, 0, 0)),
+        whole((1, mem)),
+        pl.BlockSpec((None, mem, 128), lambda i: (parts - 1, 0, 0)),
+    ]
+    args = [q, row_ok, col_ok, gathered, key_ok, gathered]
+    if mem_values is not None:
+        in_specs.append(whole((mem, channels)))
+        args.append(mem_values)
+    kernel = functools.partial(
+        step_kernel, scale=scale, step=step, with_stats=with_stats, channels=channels,
+        values_from_aux=mem_values is None,
+    )
     return pl.pallas_call(
-        lambda *refs: step_kernel(*refs, scale=scale, step=step, with_stats=with_stats),
+        kernel,
         grid=(blocks,),
-        in_specs=[
-            by_row(width), by_row(1), by_row(1),
-            pl.BlockSpec((None, mem, width), lambda i: (step, 0, 0)),
-            whole((1, mem)),
-            whole((mem, channels)),
-            pl.BlockSpec((None, mem, 128), lambda i: (parts - 1, 0, 0)),
-        ],
+        in_specs=in_specs,
         out_specs=out_specs,
         out_shape=out_shape,
         scratch_shapes=[pltpu.VMEM((channels, mem), jnp.bfloat16)] if with_stats else [],
         compiler_params=pltpu.CompilerParams(dimension_semantics=("arbitrary",)),
-    )(q, row_ok, col_ok, gathered, key_ok, mem_values, gathered)
+    )(*args)
 
 
 def body(queries, keys, label_values, class_ids, valid_pixels, keyframe_index):
@@ -171,18 +184,27 @@
     kf_queries = flat[sizes[0]:sizes[0] + sizes[1]].reshape(kf_queries.shape)
     kf_values = flat[sizes[0] + sizes[1]:].reshape(kf_values.shape)
 
-    kf_ids = jnp.take(class_ids, flat_kf, axis=0).astype(jnp.bfloat16)
+    kf_class = jnp.take(class_ids, flat_kf, axis=0)
+    kf_ok = pixel_ids[None, :] < jnp.take(valid_pixels, flat_kf)[:, None]
+    hits = (kf_class[:, :, None] == class_range[None, None, :]) & kf_ok[:, :, None]
+    partial = jnp.sum(hits.astype(jnp.int32), axis=1).reshape(total_steps, keyframes, channels)
+    partial = jnp.sum(partial, axis=1).astype(jnp.bfloat16)
+    kf_ids = kf_class.astype(jnp.bfloat16)
     kf_ids = kf_ids.reshape(total_steps, keyframes, pix_dev).transpose(1, 2, 0)
     step_keys = kf_keys.reshape(total_steps, keyframes, pix_dev, width)
     aux = jnp.concatenate([kf_values, kf_ids], axis=2)
-    aux = jnp.pad(aux, ((0, 0), (0, 0), (0, width - aux.shape[2])))
+    aux = jnp.pad(aux, ((0, 0), (0, 0), (0, 128 - aux.shape[2])))
+    tally = jnp.zeros((keyframes, pix_dev, width - 128), jnp.bfloat16)
+    tally = tally.at[0, :total_steps, :channels].set(partial)
+    aux = jnp.concatenate([aux, tally], axis=2)
     packed = jnp.concatenate([step_keys, aux[None]], axis=0)
     gathered = lax.all_gather(packed, "space", axis=2, tiled=True)
     gathered = gathered.reshape(total_steps + 1, mem_width, width)
-    mem_values = gathered[total_steps, :, :channels]
-    mem_ids = [
-        gathered[total_steps, :, channels + s].astype(jnp.int32) for s in range(total_steps)
-    ]
+    tallies = gathered[total_steps].reshape(keyframes, n_space, pix_dev, width)
+    counts = jnp.sum(
+        tallies[0, :, :total_steps, 128:128 + channels].astype(jnp.int32), axis=0
+    )
+    mem_values = None
 
     extra_queries = kf_queries.reshape(later, pix_dev, width)
     extra_valid = pixel_ids[None, :] < jnp.take(valid_pixels, flat_kf[keyframes:])[:, None]
@@ -201,7 +223,8 @@
             extra_ok = extra_valid[step * keyframes:(step + 1) * keyframes].reshape(-1, 1)
             extra_ok = extra_ok.astype(jnp.int32)
             (part,) = step_pass(
-                extra, extra_ok, extra_ok, gathered, step, key_ok, mem_values, scale, False
+                extra, extra_ok, extra_ok, gathered, step, key_ok, mem_values, channels, scale,
+                False,
             )
             part = part.reshape(keyframes, pix_dev, channels)
             next_values = gather_all(part, "space").transpose(1, 0, 2, 3).reshape(
@@ -209,7 +232,7 @@
             )
         ok = row_valid.astype(jnp.int32)[:, None]
         readout, col_max, col_total, col_num = step_pass(
-            query_rows, ok, ok, gathered, step, key_ok, mem_values, scale, True
+            query_rows, ok, ok, gathered, step, key_ok, mem_values, channels, scale, True
         )
         stats.append(jnp.stack([col_max[0], col_total[0], col_num[0]]))
         if step + 1 < total_steps:
@@ -222,27 +245,18 @@
     joined = gather_all(jnp.stack([m, t, n]), "tm")
     m, col_total, col_num = merge_stats(joined[:, 0], joined[:, 1], joined[:, 2], 0)
 
-    confidences = []
-    for step in range(total_steps):
-        chosen = keyframe_index[step]
-        key_valid = (
-            jnp.arange(pix_all, dtype=jnp.int32)[None, :]
-            < jnp.take(valid_pixels, chosen)[:, None]
-        ).reshape(mem_width)
-        class_match = mem_ids[step][None, :] == class_range[:, None]
-        hits = (class_match & key_valid[None, :]).astype(jnp.int32)
-        counts = jnp.sum(hits, axis=1)
-        all_count = jnp.sum(counts)
-        own_ids = lax.dynamic_slice_in_dim(
-            mem_ids[step].reshape(keyframes, pix_all), space_pos * pix_dev, pix_dev, 1
-        )
-        own_valid = pixel_ids[None, :] < jnp.take(valid_pixels, chosen)[:, None]
-        own = jnp.take(counts, own_ids)
-        own_safe = jnp.where(own_valid, own, 1)
-        factor = jnp.sqrt(all_count.astype(jnp.float32) / (channels * own_safe.astype(jnp.float32)))
-        conf = jnp.where(own_valid, col_num[step] / col_total[step] * factor, 0.0)
-        confidences.append(conf)
-    return (readout.reshape(fr_dev, pix_dev, channels), jnp.stack(confidences))
+    all_count = jnp.sum(counts, axis=1)
+    own_ids = kf_class.reshape(total_steps, keyframes, pix_dev)
+    own = jnp.sum(
+        jnp.where(own_ids[..., None] == class_range, counts[:, None, None, :], 0), axis=3
+    )
+    own_valid = kf_ok.reshape(total_steps, keyframes, pix_dev)
+    own_safe = jnp.where(own_valid, own, 1)
+    factor = jnp.sqrt(
+        all_count[:, None, None].astype(jnp.float32) / (channels * own_safe.astype(jnp.float32))
+    )
+    confidences = jnp.where(own_valid, col_num / col_total * factor, 0.0)
+    return (readout.reshape(fr_dev, pix_dev, channels), confidences)
 
 
 def solution(mesh):

time: 260 us -> 253 us (0.973)
  waiting for transfers between devices: 112 us -> 121 us
  starting transfers between devices: 64 us -> 57.6 us
  other arithmetic: 13.5 us -> 7.79 us
    all_gather x1, waiting for transfers between devices: 73.9 us -> 64.4 us  [body(): gathered = lax.all_gather(packed, 'space', axis=2, tiled=True)]
    ppermute x1, starting transfers between devices: 1.92 us -> 9.36 us  [broadcast_tm(): got_a = lax.ppermute(value, axis, ahead)]
    ppermute x1, starting transfers between devices: 13 us -> 5.56 us  [broadcast_tm(): got_b = lax.ppermute(value, axis, behind)]
    ppermute x1, waiting for transfers between devices: 13.3 us -> 20.6 us  [broadcast_tm(): got_b = lax.ppermute(value, axis, behind)]
    all_to_all x2, waiting for transfers between devices: 8.81 us -> 14.7 us  [gather_all(): return lax.all_to_all(spread, axis, 0, 0, tiled=True)]
    ppermute x1, waiting for transfers between devices: 1.01 us -> 4.84 us  [broadcast_tm(): got_a = lax.ppermute(value[:half], axis, ahead)]
    convert_element_type x1 -> x2, other arithmetic: 3.38 us -> 0.01 us  [the longest x1 0.01 us: body(): all_count[:, None, None].astype(jnp.float32)]
  transfers between devices with their start and end apart: 10 -> 10, of which waited for: 8 -> 9; matrix products, arithmetic and copies ran while one was open for 7% -> 5% of each run, Pallas kernels for 5% -> 5%
where the time goes in v10:
time: 253 us
  waiting for transfers between devices  121 us (48%)
  starting transfers between devices  57.6 us (23%)
  Pallas kernels  29.2 us (12%)
  local copies, waits for them, and re-layouts  23 us (9%)
  between operations  14.5 us (6%)
  other arithmetic  7.79 us (3%)
    all_gather x1, waiting for transfers between devices, body(): gathered = lax.all_gather(packed, 'space', axis=2, tiled=True)  64.4 us
    pallas_call x3, Pallas kernels, step_pass(): pl.pallas_call(kernel, grid=(blocks,), in_specs=in_specs, out_specs=out_s...  29.2 us
    ppermute x1, waiting for transfers between devices, broadcast_tm(): got_b = lax.ppermute(value, axis, behind)  20.6 us
    all_to_all x2, starting transfers between devices, gather_all(): return lax.all_to_all(spread, axis, 0, 0, tiled=True)  18.1 us
    all_to_all x2, waiting for transfers between devices, gather_all(): return lax.all_to_all(spread, axis, 0, 0, tiled=True)  14.7 us
    ppermute x1, starting transfers between devices, broadcast_tm(): got_a = lax.ppermute(value, axis, ahead)  9.36 us
    ppermute x2, starting transfers between devices, broadcast_tm(): got = lax.ppermute(value, axis, pairs)  8.93 us
    ppermute x1, starting transfers between devices, broadcast_tm(): got_a = lax.ppermute(value[:half], axis, ahead)  6.73 us
  transfers between devices with their start and end apart: 10, of which 9 were waited for; matrix products, arithmetic and copies ran while one was open for 5% of the time, Pallas kernels for 5%

profile of v10, /device:TPU:1, one launch (start us, length us, event | category | flops | bytes accessed | tf_op | source)
XLA Modules:
  0.0 252.6 jit_solution(11124603414001609692)
XLA Ops:
  9.2 1.5 gather_fusion.2
  10.9 1.5 gather_fusion.1
  13.2 4.0 %collective-permute-start = (bf16[416,256]{1,0:T(8,128)(2,1)S(1)}, bf16[416,256]{1,0:T(8,128)(2,1)S(1)}, u32[]{:S(2)}, u32[]{:S(2)}) collective-permute-start(bf16[416,256]{1,0:T(8,128)(2,1)S(1)} %pad_maximum_fusion), channel_id=1, source_target_pairs={{0,32},{32,0},{64,96},{96,64},{128,160},{160,128},{192,224},{224,1... | collective-permute-start | bytes 638984 | tf_op jit(solution)/shard_map/ppermute | solution.py:23
  22.1 4.9 %collective-permute-start.1 = (bf16[416,256]{1,0:T(8,128)(2,1)S(1)}, bf16[416,256]{1,0:T(8,128)(2,1)S(1)}, u32[]{:S(2)}, u32[]{:S(2)}) collective-permute-start(bf16[416,256]{1,0:T(8,128)(2,1)S(1)} %broadcast_select_fusion), channel_id=1, source_target_pairs={{0,64},{32,96},{64,0},{96,32},{128,192},{160,224},{192,128},{224,1... | collective-permute-start | bytes 638984 | tf_op jit(solution)/shard_map/ppermute | solution.py:23
  27.0 3.2 %collective-permute-done.1 = bf16[416,256]{1,0:T(8,128)(2,1)S(1)} collective-permute-done((bf16[416,256]{1,0:T(8,128)(2,1)S(1)}, bf16[416,256]{1,0:T(8,128)(2,1)S(1)}, u32[]{:S(2)}, u32[]{:S(2)}) %collective-permute-start.1) | collective-permute-done | bytes 213024 | tf_op jit(solution)/shard_map/ppermute | solution.py:23
  30.4 9.4 %collective-permute-start.3 = (bf16[416,256]{1,0:T(8,128)(2,1)S(1)}, bf16[416,256]{1,0:T(8,128)(2,1)S(1)}, u32[]{:S(2)}, u32[]{:S(2)}) collective-permute-start(bf16[416,256]{1,0:T(8,128)(2,1)S(1)} %broadcast_select_fusion.1), channel_id=1, source_target_pairs={{0,128},{32,160},{64,192},{96,224},{128,256},{160,288},{192,320},{... | collective-permute-start | bytes 638984 | tf_op jit(solution)/shard_map/ppermute | solution.py:38
  39.7 5.6 %collective-permute-start.2 = (bf16[416,256]{1,0:T(8,128)(2,1)S(1)}, bf16[416,256]{1,0:T(8,128)(2,1)S(1)}, u32[]{:S(2)}, u32[]{:S(2)}) collective-permute-start(bf16[416,256]{1,0:T(8,128)(2,1)S(1)} %broadcast_select_fusion.1), channel_id=1, source_target_pairs={{0,384},{32,416},{64,448},{96,480},{128,0},{160,32},{192,64},{224,... | collective-permute-start | bytes 638984 | tf_op jit(solution)/shard_map/ppermute | solution.py:39
  45.3 1.6 collective-permute-done.3
  46.9 20.6 %collective-permute-done.2 = bf16[416,256]{1,0:T(8,128)(2,1)S(1)} collective-permute-done((bf16[416,256]{1,0:T(8,128)(2,1)S(1)}, bf16[416,256]{1,0:T(8,128)(2,1)S(1)}, u32[]{:S(2)}, u32[]{:S(2)}) %collective-permute-start.2) | collective-permute-done | bytes 213024 | tf_op jit(solution)/shard_map/ppermute | solution.py:39
  67.7 6.7 %collective-permute-start.4 = (bf16[208,256]{1,0:T(8,128)(2,1)S(1)}, bf16[208,256]{1,0:T(8,128)(2,1)S(1)}, u32[]{:S(2)}, u32[]{:S(2)}) collective-permute-start(bf16[208,256]{1,0:T(8,128)(2,1)S(1)} %get-tuple-element.51), channel_id=1, source_target_pairs={{0,128},{32,160},{64,192},{96,224},{128,256},{160,288},{192,320},{... | collective-permute-start | bytes 319496 | tf_op jit(solution)/shard_map/ppermute | solution.py:33
  74.5 2.5 collective-permute-start.5
  76.9 4.8 %collective-permute-done.4 = bf16[208,256]{1,0:T(8,128)(2,1)S(1)} collective-permute-done((bf16[208,256]{1,0:T(8,128)(2,1)S(1)}, bf16[208,256]{1,0:T(8,128)(2,1)S(1)}, u32[]{:S(2)}, u32[]{:S(2)}) %collective-permute-start.4) | collective-permute-done | bytes 106528 | tf_op jit(solution)/shard_map/ppermute | solution.py:33
  81.8 4.9 %collective-permute-done.5 = bf16[208,256]{1,0:T(8,128)(2,1)S(1)} collective-permute-done((bf16[208,256]{1,0:T(8,128)(2,1)S(1)}, bf16[208,256]{1,0:T(8,128)(2,1)S(1)}, u32[]{:S(2)}, u32[]{:S(2)}) %collective-permute-start.5) | collective-permute-done | bytes 106528 | tf_op jit(solution)/shard_map/ppermute | solution.py:34
  91.3 64.4 %all-gather.2.cloned.1.call-done = bf16[3,2,2048,256]{3,2,1,0:T(8,128)(2,1)} async-done(((bf16[3,2,64,256]{3,2,1,0:T(8,128)(2,1)}), bf16[3,2,2048,256]{3,2,1,0:T(8,128)(2,1)}) %all-gather.2.cloned.1.call-update) | async-done | bytes 6291472 | tf_op jit(solution)/shard_map/all_gather | solution.py:201
  155.7 4.2 %shard_map.77 = bf16[128,64]{1,0:T(8,128)(2,1)} custom-call(bf16[128,256]{1,0:T(8,128)(2,1)} %slice.122.q_ref, s32[128,1]{1,0:T(8,128)} %reshape.763.row_ok_ref.col_ok_ref, s32[128,1]{1,0:T(8,128)} %reshape.763.row_ok_ref.col_ok_ref, bf16[3,4096,256]{2,1,0:T(8,128)(2,1)} %bitcast.100, s32[1,4096]{1,0:T(1,128)} %bitcast.114, bf16[3,4096,256]{2,1,0:T(8,128)(2,1)} %bitcast.101), custom_call_target="tpu_custom_call" | custom-call | tf_op jit(solution)/shard_map/pallas_call | solution.py:138
  161.0 1.6 reshape.764
  162.5 5.4 %all-to-all-start = ((bf16[32,2,4096]{2,1,0:T(2,128)(2,1)}), bf16[32,2,4096]{2,1,0:T(2,128)(2,1)S(1)}, u32[]{:S(2)}, u32[]{:S(2)}) async-start(bf16[32,2,4096]{2,1,0:T(2,128)(2,1)} %reshape.764), calls=%async_computation | async-start | bytes 1048576 | tf_op jit(solution)/shard_map/all_to_all | solution.py:48
  169.7 12.3 %shard_map.79 = (bf16[512,64]{1,0:T(8,128)(2,1)}, f32[1,4096]{1,0:T(1,128)}, f32[1,4096]{1,0:T(1,128)}, f32[1,4096]{1,0:T(1,128)}) custom-call(bf16[512,256]{1,0:T(8,128)(2,1)} %bitcast.109, s32[512,1]{1,0:T(8,128)} %reshape.762.row_ok_ref.col_ok_ref, s32[512,1]{1,0:T(8,128)} %reshape.762.row_ok_ref.col_ok_ref, bf16[3,4096,256]{2,1,0:T(8,128)(2,1)} %bitcast.102, ...), custom_call_target="tpu_custom_call" | custom-call | tf_op jit(solution)/shard_map/pallas_call | solution.py:138
  186.1 12.6 %shard_map.78 = (bf16[512,64]{1,0:T(8,128)(2,1)}, f32[1,4096]{1,0:T(1,128)}, f32[1,4096]{1,0:T(1,128)}, f32[1,4096]{1,0:T(1,128)}) custom-call(bf16[512,256]{1,0:T(8,128)(2,1)} %bitcast.110, s32[512,1]{1,0:T(8,128)} %reshape.762.row_ok_ref.col_ok_ref, s32[512,1]{1,0:T(8,128)} %reshape.762.row_ok_ref.col_ok_ref, bf16[3,4096,256]{2,1,0:T(8,128)(2,1)} %bitcast.104, ...), custom_call_target="tpu_custom_call" | custom-call | tf_op jit(solution)/shard_map/pallas_call | solution.py:138
  200.7 6.4 %all-to-all-start.1 = ((f32[32,1,768]{2,1,0:T(1,128)}), f32[32,1,768]{2,1,0:T(1,128)S(1)}, u32[]{:S(2)}, u32[]{:S(2)}) async-start(f32[32,1,768]{2,1,0:T(1,128)} %reshape.766), calls=%async_computation.1 | async-start | bytes 196608 | tf_op jit(solution)/shard_map/all_to_all | solution.py:243
  207.2 1.7 slice.129
  208.9 6.3 %all-to-all-done.1 = f32[32,1,768]{2,1,0:T(1,128)S(1)} async-done(((f32[32,1,768]{2,1,0:T(1,128)}), f32[32,1,768]{2,1,0:T(1,128)S(1)}, u32[]{:S(2)}, u32[]{:S(2)}) %all-to-all-start.1) | async-done | bytes 98336 | tf_op jit(solution)/shard_map/all_to_all | solution.py:243
  217.7 12.7 %all-to-all-start.2 = ((f32[16,1,768]{2,1,0:T(1,128)}), f32[16,1,768]{2,1,0:T(1,128)S(1)}, u32[]{:S(2)}, u32[]{:S(2)}) async-start(f32[16,1,768]{2,1,0:T(1,128)} %reshape.768), calls=%async_computation.2 | async-start | bytes 98304 | tf_op jit(solution)/shard_map/all_to_all | solution.py:48
  230.8 13.3 %all-to-all-done.2 = f32[16,1,768]{2,1,0:T(1,128)S(1)} async-done(((f32[16,1,768]{2,1,0:T(1,128)}), f32[16,1,768]{2,1,0:T(1,128)S(1)}, u32[]{:S(2)}, u32[]{:S(2)}) %all-to-all-start.2) | async-done | bytes 49184 | tf_op jit(solution)/shard_map/all_to_all | solution.py:48
  (110 shorter events, 25.9 us)
Async XLA Ops:
  7.2 5.3 %copy-start = (bf16[8,64,256]{2,1,0:T(8,128)(2,1)S(1)}, bf16[8,64,256]{2,1,0:T(8,128)(2,1)}, u32[]{:S(2)}) copy-start(bf16[8,64,256]{2,1,0:T(8,128)(2,1)} %param.11) | copy-start | bytes 786436
  7.2 148.5 %all-gather.2.cloned.1.call-start = ((), (), s32[]{:S(2)}) async-start(), calls=%async_computation.3 | async-start | bytes 6488064 | tf_op jit(solution)/shard_map/all_gather | solution.py:201
  13.2 8.8 %collective-permute-start = (bf16[416,256]{1,0:T(8,128)(2,1)S(1)}, bf16[416,256]{1,0:T(8,128)(2,1)S(1)}, u32[]{:S(2)}, u32[]{:S(2)}) collective-permute-start(bf16[416,256]{1,0:T(8,128)(2,1)S(1)} %pad_maximum_fusion), channel_id=1, source_target_pairs={{0,32},{32,0},{64,96},{96,64},{128,160},{160,128},{192,224},{224,1... | collective-permute-start | bytes 638984 | tf_op jit(solution)/shard_map/ppermute | solution.py:23
  22.1 65.7 %copy-start.2 = (s32[2,2]{1,0:T(2,128)S(1)}, s32[2,2]{1,0:T(2,128)}, u32[]{:S(2)}) copy-start(s32[2,2]{1,0:T(2,128)} %param.15) | copy-start | bytes 52
  22.1 65.8 %copy-start.1 = (s32[128]{0:T(128)S(1)}, s32[128]{0:T(128)}, u32[]{:S(2)}) copy-start(s32[128]{0:T(128)} %param.14) | copy-start | bytes 1540
  22.1 8.1 %collective-permute-start.1 = (bf16[416,256]{1,0:T(8,128)(2,1)S(1)}, bf16[416,256]{1,0:T(8,128)(2,1)S(1)}, u32[]{:S(2)}, u32[]{:S(2)}) collective-permute-start(bf16[416,256]{1,0:T(8,128)(2,1)S(1)} %broadcast_select_fusion), channel_id=1, source_target_pairs={{0,64},{32,96},{64,0},{96,32},{128,192},{160,224},{192,128},{224,1... | collective-permute-start | bytes 638984 | tf_op jit(solution)/shard_map/ppermute | solution.py:23
  30.4 16.5 %collective-permute-start.3 = (bf16[416,256]{1,0:T(8,128)(2,1)S(1)}, bf16[416,256]{1,0:T(8,128)(2,1)S(1)}, u32[]{:S(2)}, u32[]{:S(2)}) collective-permute-start(bf16[416,256]{1,0:T(8,128)(2,1)S(1)} %broadcast_select_fusion.1), channel_id=1, source_target_pairs={{0,128},{32,160},{64,192},{96,224},{128,256},{160,288},{192,320},{... | collective-permute-start | bytes 638984 | tf_op jit(solution)/shard_map/ppermute | solution.py:38
  39.7 27.8 %collective-permute-start.2 = (bf16[416,256]{1,0:T(8,128)(2,1)S(1)}, bf16[416,256]{1,0:T(8,128)(2,1)S(1)}, u32[]{:S(2)}, u32[]{:S(2)}) collective-permute-start(bf16[416,256]{1,0:T(8,128)(2,1)S(1)} %broadcast_select_fusion.1), channel_id=1, source_target_pairs={{0,384},{32,416},{64,448},{96,480},{128,0},{160,32},{192,64},{224,... | collective-permute-start | bytes 638984 | tf_op jit(solution)/shard_map/ppermute | solution.py:39
  67.7 14.1 %collective-permute-start.4 = (bf16[208,256]{1,0:T(8,128)(2,1)S(1)}, bf16[208,256]{1,0:T(8,128)(2,1)S(1)}, u32[]{:S(2)}, u32[]{:S(2)}) collective-permute-start(bf16[208,256]{1,0:T(8,128)(2,1)S(1)} %get-tuple-element.51), channel_id=1, source_target_pairs={{0,128},{32,160},{64,192},{96,224},{128,256},{160,288},{192,320},{... | collective-permute-start | bytes 319496 | tf_op jit(solution)/shard_map/ppermute | solution.py:33
  74.5 12.3 %collective-permute-start.5 = (bf16[208,256]{1,0:T(8,128)(2,1)S(1)}, bf16[208,256]{1,0:T(8,128)(2,1)S(1)}, u32[]{:S(2)}, u32[]{:S(2)}) collective-permute-start(bf16[208,256]{1,0:T(8,128)(2,1)S(1)} %get-tuple-element.52), channel_id=1, source_target_pairs={{0,384},{32,416},{64,448},{96,480},{128,0},{160,32},{192,64},{224,... | collective-permute-start | bytes 319496 | tf_op jit(solution)/shard_map/ppermute | solution.py:34
  162.5 21.8 %all-to-all-start = ((bf16[32,2,4096]{2,1,0:T(2,128)(2,1)}), bf16[32,2,4096]{2,1,0:T(2,128)(2,1)S(1)}, u32[]{:S(2)}, u32[]{:S(2)}) async-start(bf16[32,2,4096]{2,1,0:T(2,128)(2,1)} %reshape.764), calls=%async_computation | async-start | bytes 1048576 | tf_op jit(solution)/shard_map/all_to_all | solution.py:48
  200.7 14.5 %all-to-all-start.1 = ((f32[32,1,768]{2,1,0:T(1,128)}), f32[32,1,768]{2,1,0:T(1,128)S(1)}, u32[]{:S(2)}, u32[]{:S(2)}) async-start(f32[32,1,768]{2,1,0:T(1,128)} %reshape.766), calls=%async_computation.1 | async-start | bytes 196608 | tf_op jit(solution)/shard_map/all_to_all | solution.py:243
  217.7 26.4 %all-to-all-start.2 = ((f32[16,1,768]{2,1,0:T(1,128)}), f32[16,1,768]{2,1,0:T(1,128)S(1)}, u32[]{:S(2)}, u32[]{:S(2)}) async-start(f32[16,1,768]{2,1,0:T(1,128)} %reshape.768), calls=%async_computation.2 | async-start | bytes 98304 | tf_op jit(solution)/shard_map/all_to_all | solution.py:48
Sparse Core Ops, SparseCore 0:
  87.9 67.7 all-gather.1

commit v11 on v10

--- a/solution.py
+++ b/solution.py
@@ -95,7 +95,7 @@
         onehot = (ids == classes).astype(jnp.float32)
         onehot_ref[...] = jnp.transpose(onehot).astype(jnp.bfloat16)
 
-    picked = jnp.dot(out, onehot_ref[...], preferred_element_type=jnp.float32)
+    out_t = jnp.transpose(out.astype(jnp.float32)).astype(jnp.bfloat16)
     col_ok = col_ok_ref[...] != 0
     old_max = cmax_ref[...]
     local = jnp.max(jnp.where(col_ok, scores, LOWEST), axis=0, keepdims=True)
@@ -103,7 +103,13 @@
     keep = jnp.exp(old_max - new_max)
     expo = jnp.where(col_ok, jnp.exp(scores - new_max), 0.0)
     ctot_ref[...] = ctot_ref[...] * keep + jnp.sum(expo, axis=0, keepdims=True)
-    cnum_ref[...] = cnum_ref[...] * keep + jnp.sum(expo * picked, axis=0, keepdims=True)
+    high = expo.astype(jnp.bfloat16)
+    low = (expo - high.astype(jnp.float32)).astype(jnp.bfloat16)
+    by_class = jnp.dot(out_t, high, preferred_element_type=jnp.float32) + jnp.dot(
+        out_t, low, preferred_element_type=jnp.float32
+    )
+    num = jnp.sum(by_class * onehot_ref[...].astype(jnp.float32), axis=0, keepdims=True)
+    cnum_ref[...] = cnum_ref[...] * keep + num
     cmax_ref[...] = new_max
 
 

time: 253 us -> 255 us (level)
  no operation moved by 1% of the time
where the time goes in v11:
time: 255 us
  waiting for transfers between devices  120 us (47%)
  starting transfers between devices  58.6 us (23%)
  Pallas kernels  31.1 us (12%)
  local copies, waits for them, and re-layouts  23 us (9%)
  between operations  14.5 us (6%)
  other arithmetic  7.79 us (3%)
    all_gather x1, waiting for transfers between devices, body(): gathered = lax.all_gather(packed, 'space', axis=2, tiled=True)  64.4 us
    pallas_call x3, Pallas kernels, step_pass(): pl.pallas_call(kernel, grid=(blocks,), in_specs=in_specs, out_specs=out_s...  31.1 us
    ppermute x1, waiting for transfers between devices, broadcast_tm(): got_b = lax.ppermute(value, axis, behind)  20.6 us
    all_to_all x2, starting transfers between devices, gather_all(): return lax.all_to_all(spread, axis, 0, 0, tiled=True)  18.1 us
    all_to_all x2, waiting for transfers between devices, gather_all(): return lax.all_to_all(spread, axis, 0, 0, tiled=True)  13.7 us
    ppermute x1, starting transfers between devices, broadcast_tm(): got_a = lax.ppermute(value, axis, ahead)  9.36 us
    ppermute x2, starting transfers between devices, broadcast_tm(): got = lax.ppermute(value, axis, pairs)  8.93 us
    all_to_all x1, starting transfers between devices, body(): spread = lax.all_to_all(local, 'space', 0, 0, tiled=True)  7.37 us
  transfers between devices with their start and end apart: 10, of which 9 were waited for; matrix products, arithmetic and copies ran while one was open for 5% of the time, Pallas kernels for 5%

profile of v11, /device:TPU:1, one launch (start us, length us, event | category | flops | bytes accessed | tf_op | source)
XLA Modules:
  0.0 254.6 jit_solution(4375945525682165424)
XLA Ops:
  9.2 1.5 gather_fusion.2
  10.9 1.5 gather_fusion.1
  13.2 4.0 %collective-permute-start = (bf16[416,256]{1,0:T(8,128)(2,1)S(1)}, bf16[416,256]{1,0:T(8,128)(2,1)S(1)}, u32[]{:S(2)}, u32[]{:S(2)}) collective-permute-start(bf16[416,256]{1,0:T(8,128)(2,1)S(1)} %pad_maximum_fusion), channel_id=1, source_target_pairs={{0,32},{32,0},{64,96},{96,64},{128,160},{160,128},{192,224},{224,1... | collective-permute-start | bytes 638984 | tf_op jit(solution)/shard_map/ppermute | solution.py:23
  22.1 4.9 %collective-permute-start.1 = (bf16[416,256]{1,0:T(8,128)(2,1)S(1)}, bf16[416,256]{1,0:T(8,128)(2,1)S(1)}, u32[]{:S(2)}, u32[]{:S(2)}) collective-permute-start(bf16[416,256]{1,0:T(8,128)(2,1)S(1)} %broadcast_select_fusion), channel_id=1, source_target_pairs={{0,64},{32,96},{64,0},{96,32},{128,192},{160,224},{192,128},{224,1... | collective-permute-start | bytes 638984 | tf_op jit(solution)/shard_map/ppermute | solution.py:23
  27.0 3.2 %collective-permute-done.1 = bf16[416,256]{1,0:T(8,128)(2,1)S(1)} collective-permute-done((bf16[416,256]{1,0:T(8,128)(2,1)S(1)}, bf16[416,256]{1,0:T(8,128)(2,1)S(1)}, u32[]{:S(2)}, u32[]{:S(2)}) %collective-permute-start.1) | collective-permute-done | bytes 213024 | tf_op jit(solution)/shard_map/ppermute | solution.py:23
  30.4 9.4 %collective-permute-start.3 = (bf16[416,256]{1,0:T(8,128)(2,1)S(1)}, bf16[416,256]{1,0:T(8,128)(2,1)S(1)}, u32[]{:S(2)}, u32[]{:S(2)}) collective-permute-start(bf16[416,256]{1,0:T(8,128)(2,1)S(1)} %broadcast_select_fusion.1), channel_id=1, source_target_pairs={{0,128},{32,160},{64,192},{96,224},{128,256},{160,288},{192,320},{... | collective-permute-start | bytes 638984 | tf_op jit(solution)/shard_map/ppermute | solution.py:38
  39.7 5.6 %collective-permute-start.2 = (bf16[416,256]{1,0:T(8,128)(2,1)S(1)}, bf16[416,256]{1,0:T(8,128)(2,1)S(1)}, u32[]{:S(2)}, u32[]{:S(2)}) collective-permute-start(bf16[416,256]{1,0:T(8,128)(2,1)S(1)} %broadcast_select_fusion.1), channel_id=1, source_target_pairs={{0,384},{32,416},{64,448},{96,480},{128,0},{160,32},{192,64},{224,... | collective-permute-start | bytes 638984 | tf_op jit(solution)/shard_map/ppermute | solution.py:39
  45.3 1.6 collective-permute-done.3
  46.9 20.6 %collective-permute-done.2 = bf16[416,256]{1,0:T(8,128)(2,1)S(1)} collective-permute-done((bf16[416,256]{1,0:T(8,128)(2,1)S(1)}, bf16[416,256]{1,0:T(8,128)(2,1)S(1)}, u32[]{:S(2)}, u32[]{:S(2)}) %collective-permute-start.2) | collective-permute-done | bytes 213024 | tf_op jit(solution)/shard_map/ppermute | solution.py:39
  67.7 6.7 %collective-permute-start.4 = (bf16[208,256]{1,0:T(8,128)(2,1)S(1)}, bf16[208,256]{1,0:T(8,128)(2,1)S(1)}, u32[]{:S(2)}, u32[]{:S(2)}) collective-permute-start(bf16[208,256]{1,0:T(8,128)(2,1)S(1)} %get-tuple-element.51), channel_id=1, source_target_pairs={{0,128},{32,160},{64,192},{96,224},{128,256},{160,288},{192,320},{... | collective-permute-start | bytes 319496 | tf_op jit(solution)/shard_map/ppermute | solution.py:33
  74.5 2.5 collective-permute-start.5
  76.9 4.8 %collective-permute-done.4 = bf16[208,256]{1,0:T(8,128)(2,1)S(1)} collective-permute-done((bf16[208,256]{1,0:T(8,128)(2,1)S(1)}, bf16[208,256]{1,0:T(8,128)(2,1)S(1)}, u32[]{:S(2)}, u32[]{:S(2)}) %collective-permute-start.4) | collective-permute-done | bytes 106528 | tf_op jit(solution)/shard_map/ppermute | solution.py:33
  81.8 4.9 %collective-permute-done.5 = bf16[208,256]{1,0:T(8,128)(2,1)S(1)} collective-permute-done((bf16[208,256]{1,0:T(8,128)(2,1)S(1)}, bf16[208,256]{1,0:T(8,128)(2,1)S(1)}, u32[]{:S(2)}, u32[]{:S(2)}) %collective-permute-start.5) | collective-permute-done | bytes 106528 | tf_op jit(solution)/shard_map/ppermute | solution.py:34
  91.3 64.4 %all-gather.2.cloned.1.call-done = bf16[3,2,2048,256]{3,2,1,0:T(8,128)(2,1)} async-done(((bf16[3,2,64,256]{3,2,1,0:T(8,128)(2,1)}), bf16[3,2,2048,256]{3,2,1,0:T(8,128)(2,1)}) %all-gather.2.cloned.1.call-update) | async-done | bytes 6291472 | tf_op jit(solution)/shard_map/all_gather | solution.py:207
  155.7 4.2 %shard_map.77 = bf16[128,64]{1,0:T(8,128)(2,1)} custom-call(bf16[128,256]{1,0:T(8,128)(2,1)} %slice.122.q_ref, s32[128,1]{1,0:T(8,128)} %reshape.763.row_ok_ref.col_ok_ref, s32[128,1]{1,0:T(8,128)} %reshape.763.row_ok_ref.col_ok_ref, bf16[3,4096,256]{2,1,0:T(8,128)(2,1)} %bitcast.100, s32[1,4096]{1,0:T(1,128)} %bitcast.114, bf16[3,4096,256]{2,1,0:T(8,128)(2,1)} %bitcast.101), custom_call_target="tpu_custom_call" | custom-call | tf_op jit(solution)/shard_map/pallas_call | solution.py:144
  161.0 1.6 reshape.764
  162.5 5.4 %all-to-all-start = ((bf16[32,2,4096]{2,1,0:T(2,128)(2,1)}), bf16[32,2,4096]{2,1,0:T(2,128)(2,1)S(1)}, u32[]{:S(2)}, u32[]{:S(2)}) async-start(bf16[32,2,4096]{2,1,0:T(2,128)(2,1)} %reshape.764), calls=%async_computation | async-start | bytes 1048576 | tf_op jit(solution)/shard_map/all_to_all | solution.py:48
  169.7 13.3 %shard_map.79 = (bf16[512,64]{1,0:T(8,128)(2,1)}, f32[1,4096]{1,0:T(1,128)}, f32[1,4096]{1,0:T(1,128)}, f32[1,4096]{1,0:T(1,128)}) custom-call(bf16[512,256]{1,0:T(8,128)(2,1)} %bitcast.109, s32[512,1]{1,0:T(8,128)} %reshape.762.row_ok_ref.col_ok_ref, s32[512,1]{1,0:T(8,128)} %reshape.762.row_ok_ref.col_ok_ref, bf16[3,4096,256]{2,1,0:T(8,128)(2,1)} %bitcast.102, ...), custom_call_target="tpu_custom_call" | custom-call | tf_op jit(solution)/shard_map/pallas_call | solution.py:144
  186.1 13.6 %shard_map.78 = (bf16[512,64]{1,0:T(8,128)(2,1)}, f32[1,4096]{1,0:T(1,128)}, f32[1,4096]{1,0:T(1,128)}, f32[1,4096]{1,0:T(1,128)}) custom-call(bf16[512,256]{1,0:T(8,128)(2,1)} %bitcast.110, s32[512,1]{1,0:T(8,128)} %reshape.762.row_ok_ref.col_ok_ref, s32[512,1]{1,0:T(8,128)} %reshape.762.row_ok_ref.col_ok_ref, bf16[3,4096,256]{2,1,0:T(8,128)(2,1)} %bitcast.104, ...), custom_call_target="tpu_custom_call" | custom-call | tf_op jit(solution)/shard_map/pallas_call | solution.py:144
  201.7 7.4 %all-to-all-start.1 = ((f32[32,1,768]{2,1,0:T(1,128)}), f32[32,1,768]{2,1,0:T(1,128)S(1)}, u32[]{:S(2)}, u32[]{:S(2)}) async-start(f32[32,1,768]{2,1,0:T(1,128)} %reshape.766), calls=%async_computation.1 | async-start | bytes 196608 | tf_op jit(solution)/shard_map/all_to_all | solution.py:249
  209.1 1.7 slice.129
  210.9 6.3 %all-to-all-done.1 = f32[32,1,768]{2,1,0:T(1,128)S(1)} async-done(((f32[32,1,768]{2,1,0:T(1,128)}), f32[32,1,768]{2,1,0:T(1,128)S(1)}, u32[]{:S(2)}, u32[]{:S(2)}) %all-to-all-start.1) | async-done | bytes 98336 | tf_op jit(solution)/shard_map/all_to_all | solution.py:249
  219.6 12.7 %all-to-all-start.2 = ((f32[16,1,768]{2,1,0:T(1,128)}), f32[16,1,768]{2,1,0:T(1,128)S(1)}, u32[]{:S(2)}, u32[]{:S(2)}) async-start(f32[16,1,768]{2,1,0:T(1,128)} %reshape.768), calls=%async_computation.2 | async-start | bytes 98304 | tf_op jit(solution)/shard_map/all_to_all | solution.py:48
  232.7 13.3 %all-to-all-done.2 = f32[16,1,768]{2,1,0:T(1,128)S(1)} async-done(((f32[16,1,768]{2,1,0:T(1,128)}), f32[16,1,768]{2,1,0:T(1,128)S(1)}, u32[]{:S(2)}, u32[]{:S(2)}) %all-to-all-start.2) | async-done | bytes 49184 | tf_op jit(solution)/shard_map/all_to_all | solution.py:48
  (110 shorter events, 25.0 us)
Async XLA Ops:
  7.2 5.3 %copy-start = (bf16[8,64,256]{2,1,0:T(8,128)(2,1)S(1)}, bf16[8,64,256]{2,1,0:T(8,128)(2,1)}, u32[]{:S(2)}) copy-start(bf16[8,64,256]{2,1,0:T(8,128)(2,1)} %param.11) | copy-start | bytes 786436
  7.2 148.5 %all-gather.2.cloned.1.call-start = ((), (), s32[]{:S(2)}) async-start(), calls=%async_computation.3 | async-start | bytes 6488064 | tf_op jit(solution)/shard_map/all_gather | solution.py:207
  13.2 8.8 %collective-permute-start = (bf16[416,256]{1,0:T(8,128)(2,1)S(1)}, bf16[416,256]{1,0:T(8,128)(2,1)S(1)}, u32[]{:S(2)}, u32[]{:S(2)}) collective-permute-start(bf16[416,256]{1,0:T(8,128)(2,1)S(1)} %pad_maximum_fusion), channel_id=1, source_target_pairs={{0,32},{32,0},{64,96},{96,64},{128,160},{160,128},{192,224},{224,1... | collective-permute-start | bytes 638984 | tf_op jit(solution)/shard_map/ppermute | solution.py:23
  22.1 65.7 %copy-start.2 = (s32[2,2]{1,0:T(2,128)S(1)}, s32[2,2]{1,0:T(2,128)}, u32[]{:S(2)}) copy-start(s32[2,2]{1,0:T(2,128)} %param.15) | copy-start | bytes 52
  22.1 65.8 %copy-start.1 = (s32[128]{0:T(128)S(1)}, s32[128]{0:T(128)}, u32[]{:S(2)}) copy-start(s32[128]{0:T(128)} %param.14) | copy-start | bytes 1540
  22.1 8.1 %collective-permute-start.1 = (bf16[416,256]{1,0:T(8,128)(2,1)S(1)}, bf16[416,256]{1,0:T(8,128)(2,1)S(1)}, u32[]{:S(2)}, u32[]{:S(2)}) collective-permute-start(bf16[416,256]{1,0:T(8,128)(2,1)S(1)} %broadcast_select_fusion), channel_id=1, source_target_pairs={{0,64},{32,96},{64,0},{96,32},{128,192},{160,224},{192,128},{224,1... | collective-permute-start | bytes 638984 | tf_op jit(solution)/shard_map/ppermute | solution.py:23
  30.4 16.5 %collective-permute-start.3 = (bf16[416,256]{1,0:T(8,128)(2,1)S(1)}, bf16[416,256]{1,0:T(8,128)(2,1)S(1)}, u32[]{:S(2)}, u32[]{:S(2)}) collective-permute-start(bf16[416,256]{1,0:T(8,128)(2,1)S(1)} %broadcast_select_fusion.1), channel_id=1, source_target_pairs={{0,128},{32,160},{64,192},{96,224},{128,256},{160,288},{192,320},{... | collective-permute-start | bytes 638984 | tf_op jit(solution)/shard_map/ppermute | solution.py:38
  39.7 27.8 %collective-permute-start.2 = (bf16[416,256]{1,0:T(8,128)(2,1)S(1)}, bf16[416,256]{1,0:T(8,128)(2,1)S(1)}, u32[]{:S(2)}, u32[]{:S(2)}) collective-permute-start(bf16[416,256]{1,0:T(8,128)(2,1)S(1)} %broadcast_select_fusion.1), channel_id=1, source_target_pairs={{0,384},{32,416},{64,448},{96,480},{128,0},{160,32},{192,64},{224,... | collective-permute-start | bytes 638984 | tf_op jit(solution)/shard_map/ppermute | solution.py:39
  67.7 14.1 %collective-permute-start.4 = (bf16[208,256]{1,0:T(8,128)(2,1)S(1)}, bf16[208,256]{1,0:T(8,128)(2,1)S(1)}, u32[]{:S(2)}, u32[]{:S(2)}) collective-permute-start(bf16[208,256]{1,0:T(8,128)(2,1)S(1)} %get-tuple-element.51), channel_id=1, source_target_pairs={{0,128},{32,160},{64,192},{96,224},{128,256},{160,288},{192,320},{... | collective-permute-start | bytes 319496 | tf_op jit(solution)/shard_map/ppermute | solution.py:33
  74.5 12.3 %collective-permute-start.5 = (bf16[208,256]{1,0:T(8,128)(2,1)S(1)}, bf16[208,256]{1,0:T(8,128)(2,1)S(1)}, u32[]{:S(2)}, u32[]{:S(2)}) collective-permute-start(bf16[208,256]{1,0:T(8,128)(2,1)S(1)} %get-tuple-element.52), channel_id=1, source_target_pairs={{0,384},{32,416},{64,448},{96,480},{128,0},{160,32},{192,64},{224,... | collective-permute-start | bytes 319496 | tf_op jit(solution)/shard_map/ppermute | solution.py:34
  162.5 21.8 %all-to-all-start = ((bf16[32,2,4096]{2,1,0:T(2,128)(2,1)}), bf16[32,2,4096]{2,1,0:T(2,128)(2,1)S(1)}, u32[]{:S(2)}, u32[]{:S(2)}) async-start(bf16[32,2,4096]{2,1,0:T(2,128)(2,1)} %reshape.764), calls=%async_computation | async-start | bytes 1048576 | tf_op jit(solution)/shard_map/all_to_all | solution.py:48
  201.7 15.5 %all-to-all-start.1 = ((f32[32,1,768]{2,1,0:T(1,128)}), f32[32,1,768]{2,1,0:T(1,128)S(1)}, u32[]{:S(2)}, u32[]{:S(2)}) async-start(f32[32,1,768]{2,1,0:T(1,128)} %reshape.766), calls=%async_computation.1 | async-start | bytes 196608 | tf_op jit(solution)/shard_map/all_to_all | solution.py:249
  219.6 26.4 %all-to-all-start.2 = ((f32[16,1,768]{2,1,0:T(1,128)}), f32[16,1,768]{2,1,0:T(1,128)S(1)}, u32[]{:S(2)}, u32[]{:S(2)}) async-start(f32[16,1,768]{2,1,0:T(1,128)} %reshape.768), calls=%async_computation.2 | async-start | bytes 98304 | tf_op jit(solution)/shard_map/all_to_all | solution.py:48
Sparse Core Ops, SparseCore 0:
  87.9 67.7 all-gather.1

commit v12 on v10

--- a/solution.py
+++ b/solution.py
@@ -74,7 +74,7 @@
     row_ok = row_ok_ref[...] != 0
     masked = jnp.where(key_ok, scores, LOWEST)
     row_max = jnp.max(masked, axis=1, keepdims=True)
-    weights = jnp.where(key_ok, jnp.exp(scores - row_max), 0.0)
+    weights = jnp.exp(masked - row_max)
     total = jnp.sum(weights, axis=1, keepdims=True)
     mixed = jnp.dot(
         weights.astype(jnp.bfloat16), values, preferred_element_type=jnp.float32
@@ -98,10 +98,11 @@
     picked = jnp.dot(out, onehot_ref[...], preferred_element_type=jnp.float32)
     col_ok = col_ok_ref[...] != 0
     old_max = cmax_ref[...]
-    local = jnp.max(jnp.where(col_ok, scores, LOWEST), axis=0, keepdims=True)
+    col_scores = jnp.where(col_ok, scores, LOWEST)
+    local = jnp.max(col_scores, axis=0, keepdims=True)
     new_max = jnp.maximum(old_max, local)
     keep = jnp.exp(old_max - new_max)
-    expo = jnp.where(col_ok, jnp.exp(scores - new_max), 0.0)
+    expo = jnp.exp(col_scores - new_max)
     ctot_ref[...] = ctot_ref[...] * keep + jnp.sum(expo, axis=0, keepdims=True)
     cnum_ref[...] = cnum_ref[...] * keep + jnp.sum(expo * picked, axis=0, keepdims=True)
     cmax_ref[...] = new_max

time: 253 us -> 251 us (level)
  no operation moved by 1% of the time
where the time goes in v12:
time: 251 us; the launch traced here: 250 us
  waiting for transfers between devices  122 us (49%)
  starting transfers between devices  56.6 us (23%)
  Pallas kernels  27 us (11%)
  local copies, waits for them, and re-layouts  23 us (9%)
  between operations  14.5 us (6%)
  other arithmetic  7.79 us (3%)
    all_gather x1, waiting for transfers between devices, body(): gathered = lax.all_gather(packed, 'space', axis=2, tiled=True)  64.4 us
    pallas_call x3, Pallas kernels, step_pass(): pl.pallas_call(kernel, grid=(blocks,), in_specs=in_specs, out_specs=out_s...  27 us
    ppermute x1, waiting for transfers between devices, broadcast_tm(): got_b = lax.ppermute(value, axis, behind)  20.6 us
    all_to_all x2, starting transfers between devices, gather_all(): return lax.all_to_all(spread, axis, 0, 0, tiled=True)  18.1 us
    all_to_all x2, waiting for transfers between devices, gather_all(): return lax.all_to_all(spread, axis, 0, 0, tiled=True)  15.7 us
    ppermute x1, starting transfers between devices, broadcast_tm(): got_a = lax.ppermute(value, axis, ahead)  9.36 us
    ppermute x2, starting transfers between devices, broadcast_tm(): got = lax.ppermute(value, axis, pairs)  8.93 us
    ppermute x1, starting transfers between devices, broadcast_tm(): got_a = lax.ppermute(value[:half], axis, ahead)  6.73 us
  transfers between devices with their start and end apart: 10, of which 9 were waited for; matrix products, arithmetic and copies ran while one was open for 5% of the time, Pallas kernels for 5%

profile of v12, /device:TPU:1, one launch (start us, length us, event | category | flops | bytes accessed | tf_op | source)
XLA Modules:
  0.0 250.5 jit_solution(7375566482293162701)
XLA Ops:
  10.9 1.5 gather_fusion.1
  13.2 4.0 %collective-permute-start = (bf16[416,256]{1,0:T(8,128)(2,1)S(1)}, bf16[416,256]{1,0:T(8,128)(2,1)S(1)}, u32[]{:S(2)}, u32[]{:S(2)}) collective-permute-start(bf16[416,256]{1,0:T(8,128)(2,1)S(1)} %pad_maximum_fusion), channel_id=1, source_target_pairs={{0,32},{32,0},{64,96},{96,64},{128,160},{160,128},{192,224},{224,1... | collective-permute-start | bytes 638984 | tf_op jit(solution)/shard_map/ppermute | solution.py:23
  22.1 4.9 %collective-permute-start.1 = (bf16[416,256]{1,0:T(8,128)(2,1)S(1)}, bf16[416,256]{1,0:T(8,128)(2,1)S(1)}, u32[]{:S(2)}, u32[]{:S(2)}) collective-permute-start(bf16[416,256]{1,0:T(8,128)(2,1)S(1)} %broadcast_select_fusion), channel_id=1, source_target_pairs={{0,64},{32,96},{64,0},{96,32},{128,192},{160,224},{192,128},{224,1... | collective-permute-start | bytes 638984 | tf_op jit(solution)/shard_map/ppermute | solution.py:23
  27.0 3.2 %collective-permute-done.1 = bf16[416,256]{1,0:T(8,128)(2,1)S(1)} collective-permute-done((bf16[416,256]{1,0:T(8,128)(2,1)S(1)}, bf16[416,256]{1,0:T(8,128)(2,1)S(1)}, u32[]{:S(2)}, u32[]{:S(2)}) %collective-permute-start.1) | collective-permute-done | bytes 213024 | tf_op jit(solution)/shard_map/ppermute | solution.py:23
  30.4 9.4 %collective-permute-start.3 = (bf16[416,256]{1,0:T(8,128)(2,1)S(1)}, bf16[416,256]{1,0:T(8,128)(2,1)S(1)}, u32[]{:S(2)}, u32[]{:S(2)}) collective-permute-start(bf16[416,256]{1,0:T(8,128)(2,1)S(1)} %broadcast_select_fusion.1), channel_id=1, source_target_pairs={{0,128},{32,160},{64,192},{96,224},{128,256},{160,288},{192,320},{... | collective-permute-start | bytes 638984 | tf_op jit(solution)/shard_map/ppermute | solution.py:38
  39.7 5.6 %collective-permute-start.2 = (bf16[416,256]{1,0:T(8,128)(2,1)S(1)}, bf16[416,256]{1,0:T(8,128)(2,1)S(1)}, u32[]{:S(2)}, u32[]{:S(2)}) collective-permute-start(bf16[416,256]{1,0:T(8,128)(2,1)S(1)} %broadcast_select_fusion.1), channel_id=1, source_target_pairs={{0,384},{32,416},{64,448},{96,480},{128,0},{160,32},{192,64},{224,... | collective-permute-start | bytes 638984 | tf_op jit(solution)/shard_map/ppermute | solution.py:39
  45.3 1.6 collective-permute-done.3
  46.9 20.6 %collective-permute-done.2 = bf16[416,256]{1,0:T(8,128)(2,1)S(1)} collective-permute-done((bf16[416,256]{1,0:T(8,128)(2,1)S(1)}, bf16[416,256]{1,0:T(8,128)(2,1)S(1)}, u32[]{:S(2)}, u32[]{:S(2)}) %collective-permute-start.2) | collective-permute-done | bytes 213024 | tf_op jit(solution)/shard_map/ppermute | solution.py:39
  67.7 6.7 %collective-permute-start.4 = (bf16[208,256]{1,0:T(8,128)(2,1)S(1)}, bf16[208,256]{1,0:T(8,128)(2,1)S(1)}, u32[]{:S(2)}, u32[]{:S(2)}) collective-permute-start(bf16[208,256]{1,0:T(8,128)(2,1)S(1)} %get-tuple-element.51), channel_id=1, source_target_pairs={{0,128},{32,160},{64,192},{96,224},{128,256},{160,288},{192,320},{... | collective-permute-start | bytes 319496 | tf_op jit(solution)/shard_map/ppermute | solution.py:33
  74.5 2.5 collective-permute-start.5
  76.9 4.8 %collective-permute-done.4 = bf16[208,256]{1,0:T(8,128)(2,1)S(1)} collective-permute-done((bf16[208,256]{1,0:T(8,128)(2,1)S(1)}, bf16[208,256]{1,0:T(8,128)(2,1)S(1)}, u32[]{:S(2)}, u32[]{:S(2)}) %collective-permute-start.4) | collective-permute-done | bytes 106528 | tf_op jit(solution)/shard_map/ppermute | solution.py:33
  81.8 4.9 %collective-permute-done.5 = bf16[208,256]{1,0:T(8,128)(2,1)S(1)} collective-permute-done((bf16[208,256]{1,0:T(8,128)(2,1)S(1)}, bf16[208,256]{1,0:T(8,128)(2,1)S(1)}, u32[]{:S(2)}, u32[]{:S(2)}) %collective-permute-start.5) | collective-permute-done | bytes 106528 | tf_op jit(solution)/shard_map/ppermute | solution.py:34
  91.3 64.4 %all-gather.2.cloned.1.call-done = bf16[3,2,2048,256]{3,2,1,0:T(8,128)(2,1)} async-done(((bf16[3,2,64,256]{3,2,1,0:T(8,128)(2,1)}), bf16[3,2,2048,256]{3,2,1,0:T(8,128)(2,1)}) %all-gather.2.cloned.1.call-update) | async-done | bytes 6291472 | tf_op jit(solution)/shard_map/all_gather | solution.py:202
  155.7 4.1 %shard_map.77 = bf16[128,64]{1,0:T(8,128)(2,1)} custom-call(bf16[128,256]{1,0:T(8,128)(2,1)} %slice.122.q_ref, s32[128,1]{1,0:T(8,128)} %reshape.763.row_ok_ref.col_ok_ref, s32[128,1]{1,0:T(8,128)} %reshape.763.row_ok_ref.col_ok_ref, bf16[3,4096,256]{2,1,0:T(8,128)(2,1)} %bitcast.100, s32[1,4096]{1,0:T(1,128)} %bitcast.114, bf16[3,4096,256]{2,1,0:T(8,128)(2,1)} %bitcast.101), custom_call_target="tpu_custom_call" | custom-call | tf_op jit(solution)/shard_map/pallas_call | solution.py:139
  160.8 1.6 reshape.764
  162.4 5.4 %all-to-all-start = ((bf16[32,2,4096]{2,1,0:T(2,128)(2,1)}), bf16[32,2,4096]{2,1,0:T(2,128)(2,1)S(1)}, u32[]{:S(2)}, u32[]{:S(2)}) async-start(bf16[32,2,4096]{2,1,0:T(2,128)(2,1)} %reshape.764), calls=%async_computation | async-start | bytes 1048576 | tf_op jit(solution)/shard_map/all_to_all | solution.py:48
  169.6 11.3 %shard_map.79 = (bf16[512,64]{1,0:T(8,128)(2,1)}, f32[1,4096]{1,0:T(1,128)}, f32[1,4096]{1,0:T(1,128)}, f32[1,4096]{1,0:T(1,128)}) custom-call(bf16[512,256]{1,0:T(8,128)(2,1)} %bitcast.109, s32[512,1]{1,0:T(8,128)} %reshape.762.row_ok_ref.col_ok_ref, s32[512,1]{1,0:T(8,128)} %reshape.762.row_ok_ref.col_ok_ref, bf16[3,4096,256]{2,1,0:T(8,128)(2,1)} %bitcast.102, ...), custom_call_target="tpu_custom_call" | custom-call | tf_op jit(solution)/shard_map/pallas_call | solution.py:139
  181.9 2.3 all-to-all-done
  186.0 11.6 %shard_map.78 = (bf16[512,64]{1,0:T(8,128)(2,1)}, f32[1,4096]{1,0:T(1,128)}, f32[1,4096]{1,0:T(1,128)}, f32[1,4096]{1,0:T(1,128)}) custom-call(bf16[512,256]{1,0:T(8,128)(2,1)} %bitcast.110, s32[512,1]{1,0:T(8,128)} %reshape.762.row_ok_ref.col_ok_ref, s32[512,1]{1,0:T(8,128)} %reshape.762.row_ok_ref.col_ok_ref, bf16[3,4096,256]{2,1,0:T(8,128)(2,1)} %bitcast.104, ...), custom_call_target="tpu_custom_call" | custom-call | tf_op jit(solution)/shard_map/pallas_call | solution.py:139
  199.5 5.4 %all-to-all-start.1 = ((f32[32,1,768]{2,1,0:T(1,128)}), f32[32,1,768]{2,1,0:T(1,128)S(1)}, u32[]{:S(2)}, u32[]{:S(2)}) async-start(f32[32,1,768]{2,1,0:T(1,128)} %reshape.766), calls=%async_computation.1 | async-start | bytes 196608 | tf_op jit(solution)/shard_map/all_to_all | solution.py:244
  205.0 1.7 slice.129
  206.8 6.3 %all-to-all-done.1 = f32[32,1,768]{2,1,0:T(1,128)S(1)} async-done(((f32[32,1,768]{2,1,0:T(1,128)}), f32[32,1,768]{2,1,0:T(1,128)S(1)}, u32[]{:S(2)}, u32[]{:S(2)}) %all-to-all-start.1) | async-done | bytes 98336 | tf_op jit(solution)/shard_map/all_to_all | solution.py:244
  215.5 12.7 %all-to-all-start.2 = ((f32[16,1,768]{2,1,0:T(1,128)}), f32[16,1,768]{2,1,0:T(1,128)S(1)}, u32[]{:S(2)}, u32[]{:S(2)}) async-start(f32[16,1,768]{2,1,0:T(1,128)} %reshape.768), calls=%async_computation.2 | async-start | bytes 98304 | tf_op jit(solution)/shard_map/all_to_all | solution.py:48
  228.6 13.3 %all-to-all-done.2 = f32[16,1,768]{2,1,0:T(1,128)S(1)} async-done(((f32[16,1,768]{2,1,0:T(1,128)}), f32[16,1,768]{2,1,0:T(1,128)S(1)}, u32[]{:S(2)}, u32[]{:S(2)}) %all-to-all-start.2) | async-done | bytes 49184 | tf_op jit(solution)/shard_map/all_to_all | solution.py:48
  (110 shorter events, 26.1 us)
Async XLA Ops:
  7.2 5.3 %copy-start = (bf16[8,64,256]{2,1,0:T(8,128)(2,1)S(1)}, bf16[8,64,256]{2,1,0:T(8,128)(2,1)}, u32[]{:S(2)}) copy-start(bf16[8,64,256]{2,1,0:T(8,128)(2,1)} %param.11) | copy-start | bytes 786436
  7.2 148.5 %all-gather.2.cloned.1.call-start = ((), (), s32[]{:S(2)}) async-start(), calls=%async_computation.3 | async-start | bytes 6488064 | tf_op jit(solution)/shard_map/all_gather | solution.py:202
  13.2 8.8 %collective-permute-start = (bf16[416,256]{1,0:T(8,128)(2,1)S(1)}, bf16[416,256]{1,0:T(8,128)(2,1)S(1)}, u32[]{:S(2)}, u32[]{:S(2)}) collective-permute-start(bf16[416,256]{1,0:T(8,128)(2,1)S(1)} %pad_maximum_fusion), channel_id=1, source_target_pairs={{0,32},{32,0},{64,96},{96,64},{128,160},{160,128},{192,224},{224,1... | collective-permute-start | bytes 638984 | tf_op jit(solution)/shard_map/ppermute | solution.py:23
  22.1 65.7 %copy-start.2 = (s32[2,2]{1,0:T(2,128)S(1)}, s32[2,2]{1,0:T(2,128)}, u32[]{:S(2)}) copy-start(s32[2,2]{1,0:T(2,128)} %param.15) | copy-start | bytes 52
  22.1 65.8 %copy-start.1 = (s32[128]{0:T(128)S(1)}, s32[128]{0:T(128)}, u32[]{:S(2)}) copy-start(s32[128]{0:T(128)} %param.14) | copy-start | bytes 1540
  22.1 8.1 %collective-permute-start.1 = (bf16[416,256]{1,0:T(8,128)(2,1)S(1)}, bf16[416,256]{1,0:T(8,128)(2,1)S(1)}, u32[]{:S(2)}, u32[]{:S(2)}) collective-permute-start(bf16[416,256]{1,0:T(8,128)(2,1)S(1)} %broadcast_select_fusion), channel_id=1, source_target_pairs={{0,64},{32,96},{64,0},{96,32},{128,192},{160,224},{192,128},{224,1... | collective-permute-start | bytes 638984 | tf_op jit(solution)/shard_map/ppermute | solution.py:23
  30.4 16.5 %collective-permute-start.3 = (bf16[416,256]{1,0:T(8,128)(2,1)S(1)}, bf16[416,256]{1,0:T(8,128)(2,1)S(1)}, u32[]{:S(2)}, u32[]{:S(2)}) collective-permute-start(bf16[416,256]{1,0:T(8,128)(2,1)S(1)} %broadcast_select_fusion.1), channel_id=1, source_target_pairs={{0,128},{32,160},{64,192},{96,224},{128,256},{160,288},{192,320},{... | collective-permute-start | bytes 638984 | tf_op jit(solution)/shard_map/ppermute | solution.py:38
  39.7 27.8 %collective-permute-start.2 = (bf16[416,256]{1,0:T(8,128)(2,1)S(1)}, bf16[416,256]{1,0:T(8,128)(2,1)S(1)}, u32[]{:S(2)}, u32[]{:S(2)}) collective-permute-start(bf16[416,256]{1,0:T(8,128)(2,1)S(1)} %broadcast_select_fusion.1), channel_id=1, source_target_pairs={{0,384},{32,416},{64,448},{96,480},{128,0},{160,32},{192,64},{224,... | collective-permute-start | bytes 638984 | tf_op jit(solution)/shard_map/ppermute | solution.py:39
  67.7 14.1 %collective-permute-start.4 = (bf16[208,256]{1,0:T(8,128)(2,1)S(1)}, bf16[208,256]{1,0:T(8,128)(2,1)S(1)}, u32[]{:S(2)}, u32[]{:S(2)}) collective-permute-start(bf16[208,256]{1,0:T(8,128)(2,1)S(1)} %get-tuple-element.51), channel_id=1, source_target_pairs={{0,128},{32,160},{64,192},{96,224},{128,256},{160,288},{192,320},{... | collective-permute-start | bytes 319496 | tf_op jit(solution)/shard_map/ppermute | solution.py:33
  74.5 12.3 %collective-permute-start.5 = (bf16[208,256]{1,0:T(8,128)(2,1)S(1)}, bf16[208,256]{1,0:T(8,128)(2,1)S(1)}, u32[]{:S(2)}, u32[]{:S(2)}) collective-permute-start(bf16[208,256]{1,0:T(8,128)(2,1)S(1)} %get-tuple-element.52), channel_id=1, source_target_pairs={{0,384},{32,416},{64,448},{96,480},{128,0},{160,32},{192,64},{224,... | collective-permute-start | bytes 319496 | tf_op jit(solution)/shard_map/ppermute | solution.py:34
  162.4 21.8 %all-to-all-start = ((bf16[32,2,4096]{2,1,0:T(2,128)(2,1)}), bf16[32,2,4096]{2,1,0:T(2,128)(2,1)S(1)}, u32[]{:S(2)}, u32[]{:S(2)}) async-start(bf16[32,2,4096]{2,1,0:T(2,128)(2,1)} %reshape.764), calls=%async_computation | async-start | bytes 1048576 | tf_op jit(solution)/shard_map/all_to_all | solution.py:48
  199.5 13.5 %all-to-all-start.1 = ((f32[32,1,768]{2,1,0:T(1,128)}), f32[32,1,768]{2,1,0:T(1,128)S(1)}, u32[]{:S(2)}, u32[]{:S(2)}) async-start(f32[32,1,768]{2,1,0:T(1,128)} %reshape.766), calls=%async_computation.1 | async-start | bytes 196608 | tf_op jit(solution)/shard_map/all_to_all | solution.py:244
  215.5 26.4 %all-to-all-start.2 = ((f32[16,1,768]{2,1,0:T(1,128)}), f32[16,1,768]{2,1,0:T(1,128)S(1)}, u32[]{:S(2)}, u32[]{:S(2)}) async-start(f32[16,1,768]{2,1,0:T(1,128)} %reshape.768), calls=%async_computation.2 | async-start | bytes 98304 | tf_op jit(solution)/shard_map/all_to_all | solution.py:48
Sparse Core Ops, SparseCore 0:
  87.9 67.7 all-gather.1

commit v13 on v12

--- a/solution.py
+++ b/solution.py
@@ -56,6 +56,22 @@
     return jnp.squeeze(top, axis), total, num
 
 
+def reduce_tm(m, t, n, axis):
+    size = lax.axis_size(axis)
+    rounds = size.bit_length() - 1
+    assert (1 << rounds) == size
+    for r in range(rounds):
+        bit = 1 << r
+        pairs = [(i, i ^ bit) for i in range(size)]
+        gm, gt, gn = lax.ppermute(jnp.stack([m, t, n]), axis, pairs)
+        top = jnp.maximum(m, gm)
+        keep, got_keep = jnp.exp(m - top), jnp.exp(gm - top)
+        t = t * keep + gt * got_keep
+        n = n * keep + gn * got_keep
+        m = top
+    return m, t, n
+
+
 BLOCK_ROWS = 256
 
 
@@ -243,8 +259,7 @@
     local = local.transpose(3, 1, 0, 2, 4)
     spread = lax.all_to_all(local, "space", 0, 0, tiled=True)
     m, t, n = merge_stats(spread[:, 0], spread[:, 1], spread[:, 2], 0)
-    joined = gather_all(jnp.stack([m, t, n]), "tm")
-    m, col_total, col_num = merge_stats(joined[:, 0], joined[:, 1], joined[:, 2], 0)
+    m, col_total, col_num = reduce_tm(m, t, n, "tm")
 
     all_count = jnp.sum(counts, axis=1)
     own_ids = kf_class.reshape(total_steps, keyframes, pix_dev)

time: 251 us -> 257 us (1.024); the launches traced: 250 us -> 254 us
  waiting for transfers between devices: 122 us -> 106 us
  blocking collectives: 0 us -> 13.3 us
  starting transfers between devices: 56.6 us -> 64.3 us
    ppermute x0 -> x4, starting transfers between devices: none -> 25.8 us  [reduce_tm(): gm, gt, gn = lax.ppermute(jnp.stack([m, t, n]), axis, pairs)]
    all_to_all x2 -> x1, waiting for transfers between devices: 15.7 us -> 2.36 us  [gather_all(): return lax.all_to_all(spread, axis, 0, 0, tiled=True)]
    all_to_all x0 -> x1, blocking collectives: none -> 13.3 us  [body(): spread = lax.all_to_all(local, 'space', 0, 0, tiled=True)]
    all_to_all x2 -> x1, starting transfers between devices: 18.1 us -> 5.43 us  [gather_all(): return lax.all_to_all(spread, axis, 0, 0, tiled=True)]
    all_to_all x1 -> x0, waiting for transfers between devices: 6.27 us -> none  [body(): spread = lax.all_to_all(local, 'space', 0, 0, tiled=True)]
    all_to_all x1 -> x0, starting transfers between devices: 5.4 us -> none  [body(): spread = lax.all_to_all(local, 'space', 0, 0, tiled=True)]
    ppermute x0 -> x4, waiting for transfers between devices: none -> 4.27 us  [reduce_tm(): gm, gt, gn = lax.ppermute(jnp.stack([m, t, n]), axis, pairs)]
    unnamed x17 -> x15, local copies, waits for them, and re-layouts: 6.23 us -> 4.73 us
  transfers between devices with their start and end apart: 10 -> 12, of which waited for: 9 -> 10; matrix products, arithmetic and copies ran while one was open for 5% -> 5% of each run, Pallas kernels for 5% -> 4%
where the time goes in v13:
time: 257 us; the launch traced here: 254 us
  waiting for transfers between devices  106 us (41%)
  starting transfers between devices  64.3 us (25%)
  Pallas kernels  27 us (11%)
  local copies, waits for them, and re-layouts  21.5 us (8%)
  between operations  14.6 us (6%)
  blocking collectives  13.3 us (5%)
  other arithmetic  7.01 us (3%)
    all_gather x1, waiting for transfers between devices, body(): gathered = lax.all_gather(packed, 'space', axis=2, tiled=True)  64.4 us
    pallas_call x3, Pallas kernels, step_pass(): pl.pallas_call(kernel, grid=(blocks,), in_specs=in_specs, out_specs=out_s...  27 us
    ppermute x4, starting transfers between devices, reduce_tm(): gm, gt, gn = lax.ppermute(jnp.stack([m, t, n]), axis, pairs)  25.8 us
    ppermute x1, waiting for transfers between devices, broadcast_tm(): got_b = lax.ppermute(value, axis, behind)  20.6 us
    all_to_all x1, blocking collectives, body(): spread = lax.all_to_all(local, 'space', 0, 0, tiled=True)  13.3 us
    ppermute x1, starting transfers between devices, broadcast_tm(): got_a = lax.ppermute(value, axis, ahead)  9.36 us
    ppermute x2, starting transfers between devices, broadcast_tm(): got = lax.ppermute(value, axis, pairs)  8.93 us
    ppermute x1, starting transfers between devices, broadcast_tm(): got_a = lax.ppermute(value[:half], axis, ahead)  6.73 us
  transfers between devices with their start and end apart: 12, of which 10 were waited for; matrix products, arithmetic and copies ran while one was open for 5% of the time, Pallas kernels for 4%

profile of v13, /device:TPU:1, one launch (start us, length us, event | category | flops | bytes accessed | tf_op | source)
XLA Modules:
  0.0 253.9 jit_solution(10166862362693722349)
XLA Ops:
  13.2 4.0 %collective-permute-start = (bf16[416,256]{1,0:T(8,128)(2,1)S(1)}, bf16[416,256]{1,0:T(8,128)(2,1)S(1)}, u32[]{:S(2)}, u32[]{:S(2)}) collective-permute-start(bf16[416,256]{1,0:T(8,128)(2,1)S(1)} %pad_maximum_fusion), channel_id=1, source_target_pairs={{0,32},{32,0},{64,96},{96,64},{128,160},{160,128},{192,224},{224,1... | collective-permute-start | bytes 638984 | tf_op jit(solution)/shard_map/ppermute | solution.py:23
  22.1 4.9 %collective-permute-start.1 = (bf16[416,256]{1,0:T(8,128)(2,1)S(1)}, bf16[416,256]{1,0:T(8,128)(2,1)S(1)}, u32[]{:S(2)}, u32[]{:S(2)}) collective-permute-start(bf16[416,256]{1,0:T(8,128)(2,1)S(1)} %broadcast_select_fusion), channel_id=1, source_target_pairs={{0,64},{32,96},{64,0},{96,32},{128,192},{160,224},{192,128},{224,1... | collective-permute-start | bytes 638984 | tf_op jit(solution)/shard_map/ppermute | solution.py:23
  27.0 3.2 %collective-permute-done.1 = bf16[416,256]{1,0:T(8,128)(2,1)S(1)} collective-permute-done((bf16[416,256]{1,0:T(8,128)(2,1)S(1)}, bf16[416,256]{1,0:T(8,128)(2,1)S(1)}, u32[]{:S(2)}, u32[]{:S(2)}) %collective-permute-start.1) | collective-permute-done | bytes 213024 | tf_op jit(solution)/shard_map/ppermute | solution.py:23
  30.4 9.4 %collective-permute-start.3 = (bf16[416,256]{1,0:T(8,128)(2,1)S(1)}, bf16[416,256]{1,0:T(8,128)(2,1)S(1)}, u32[]{:S(2)}, u32[]{:S(2)}) collective-permute-start(bf16[416,256]{1,0:T(8,128)(2,1)S(1)} %broadcast_select_fusion.1), channel_id=1, source_target_pairs={{0,128},{32,160},{64,192},{96,224},{128,256},{160,288},{192,320},{... | collective-permute-start | bytes 638984 | tf_op jit(solution)/shard_map/ppermute | solution.py:38
  39.7 5.6 %collective-permute-start.2 = (bf16[416,256]{1,0:T(8,128)(2,1)S(1)}, bf16[416,256]{1,0:T(8,128)(2,1)S(1)}, u32[]{:S(2)}, u32[]{:S(2)}) collective-permute-start(bf16[416,256]{1,0:T(8,128)(2,1)S(1)} %broadcast_select_fusion.1), channel_id=1, source_target_pairs={{0,384},{32,416},{64,448},{96,480},{128,0},{160,32},{192,64},{224,... | collective-permute-start | bytes 638984 | tf_op jit(solution)/shard_map/ppermute | solution.py:39
  45.3 1.6 collective-permute-done.3
  46.9 20.6 %collective-permute-done.2 = bf16[416,256]{1,0:T(8,128)(2,1)S(1)} collective-permute-done((bf16[416,256]{1,0:T(8,128)(2,1)S(1)}, bf16[416,256]{1,0:T(8,128)(2,1)S(1)}, u32[]{:S(2)}, u32[]{:S(2)}) %collective-permute-start.2) | collective-permute-done | bytes 213024 | tf_op jit(solution)/shard_map/ppermute | solution.py:39
  67.7 6.7 %collective-permute-start.4 = (bf16[208,256]{1,0:T(8,128)(2,1)S(1)}, bf16[208,256]{1,0:T(8,128)(2,1)S(1)}, u32[]{:S(2)}, u32[]{:S(2)}) collective-permute-start(bf16[208,256]{1,0:T(8,128)(2,1)S(1)} %get-tuple-element.53), channel_id=1, source_target_pairs={{0,128},{32,160},{64,192},{96,224},{128,256},{160,288},{192,320},{... | collective-permute-start | bytes 319496 | tf_op jit(solution)/shard_map/ppermute | solution.py:33
  74.5 2.5 collective-permute-start.5
  76.9 4.8 %collective-permute-done.4 = bf16[208,256]{1,0:T(8,128)(2,1)S(1)} collective-permute-done((bf16[208,256]{1,0:T(8,128)(2,1)S(1)}, bf16[208,256]{1,0:T(8,128)(2,1)S(1)}, u32[]{:S(2)}, u32[]{:S(2)}) %collective-permute-start.4) | collective-permute-done | bytes 106528 | tf_op jit(solution)/shard_map/ppermute | solution.py:33
  81.8 4.9 %collective-permute-done.5 = bf16[208,256]{1,0:T(8,128)(2,1)S(1)} collective-permute-done((bf16[208,256]{1,0:T(8,128)(2,1)S(1)}, bf16[208,256]{1,0:T(8,128)(2,1)S(1)}, u32[]{:S(2)}, u32[]{:S(2)}) %collective-permute-start.5) | collective-permute-done | bytes 106528 | tf_op jit(solution)/shard_map/ppermute | solution.py:34
  91.3 64.4 %all-gather.2.cloned.1.call-done = bf16[3,2,2048,256]{3,2,1,0:T(8,128)(2,1)} async-done(((bf16[3,2,64,256]{3,2,1,0:T(8,128)(2,1)}), bf16[3,2,2048,256]{3,2,1,0:T(8,128)(2,1)}) %all-gather.2.cloned.1.call-update) | async-done | bytes 6291472 | tf_op jit(solution)/shard_map/all_gather | solution.py:218
  155.7 4.1 %shard_map.77 = bf16[128,64]{1,0:T(8,128)(2,1)} custom-call(bf16[128,256]{1,0:T(8,128)(2,1)} %slice.110.q_ref, s32[128,1]{1,0:T(8,128)} %reshape.776.row_ok_ref.col_ok_ref, s32[128,1]{1,0:T(8,128)} %reshape.776.row_ok_ref.col_ok_ref, bf16[3,4096,256]{2,1,0:T(8,128)(2,1)} %bitcast.218, s32[1,4096]{1,0:T(1,128)} %bitcast.232, bf16[3,4096,256]{2,1,0:T(8,128)(2,1)} %bitcast.219), custom_call_target="tpu_custom_call" | custom-call | tf_op jit(solution)/shard_map/pallas_call | solution.py:155
  162.4 5.4 %all-to-all-start = ((bf16[32,2,4096]{2,1,0:T(2,128)(2,1)}), bf16[32,2,4096]{2,1,0:T(2,128)(2,1)S(1)}, u32[]{:S(2)}, u32[]{:S(2)}) async-start(bf16[32,2,4096]{2,1,0:T(2,128)(2,1)} %reshape.777), calls=%async_computation | async-start | bytes 1048576 | tf_op jit(solution)/shard_map/all_to_all | solution.py:48
  169.5 11.3 %shard_map.79 = (bf16[512,64]{1,0:T(8,128)(2,1)}, f32[1,4096]{1,0:T(1,128)}, f32[1,4096]{1,0:T(1,128)}, f32[1,4096]{1,0:T(1,128)}) custom-call(bf16[512,256]{1,0:T(8,128)(2,1)} %bitcast.227, s32[512,1]{1,0:T(8,128)} %reshape.775.row_ok_ref.col_ok_ref, s32[512,1]{1,0:T(8,128)} %reshape.775.row_ok_ref.col_ok_ref, bf16[3,4096,256]{2,1,0:T(8,128)(2,1)} %bitcast.220, ...), custom_call_target="tpu_custom_call" | custom-call | tf_op jit(solution)/shard_map/pallas_call | solution.py:155
  181.8 2.4 all-to-all-done
  185.9 11.6 %shard_map.78 = (bf16[512,64]{1,0:T(8,128)(2,1)}, f32[1,4096]{1,0:T(1,128)}, f32[1,4096]{1,0:T(1,128)}, f32[1,4096]{1,0:T(1,128)}) custom-call(bf16[512,256]{1,0:T(8,128)(2,1)} %bitcast.228, s32[512,1]{1,0:T(8,128)} %reshape.775.row_ok_ref.col_ok_ref, s32[512,1]{1,0:T(8,128)} %reshape.775.row_ok_ref.col_ok_ref, bf16[3,4096,256]{2,1,0:T(8,128)(2,1)} %bitcast.222, ...), custom_call_target="tpu_custom_call" | custom-call | tf_op jit(solution)/shard_map/pallas_call | solution.py:155
  198.9 13.3 %all_to_all.10 = f32[32,1,768]{2,1,0:T(1,128)S(1)} all-to-all(f32[32,1,768]{2,1,0:T(1,128)S(1)} %reshape.779), channel_id=1, replica_groups=mesh['tm'=16,'space'=32] {'space'}, dimensions={0} | all-to-all | bytes 196608 | tf_op jit(solution)/shard_map/all_to_all | solution.py:260
  213.9 3.1 %collective-permute-start.6 = (f32[3,2,2,64]{3,2,1,0:T(2,128)S(1)}, f32[3,2,2,64]{3,2,1,0:T(2,128)S(1)}, u32[]{:S(2)}, u32[]{:S(2)}) collective-permute-start(f32[3,2,2,64]{3,2,1,0:T(2,128)S(1)} %pad_maximum_fusion.4), channel_id=1, source_target_pairs={{0,32},{32,0},{64,96},{96,64},{128,160},{160,128},{192,224},{224,1... | collective-permute-start | bytes 9224 | tf_op jit(solution)/shard_map/ppermute | solution.py:66
  218.3 4.6 %collective-permute-start.7 = (f32[3,2,2,64]{3,2,1,0:T(2,128)S(1)}, f32[3,2,2,64]{3,2,1,0:T(2,128)S(1)}, u32[]{:S(2)}, u32[]{:S(2)}) collective-permute-start(f32[3,2,2,64]{3,2,1,0:T(2,128)S(1)} %pad_maximum_fusion.5), channel_id=1, source_target_pairs={{0,64},{32,96},{64,0},{96,32},{128,192},{160,224},{192,128},{224,1... | collective-permute-start | bytes 9224 | tf_op jit(solution)/shard_map/ppermute | solution.py:66
  223.1 1.7 slice.114
  224.9 7.4 %collective-permute-start.8 = (f32[3,2,2,64]{3,2,1,0:T(2,128)S(1)}, f32[3,2,2,64]{3,2,1,0:T(2,128)S(1)}, u32[]{:S(2)}, u32[]{:S(2)}) collective-permute-start(f32[3,2,2,64]{3,2,1,0:T(2,128)S(1)} %pad_maximum_fusion.6), channel_id=1, source_target_pairs={{0,128},{32,160},{64,192},{96,224},{128,0},{160,32},{192,64},{224,... | collective-permute-start | bytes 9224 | tf_op jit(solution)/shard_map/ppermute | solution.py:66
  233.3 10.7 %collective-permute-start.9 = (f32[3,2,2,64]{3,2,1,0:T(2,128)S(1)}, f32[3,2,2,64]{3,2,1,0:T(2,128)S(1)}, u32[]{:S(2)}, u32[]{:S(2)}) collective-permute-start(f32[3,2,2,64]{3,2,1,0:T(2,128)S(1)} %pad_maximum_fusion.7), channel_id=1, source_target_pairs={{0,256},{32,288},{64,320},{96,352},{128,384},{160,416},{192,448},{... | collective-permute-start | bytes 9224 | tf_op jit(solution)/shard_map/ppermute | solution.py:66
  244.2 2.2 collective-permute-done.9
  (117 shorter events, 28.9 us)
Async XLA Ops:
  7.2 5.3 %copy-start = (bf16[8,64,256]{2,1,0:T(8,128)(2,1)S(1)}, bf16[8,64,256]{2,1,0:T(8,128)(2,1)}, u32[]{:S(2)}) copy-start(bf16[8,64,256]{2,1,0:T(8,128)(2,1)} %param.11) | copy-start | bytes 786436
  7.2 148.5 %all-gather.2.cloned.1.call-start = ((), (), s32[]{:S(2)}) async-start(), calls=%async_computation.2 | async-start | bytes 6488064 | tf_op jit(solution)/shard_map/all_gather | solution.py:218
  13.2 8.8 %collective-permute-start = (bf16[416,256]{1,0:T(8,128)(2,1)S(1)}, bf16[416,256]{1,0:T(8,128)(2,1)S(1)}, u32[]{:S(2)}, u32[]{:S(2)}) collective-permute-start(bf16[416,256]{1,0:T(8,128)(2,1)S(1)} %pad_maximum_fusion), channel_id=1, source_target_pairs={{0,32},{32,0},{64,96},{96,64},{128,160},{160,128},{192,224},{224,1... | collective-permute-start | bytes 638984 | tf_op jit(solution)/shard_map/ppermute | solution.py:23
  22.1 65.7 %copy-start.2 = (s32[2,2]{1,0:T(2,128)S(1)}, s32[2,2]{1,0:T(2,128)}, u32[]{:S(2)}) copy-start(s32[2,2]{1,0:T(2,128)} %param.15) | copy-start | bytes 52
  22.1 65.8 %copy-start.1 = (s32[128]{0:T(128)S(1)}, s32[128]{0:T(128)}, u32[]{:S(2)}) copy-start(s32[128]{0:T(128)} %param.14) | copy-start | bytes 1540
  22.1 8.1 %collective-permute-start.1 = (bf16[416,256]{1,0:T(8,128)(2,1)S(1)}, bf16[416,256]{1,0:T(8,128)(2,1)S(1)}, u32[]{:S(2)}, u32[]{:S(2)}) collective-permute-start(bf16[416,256]{1,0:T(8,128)(2,1)S(1)} %broadcast_select_fusion), channel_id=1, source_target_pairs={{0,64},{32,96},{64,0},{96,32},{128,192},{160,224},{192,128},{224,1... | collective-permute-start | bytes 638984 | tf_op jit(solution)/shard_map/ppermute | solution.py:23
  30.4 16.5 %collective-permute-start.3 = (bf16[416,256]{1,0:T(8,128)(2,1)S(1)}, bf16[416,256]{1,0:T(8,128)(2,1)S(1)}, u32[]{:S(2)}, u32[]{:S(2)}) collective-permute-start(bf16[416,256]{1,0:T(8,128)(2,1)S(1)} %broadcast_select_fusion.1), channel_id=1, source_target_pairs={{0,128},{32,160},{64,192},{96,224},{128,256},{160,288},{192,320},{... | collective-permute-start | bytes 638984 | tf_op jit(solution)/shard_map/ppermute | solution.py:38
  39.7 27.8 %collective-permute-start.2 = (bf16[416,256]{1,0:T(8,128)(2,1)S(1)}, bf16[416,256]{1,0:T(8,128)(2,1)S(1)}, u32[]{:S(2)}, u32[]{:S(2)}) collective-permute-start(bf16[416,256]{1,0:T(8,128)(2,1)S(1)} %broadcast_select_fusion.1), channel_id=1, source_target_pairs={{0,384},{32,416},{64,448},{96,480},{128,0},{160,32},{192,64},{224,... | collective-permute-start | bytes 638984 | tf_op jit(solution)/shard_map/ppermute | solution.py:39
  67.7 14.1 %collective-permute-start.4 = (bf16[208,256]{1,0:T(8,128)(2,1)S(1)}, bf16[208,256]{1,0:T(8,128)(2,1)S(1)}, u32[]{:S(2)}, u32[]{:S(2)}) collective-permute-start(bf16[208,256]{1,0:T(8,128)(2,1)S(1)} %get-tuple-element.53), channel_id=1, source_target_pairs={{0,128},{32,160},{64,192},{96,224},{128,256},{160,288},{192,320},{... | collective-permute-start | bytes 319496 | tf_op jit(solution)/shard_map/ppermute | solution.py:33
  74.5 12.3 %collective-permute-start.5 = (bf16[208,256]{1,0:T(8,128)(2,1)S(1)}, bf16[208,256]{1,0:T(8,128)(2,1)S(1)}, u32[]{:S(2)}, u32[]{:S(2)}) collective-permute-start(bf16[208,256]{1,0:T(8,128)(2,1)S(1)} %get-tuple-element.54), channel_id=1, source_target_pairs={{0,384},{32,416},{64,448},{96,480},{128,0},{160,32},{192,64},{224,... | collective-permute-start | bytes 319496 | tf_op jit(solution)/shard_map/ppermute | solution.py:34
  162.4 21.8 %all-to-all-start = ((bf16[32,2,4096]{2,1,0:T(2,128)(2,1)}), bf16[32,2,4096]{2,1,0:T(2,128)(2,1)S(1)}, u32[]{:S(2)}, u32[]{:S(2)}) async-start(bf16[32,2,4096]{2,1,0:T(2,128)(2,1)} %reshape.777), calls=%async_computation | async-start | bytes 1048576 | tf_op jit(solution)/shard_map/all_to_all | solution.py:48
  213.9 4.4 %collective-permute-start.6 = (f32[3,2,2,64]{3,2,1,0:T(2,128)S(1)}, f32[3,2,2,64]{3,2,1,0:T(2,128)S(1)}, u32[]{:S(2)}, u32[]{:S(2)}) collective-permute-start(f32[3,2,2,64]{3,2,1,0:T(2,128)S(1)} %pad_maximum_fusion.4), channel_id=1, source_target_pairs={{0,32},{32,0},{64,96},{96,64},{128,160},{160,128},{192,224},{224,1... | collective-permute-start | bytes 9224 | tf_op jit(solution)/shard_map/ppermute | solution.py:66
  218.3 6.5 %collective-permute-start.7 = (f32[3,2,2,64]{3,2,1,0:T(2,128)S(1)}, f32[3,2,2,64]{3,2,1,0:T(2,128)S(1)}, u32[]{:S(2)}, u32[]{:S(2)}) collective-permute-start(f32[3,2,2,64]{3,2,1,0:T(2,128)S(1)} %pad_maximum_fusion.5), channel_id=1, source_target_pairs={{0,64},{32,96},{64,0},{96,32},{128,192},{160,224},{192,128},{224,1... | collective-permute-start | bytes 9224 | tf_op jit(solution)/shard_map/ppermute | solution.py:66
  224.9 8.4 %collective-permute-start.8 = (f32[3,2,2,64]{3,2,1,0:T(2,128)S(1)}, f32[3,2,2,64]{3,2,1,0:T(2,128)S(1)}, u32[]{:S(2)}, u32[]{:S(2)}) collective-permute-start(f32[3,2,2,64]{3,2,1,0:T(2,128)S(1)} %pad_maximum_fusion.6), channel_id=1, source_target_pairs={{0,128},{32,160},{64,192},{96,224},{128,0},{160,32},{192,64},{224,... | collective-permute-start | bytes 9224 | tf_op jit(solution)/shard_map/ppermute | solution.py:66
  233.3 13.1 %collective-permute-start.9 = (f32[3,2,2,64]{3,2,1,0:T(2,128)S(1)}, f32[3,2,2,64]{3,2,1,0:T(2,128)S(1)}, u32[]{:S(2)}, u32[]{:S(2)}) collective-permute-start(f32[3,2,2,64]{3,2,1,0:T(2,128)S(1)} %pad_maximum_fusion.7), channel_id=1, source_target_pairs={{0,256},{32,288},{64,320},{96,352},{128,384},{160,416},{192,448},{... | collective-permute-start | bytes 9224 | tf_op jit(solution)/shard_map/ppermute | solution.py:66
Sparse Core Ops, SparseCore 0:
  87.9 67.7 all-gather.1

commit v14 on v12

--- a/solution.py
+++ b/solution.py
@@ -56,7 +56,7 @@
     return jnp.squeeze(top, axis), total, num
 
 
-BLOCK_ROWS = 256
+BLOCK_ROWS = 512
 
 
 def step_kernel(q_ref, row_ok_ref, col_ok_ref, keys_ref, key_ok_ref, aux_ref, *refs,

time: 251 us -> 251 us (level)
  transfers between devices with their start and end apart: 10 -> 10, of which waited for: 9 -> 9; matrix products, arithmetic and copies ran while one was open for 5% -> 5% of each run, Pallas kernels for 5% -> 4%
where the time goes in v14:
time: 251 us; the launch traced here: 250 us
  waiting for transfers between devices  122 us (49%)
  starting transfers between devices  56.6 us (23%)
  Pallas kernels  26.5 us (11%)
  local copies, waits for them, and re-layouts  23 us (9%)
  between operations  14.5 us (6%)
  other arithmetic  7.79 us (3%)
    all_gather x1, waiting for transfers between devices, body(): gathered = lax.all_gather(packed, 'space', axis=2, tiled=True)  64.4 us
    pallas_call x3, Pallas kernels, step_pass(): pl.pallas_call(kernel, grid=(blocks,), in_specs=in_specs, out_specs=out_s...  26.5 us
    ppermute x1, waiting for transfers between devices, broadcast_tm(): got_b = lax.ppermute(value, axis, behind)  20.6 us
    all_to_all x2, starting transfers between devices, gather_all(): return lax.all_to_all(spread, axis, 0, 0, tiled=True)  18.3 us
    all_to_all x2, waiting for transfers between devices, gather_all(): return lax.all_to_all(spread, axis, 0, 0, tiled=True)  15.8 us
    ppermute x1, starting transfers between devices, broadcast_tm(): got_a = lax.ppermute(value, axis, ahead)  9.36 us
    ppermute x2, starting transfers between devices, broadcast_tm(): got = lax.ppermute(value, axis, pairs)  8.93 us
    ppermute x1, starting transfers between devices, broadcast_tm(): got_a = lax.ppermute(value[:half], axis, ahead)  6.73 us
  transfers between devices with their start and end apart: 10, of which 9 were waited for; matrix products, arithmetic and copies ran while one was open for 5% of the time, Pallas kernels for 4%

profile of v14, /device:TPU:1, one launch (start us, length us, event | category | flops | bytes accessed | tf_op | source)
XLA Modules:
  0.0 250.2 jit_solution(7236777886803802629)
XLA Ops:
  10.9 1.5 gather_fusion.1
  13.2 4.0 %collective-permute-start = (bf16[416,256]{1,0:T(8,128)(2,1)S(1)}, bf16[416,256]{1,0:T(8,128)(2,1)S(1)}, u32[]{:S(2)}, u32[]{:S(2)}) collective-permute-start(bf16[416,256]{1,0:T(8,128)(2,1)S(1)} %pad_maximum_fusion), channel_id=1, source_target_pairs={{0,32},{32,0},{64,96},{96,64},{128,160},{160,128},{192,224},{224,1... | collective-permute-start | bytes 638984 | tf_op jit(solution)/shard_map/ppermute | solution.py:23
  22.1 4.9 %collective-permute-start.1 = (bf16[416,256]{1,0:T(8,128)(2,1)S(1)}, bf16[416,256]{1,0:T(8,128)(2,1)S(1)}, u32[]{:S(2)}, u32[]{:S(2)}) collective-permute-start(bf16[416,256]{1,0:T(8,128)(2,1)S(1)} %broadcast_select_fusion), channel_id=1, source_target_pairs={{0,64},{32,96},{64,0},{96,32},{128,192},{160,224},{192,128},{224,1... | collective-permute-start | bytes 638984 | tf_op jit(solution)/shard_map/ppermute | solution.py:23
  27.0 3.2 %collective-permute-done.1 = bf16[416,256]{1,0:T(8,128)(2,1)S(1)} collective-permute-done((bf16[416,256]{1,0:T(8,128)(2,1)S(1)}, bf16[416,256]{1,0:T(8,128)(2,1)S(1)}, u32[]{:S(2)}, u32[]{:S(2)}) %collective-permute-start.1) | collective-permute-done | bytes 213024 | tf_op jit(solution)/shard_map/ppermute | solution.py:23
  30.4 9.4 %collective-permute-start.3 = (bf16[416,256]{1,0:T(8,128)(2,1)S(1)}, bf16[416,256]{1,0:T(8,128)(2,1)S(1)}, u32[]{:S(2)}, u32[]{:S(2)}) collective-permute-start(bf16[416,256]{1,0:T(8,128)(2,1)S(1)} %broadcast_select_fusion.1), channel_id=1, source_target_pairs={{0,128},{32,160},{64,192},{96,224},{128,256},{160,288},{192,320},{... | collective-permute-start | bytes 638984 | tf_op jit(solution)/shard_map/ppermute | solution.py:38
  39.7 5.6 %collective-permute-start.2 = (bf16[416,256]{1,0:T(8,128)(2,1)S(1)}, bf16[416,256]{1,0:T(8,128)(2,1)S(1)}, u32[]{:S(2)}, u32[]{:S(2)}) collective-permute-start(bf16[416,256]{1,0:T(8,128)(2,1)S(1)} %broadcast_select_fusion.1), channel_id=1, source_target_pairs={{0,384},{32,416},{64,448},{96,480},{128,0},{160,32},{192,64},{224,... | collective-permute-start | bytes 638984 | tf_op jit(solution)/shard_map/ppermute | solution.py:39
  45.3 1.6 collective-permute-done.3
  46.9 20.6 %collective-permute-done.2 = bf16[416,256]{1,0:T(8,128)(2,1)S(1)} collective-permute-done((bf16[416,256]{1,0:T(8,128)(2,1)S(1)}, bf16[416,256]{1,0:T(8,128)(2,1)S(1)}, u32[]{:S(2)}, u32[]{:S(2)}) %collective-permute-start.2) | collective-permute-done | bytes 213024 | tf_op jit(solution)/shard_map/ppermute | solution.py:39
  67.7 6.7 %collective-permute-start.4 = (bf16[208,256]{1,0:T(8,128)(2,1)S(1)}, bf16[208,256]{1,0:T(8,128)(2,1)S(1)}, u32[]{:S(2)}, u32[]{:S(2)}) collective-permute-start(bf16[208,256]{1,0:T(8,128)(2,1)S(1)} %get-tuple-element.51), channel_id=1, source_target_pairs={{0,128},{32,160},{64,192},{96,224},{128,256},{160,288},{192,320},{... | collective-permute-start | bytes 319496 | tf_op jit(solution)/shard_map/ppermute | solution.py:33
  74.5 2.5 collective-permute-start.5
  76.9 4.8 %collective-permute-done.4 = bf16[208,256]{1,0:T(8,128)(2,1)S(1)} collective-permute-done((bf16[208,256]{1,0:T(8,128)(2,1)S(1)}, bf16[208,256]{1,0:T(8,128)(2,1)S(1)}, u32[]{:S(2)}, u32[]{:S(2)}) %collective-permute-start.4) | collective-permute-done | bytes 106528 | tf_op jit(solution)/shard_map/ppermute | solution.py:33
  81.8 4.9 %collective-permute-done.5 = bf16[208,256]{1,0:T(8,128)(2,1)S(1)} collective-permute-done((bf16[208,256]{1,0:T(8,128)(2,1)S(1)}, bf16[208,256]{1,0:T(8,128)(2,1)S(1)}, u32[]{:S(2)}, u32[]{:S(2)}) %collective-permute-start.5) | collective-permute-done | bytes 106528 | tf_op jit(solution)/shard_map/ppermute | solution.py:34
  91.3 64.4 %all-gather.2.cloned.1.call-done = bf16[3,2,2048,256]{3,2,1,0:T(8,128)(2,1)} async-done(((bf16[3,2,64,256]{3,2,1,0:T(8,128)(2,1)}), bf16[3,2,2048,256]{3,2,1,0:T(8,128)(2,1)}) %all-gather.2.cloned.1.call-update) | async-done | bytes 6291472 | tf_op jit(solution)/shard_map/all_gather | solution.py:202
  155.7 4.1 %shard_map.77 = bf16[128,64]{1,0:T(8,128)(2,1)} custom-call(bf16[128,256]{1,0:T(8,128)(2,1)} %slice.122.q_ref, s32[128,1]{1,0:T(8,128)} %reshape.763.row_ok_ref.col_ok_ref, s32[128,1]{1,0:T(8,128)} %reshape.763.row_ok_ref.col_ok_ref, bf16[3,4096,256]{2,1,0:T(8,128)(2,1)} %bitcast.100, s32[1,4096]{1,0:T(1,128)} %bitcast.114, bf16[3,4096,256]{2,1,0:T(8,128)(2,1)} %bitcast.101), custom_call_target="tpu_custom_call" | custom-call | tf_op jit(solution)/shard_map/pallas_call | solution.py:139
  160.8 1.6 reshape.764
  162.4 5.6 %all-to-all-start = ((bf16[32,2,4096]{2,1,0:T(2,128)(2,1)}), bf16[32,2,4096]{2,1,0:T(2,128)(2,1)S(1)}, u32[]{:S(2)}, u32[]{:S(2)}) async-start(bf16[32,2,4096]{2,1,0:T(2,128)(2,1)} %reshape.764), calls=%async_computation | async-start | bytes 1048576 | tf_op jit(solution)/shard_map/all_to_all | solution.py:48
  169.7 11.0 %shard_map.79 = (bf16[512,64]{1,0:T(8,128)(2,1)}, f32[1,4096]{1,0:T(1,128)}, f32[1,4096]{1,0:T(1,128)}, f32[1,4096]{1,0:T(1,128)}) custom-call(bf16[512,256]{1,0:T(8,128)(2,1)} %bitcast.109, s32[512,1]{1,0:T(8,128)} %reshape.762.row_ok_ref.col_ok_ref, s32[512,1]{1,0:T(8,128)} %reshape.762.row_ok_ref.col_ok_ref, bf16[3,4096,256]{2,1,0:T(8,128)(2,1)} %bitcast.102, ...), custom_call_target="tpu_custom_call" | custom-call | tf_op jit(solution)/shard_map/pallas_call | solution.py:139
  181.7 2.5 %all-to-all-done = bf16[32,2,4096]{2,1,0:T(2,128)(2,1)S(1)} async-done(((bf16[32,2,4096]{2,1,0:T(2,128)(2,1)}), bf16[32,2,4096]{2,1,0:T(2,128)(2,1)S(1)}, u32[]{:S(2)}, u32[]{:S(2)}) %all-to-all-start) | async-done | bytes 524320 | tf_op jit(solution)/shard_map/all_to_all | solution.py:48
  186.0 11.5 %shard_map.78 = (bf16[512,64]{1,0:T(8,128)(2,1)}, f32[1,4096]{1,0:T(1,128)}, f32[1,4096]{1,0:T(1,128)}, f32[1,4096]{1,0:T(1,128)}) custom-call(bf16[512,256]{1,0:T(8,128)(2,1)} %bitcast.110, s32[512,1]{1,0:T(8,128)} %reshape.762.row_ok_ref.col_ok_ref, s32[512,1]{1,0:T(8,128)} %reshape.762.row_ok_ref.col_ok_ref, bf16[3,4096,256]{2,1,0:T(8,128)(2,1)} %bitcast.104, ...), custom_call_target="tpu_custom_call" | custom-call | tf_op jit(solution)/shard_map/pallas_call | solution.py:139
  199.4 5.2 %all-to-all-start.1 = ((f32[32,1,768]{2,1,0:T(1,128)}), f32[32,1,768]{2,1,0:T(1,128)S(1)}, u32[]{:S(2)}, u32[]{:S(2)}) async-start(f32[32,1,768]{2,1,0:T(1,128)} %reshape.766), calls=%async_computation.1 | async-start | bytes 196608 | tf_op jit(solution)/shard_map/all_to_all | solution.py:244
  204.7 1.7 slice.129
  206.5 6.3 %all-to-all-done.1 = f32[32,1,768]{2,1,0:T(1,128)S(1)} async-done(((f32[32,1,768]{2,1,0:T(1,128)}), f32[32,1,768]{2,1,0:T(1,128)S(1)}, u32[]{:S(2)}, u32[]{:S(2)}) %all-to-all-start.1) | async-done | bytes 98336 | tf_op jit(solution)/shard_map/all_to_all | solution.py:244
  215.2 12.7 %all-to-all-start.2 = ((f32[16,1,768]{2,1,0:T(1,128)}), f32[16,1,768]{2,1,0:T(1,128)S(1)}, u32[]{:S(2)}, u32[]{:S(2)}) async-start(f32[16,1,768]{2,1,0:T(1,128)} %reshape.768), calls=%async_computation.2 | async-start | bytes 98304 | tf_op jit(solution)/shard_map/all_to_all | solution.py:48
  228.3 13.3 %all-to-all-done.2 = f32[16,1,768]{2,1,0:T(1,128)S(1)} async-done(((f32[16,1,768]{2,1,0:T(1,128)}), f32[16,1,768]{2,1,0:T(1,128)S(1)}, u32[]{:S(2)}, u32[]{:S(2)}) %all-to-all-start.2) | async-done | bytes 49184 | tf_op jit(solution)/shard_map/all_to_all | solution.py:48
  (110 shorter events, 26.1 us)
Async XLA Ops:
  7.2 5.3 %copy-start = (bf16[8,64,256]{2,1,0:T(8,128)(2,1)S(1)}, bf16[8,64,256]{2,1,0:T(8,128)(2,1)}, u32[]{:S(2)}) copy-start(bf16[8,64,256]{2,1,0:T(8,128)(2,1)} %param.11) | copy-start | bytes 786436
  7.2 148.5 %all-gather.2.cloned.1.call-start = ((), (), s32[]{:S(2)}) async-start(), calls=%async_computation.3 | async-start | bytes 6488064 | tf_op jit(solution)/shard_map/all_gather | solution.py:202
  13.2 8.8 %collective-permute-start = (bf16[416,256]{1,0:T(8,128)(2,1)S(1)}, bf16[416,256]{1,0:T(8,128)(2,1)S(1)}, u32[]{:S(2)}, u32[]{:S(2)}) collective-permute-start(bf16[416,256]{1,0:T(8,128)(2,1)S(1)} %pad_maximum_fusion), channel_id=1, source_target_pairs={{0,32},{32,0},{64,96},{96,64},{128,160},{160,128},{192,224},{224,1... | collective-permute-start | bytes 638984 | tf_op jit(solution)/shard_map/ppermute | solution.py:23
  22.1 65.7 %copy-start.2 = (s32[2,2]{1,0:T(2,128)S(1)}, s32[2,2]{1,0:T(2,128)}, u32[]{:S(2)}) copy-start(s32[2,2]{1,0:T(2,128)} %param.15) | copy-start | bytes 52
  22.1 65.8 %copy-start.1 = (s32[128]{0:T(128)S(1)}, s32[128]{0:T(128)}, u32[]{:S(2)}) copy-start(s32[128]{0:T(128)} %param.14) | copy-start | bytes 1540
  22.1 8.1 %collective-permute-start.1 = (bf16[416,256]{1,0:T(8,128)(2,1)S(1)}, bf16[416,256]{1,0:T(8,128)(2,1)S(1)}, u32[]{:S(2)}, u32[]{:S(2)}) collective-permute-start(bf16[416,256]{1,0:T(8,128)(2,1)S(1)} %broadcast_select_fusion), channel_id=1, source_target_pairs={{0,64},{32,96},{64,0},{96,32},{128,192},{160,224},{192,128},{224,1... | collective-permute-start | bytes 638984 | tf_op jit(solution)/shard_map/ppermute | solution.py:23
  30.4 16.5 %collective-permute-start.3 = (bf16[416,256]{1,0:T(8,128)(2,1)S(1)}, bf16[416,256]{1,0:T(8,128)(2,1)S(1)}, u32[]{:S(2)}, u32[]{:S(2)}) collective-permute-start(bf16[416,256]{1,0:T(8,128)(2,1)S(1)} %broadcast_select_fusion.1), channel_id=1, source_target_pairs={{0,128},{32,160},{64,192},{96,224},{128,256},{160,288},{192,320},{... | collective-permute-start | bytes 638984 | tf_op jit(solution)/shard_map/ppermute | solution.py:38
  39.7 27.8 %collective-permute-start.2 = (bf16[416,256]{1,0:T(8,128)(2,1)S(1)}, bf16[416,256]{1,0:T(8,128)(2,1)S(1)}, u32[]{:S(2)}, u32[]{:S(2)}) collective-permute-start(bf16[416,256]{1,0:T(8,128)(2,1)S(1)} %broadcast_select_fusion.1), channel_id=1, source_target_pairs={{0,384},{32,416},{64,448},{96,480},{128,0},{160,32},{192,64},{224,... | collective-permute-start | bytes 638984 | tf_op jit(solution)/shard_map/ppermute | solution.py:39
  67.7 14.1 %collective-permute-start.4 = (bf16[208,256]{1,0:T(8,128)(2,1)S(1)}, bf16[208,256]{1,0:T(8,128)(2,1)S(1)}, u32[]{:S(2)}, u32[]{:S(2)}) collective-permute-start(bf16[208,256]{1,0:T(8,128)(2,1)S(1)} %get-tuple-element.51), channel_id=1, source_target_pairs={{0,128},{32,160},{64,192},{96,224},{128,256},{160,288},{192,320},{... | collective-permute-start | bytes 319496 | tf_op jit(solution)/shard_map/ppermute | solution.py:33
  74.5 12.3 %collective-permute-start.5 = (bf16[208,256]{1,0:T(8,128)(2,1)S(1)}, bf16[208,256]{1,0:T(8,128)(2,1)S(1)}, u32[]{:S(2)}, u32[]{:S(2)}) collective-permute-start(bf16[208,256]{1,0:T(8,128)(2,1)S(1)} %get-tuple-element.52), channel_id=1, source_target_pairs={{0,384},{32,416},{64,448},{96,480},{128,0},{160,32},{192,64},{224,... | collective-permute-start | bytes 319496 | tf_op jit(solution)/shard_map/ppermute | solution.py:34
  162.4 21.8 %all-to-all-start = ((bf16[32,2,4096]{2,1,0:T(2,128)(2,1)}), bf16[32,2,4096]{2,1,0:T(2,128)(2,1)S(1)}, u32[]{:S(2)}, u32[]{:S(2)}) async-start(bf16[32,2,4096]{2,1,0:T(2,128)(2,1)} %reshape.764), calls=%async_computation | async-start | bytes 1048576 | tf_op jit(solution)/shard_map/all_to_all | solution.py:48
  199.4 13.3 %all-to-all-start.1 = ((f32[32,1,768]{2,1,0:T(1,128)}), f32[32,1,768]{2,1,0:T(1,128)S(1)}, u32[]{:S(2)}, u32[]{:S(2)}) async-start(f32[32,1,768]{2,1,0:T(1,128)} %reshape.766), calls=%async_computation.1 | async-start | bytes 196608 | tf_op jit(solution)/shard_map/all_to_all | solution.py:244
  215.2 26.4 %all-to-all-start.2 = ((f32[16,1,768]{2,1,0:T(1,128)}), f32[16,1,768]{2,1,0:T(1,128)S(1)}, u32[]{:S(2)}, u32[]{:S(2)}) async-start(f32[16,1,768]{2,1,0:T(1,128)} %reshape.768), calls=%async_computation.2 | async-start | bytes 98304 | tf_op jit(solution)/shard_map/all_to_all | solution.py:48
Sparse Core Ops, SparseCore 0:
  87.9 67.7 all-gather.1

commit v15 on v14

--- a/solution.py
+++ b/solution.py
@@ -227,10 +227,10 @@
                 extra, extra_ok, extra_ok, gathered, step, key_ok, mem_values, channels, scale,
                 False,
             )
-            part = part.reshape(keyframes, pix_dev, channels)
-            next_values = gather_all(part, "space").transpose(1, 0, 2, 3).reshape(
-                mem_width, channels
-            )
+            part = part.reshape(keyframes, pix_dev * channels)
+            next_values = gather_all(part, "space").reshape(
+                n_space, keyframes, pix_dev, channels
+            ).transpose(1, 0, 2, 3).reshape(mem_width, channels)
         ok = row_valid.astype(jnp.int32)[:, None]
         readout, col_max, col_total, col_num = step_pass(
             query_rows, ok, ok, gathered, step, key_ok, mem_values, channels, scale, True

time: 251 us -> 251 us (level)
    unnamed x17 -> x15, local copies, waits for them, and re-layouts: 6.23 us -> 3.99 us
where the time goes in v15:
time: 251 us; the launch traced here: 250 us
  waiting for transfers between devices  122 us (49%)
  starting transfers between devices  56.6 us (23%)
  Pallas kernels  26.5 us (11%)
  local copies, waits for them, and re-layouts  22.6 us (9%)
  between operations  14.5 us (6%)
  other arithmetic  7.77 us (3%)
    all_gather x1, waiting for transfers between devices, body(): gathered = lax.all_gather(packed, 'space', axis=2, tiled=True)  64.4 us
    pallas_call x3, Pallas kernels, step_pass(): pl.pallas_call(kernel, grid=(blocks,), in_specs=in_specs, out_specs=out_s...  26.5 us
    ppermute x1, waiting for transfers between devices, broadcast_tm(): got_b = lax.ppermute(value, axis, behind)  20.6 us
    all_to_all x2, starting transfers between devices, gather_all(): return lax.all_to_all(spread, axis, 0, 0, tiled=True)  18.3 us
    all_to_all x2, waiting for transfers between devices, gather_all(): return lax.all_to_all(spread, axis, 0, 0, tiled=True)  15.8 us
    ppermute x1, starting transfers between devices, broadcast_tm(): got_a = lax.ppermute(value, axis, ahead)  9.36 us
    ppermute x2, starting transfers between devices, broadcast_tm(): got = lax.ppermute(value, axis, pairs)  8.93 us
    ppermute x1, starting transfers between devices, broadcast_tm(): got_a = lax.ppermute(value[:half], axis, ahead)  6.73 us
  transfers between devices with their start and end apart: 10, of which 9 were waited for; matrix products, arithmetic and copies ran while one was open for 5% of the time, Pallas kernels for 4%

profile of v15, /device:TPU:1, one launch (start us, length us, event | category | flops | bytes accessed | tf_op | source)
XLA Modules:
  0.0 249.7 jit_solution(16573796569570467408)
XLA Ops:
  9.2 1.5 gather_fusion.2
  10.9 1.5 gather_fusion.1
  13.2 4.0 %collective-permute-start = (bf16[416,256]{1,0:T(8,128)(2,1)S(1)}, bf16[416,256]{1,0:T(8,128)(2,1)S(1)}, u32[]{:S(2)}, u32[]{:S(2)}) collective-permute-start(bf16[416,256]{1,0:T(8,128)(2,1)S(1)} %pad_maximum_fusion), channel_id=1, source_target_pairs={{0,32},{32,0},{64,96},{96,64},{128,160},{160,128},{192,224},{224,1... | collective-permute-start | bytes 638984 | tf_op jit(solution)/shard_map/ppermute | solution.py:23
  22.1 4.9 %collective-permute-start.1 = (bf16[416,256]{1,0:T(8,128)(2,1)S(1)}, bf16[416,256]{1,0:T(8,128)(2,1)S(1)}, u32[]{:S(2)}, u32[]{:S(2)}) collective-permute-start(bf16[416,256]{1,0:T(8,128)(2,1)S(1)} %broadcast_select_fusion), channel_id=1, source_target_pairs={{0,64},{32,96},{64,0},{96,32},{128,192},{160,224},{192,128},{224,1... | collective-permute-start | bytes 638984 | tf_op jit(solution)/shard_map/ppermute | solution.py:23
  27.0 3.2 %collective-permute-done.1 = bf16[416,256]{1,0:T(8,128)(2,1)S(1)} collective-permute-done((bf16[416,256]{1,0:T(8,128)(2,1)S(1)}, bf16[416,256]{1,0:T(8,128)(2,1)S(1)}, u32[]{:S(2)}, u32[]{:S(2)}) %collective-permute-start.1) | collective-permute-done | bytes 213024 | tf_op jit(solution)/shard_map/ppermute | solution.py:23
  30.4 9.4 %collective-permute-start.3 = (bf16[416,256]{1,0:T(8,128)(2,1)S(1)}, bf16[416,256]{1,0:T(8,128)(2,1)S(1)}, u32[]{:S(2)}, u32[]{:S(2)}) collective-permute-start(bf16[416,256]{1,0:T(8,128)(2,1)S(1)} %broadcast_select_fusion.1), channel_id=1, source_target_pairs={{0,128},{32,160},{64,192},{96,224},{128,256},{160,288},{192,320},{... | collective-permute-start | bytes 638984 | tf_op jit(solution)/shard_map/ppermute | solution.py:38
  39.7 5.6 %collective-permute-start.2 = (bf16[416,256]{1,0:T(8,128)(2,1)S(1)}, bf16[416,256]{1,0:T(8,128)(2,1)S(1)}, u32[]{:S(2)}, u32[]{:S(2)}) collective-permute-start(bf16[416,256]{1,0:T(8,128)(2,1)S(1)} %broadcast_select_fusion.1), channel_id=1, source_target_pairs={{0,384},{32,416},{64,448},{96,480},{128,0},{160,32},{192,64},{224,... | collective-permute-start | bytes 638984 | tf_op jit(solution)/shard_map/ppermute | solution.py:39
  45.3 1.6 collective-permute-done.3
  46.9 20.6 %collective-permute-done.2 = bf16[416,256]{1,0:T(8,128)(2,1)S(1)} collective-permute-done((bf16[416,256]{1,0:T(8,128)(2,1)S(1)}, bf16[416,256]{1,0:T(8,128)(2,1)S(1)}, u32[]{:S(2)}, u32[]{:S(2)}) %collective-permute-start.2) | collective-permute-done | bytes 213024 | tf_op jit(solution)/shard_map/ppermute | solution.py:39
  67.7 6.7 %collective-permute-start.4 = (bf16[208,256]{1,0:T(8,128)(2,1)S(1)}, bf16[208,256]{1,0:T(8,128)(2,1)S(1)}, u32[]{:S(2)}, u32[]{:S(2)}) collective-permute-start(bf16[208,256]{1,0:T(8,128)(2,1)S(1)} %get-tuple-element.51), channel_id=1, source_target_pairs={{0,128},{32,160},{64,192},{96,224},{128,256},{160,288},{192,320},{... | collective-permute-start | bytes 319496 | tf_op jit(solution)/shard_map/ppermute | solution.py:33
  74.5 2.5 collective-permute-start.5
  76.9 4.8 %collective-permute-done.4 = bf16[208,256]{1,0:T(8,128)(2,1)S(1)} collective-permute-done((bf16[208,256]{1,0:T(8,128)(2,1)S(1)}, bf16[208,256]{1,0:T(8,128)(2,1)S(1)}, u32[]{:S(2)}, u32[]{:S(2)}) %collective-permute-start.4) | collective-permute-done | bytes 106528 | tf_op jit(solution)/shard_map/ppermute | solution.py:33
  81.8 4.9 %collective-permute-done.5 = bf16[208,256]{1,0:T(8,128)(2,1)S(1)} collective-permute-done((bf16[208,256]{1,0:T(8,128)(2,1)S(1)}, bf16[208,256]{1,0:T(8,128)(2,1)S(1)}, u32[]{:S(2)}, u32[]{:S(2)}) %collective-permute-start.5) | collective-permute-done | bytes 106528 | tf_op jit(solution)/shard_map/ppermute | solution.py:34
  91.3 64.4 %all-gather.2.cloned.1.call-done = bf16[3,2,2048,256]{3,2,1,0:T(8,128)(2,1)} async-done(((bf16[3,2,64,256]{3,2,1,0:T(8,128)(2,1)}), bf16[3,2,2048,256]{3,2,1,0:T(8,128)(2,1)}) %all-gather.2.cloned.1.call-update) | async-done | bytes 6291472 | tf_op jit(solution)/shard_map/all_gather | solution.py:202
  155.7 4.1 %shard_map.77 = bf16[128,64]{1,0:T(8,128)(2,1)} custom-call(bf16[128,256]{1,0:T(8,128)(2,1)} %slice.122.q_ref, s32[128,1]{1,0:T(8,128)} %reshape.767.row_ok_ref.col_ok_ref, s32[128,1]{1,0:T(8,128)} %reshape.767.row_ok_ref.col_ok_ref, bf16[3,4096,256]{2,1,0:T(8,128)(2,1)} %bitcast.100, s32[1,4096]{1,0:T(1,128)} %bitcast.113, bf16[3,4096,256]{2,1,0:T(8,128)(2,1)} %bitcast.101), custom_call_target="tpu_custom_call" | custom-call | tf_op jit(solution)/shard_map/pallas_call | solution.py:139
  161.9 5.6 %all-to-all-start = ((bf16[32,2,4096]{2,1,0:T(2,128)(2,1)}), bf16[32,2,4096]{2,1,0:T(2,128)(2,1)S(1)}, u32[]{:S(2)}, u32[]{:S(2)}) async-start(bf16[32,2,4096]{2,1,0:T(2,128)(2,1)} %broadcast_in_dim.190), calls=%async_computation | async-start | bytes 1048576 | tf_op jit(solution)/shard_map/all_to_all | solution.py:48
  169.3 11.0 %shard_map.79 = (bf16[512,64]{1,0:T(8,128)(2,1)}, f32[1,4096]{1,0:T(1,128)}, f32[1,4096]{1,0:T(1,128)}, f32[1,4096]{1,0:T(1,128)}) custom-call(bf16[512,256]{1,0:T(8,128)(2,1)} %bitcast.108, s32[512,1]{1,0:T(8,128)} %reshape.766.row_ok_ref.col_ok_ref, s32[512,1]{1,0:T(8,128)} %reshape.766.row_ok_ref.col_ok_ref, bf16[3,4096,256]{2,1,0:T(8,128)(2,1)} %bitcast.102, ...), custom_call_target="tpu_custom_call" | custom-call | tf_op jit(solution)/shard_map/pallas_call | solution.py:139
  181.2 2.5 %all-to-all-done = bf16[32,2,4096]{2,1,0:T(2,128)(2,1)S(1)} async-done(((bf16[32,2,4096]{2,1,0:T(2,128)(2,1)}), bf16[32,2,4096]{2,1,0:T(2,128)(2,1)S(1)}, u32[]{:S(2)}, u32[]{:S(2)}) %all-to-all-start) | async-done | bytes 524320 | tf_op jit(solution)/shard_map/all_to_all | solution.py:48
  185.5 11.5 %shard_map.78 = (bf16[512,64]{1,0:T(8,128)(2,1)}, f32[1,4096]{1,0:T(1,128)}, f32[1,4096]{1,0:T(1,128)}, f32[1,4096]{1,0:T(1,128)}) custom-call(bf16[512,256]{1,0:T(8,128)(2,1)} %bitcast.109, s32[512,1]{1,0:T(8,128)} %reshape.766.row_ok_ref.col_ok_ref, s32[512,1]{1,0:T(8,128)} %reshape.766.row_ok_ref.col_ok_ref, bf16[3,4096,256]{2,1,0:T(8,128)(2,1)} %bitcast.104, ...), custom_call_target="tpu_custom_call" | custom-call | tf_op jit(solution)/shard_map/pallas_call | solution.py:139
  198.9 5.2 %all-to-all-start.1 = ((f32[32,1,768]{2,1,0:T(1,128)}), f32[32,1,768]{2,1,0:T(1,128)S(1)}, u32[]{:S(2)}, u32[]{:S(2)}) async-start(f32[32,1,768]{2,1,0:T(1,128)} %reshape.768), calls=%async_computation.1 | async-start | bytes 196608 | tf_op jit(solution)/shard_map/all_to_all | solution.py:244
  204.3 1.7 slice.129
  206.0 6.3 %all-to-all-done.1 = f32[32,1,768]{2,1,0:T(1,128)S(1)} async-done(((f32[32,1,768]{2,1,0:T(1,128)}), f32[32,1,768]{2,1,0:T(1,128)S(1)}, u32[]{:S(2)}, u32[]{:S(2)}) %all-to-all-start.1) | async-done | bytes 98336 | tf_op jit(solution)/shard_map/all_to_all | solution.py:244
  214.8 12.7 %all-to-all-start.2 = ((f32[16,1,768]{2,1,0:T(1,128)}), f32[16,1,768]{2,1,0:T(1,128)S(1)}, u32[]{:S(2)}, u32[]{:S(2)}) async-start(f32[16,1,768]{2,1,0:T(1,128)} %reshape.770), calls=%async_computation.2 | async-start | bytes 98304 | tf_op jit(solution)/shard_map/all_to_all | solution.py:48
  227.9 13.3 %all-to-all-done.2 = f32[16,1,768]{2,1,0:T(1,128)S(1)} async-done(((f32[16,1,768]{2,1,0:T(1,128)}), f32[16,1,768]{2,1,0:T(1,128)S(1)}, u32[]{:S(2)}, u32[]{:S(2)}) %all-to-all-start.2) | async-done | bytes 49184 | tf_op jit(solution)/shard_map/all_to_all | solution.py:48
  (110 shorter events, 25.7 us)
Async XLA Ops:
  7.2 5.3 %copy-start = (bf16[8,64,256]{2,1,0:T(8,128)(2,1)S(1)}, bf16[8,64,256]{2,1,0:T(8,128)(2,1)}, u32[]{:S(2)}) copy-start(bf16[8,64,256]{2,1,0:T(8,128)(2,1)} %param.11) | copy-start | bytes 786436
  7.2 148.5 %all-gather.2.cloned.1.call-start = ((), (), s32[]{:S(2)}) async-start(), calls=%async_computation.3 | async-start | bytes 6488064 | tf_op jit(solution)/shard_map/all_gather | solution.py:202
  13.2 8.8 %collective-permute-start = (bf16[416,256]{1,0:T(8,128)(2,1)S(1)}, bf16[416,256]{1,0:T(8,128)(2,1)S(1)}, u32[]{:S(2)}, u32[]{:S(2)}) collective-permute-start(bf16[416,256]{1,0:T(8,128)(2,1)S(1)} %pad_maximum_fusion), channel_id=1, source_target_pairs={{0,32},{32,0},{64,96},{96,64},{128,160},{160,128},{192,224},{224,1... | collective-permute-start | bytes 638984 | tf_op jit(solution)/shard_map/ppermute | solution.py:23
  22.1 65.7 %copy-start.2 = (s32[2,2]{1,0:T(2,128)S(1)}, s32[2,2]{1,0:T(2,128)}, u32[]{:S(2)}) copy-start(s32[2,2]{1,0:T(2,128)} %param.15) | copy-start | bytes 52
  22.1 65.8 %copy-start.1 = (s32[128]{0:T(128)S(1)}, s32[128]{0:T(128)}, u32[]{:S(2)}) copy-start(s32[128]{0:T(128)} %param.14) | copy-start | bytes 1540
  22.1 8.1 %collective-permute-start.1 = (bf16[416,256]{1,0:T(8,128)(2,1)S(1)}, bf16[416,256]{1,0:T(8,128)(2,1)S(1)}, u32[]{:S(2)}, u32[]{:S(2)}) collective-permute-start(bf16[416,256]{1,0:T(8,128)(2,1)S(1)} %broadcast_select_fusion), channel_id=1, source_target_pairs={{0,64},{32,96},{64,0},{96,32},{128,192},{160,224},{192,128},{224,1... | collective-permute-start | bytes 638984 | tf_op jit(solution)/shard_map/ppermute | solution.py:23
  30.4 16.5 %collective-permute-start.3 = (bf16[416,256]{1,0:T(8,128)(2,1)S(1)}, bf16[416,256]{1,0:T(8,128)(2,1)S(1)}, u32[]{:S(2)}, u32[]{:S(2)}) collective-permute-start(bf16[416,256]{1,0:T(8,128)(2,1)S(1)} %broadcast_select_fusion.1), channel_id=1, source_target_pairs={{0,128},{32,160},{64,192},{96,224},{128,256},{160,288},{192,320},{... | collective-permute-start | bytes 638984 | tf_op jit(solution)/shard_map/ppermute | solution.py:38
  39.7 27.8 %collective-permute-start.2 = (bf16[416,256]{1,0:T(8,128)(2,1)S(1)}, bf16[416,256]{1,0:T(8,128)(2,1)S(1)}, u32[]{:S(2)}, u32[]{:S(2)}) collective-permute-start(bf16[416,256]{1,0:T(8,128)(2,1)S(1)} %broadcast_select_fusion.1), channel_id=1, source_target_pairs={{0,384},{32,416},{64,448},{96,480},{128,0},{160,32},{192,64},{224,... | collective-permute-start | bytes 638984 | tf_op jit(solution)/shard_map/ppermute | solution.py:39
  67.7 14.1 %collective-permute-start.4 = (bf16[208,256]{1,0:T(8,128)(2,1)S(1)}, bf16[208,256]{1,0:T(8,128)(2,1)S(1)}, u32[]{:S(2)}, u32[]{:S(2)}) collective-permute-start(bf16[208,256]{1,0:T(8,128)(2,1)S(1)} %get-tuple-element.51), channel_id=1, source_target_pairs={{0,128},{32,160},{64,192},{96,224},{128,256},{160,288},{192,320},{... | collective-permute-start | bytes 319496 | tf_op jit(solution)/shard_map/ppermute | solution.py:33
  74.5 12.3 %collective-permute-start.5 = (bf16[208,256]{1,0:T(8,128)(2,1)S(1)}, bf16[208,256]{1,0:T(8,128)(2,1)S(1)}, u32[]{:S(2)}, u32[]{:S(2)}) collective-permute-start(bf16[208,256]{1,0:T(8,128)(2,1)S(1)} %get-tuple-element.52), channel_id=1, source_target_pairs={{0,384},{32,416},{64,448},{96,480},{128,0},{160,32},{192,64},{224,... | collective-permute-start | bytes 319496 | tf_op jit(solution)/shard_map/ppermute | solution.py:34
  161.9 21.8 %all-to-all-start = ((bf16[32,2,4096]{2,1,0:T(2,128)(2,1)}), bf16[32,2,4096]{2,1,0:T(2,128)(2,1)S(1)}, u32[]{:S(2)}, u32[]{:S(2)}) async-start(bf16[32,2,4096]{2,1,0:T(2,128)(2,1)} %broadcast_in_dim.190), calls=%async_computation | async-start | bytes 1048576 | tf_op jit(solution)/shard_map/all_to_all | solution.py:48
  198.9 13.3 %all-to-all-start.1 = ((f32[32,1,768]{2,1,0:T(1,128)}), f32[32,1,768]{2,1,0:T(1,128)S(1)}, u32[]{:S(2)}, u32[]{:S(2)}) async-start(f32[32,1,768]{2,1,0:T(1,128)} %reshape.768), calls=%async_computation.1 | async-start | bytes 196608 | tf_op jit(solution)/shard_map/all_to_all | solution.py:244
  214.8 26.4 %all-to-all-start.2 = ((f32[16,1,768]{2,1,0:T(1,128)}), f32[16,1,768]{2,1,0:T(1,128)S(1)}, u32[]{:S(2)}, u32[]{:S(2)}) async-start(f32[16,1,768]{2,1,0:T(1,128)} %reshape.770), calls=%async_computation.2 | async-start | bytes 98304 | tf_op jit(solution)/shard_map/all_to_all | solution.py:48
Sparse Core Ops, SparseCore 0:
  87.9 67.7 all-gather.1

commit v16 on v14

--- a/solution.py
+++ b/solution.py
@@ -170,9 +170,12 @@
     slots = flat_kf % fr_dev
     later = keyframes * (total_steps - 1)
 
-    kf_keys = jnp.take(keys, slots, axis=0)
-    kf_values = jnp.take(label_values, slots[:keyframes], axis=0)
-    kf_queries = jnp.take(queries, slots[keyframes:], axis=0)
+    pick = lambda array, which: jnp.stack(
+        [lax.dynamic_index_in_dim(array, w, 0, keepdims=False) for w in which]
+    )
+    kf_keys = pick(keys, [slots[i] for i in range(total_steps * keyframes)])
+    kf_values = pick(label_values, [slots[i] for i in range(keyframes)])
+    kf_queries = pick(queries, [slots[i] for i in range(keyframes, total_steps * keyframes)])
     parts = [kf_keys, kf_queries, kf_values]
     part_owners = [owners, owners[keyframes:], owners[:keyframes]]
     flat = jnp.concatenate([p.reshape(-1, width) for p in parts], axis=0)

time: 251 us -> 258 us (1.028)
  between operations: 14.5 us -> 22.1 us
    gather x3 -> x0, local copies, waits for them, and re-layouts: 3.52 us -> none  [the longest x1 1.5 us: body(): kf_queries = jnp.take(queries, slots[keyframes:], axis=0)]
    unnamed x17 -> x15, local copies, waits for them, and re-layouts: 6.23 us -> 6.22 us
where the time goes in v16:
time: 258 us; the launch traced here: 257 us
  waiting for transfers between devices  122 us (47%)
  starting transfers between devices  57.9 us (22%)
  Pallas kernels  26.5 us (10%)
  between operations  22.1 us (9%)
  local copies, waits for them, and re-layouts  21.4 us (8%)
  other arithmetic  7.46 us (3%)
    all_gather x1, waiting for transfers between devices, body(): gathered = lax.all_gather(packed, 'space', axis=2, tiled=True)  64.4 us
    pallas_call x3, Pallas kernels, step_pass(): pl.pallas_call(kernel, grid=(blocks,), in_specs=in_specs, out_specs=out_s...  26.5 us
    ppermute x1, waiting for transfers between devices, broadcast_tm(): got_b = lax.ppermute(value, axis, behind)  20.6 us
    all_to_all x2, starting transfers between devices, gather_all(): return lax.all_to_all(spread, axis, 0, 0, tiled=True)  18.3 us
    all_to_all x2, waiting for transfers between devices, gather_all(): return lax.all_to_all(spread, axis, 0, 0, tiled=True)  15.8 us
    ppermute x2, starting transfers between devices, broadcast_tm(): got = lax.ppermute(value, axis, pairs)  10.3 us
    ppermute x1, starting transfers between devices, broadcast_tm(): got_a = lax.ppermute(value, axis, ahead)  9.36 us
    ppermute x1, starting transfers between devices, broadcast_tm(): got_a = lax.ppermute(value[:half], axis, ahead)  6.73 us
  transfers between devices with their start and end apart: 10, of which 9 were waited for; matrix products, arithmetic and copies ran while one was open for 5% of the time, Pallas kernels for 4%

profile of v16, /device:TPU:1, one launch (start us, length us, event | category | flops | bytes accessed | tf_op | source)
XLA Modules:
  0.0 257.1 jit_solution(5719867528481353044)
XLA Ops:
  8.7 1.3 gather_fusion.1
  20.2 4.0 %collective-permute-start = (bf16[416,256]{1,0:T(8,128)(2,1)S(1)}, bf16[416,256]{1,0:T(8,128)(2,1)S(1)}, u32[]{:S(2)}, u32[]{:S(2)}) collective-permute-start(bf16[416,256]{1,0:T(8,128)(2,1)S(1)} %pad_maximum_fusion), channel_id=1, source_target_pairs={{0,32},{32,0},{64,96},{96,64},{128,160},{160,128},{192,224},{224,1... | collective-permute-start | bytes 638984 | tf_op jit(solution)/shard_map/ppermute | solution.py:23
  27.8 6.2 %collective-permute-start.1 = (bf16[416,256]{1,0:T(8,128)(2,1)S(1)}, bf16[416,256]{1,0:T(8,128)(2,1)S(1)}, u32[]{:S(2)}, u32[]{:S(2)}) collective-permute-start(bf16[416,256]{1,0:T(8,128)(2,1)S(1)} %broadcast_select_fusion), channel_id=1, source_target_pairs={{0,64},{32,96},{64,0},{96,32},{128,192},{160,224},{192,128},{224,1... | collective-permute-start | bytes 638984 | tf_op jit(solution)/shard_map/ppermute | solution.py:23
  34.0 3.2 %collective-permute-done.1 = bf16[416,256]{1,0:T(8,128)(2,1)S(1)} collective-permute-done((bf16[416,256]{1,0:T(8,128)(2,1)S(1)}, bf16[416,256]{1,0:T(8,128)(2,1)S(1)}, u32[]{:S(2)}, u32[]{:S(2)}) %collective-permute-start.1) | collective-permute-done | bytes 213024 | tf_op jit(solution)/shard_map/ppermute | solution.py:23
  37.3 9.4 %collective-permute-start.3 = (bf16[416,256]{1,0:T(8,128)(2,1)S(1)}, bf16[416,256]{1,0:T(8,128)(2,1)S(1)}, u32[]{:S(2)}, u32[]{:S(2)}) collective-permute-start(bf16[416,256]{1,0:T(8,128)(2,1)S(1)} %broadcast_select_fusion.1), channel_id=1, source_target_pairs={{0,128},{32,160},{64,192},{96,224},{128,256},{160,288},{192,320},{... | collective-permute-start | bytes 638984 | tf_op jit(solution)/shard_map/ppermute | solution.py:38
  46.7 5.6 %collective-permute-start.2 = (bf16[416,256]{1,0:T(8,128)(2,1)S(1)}, bf16[416,256]{1,0:T(8,128)(2,1)S(1)}, u32[]{:S(2)}, u32[]{:S(2)}) collective-permute-start(bf16[416,256]{1,0:T(8,128)(2,1)S(1)} %broadcast_select_fusion.1), channel_id=1, source_target_pairs={{0,384},{32,416},{64,448},{96,480},{128,0},{160,32},{192,64},{224,... | collective-permute-start | bytes 638984 | tf_op jit(solution)/shard_map/ppermute | solution.py:39
  52.3 1.6 collective-permute-done.3
  53.9 20.6 %collective-permute-done.2 = bf16[416,256]{1,0:T(8,128)(2,1)S(1)} collective-permute-done((bf16[416,256]{1,0:T(8,128)(2,1)S(1)}, bf16[416,256]{1,0:T(8,128)(2,1)S(1)}, u32[]{:S(2)}, u32[]{:S(2)}) %collective-permute-start.2) | collective-permute-done | bytes 213024 | tf_op jit(solution)/shard_map/ppermute | solution.py:39
  74.7 6.7 %collective-permute-start.4 = (bf16[208,256]{1,0:T(8,128)(2,1)S(1)}, bf16[208,256]{1,0:T(8,128)(2,1)S(1)}, u32[]{:S(2)}, u32[]{:S(2)}) collective-permute-start(bf16[208,256]{1,0:T(8,128)(2,1)S(1)} %get-tuple-element.51), channel_id=1, source_target_pairs={{0,128},{32,160},{64,192},{96,224},{128,256},{160,288},{192,320},{... | collective-permute-start | bytes 319496 | tf_op jit(solution)/shard_map/ppermute | solution.py:33
  81.4 2.5 collective-permute-start.5
  83.9 4.8 %collective-permute-done.4 = bf16[208,256]{1,0:T(8,128)(2,1)S(1)} collective-permute-done((bf16[208,256]{1,0:T(8,128)(2,1)S(1)}, bf16[208,256]{1,0:T(8,128)(2,1)S(1)}, u32[]{:S(2)}, u32[]{:S(2)}) %collective-permute-start.4) | collective-permute-done | bytes 106528 | tf_op jit(solution)/shard_map/ppermute | solution.py:33
  88.8 4.9 %collective-permute-done.5 = bf16[208,256]{1,0:T(8,128)(2,1)S(1)} collective-permute-done((bf16[208,256]{1,0:T(8,128)(2,1)S(1)}, bf16[208,256]{1,0:T(8,128)(2,1)S(1)}, u32[]{:S(2)}, u32[]{:S(2)}) %collective-permute-start.5) | collective-permute-done | bytes 106528 | tf_op jit(solution)/shard_map/ppermute | solution.py:34
  98.3 64.4 %all-gather.2.cloned.1.call-done = bf16[3,2,2048,256]{3,2,1,0:T(8,128)(2,1)} async-done(((bf16[3,2,64,256]{3,2,1,0:T(8,128)(2,1)}), bf16[3,2,2048,256]{3,2,1,0:T(8,128)(2,1)}) %all-gather.2.cloned.1.call-update) | async-done | bytes 6291472 | tf_op jit(solution)/shard_map/all_gather | solution.py:205
  162.7 4.1 %shard_map.77 = bf16[128,64]{1,0:T(8,128)(2,1)} custom-call(bf16[128,256]{1,0:T(8,128)(2,1)} %slice.128.q_ref, s32[128,1]{1,0:T(8,128)} %reshape.665.row_ok_ref.col_ok_ref, s32[128,1]{1,0:T(8,128)} %reshape.665.row_ok_ref.col_ok_ref, bf16[3,4096,256]{2,1,0:T(8,128)(2,1)} %bitcast.100, s32[1,4096]{1,0:T(1,128)} %bitcast.118, bf16[3,4096,256]{2,1,0:T(8,128)(2,1)} %bitcast.101), custom_call_target="tpu_custom_call" | custom-call | tf_op jit(solution)/shard_map/pallas_call | solution.py:139
  167.8 1.6 reshape.666
  169.3 5.6 %all-to-all-start = ((bf16[32,2,4096]{2,1,0:T(2,128)(2,1)}), bf16[32,2,4096]{2,1,0:T(2,128)(2,1)S(1)}, u32[]{:S(2)}, u32[]{:S(2)}) async-start(bf16[32,2,4096]{2,1,0:T(2,128)(2,1)} %reshape.666), calls=%async_computation | async-start | bytes 1048576 | tf_op jit(solution)/shard_map/all_to_all | solution.py:48
  176.7 11.0 %shard_map.79 = (bf16[512,64]{1,0:T(8,128)(2,1)}, f32[1,4096]{1,0:T(1,128)}, f32[1,4096]{1,0:T(1,128)}, f32[1,4096]{1,0:T(1,128)}) custom-call(bf16[512,256]{1,0:T(8,128)(2,1)} %bitcast.109, s32[512,1]{1,0:T(8,128)} %reshape.664.row_ok_ref.col_ok_ref, s32[512,1]{1,0:T(8,128)} %reshape.664.row_ok_ref.col_ok_ref, bf16[3,4096,256]{2,1,0:T(8,128)(2,1)} %bitcast.102, ...), custom_call_target="tpu_custom_call" | custom-call | tf_op jit(solution)/shard_map/pallas_call | solution.py:139
  188.7 2.5 all-to-all-done
  192.9 11.5 %shard_map.78 = (bf16[512,64]{1,0:T(8,128)(2,1)}, f32[1,4096]{1,0:T(1,128)}, f32[1,4096]{1,0:T(1,128)}, f32[1,4096]{1,0:T(1,128)}) custom-call(bf16[512,256]{1,0:T(8,128)(2,1)} %bitcast.110, s32[512,1]{1,0:T(8,128)} %reshape.664.row_ok_ref.col_ok_ref, s32[512,1]{1,0:T(8,128)} %reshape.664.row_ok_ref.col_ok_ref, bf16[3,4096,256]{2,1,0:T(8,128)(2,1)} %bitcast.104, ...), custom_call_target="tpu_custom_call" | custom-call | tf_op jit(solution)/shard_map/pallas_call | solution.py:139
  206.4 5.2 %all-to-all-start.1 = ((f32[32,1,768]{2,1,0:T(1,128)}), f32[32,1,768]{2,1,0:T(1,128)S(1)}, u32[]{:S(2)}, u32[]{:S(2)}) async-start(f32[32,1,768]{2,1,0:T(1,128)} %reshape.668), calls=%async_computation.1 | async-start | bytes 196608 | tf_op jit(solution)/shard_map/all_to_all | solution.py:247
  211.7 1.7 slice.135
  213.4 6.3 %all-to-all-done.1 = f32[32,1,768]{2,1,0:T(1,128)S(1)} async-done(((f32[32,1,768]{2,1,0:T(1,128)}), f32[32,1,768]{2,1,0:T(1,128)S(1)}, u32[]{:S(2)}, u32[]{:S(2)}) %all-to-all-start.1) | async-done | bytes 98336 | tf_op jit(solution)/shard_map/all_to_all | solution.py:247
  222.2 12.7 %all-to-all-start.2 = ((f32[16,1,768]{2,1,0:T(1,128)}), f32[16,1,768]{2,1,0:T(1,128)S(1)}, u32[]{:S(2)}, u32[]{:S(2)}) async-start(f32[16,1,768]{2,1,0:T(1,128)} %reshape.670), calls=%async_computation.2 | async-start | bytes 98304 | tf_op jit(solution)/shard_map/all_to_all | solution.py:48
  235.3 13.3 %all-to-all-done.2 = f32[16,1,768]{2,1,0:T(1,128)S(1)} async-done(((f32[16,1,768]{2,1,0:T(1,128)}), f32[16,1,768]{2,1,0:T(1,128)S(1)}, u32[]{:S(2)}, u32[]{:S(2)}) %all-to-all-start.2) | async-done | bytes 49184 | tf_op jit(solution)/shard_map/all_to_all | solution.py:48
  (101 shorter events, 24.3 us)
Async XLA Ops:
  7.2 155.5 %all-gather.2.cloned.1.call-start = ((), (), s32[]{:S(2)}) async-start(), calls=%async_computation.3 | async-start | bytes 6488064 | tf_op jit(solution)/shard_map/all_gather | solution.py:205
  20.2 7.4 %collective-permute-start = (bf16[416,256]{1,0:T(8,128)(2,1)S(1)}, bf16[416,256]{1,0:T(8,128)(2,1)S(1)}, u32[]{:S(2)}, u32[]{:S(2)}) collective-permute-start(bf16[416,256]{1,0:T(8,128)(2,1)S(1)} %pad_maximum_fusion), channel_id=1, source_target_pairs={{0,32},{32,0},{64,96},{96,64},{128,160},{160,128},{192,224},{224,1... | collective-permute-start | bytes 638984 | tf_op jit(solution)/shard_map/ppermute | solution.py:23
  27.7 67.1 %copy-start.1 = (s32[2,2]{1,0:T(2,128)S(1)}, s32[2,2]{1,0:T(2,128)}, u32[]{:S(2)}) copy-start(s32[2,2]{1,0:T(2,128)} %param.15) | copy-start | bytes 52
  27.7 67.1 %copy-start = (s32[128]{0:T(128)S(1)}, s32[128]{0:T(128)}, u32[]{:S(2)}) copy-start(s32[128]{0:T(128)} %param.14) | copy-start | bytes 1540
  27.8 9.5 %collective-permute-start.1 = (bf16[416,256]{1,0:T(8,128)(2,1)S(1)}, bf16[416,256]{1,0:T(8,128)(2,1)S(1)}, u32[]{:S(2)}, u32[]{:S(2)}) collective-permute-start(bf16[416,256]{1,0:T(8,128)(2,1)S(1)} %broadcast_select_fusion), channel_id=1, source_target_pairs={{0,64},{32,96},{64,0},{96,32},{128,192},{160,224},{192,128},{224,1... | collective-permute-start | bytes 638984 | tf_op jit(solution)/shard_map/ppermute | solution.py:23
  37.3 16.5 %collective-permute-start.3 = (bf16[416,256]{1,0:T(8,128)(2,1)S(1)}, bf16[416,256]{1,0:T(8,128)(2,1)S(1)}, u32[]{:S(2)}, u32[]{:S(2)}) collective-permute-start(bf16[416,256]{1,0:T(8,128)(2,1)S(1)} %broadcast_select_fusion.1), channel_id=1, source_target_pairs={{0,128},{32,160},{64,192},{96,224},{128,256},{160,288},{192,320},{... | collective-permute-start | bytes 638984 | tf_op jit(solution)/shard_map/ppermute | solution.py:38
  46.7 27.8 %collective-permute-start.2 = (bf16[416,256]{1,0:T(8,128)(2,1)S(1)}, bf16[416,256]{1,0:T(8,128)(2,1)S(1)}, u32[]{:S(2)}, u32[]{:S(2)}) collective-permute-start(bf16[416,256]{1,0:T(8,128)(2,1)S(1)} %broadcast_select_fusion.1), channel_id=1, source_target_pairs={{0,384},{32,416},{64,448},{96,480},{128,0},{160,32},{192,64},{224,... | collective-permute-start | bytes 638984 | tf_op jit(solution)/shard_map/ppermute | solution.py:39
  74.7 14.1 %collective-permute-start.4 = (bf16[208,256]{1,0:T(8,128)(2,1)S(1)}, bf16[208,256]{1,0:T(8,128)(2,1)S(1)}, u32[]{:S(2)}, u32[]{:S(2)}) collective-permute-start(bf16[208,256]{1,0:T(8,128)(2,1)S(1)} %get-tuple-element.51), channel_id=1, source_target_pairs={{0,128},{32,160},{64,192},{96,224},{128,256},{160,288},{192,320},{... | collective-permute-start | bytes 319496 | tf_op jit(solution)/shard_map/ppermute | solution.py:33
  81.4 12.3 %collective-permute-start.5 = (bf16[208,256]{1,0:T(8,128)(2,1)S(1)}, bf16[208,256]{1,0:T(8,128)(2,1)S(1)}, u32[]{:S(2)}, u32[]{:S(2)}) collective-permute-start(bf16[208,256]{1,0:T(8,128)(2,1)S(1)} %get-tuple-element.52), channel_id=1, source_target_pairs={{0,384},{32,416},{64,448},{96,480},{128,0},{160,32},{192,64},{224,... | collective-permute-start | bytes 319496 | tf_op jit(solution)/shard_map/ppermute | solution.py:34
  169.3 21.8 %all-to-all-start = ((bf16[32,2,4096]{2,1,0:T(2,128)(2,1)}), bf16[32,2,4096]{2,1,0:T(2,128)(2,1)S(1)}, u32[]{:S(2)}, u32[]{:S(2)}) async-start(bf16[32,2,4096]{2,1,0:T(2,128)(2,1)} %reshape.666), calls=%async_computation | async-start | bytes 1048576 | tf_op jit(solution)/shard_map/all_to_all | solution.py:48
  206.4 13.3 %all-to-all-start.1 = ((f32[32,1,768]{2,1,0:T(1,128)}), f32[32,1,768]{2,1,0:T(1,128)S(1)}, u32[]{:S(2)}, u32[]{:S(2)}) async-start(f32[32,1,768]{2,1,0:T(1,128)} %reshape.668), calls=%async_computation.1 | async-start | bytes 196608 | tf_op jit(solution)/shard_map/all_to_all | solution.py:247
  222.2 26.4 %all-to-all-start.2 = ((f32[16,1,768]{2,1,0:T(1,128)}), f32[16,1,768]{2,1,0:T(1,128)S(1)}, u32[]{:S(2)}, u32[]{:S(2)}) async-start(f32[16,1,768]{2,1,0:T(1,128)} %reshape.670), calls=%async_computation.2 | async-start | bytes 98304 | tf_op jit(solution)/shard_map/all_to_all | solution.py:48
Sparse Core Ops, SparseCore 0:
  94.9 67.7 all-gather.1

commit v17 on v14

--- a/solution.py
+++ b/solution.py
@@ -59,7 +59,7 @@
 BLOCK_ROWS = 512
 
 
-def step_kernel(q_ref, row_ok_ref, col_ok_ref, keys_ref, key_ok_ref, aux_ref, *refs,
+def step_kernel(q_ref, row_ok_ref, keys_ref, key_ok_ref, aux_ref, *refs,
                 scale, step, with_stats, channels, values_from_aux):
     if values_from_aux:
         values = aux_ref[:, :channels]
@@ -96,7 +96,7 @@
         onehot_ref[...] = jnp.transpose(onehot).astype(jnp.bfloat16)
 
     picked = jnp.dot(out, onehot_ref[...], preferred_element_type=jnp.float32)
-    col_ok = col_ok_ref[...] != 0
+    col_ok = row_ok
     old_max = cmax_ref[...]
     col_scores = jnp.where(col_ok, scores, LOWEST)
     local = jnp.max(col_scores, axis=0, keepdims=True)
@@ -108,7 +108,7 @@
     cmax_ref[...] = new_max
 
 
-def step_pass(q, row_ok, col_ok, gathered, step, key_ok, mem_values, channels, scale, with_stats):
+def step_pass(q, row_ok, gathered, step, key_ok, mem_values, channels, scale, with_stats):
     rows, width = q.shape
     parts, mem, _ = gathered.shape
     block = min(BLOCK_ROWS, rows)
@@ -123,12 +123,12 @@
         out_specs += [whole((1, mem))] * 3
         out_shape += [stat] * 3
     in_specs = [
-        by_row(width), by_row(1), by_row(1),
+        by_row(width), by_row(1),
         pl.BlockSpec((None, mem, width), lambda i: (step, 0, 0)),
         whole((1, mem)),
         pl.BlockSpec((None, mem, 128), lambda i: (parts - 1, 0, 0)),
     ]
-    args = [q, row_ok, col_ok, gathered, key_ok, gathered]
+    args = [q, row_ok, gathered, key_ok, gathered]
     if mem_values is not None:
         in_specs.append(whole((mem, channels)))
         args.append(mem_values)
@@ -224,7 +224,7 @@
             extra_ok = extra_valid[step * keyframes:(step + 1) * keyframes].reshape(-1, 1)
             extra_ok = extra_ok.astype(jnp.int32)
             (part,) = step_pass(
-                extra, extra_ok, extra_ok, gathered, step, key_ok, mem_values, channels, scale,
+                extra, extra_ok, gathered, step, key_ok, mem_values, channels, scale,
                 False,
             )
             part = part.reshape(keyframes, pix_dev, channels)
@@ -233,7 +233,7 @@
             )
         ok = row_valid.astype(jnp.int32)[:, None]
         readout, col_max, col_total, col_num = step_pass(
-            query_rows, ok, ok, gathered, step, key_ok, mem_values, channels, scale, True
+            query_rows, ok, gathered, step, key_ok, mem_values, channels, scale, True
         )
         stats.append(jnp.stack([col_max[0], col_total[0], col_num[0]]))
         if step + 1 < total_steps:

time: 251 us -> 251 us (level)
  no operation moved by 1% of the time
where the time goes in v17:
time: 251 us; the launch traced here: 250 us
  waiting for transfers between devices  122 us (49%)
  starting transfers between devices  56.4 us (22%)
  Pallas kernels  26.1 us (10%)
  local copies, waits for them, and re-layouts  23 us (9%)
  between operations  14.5 us (6%)
  other arithmetic  7.79 us (3%)
    all_gather x1, waiting for transfers between devices, body(): gathered = lax.all_gather(packed, 'space', axis=2, tiled=True)  64.4 us
    pallas_call x3, Pallas kernels, step_pass(): pl.pallas_call(kernel, grid=(blocks,), in_specs=in_specs, out_specs=out_s...  26.1 us
    ppermute x1, waiting for transfers between devices, broadcast_tm(): got_b = lax.ppermute(value, axis, behind)  20.6 us
    all_to_all x2, starting transfers between devices, gather_all(): return lax.all_to_all(spread, axis, 0, 0, tiled=True)  18.3 us
    all_to_all x2, waiting for transfers between devices, gather_all(): return lax.all_to_all(spread, axis, 0, 0, tiled=True)  16.1 us
    ppermute x1, starting transfers between devices, broadcast_tm(): got_a = lax.ppermute(value, axis, ahead)  9.36 us
    ppermute x2, starting transfers between devices, broadcast_tm(): got = lax.ppermute(value, axis, pairs)  8.93 us
    ppermute x1, starting transfers between devices, broadcast_tm(): got_a = lax.ppermute(value[:half], axis, ahead)  6.73 us
  transfers between devices with their start and end apart: 10, of which 9 were waited for; matrix products, arithmetic and copies ran while one was open for 5% of the time, Pallas kernels for 4%

profile of v17, /device:TPU:1, one launch (start us, length us, event | category | flops | bytes accessed | tf_op | source)
XLA Modules:
  0.0 249.7 jit_solution(16729658401492046959)
XLA Ops:
  10.9 1.5 gather_fusion.1
  13.2 4.0 %collective-permute-start = (bf16[416,256]{1,0:T(8,128)(2,1)S(1)}, bf16[416,256]{1,0:T(8,128)(2,1)S(1)}, u32[]{:S(2)}, u32[]{:S(2)}) collective-permute-start(bf16[416,256]{1,0:T(8,128)(2,1)S(1)} %pad_maximum_fusion), channel_id=1, source_target_pairs={{0,32},{32,0},{64,96},{96,64},{128,160},{160,128},{192,224},{224,1... | collective-permute-start | bytes 638984 | tf_op jit(solution)/shard_map/ppermute | solution.py:23
  22.1 4.9 %collective-permute-start.1 = (bf16[416,256]{1,0:T(8,128)(2,1)S(1)}, bf16[416,256]{1,0:T(8,128)(2,1)S(1)}, u32[]{:S(2)}, u32[]{:S(2)}) collective-permute-start(bf16[416,256]{1,0:T(8,128)(2,1)S(1)} %broadcast_select_fusion), channel_id=1, source_target_pairs={{0,64},{32,96},{64,0},{96,32},{128,192},{160,224},{192,128},{224,1... | collective-permute-start | bytes 638984 | tf_op jit(solution)/shard_map/ppermute | solution.py:23
  27.0 3.2 %collective-permute-done.1 = bf16[416,256]{1,0:T(8,128)(2,1)S(1)} collective-permute-done((bf16[416,256]{1,0:T(8,128)(2,1)S(1)}, bf16[416,256]{1,0:T(8,128)(2,1)S(1)}, u32[]{:S(2)}, u32[]{:S(2)}) %collective-permute-start.1) | collective-permute-done | bytes 213024 | tf_op jit(solution)/shard_map/ppermute | solution.py:23
  30.4 9.4 %collective-permute-start.3 = (bf16[416,256]{1,0:T(8,128)(2,1)S(1)}, bf16[416,256]{1,0:T(8,128)(2,1)S(1)}, u32[]{:S(2)}, u32[]{:S(2)}) collective-permute-start(bf16[416,256]{1,0:T(8,128)(2,1)S(1)} %broadcast_select_fusion.1), channel_id=1, source_target_pairs={{0,128},{32,160},{64,192},{96,224},{128,256},{160,288},{192,320},{... | collective-permute-start | bytes 638984 | tf_op jit(solution)/shard_map/ppermute | solution.py:38
  39.7 5.6 %collective-permute-start.2 = (bf16[416,256]{1,0:T(8,128)(2,1)S(1)}, bf16[416,256]{1,0:T(8,128)(2,1)S(1)}, u32[]{:S(2)}, u32[]{:S(2)}) collective-permute-start(bf16[416,256]{1,0:T(8,128)(2,1)S(1)} %broadcast_select_fusion.1), channel_id=1, source_target_pairs={{0,384},{32,416},{64,448},{96,480},{128,0},{160,32},{192,64},{224,... | collective-permute-start | bytes 638984 | tf_op jit(solution)/shard_map/ppermute | solution.py:39
  45.3 1.6 collective-permute-done.3
  46.9 20.6 %collective-permute-done.2 = bf16[416,256]{1,0:T(8,128)(2,1)S(1)} collective-permute-done((bf16[416,256]{1,0:T(8,128)(2,1)S(1)}, bf16[416,256]{1,0:T(8,128)(2,1)S(1)}, u32[]{:S(2)}, u32[]{:S(2)}) %collective-permute-start.2) | collective-permute-done | bytes 213024 | tf_op jit(solution)/shard_map/ppermute | solution.py:39
  67.7 6.7 %collective-permute-start.4 = (bf16[208,256]{1,0:T(8,128)(2,1)S(1)}, bf16[208,256]{1,0:T(8,128)(2,1)S(1)}, u32[]{:S(2)}, u32[]{:S(2)}) collective-permute-start(bf16[208,256]{1,0:T(8,128)(2,1)S(1)} %get-tuple-element.51), channel_id=1, source_target_pairs={{0,128},{32,160},{64,192},{96,224},{128,256},{160,288},{192,320},{... | collective-permute-start | bytes 319496 | tf_op jit(solution)/shard_map/ppermute | solution.py:33
  74.5 2.5 collective-permute-start.5
  76.9 4.8 %collective-permute-done.4 = bf16[208,256]{1,0:T(8,128)(2,1)S(1)} collective-permute-done((bf16[208,256]{1,0:T(8,128)(2,1)S(1)}, bf16[208,256]{1,0:T(8,128)(2,1)S(1)}, u32[]{:S(2)}, u32[]{:S(2)}) %collective-permute-start.4) | collective-permute-done | bytes 106528 | tf_op jit(solution)/shard_map/ppermute | solution.py:33
  81.8 4.9 %collective-permute-done.5 = bf16[208,256]{1,0:T(8,128)(2,1)S(1)} collective-permute-done((bf16[208,256]{1,0:T(8,128)(2,1)S(1)}, bf16[208,256]{1,0:T(8,128)(2,1)S(1)}, u32[]{:S(2)}, u32[]{:S(2)}) %collective-permute-start.5) | collective-permute-done | bytes 106528 | tf_op jit(solution)/shard_map/ppermute | solution.py:34
  91.3 64.4 %all-gather.2.cloned.1.call-done = bf16[3,2,2048,256]{3,2,1,0:T(8,128)(2,1)} async-done(((bf16[3,2,64,256]{3,2,1,0:T(8,128)(2,1)}), bf16[3,2,2048,256]{3,2,1,0:T(8,128)(2,1)}) %all-gather.2.cloned.1.call-update) | async-done | bytes 6291472 | tf_op jit(solution)/shard_map/all_gather | solution.py:202
  155.7 4.1 %shard_map.77 = bf16[128,64]{1,0:T(8,128)(2,1)} custom-call(bf16[128,256]{1,0:T(8,128)(2,1)} %slice.122.q_ref, s32[128,1]{1,0:T(8,128)} %reshape.763.row_ok_ref, bf16[3,4096,256]{2,1,0:T(8,128)(2,1)} %bitcast.100, s32[1,4096]{1,0:T(1,128)} %bitcast.114, bf16[3,4096,256]{2,1,0:T(8,128)(2,1)} %bitcast.101), custom_call_target="tpu_custom_call" | custom-call | tf_op jit(solution)/shard_map/pallas_call | solution.py:139
  160.8 1.6 reshape.764
  162.4 5.6 %all-to-all-start = ((bf16[32,2,4096]{2,1,0:T(2,128)(2,1)}), bf16[32,2,4096]{2,1,0:T(2,128)(2,1)S(1)}, u32[]{:S(2)}, u32[]{:S(2)}) async-start(bf16[32,2,4096]{2,1,0:T(2,128)(2,1)} %reshape.764), calls=%async_computation | async-start | bytes 1048576 | tf_op jit(solution)/shard_map/all_to_all | solution.py:48
  169.7 10.7 %shard_map.79 = (bf16[512,64]{1,0:T(8,128)(2,1)}, f32[1,4096]{1,0:T(1,128)}, f32[1,4096]{1,0:T(1,128)}, f32[1,4096]{1,0:T(1,128)}) custom-call(bf16[512,256]{1,0:T(8,128)(2,1)} %bitcast.109, s32[512,1]{1,0:T(8,128)} %reshape.762.row_ok_ref, bf16[3,4096,256]{2,1,0:T(8,128)(2,1)} %bitcast.102, s32[1,4096]{1,0:T(1,128)} %bitcast.115, ...), custom_call_target="tpu_custom_call" | custom-call | tf_op jit(solution)/shard_map/pallas_call | solution.py:139
  181.5 2.7 %all-to-all-done = bf16[32,2,4096]{2,1,0:T(2,128)(2,1)S(1)} async-done(((bf16[32,2,4096]{2,1,0:T(2,128)(2,1)}), bf16[32,2,4096]{2,1,0:T(2,128)(2,1)S(1)}, u32[]{:S(2)}, u32[]{:S(2)}) %all-to-all-start) | async-done | bytes 524320 | tf_op jit(solution)/shard_map/all_to_all | solution.py:48
  186.0 11.3 %shard_map.78 = (bf16[512,64]{1,0:T(8,128)(2,1)}, f32[1,4096]{1,0:T(1,128)}, f32[1,4096]{1,0:T(1,128)}, f32[1,4096]{1,0:T(1,128)}) custom-call(bf16[512,256]{1,0:T(8,128)(2,1)} %bitcast.110, s32[512,1]{1,0:T(8,128)} %reshape.762.row_ok_ref, bf16[3,4096,256]{2,1,0:T(8,128)(2,1)} %bitcast.104, s32[1,4096]{1,0:T(1,128)} %bitcast.117, ...), custom_call_target="tpu_custom_call" | custom-call | tf_op jit(solution)/shard_map/pallas_call | solution.py:139
  199.2 5.0 %all-to-all-start.1 = ((f32[32,1,768]{2,1,0:T(1,128)}), f32[32,1,768]{2,1,0:T(1,128)S(1)}, u32[]{:S(2)}, u32[]{:S(2)}) async-start(f32[32,1,768]{2,1,0:T(1,128)} %reshape.766), calls=%async_computation.1 | async-start | bytes 196608 | tf_op jit(solution)/shard_map/all_to_all | solution.py:244
  204.3 1.7 slice.129
  206.0 6.3 %all-to-all-done.1 = f32[32,1,768]{2,1,0:T(1,128)S(1)} async-done(((f32[32,1,768]{2,1,0:T(1,128)}), f32[32,1,768]{2,1,0:T(1,128)S(1)}, u32[]{:S(2)}, u32[]{:S(2)}) %all-to-all-start.1) | async-done | bytes 98336 | tf_op jit(solution)/shard_map/all_to_all | solution.py:244
  214.8 12.7 %all-to-all-start.2 = ((f32[16,1,768]{2,1,0:T(1,128)}), f32[16,1,768]{2,1,0:T(1,128)S(1)}, u32[]{:S(2)}, u32[]{:S(2)}) async-start(f32[16,1,768]{2,1,0:T(1,128)} %reshape.768), calls=%async_computation.2 | async-start | bytes 98304 | tf_op jit(solution)/shard_map/all_to_all | solution.py:48
  227.9 13.3 %all-to-all-done.2 = f32[16,1,768]{2,1,0:T(1,128)S(1)} async-done(((f32[16,1,768]{2,1,0:T(1,128)}), f32[16,1,768]{2,1,0:T(1,128)S(1)}, u32[]{:S(2)}, u32[]{:S(2)}) %all-to-all-start.2) | async-done | bytes 49184 | tf_op jit(solution)/shard_map/all_to_all | solution.py:48
  (110 shorter events, 26.1 us)
Async XLA Ops:
  7.2 5.3 %copy-start = (bf16[8,64,256]{2,1,0:T(8,128)(2,1)S(1)}, bf16[8,64,256]{2,1,0:T(8,128)(2,1)}, u32[]{:S(2)}) copy-start(bf16[8,64,256]{2,1,0:T(8,128)(2,1)} %param.11) | copy-start | bytes 786436
  7.2 148.5 %all-gather.2.cloned.1.call-start = ((), (), s32[]{:S(2)}) async-start(), calls=%async_computation.3 | async-start | bytes 6488064 | tf_op jit(solution)/shard_map/all_gather | solution.py:202
  13.2 8.8 %collective-permute-start = (bf16[416,256]{1,0:T(8,128)(2,1)S(1)}, bf16[416,256]{1,0:T(8,128)(2,1)S(1)}, u32[]{:S(2)}, u32[]{:S(2)}) collective-permute-start(bf16[416,256]{1,0:T(8,128)(2,1)S(1)} %pad_maximum_fusion), channel_id=1, source_target_pairs={{0,32},{32,0},{64,96},{96,64},{128,160},{160,128},{192,224},{224,1... | collective-permute-start | bytes 638984 | tf_op jit(solution)/shard_map/ppermute | solution.py:23
  22.1 65.7 %copy-start.2 = (s32[2,2]{1,0:T(2,128)S(1)}, s32[2,2]{1,0:T(2,128)}, u32[]{:S(2)}) copy-start(s32[2,2]{1,0:T(2,128)} %param.15) | copy-start | bytes 52
  22.1 65.8 %copy-start.1 = (s32[128]{0:T(128)S(1)}, s32[128]{0:T(128)}, u32[]{:S(2)}) copy-start(s32[128]{0:T(128)} %param.14) | copy-start | bytes 1540
  22.1 8.1 %collective-permute-start.1 = (bf16[416,256]{1,0:T(8,128)(2,1)S(1)}, bf16[416,256]{1,0:T(8,128)(2,1)S(1)}, u32[]{:S(2)}, u32[]{:S(2)}) collective-permute-start(bf16[416,256]{1,0:T(8,128)(2,1)S(1)} %broadcast_select_fusion), channel_id=1, source_target_pairs={{0,64},{32,96},{64,0},{96,32},{128,192},{160,224},{192,128},{224,1... | collective-permute-start | bytes 638984 | tf_op jit(solution)/shard_map/ppermute | solution.py:23
  30.4 16.5 %collective-permute-start.3 = (bf16[416,256]{1,0:T(8,128)(2,1)S(1)}, bf16[416,256]{1,0:T(8,128)(2,1)S(1)}, u32[]{:S(2)}, u32[]{:S(2)}) collective-permute-start(bf16[416,256]{1,0:T(8,128)(2,1)S(1)} %broadcast_select_fusion.1), channel_id=1, source_target_pairs={{0,128},{32,160},{64,192},{96,224},{128,256},{160,288},{192,320},{... | collective-permute-start | bytes 638984 | tf_op jit(solution)/shard_map/ppermute | solution.py:38
  39.7 27.8 %collective-permute-start.2 = (bf16[416,256]{1,0:T(8,128)(2,1)S(1)}, bf16[416,256]{1,0:T(8,128)(2,1)S(1)}, u32[]{:S(2)}, u32[]{:S(2)}) collective-permute-start(bf16[416,256]{1,0:T(8,128)(2,1)S(1)} %broadcast_select_fusion.1), channel_id=1, source_target_pairs={{0,384},{32,416},{64,448},{96,480},{128,0},{160,32},{192,64},{224,... | collective-permute-start | bytes 638984 | tf_op jit(solution)/shard_map/ppermute | solution.py:39
  67.7 14.1 %collective-permute-start.4 = (bf16[208,256]{1,0:T(8,128)(2,1)S(1)}, bf16[208,256]{1,0:T(8,128)(2,1)S(1)}, u32[]{:S(2)}, u32[]{:S(2)}) collective-permute-start(bf16[208,256]{1,0:T(8,128)(2,1)S(1)} %get-tuple-element.51), channel_id=1, source_target_pairs={{0,128},{32,160},{64,192},{96,224},{128,256},{160,288},{192,320},{... | collective-permute-start | bytes 319496 | tf_op jit(solution)/shard_map/ppermute | solution.py:33
  74.5 12.3 %collective-permute-start.5 = (bf16[208,256]{1,0:T(8,128)(2,1)S(1)}, bf16[208,256]{1,0:T(8,128)(2,1)S(1)}, u32[]{:S(2)}, u32[]{:S(2)}) collective-permute-start(bf16[208,256]{1,0:T(8,128)(2,1)S(1)} %get-tuple-element.52), channel_id=1, source_target_pairs={{0,384},{32,416},{64,448},{96,480},{128,0},{160,32},{192,64},{224,... | collective-permute-start | bytes 319496 | tf_op jit(solution)/shard_map/ppermute | solution.py:34
  162.4 21.8 %all-to-all-start = ((bf16[32,2,4096]{2,1,0:T(2,128)(2,1)}), bf16[32,2,4096]{2,1,0:T(2,128)(2,1)S(1)}, u32[]{:S(2)}, u32[]{:S(2)}) async-start(bf16[32,2,4096]{2,1,0:T(2,128)(2,1)} %reshape.764), calls=%async_computation | async-start | bytes 1048576 | tf_op jit(solution)/shard_map/all_to_all | solution.py:48
  199.2 13.1 %all-to-all-start.1 = ((f32[32,1,768]{2,1,0:T(1,128)}), f32[32,1,768]{2,1,0:T(1,128)S(1)}, u32[]{:S(2)}, u32[]{:S(2)}) async-start(f32[32,1,768]{2,1,0:T(1,128)} %reshape.766), calls=%async_computation.1 | async-start | bytes 196608 | tf_op jit(solution)/shard_map/all_to_all | solution.py:244
  214.8 26.4 %all-to-all-start.2 = ((f32[16,1,768]{2,1,0:T(1,128)}), f32[16,1,768]{2,1,0:T(1,128)S(1)}, u32[]{:S(2)}, u32[]{:S(2)}) async-start(f32[16,1,768]{2,1,0:T(1,128)} %reshape.768), calls=%async_computation.2 | async-start | bytes 98304 | tf_op jit(solution)/shard_map/all_to_all | solution.py:48
Sparse Core Ops, SparseCore 0:
  87.9 67.7 all-gather.1
